TPU v7x, 32 devices: a whole 2x2x4 slice. The times are simulated.
32 devices in a mesh: groups: 2 (over y), feat: 4 (over z), tower: 4 (over x, core).
Axes of the slice: x: 2, y: 2, z: 4, core: 2. Of those that a mesh axis runs over, the one named last changes fastest.
Arguments:
- pooled_first: bfloat16 [4, 16, 3072, 128], P('tower', 'feat', 'groups'), parts along dimension 2, may hold values from -6 to 6
- pooled_second: bfloat16 [4, 16, 3072, 128], P('tower', 'feat', 'groups'), parts along dimension 2, may hold values from -6 to 6
- feature_order: int32 [4, 32], P('tower'), may hold values from 0 to 31, each once within a row
- cross_down: bfloat16 [4, 4096, 256], P('tower', 'feat'), may hold values from -0.09375 to 0.09375
- cross_up: bfloat16 [4, 4096, 256], P('tower', 'feat'), may hold values from -0.375 to 0.375
- cross_bias: float32 [4, 4096], P('tower'), may hold values from -3 to 3
- compress_weight: bfloat16 [4, 4096, 512], P('tower', 'feat'), may hold values from -0.09375 to 0.09375
- compress_bias: float32 [4, 512], P('tower'), may hold values from -3 to 3
- dense_vector: bfloat16 [3072, 128], P(('groups', 'feat', 'tower')), parts along dimension 0, may hold values from -6 to 6
- mlp_weight: bfloat16 [248, 1024], P('tower'), may hold values from -0.375 to 0.375
- mlp_bias: float32 [1024], replicated, may hold values from -3 to 3
Outputs:
- top_hidden: bfloat16 [3072, 1024], P(('groups', 'feat', 'tower')), parts along dimension 0
There are 2 independent parts, one for each index of `groups`. A program takes and returns all parts, laid end to end along the dimension named above; an argument that names none is the same for every part. Nothing has to cross between parts.
Inputs may be any that keep to these rules, and one draw needn't show every extreme that they name: Each row of feature_order names every number from 0 to 31 once.
All inputs are finite; a program needn't handle non-finite values.
Results may differ from a plain program's by a relative error of at most 0.0072.
Values may be sent and summed in bfloat16 or wider, within the bound.
No kernel may reach another device: no remote copies, remote signals or barrier semaphores. Data moves between devices by JAX's collectives and lax.ppermute only.
A program may use at most 64 MiB of HBM per device.

v0:
```python
import math

import jax
import jax.numpy as jnp
import numpy as np
from jax import lax
from jax.sharding import PartitionSpec as P


def pair_positions(vector_count):
    upper_rows, upper_cols = np.triu_indices(vector_count, 1)
    return upper_rows * vector_count + upper_cols


def on_device(
    pooled_first,
    pooled_second,
    feature_order,
    cross_down,
    cross_up,
    cross_bias,
    compress_weight,
    compress_bias,
    dense_vector,
    mlp_weight,
    mlp_bias,
):
    group_one, group_two = (
        lax.all_to_all(pooled_first, "feat", split_axis=2, concat_axis=1, tiled=True),
        lax.all_to_all(pooled_second, "feat", split_axis=2, concat_axis=1, tiled=True),
    )
    slot_data = jnp.concatenate([group_one[0], group_two[0]], 0)
    slot_count = slot_data.shape[0]
    row_count = slot_data.shape[1]
    entry_count = slot_data.shape[2]
    orders = feature_order[0]
    one_hot = (orders[None, :] == jnp.arange(slot_count, dtype=jnp.int32)[:, None]).astype(
        jnp.bfloat16
    )
    base_rows = jnp.einsum("fs,sre->rfe", one_hot, slot_data, preferred_element_type=jnp.float32)
    base_rows = base_rows.astype(jnp.bfloat16).reshape(row_count, slot_count * entry_count)
    weight_piece = lax.all_gather(cross_down[0], "feat", axis=0, tiled=True)
    columns = base_rows
    low_sum = jnp.dot(columns, weight_piece, preferred_element_type=jnp.float32)
    low_rank = low_sum.astype(jnp.bfloat16)
    shift_row = cross_bias[0]
    up_piece = lax.all_gather(cross_up[0], "feat", axis=0, tiled=True)
    squeeze_piece = lax.all_gather(compress_weight[0], "feat", axis=0, tiled=True)
    lifted = lax.dot_general(
        low_rank, up_piece, (((1,), (1,)), ((), ())), preferred_element_type=jnp.float32
    )
    columns = base_rows.astype(jnp.float32)
    crossed = (columns * (lifted + shift_row[None, :]) + columns).astype(jnp.bfloat16)
    squeezed = jnp.dot(crossed, squeeze_piece, preferred_element_type=jnp.float32)
    compressed = (squeezed + compress_bias[0][None, :]).astype(jnp.bfloat16)
    gathered = lax.all_to_all(compressed, "tower", split_axis=0, concat_axis=1, tiled=True)
    local_rows = gathered.shape[0]
    vector_count = gathered.shape[1] // entry_count
    vectors = gathered.reshape(local_rows, vector_count, entry_count)
    gram_matrix = jnp.einsum(
        "bie,bje->bij", vectors, vectors, preferred_element_type=jnp.float32
    ) * (1.0 / math.sqrt(entry_count))
    pair_terms = gram_matrix.reshape(local_rows, vector_count * vector_count)[
        :, pair_positions(vector_count)
    ]
    joined = jnp.concatenate([dense_vector.astype(jnp.float32), pair_terms], 1).astype(jnp.bfloat16)
    hidden_units = mlp_weight.shape[1]
    weight_piece = lax.all_gather(mlp_weight, "tower", axis=0, tiled=True)
    width_here = weight_piece.shape[0]
    columns = lax.slice_in_dim(joined, 0, width_here, axis=1)
    hidden_sum = jnp.zeros((local_rows, hidden_units), jnp.float32) + jnp.dot(
        columns, weight_piece, preferred_element_type=jnp.float32
    )
    return jax.nn.relu(hidden_sum + mlp_bias[None, :]).astype(jnp.bfloat16)


def solution(mesh):
    in_specs = (
        P("tower", "feat", "groups", None),
        P("tower", "feat", "groups", None),
        P("tower", None),
        P("tower", "feat", None),
        P("tower", "feat", None),
        P("tower", None),
        P("tower", "feat", None),
        P("tower", None),
        P(("groups", "feat", "tower"), None),
        P("tower", None),
        P(),
    )
    out_specs = P(("groups", "feat", "tower"), None)
    return jax.shard_map(
        on_device, mesh=mesh, in_specs=in_specs, out_specs=out_specs, check_vma=False
    )
```

profile of v0, /device:TPU:0, one launch (start us, length us, event | category | flops | bytes accessed | tf_op | source)
XLA Modules:
  0.0 278.5 jit_solution(6813317362227992565)
XLA Ops:
  6.5 0.7 all-gather.8.cloned.1.call-update
  7.3 0.7 all-gather.10.cloned.1.call-update
  8.1 0.7 all-gather.12.cloned.1.call-update
  8.8 8.2 %copy.24 = bf16[1,4,1536,128]{3,1,0,2:T(4,128)(2,1)} copy(bf16[1,4,1536,128]{3,2,1,0:T(8,128)(2,1)S(1)} %copy-done.2) | data formatting | bytes 3145728 | tf_op args[0]
  17.0 6.3 %all-to-all-start = ((bf16[1,4,1536,128]{3,1,0,2:T(4,128)(2,1)}), bf16[1,4,1536,128]{3,1,0,2:T(4,128)(2,1)S(1)}, u32[]{:S(2)}, u32[]{:S(2)}) async-start(bf16[1,4,1536,128]{3,1,0,2:T(4,128)(2,1)} %copy.24), calls=%async_computation | async-start | bytes 3145728 | tf_op jit(solution)/shard_map/all_to_all | solution.py:29
  23.3 8.2 %copy.26 = bf16[1,4,1536,128]{3,1,0,2:T(4,128)(2,1)} copy(bf16[1,4,1536,128]{3,2,1,0:T(8,128)(2,1)S(1)} %copy-done.3) | data formatting | bytes 3145728 | tf_op args[1]
  31.5 59.2 %all-to-all-done = bf16[1,4,1536,128]{3,1,0,2:T(4,128)(2,1)S(1)} async-done(((bf16[1,4,1536,128]{3,1,0,2:T(4,128)(2,1)}), bf16[1,4,1536,128]{3,1,0,2:T(4,128)(2,1)S(1)}, u32[]{:S(2)}, u32[]{:S(2)}) %all-to-all-start) | async-done | bytes 1572896 | tf_op jit(solution)/shard_map/all_to_all | solution.py:29
  90.7 3.7 %all-to-all-start.1 = ((bf16[1,4,1536,128]{3,1,0,2:T(4,128)(2,1)}), bf16[1,4,1536,128]{3,1,0,2:T(4,128)(2,1)S(1)}, u32[]{:S(2)}, u32[]{:S(2)}) async-start(bf16[1,4,1536,128]{3,1,0,2:T(4,128)(2,1)} %copy.26), calls=%async_computation.1 | async-start | bytes 3145728 | tf_op jit(solution)/shard_map/all_to_all | solution.py:30
  94.5 1.7 copy.25
  96.2 69.1 %all-to-all-done.1 = bf16[1,4,1536,128]{3,1,0,2:T(4,128)(2,1)S(1)} async-done(((bf16[1,4,1536,128]{3,1,0,2:T(4,128)(2,1)}), bf16[1,4,1536,128]{3,1,0,2:T(4,128)(2,1)S(1)}, u32[]{:S(2)}, u32[]{:S(2)}) %all-to-all-start.1) | async-done | bytes 1572896 | tf_op jit(solution)/shard_map/all_to_all | solution.py:30
  165.3 0.5 copy.27
  165.9 2.6 fusion.10
  168.5 3.8 %fusion.23 = bf16[384,256]{1,0:T(8,128)(2,1)S(1)} fusion(bf16[1,4096,256]{2,1,0:T(8,128)(2,1)} %all-gather.8.cloned.1.call-done, bf16[48,8,32,128]{3,2,1,0:T(8,128)(2,1)} %bitcast.56), kind=kOutput, calls=%fused_computation.21 | convolution fusion | flops 805404672 | bytes 5439488 | tf_op jit(solution)/shard_map/dot_general | solution.py:44
  172.3 74.9 %all-gather.12.cloned.1.call-done = bf16[1,4096,512]{2,1,0:T(8,128)(2,1)} async-done(((bf16[1,1024,512]{2,1,0:T(8,128)(2,1)}), bf16[1,4096,512]{2,1,0:T(8,128)(2,1)}) %all-gather.12.cloned.1.call-update) | async-done | bytes 4194320 | tf_op jit(solution)/shard_map/all_gather | solution.py:48
  247.2 7.0 %fusion.18 = bf16[384,512]{1,0:T(8,128)(2,1)} fusion(bf16[1,4096,512]{2,1,0:T(8,128)(2,1)} %all-gather.12.cloned.1.call-done, bf16[384,256]{1,0:T(8,128)(2,1)S(1)} %fusion.23, f32[4096]{0:T(1024)S(1)} %bitcast.63, bf16[48,8,32,128]{3,2,1,0:T(8,128)(2,1)S(1)} %bitcast.57, bf16[1,4096,256]{2,1,0:T(8,128)(2,1)} %all-gather.10.cloned.1.call-done, ...), kind=kOutput, calls=%fused_computation.17 | convolution fusion | flops 2424176640 | bytes 10045440 | tf_op jit(solution)/shard_map/dot_general | solution.py:54
  254.2 3.6 %all-to-all-start.2 = ((bf16[4,96,512]{2,1,0:T(8,128)(2,1)}), bf16[4,96,512]{2,1,0:T(8,128)(2,1)S(1)}, u32[]{:S(2)}, u32[]{:S(2)}) async-start(bf16[4,96,512]{2,1,0:T(8,128)(2,1)} %bitcast.14), calls=%async_computation.2 | async-start | bytes 786432 | tf_op jit(solution)/shard_map/all_to_all | solution.py:56
  257.8 11.1 %all-gather.3 = bf16[4,62,1024]{2,1,0:T(8,128)(2,1)S(1)} all-gather(bf16[1,62,1024]{2,1,0:T(8,128)(2,1)S(1)} %bitcast.60), channel_id=1, replica_groups=mesh['groups'=2,'feat'=4,'tower'=4] {'tower'}, dimensions={0}, use_global_device_ids=true | all-gather | bytes 634880 | tf_op jit(solution)/shard_map/all_gather | solution.py:68
  268.9 0.1 reshape.31
  269.1 0.3 copy.28
  269.4 0.2 reshape.17
  269.5 0.3 convolution_multiply_fusion
  269.9 0.3 copy.29
  270.2 0.7 gather_fusion
  271.1 0.9 fusion.22
  (30 shorter events, 0.3 us)
Async XLA Ops:
  6.5 2.2 copy-start.2
  6.5 162.0 %all-gather.8.cloned.1.call-start = ((), (), s32[]{:S(2)}) async-start(), calls=%async_computation.3 | async-start | bytes 2621440 | tf_op jit(solution)/shard_map/all_gather | solution.py:42
  7.3 165.0 %all-gather.10.cloned.1.call-start = ((), (), s32[]{:S(2)}) async-start(), calls=%async_computation.4 | async-start | bytes 2621440 | tf_op jit(solution)/shard_map/all_gather | solution.py:47
  8.0 239.2 %all-gather.12.cloned.1.call-start = ((), (), s32[]{:S(2)}) async-start(), calls=%async_computation.5 | async-start | bytes 5242880 | tf_op jit(solution)/shard_map/all_gather | solution.py:48
  8.8 14.5 %copy-start.3 = (bf16[1,4,1536,128]{3,2,1,0:T(8,128)(2,1)S(1)}, bf16[1,4,1536,128]{3,2,1,0:T(8,128)(2,1)}, u32[]{:S(2)}) copy-start(bf16[1,4,1536,128]{3,2,1,0:T(8,128)(2,1)} %param.14) | copy-start | bytes 4718596
  17.0 73.7 %all-to-all-start = ((bf16[1,4,1536,128]{3,1,0,2:T(4,128)(2,1)}), bf16[1,4,1536,128]{3,1,0,2:T(4,128)(2,1)S(1)}, u32[]{:S(2)}, u32[]{:S(2)}) async-start(bf16[1,4,1536,128]{3,1,0,2:T(4,128)(2,1)} %copy.24), calls=%async_computation | async-start | bytes 3145728 | tf_op jit(solution)/shard_map/all_to_all | solution.py:29
  90.7 74.6 %all-to-all-start.1 = ((bf16[1,4,1536,128]{3,1,0,2:T(4,128)(2,1)}), bf16[1,4,1536,128]{3,1,0,2:T(4,128)(2,1)S(1)}, u32[]{:S(2)}, u32[]{:S(2)}) async-start(bf16[1,4,1536,128]{3,1,0,2:T(4,128)(2,1)} %copy.26), calls=%async_computation.1 | async-start | bytes 3145728 | tf_op jit(solution)/shard_map/all_to_all | solution.py:30
  94.5 71.4 %copy-start.7 = (s32[1,32]{1,0:T(1,128)S(1)}, s32[1,32]{1,0:T(1,128)}, u32[]{:S(2)}) copy-start(s32[1,32]{1,0:T(1,128)} %param.15) | copy-start | bytes 388
  96.2 69.7 %copy-start = (bf16[1,4,4,384,128]{4,1,2,3,0:T(4,128)(2,1)S(1)}, bf16[1,4,4,384,128]{4,1,2,3,0:T(4,128)(2,1)}, u32[]{:S(2)}) copy-start(bf16[1,4,4,384,128]{4,1,2,3,0:T(4,128)(2,1)} %copy.25) | copy-start | bytes 4718596
  168.5 78.7 %copy-start.1 = (bf16[384,128,32]{1,2,0:T(8,128)(2,1)S(1)}, bf16[384,128,32]{1,2,0:T(8,128)(2,1)}, u32[]{:S(2)}) copy-start(bf16[384,128,32]{1,2,0:T(8,128)(2,1)} %fusion.10) | copy-start | bytes 9437188
  168.5 78.7 %copy-start.9 = (f32[1,4096]{1,0:T(1,128)S(1)}, f32[1,4096]{1,0:T(1,128)}, u32[]{:S(2)}) copy-start(f32[1,4096]{1,0:T(1,128)} %param.18) | copy-start | bytes 49156
  168.5 78.7 %copy-start.10 = (f32[1,512]{1,0:T(1,128)S(1)}, f32[1,512]{1,0:T(1,128)}, u32[]{:S(2)}) copy-start(f32[1,512]{1,0:T(1,128)} %param.20) | copy-start | bytes 6148
  247.2 10.6 %copy-start.4 = (bf16[62,1024]{1,0:T(8,128)(2,1)S(1)}, bf16[62,1024]{1,0:T(8,128)(2,1)}, u32[]{:S(2)}) copy-start(bf16[62,1024]{1,0:T(8,128)(2,1)} %param.22) | copy-start | bytes 380932
  247.2 21.8 %copy-start.8 = (s32[120]{0:T(128)S(1)}, s32[120]{0:T(128)}, u32[]{:S(2)}) copy-start(s32[120]{0:T(128)} %constant.23) | copy-start | bytes 1444
  254.2 16.8 %copy-start.5 = (bf16[96,128]{1,0:T(8,128)(2,1)S(1)}, bf16[96,128]{1,0:T(8,128)(2,1)}, u32[]{:S(2)}) copy-start(bf16[96,128]{1,0:T(8,128)(2,1)} %param.21) | copy-start | bytes 73732
  254.2 16.8 %copy-start.6 = (f32[1024]{0:T(1024)S(1)}, f32[1024]{0:T(1024)}, u32[]{:S(2)}) copy-start(f32[1024]{0:T(1024)} %param.23) | copy-start | bytes 12292
  254.2 14.8 %all-to-all-start.2 = ((bf16[4,96,512]{2,1,0:T(8,128)(2,1)}), bf16[4,96,512]{2,1,0:T(8,128)(2,1)S(1)}, u32[]{:S(2)}, u32[]{:S(2)}) async-start(bf16[4,96,512]{2,1,0:T(8,128)(2,1)} %bitcast.14), calls=%async_computation.2 | async-start | bytes 786432 | tf_op jit(solution)/shard_map/all_to_all | solution.py:56
Sparse Core Ops, SparseCore 0:
  8.9 80.3 all-gather.7
  90.9 74.7 all-gather.9
  167.3 79.9 all-gather.11
where the time goes:
time: 279 us
  waiting for transfers between devices  205 us (73%)
  local copies, waits for them, and re-layouts  20.4 us (7%)
  matrix products  14.6 us (5%)
  starting transfers between devices  13.7 us (5%)
  between operations  13.3 us (5%)
  blocking collectives  11.1 us (4%)
    all_gather x1, waiting for transfers between devices, on_device(): lax.all_gather(compress_weight[0], 'feat', axis=0, tiled=True)  74.9 us
    all_to_all x1, waiting for transfers between devices, on_device(): lax.all_to_all(pooled_second, 'feat', split_axis=2, concat_axis=1, tiled=...  69.1 us
    all_to_all x1, waiting for transfers between devices, on_device(): lax.all_to_all(pooled_first, 'feat', split_axis=2, concat_axis=1, tiled=T...  59.2 us
    unnamed x25, local copies, waits for them, and re-layouts  16.6 us
    all_gather x1, blocking collectives, on_device(): weight_piece = lax.all_gather(mlp_weight, 'tower', axis=0, tiled=True)  11.1 us
    dot_general x1, matrix products, on_device(): jnp.dot(crossed, squeeze_piece, preferred_element_type=jnp.float32)  6.96 us
    all_to_all x1, starting transfers between devices, on_device(): lax.all_to_all(pooled_first, 'feat', split_axis=2, concat_axis=1, tiled=T...  6.32 us
  transfers between devices with their start and end apart: 6, of which 3 were waited for; matrix products, arithmetic and copies ran while one was open for 9% of the time, Pallas kernels for 0%

commit v1 on v0

--- a/solution.py
+++ b/solution.py
@@ -1,3 +1,4 @@
+import functools
 import math
 
 import jax
@@ -12,6 +13,16 @@
     return upper_rows * vector_count + upper_cols
 
 
+def gathered_feature_order(rows_here, feat_count, group_count, entry_count):
+    piece = rows_here // group_count
+    positions = []
+    for group in range(group_count):
+        for owner in range(feat_count):
+            start = owner * rows_here + group * piece
+            positions.extend(range(start // entry_count, (start + piece) // entry_count))
+    return np.asarray(positions, np.int32)
+
+
 def on_device(
     pooled_first,
     pooled_second,
@@ -24,7 +35,31 @@
     dense_vector,
     mlp_weight,
     mlp_bias,
+    *,
+    feat_count,
+    group_count,
 ):
+    entry_count = pooled_first.shape[3]
+    rows_here = cross_down.shape[1]
+    rank = cross_down.shape[2]
+    split = rows_here % group_count == 0 and (rows_here // group_count) % entry_count == 0
+    gather_groups = group_count if split else 1
+    piece = rows_here // gather_groups
+
+    hidden_weight = lax.all_gather(mlp_weight, "tower", axis=0, tiled=True)
+    hidden_weight, pooled_first, pooled_second = lax.optimization_barrier(
+        (hidden_weight, pooled_first, pooled_second)
+    )
+
+    weights_here = jnp.concatenate([cross_down[0], cross_up[0], compress_weight[0]], axis=1)
+    if split:
+        group_index = lax.axis_index("groups")
+        weights_here = lax.dynamic_slice_in_dim(weights_here, group_index * piece, piece, axis=0)
+        weights = lax.all_gather(weights_here, ("groups", "feat"), axis=0, tiled=True)
+    else:
+        weights = lax.all_gather(weights_here, "feat", axis=0, tiled=True)
+    position_feature = gathered_feature_order(rows_here, feat_count, gather_groups, entry_count)
+
     group_one, group_two = (
         lax.all_to_all(pooled_first, "feat", split_axis=2, concat_axis=1, tiled=True),
         lax.all_to_all(pooled_second, "feat", split_axis=2, concat_axis=1, tiled=True),
@@ -32,20 +67,19 @@
     slot_data = jnp.concatenate([group_one[0], group_two[0]], 0)
     slot_count = slot_data.shape[0]
     row_count = slot_data.shape[1]
-    entry_count = slot_data.shape[2]
     orders = feature_order[0]
-    one_hot = (orders[None, :] == jnp.arange(slot_count, dtype=jnp.int32)[:, None]).astype(
-        jnp.bfloat16
-    )
+    one_hot = (orders[None, :] == jnp.asarray(position_feature)[:, None]).astype(jnp.bfloat16)
     base_rows = jnp.einsum("fs,sre->rfe", one_hot, slot_data, preferred_element_type=jnp.float32)
     base_rows = base_rows.astype(jnp.bfloat16).reshape(row_count, slot_count * entry_count)
-    weight_piece = lax.all_gather(cross_down[0], "feat", axis=0, tiled=True)
-    columns = base_rows
-    low_sum = jnp.dot(columns, weight_piece, preferred_element_type=jnp.float32)
+
+    width = slot_count * entry_count
+    shift_row = cross_bias[0].reshape(width // entry_count, entry_count)[position_feature].reshape(width)
+    down_piece = weights[:, :rank]
+    up_piece = weights[:, rank : 2 * rank]
+    squeeze_piece = weights[:, 2 * rank :]
+
+    low_sum = jnp.dot(base_rows, down_piece, preferred_element_type=jnp.float32)
     low_rank = low_sum.astype(jnp.bfloat16)
-    shift_row = cross_bias[0]
-    up_piece = lax.all_gather(cross_up[0], "feat", axis=0, tiled=True)
-    squeeze_piece = lax.all_gather(compress_weight[0], "feat", axis=0, tiled=True)
     lifted = lax.dot_general(
         low_rank, up_piece, (((1,), (1,)), ((), ())), preferred_element_type=jnp.float32
     )
@@ -65,11 +99,10 @@
     ]
     joined = jnp.concatenate([dense_vector.astype(jnp.float32), pair_terms], 1).astype(jnp.bfloat16)
     hidden_units = mlp_weight.shape[1]
-    weight_piece = lax.all_gather(mlp_weight, "tower", axis=0, tiled=True)
-    width_here = weight_piece.shape[0]
+    width_here = hidden_weight.shape[0]
     columns = lax.slice_in_dim(joined, 0, width_here, axis=1)
     hidden_sum = jnp.zeros((local_rows, hidden_units), jnp.float32) + jnp.dot(
-        columns, weight_piece, preferred_element_type=jnp.float32
+        columns, hidden_weight, preferred_element_type=jnp.float32
     )
     return jax.nn.relu(hidden_sum + mlp_bias[None, :]).astype(jnp.bfloat16)
 
@@ -89,6 +122,7 @@
         P(),
     )
     out_specs = P(("groups", "feat", "tower"), None)
-    return jax.shard_map(
-        on_device, mesh=mesh, in_specs=in_specs, out_specs=out_specs, check_vma=False
+    body = functools.partial(
+        on_device, feat_count=mesh.shape["feat"], group_count=mesh.shape["groups"]
     )
+    return jax.shard_map(body, mesh=mesh, in_specs=in_specs, out_specs=out_specs, check_vma=False)

time: 279 us -> 228 us (0.82)
  waiting for transfers between devices: 205 us -> 155 us
    all_gather x3 -> x1, waiting for transfers between devices: 74.9 us -> 17 us  [on_device(): lax.all_gather(weights_here, ('groups', 'feat'), axis=0, tiled=True)]
    all_to_all x1, waiting for transfers between devices: 59.2 us -> 77.5 us  [on_device(): lax.all_to_all(pooled_first, 'feat', split_axis=2, concat_axis=1, tiled=T...]
    optimization_barrier x0 -> x3, local copies, waits for them, and re-layouts: none -> 17.3 us  [on_device(): lax.optimization_barrier((hidden_weight, pooled_first, pooled_second))]
    all_to_all x1, waiting for transfers between devices: 69.1 us -> 52.6 us  [on_device(): lax.all_to_all(pooled_second, 'feat', split_axis=2, concat_axis=1, tiled=...]
    unnamed x25 -> x26, local copies, waits for them, and re-layouts: 16.6 us -> 0.05 us
    all_to_all x1, waiting for transfers between devices: 0.01 us -> 7.38 us  [on_device(): lax.all_to_all(compressed, 'tower', split_axis=0, concat_axis=1, tiled=True)]
  transfers between devices with their start and end apart: 6 -> 4, of which waited for: 3 -> 4; matrix products, arithmetic and copies ran while one was open for 9% -> 10% of each run, Pallas kernels for 0% -> 0%
where the time goes in v1:
time: 228 us
  waiting for transfers between devices  155 us (68%)
  local copies, waits for them, and re-layouts  21.8 us (10%)
  matrix products  14.7 us (6%)
  between operations  13.6 us (6%)
  starting transfers between devices  12.3 us (5%)
  blocking collectives  8.62 us (4%)
  other arithmetic  2.45 us (1%)
    all_to_all x1, waiting for transfers between devices, on_device(): lax.all_to_all(pooled_first, 'feat', split_axis=2, concat_axis=1, tiled=T...  77.5 us
    all_to_all x1, waiting for transfers between devices, on_device(): lax.all_to_all(pooled_second, 'feat', split_axis=2, concat_axis=1, tiled=...  52.6 us
    optimization_barrier x3, local copies, waits for them, and re-layouts, on_device(): lax.optimization_barrier((hidden_weight, pooled_first, pooled_second))  17.3 us
    all_gather x1, waiting for transfers between devices, on_device(): lax.all_gather(weights_here, ('groups', 'feat'), axis=0, tiled=True)  17 us
    all_gather x1, blocking collectives, on_device(): hidden_weight = lax.all_gather(mlp_weight, 'tower', axis=0, tiled=True)  8.62 us
    all_to_all x1, waiting for transfers between devices, on_device(): lax.all_to_all(compressed, 'tower', split_axis=0, concat_axis=1, tiled=True)  7.38 us
    dot_general x1, matrix products, on_device(): jnp.dot(crossed, squeeze_piece, preferred_element_type=jnp.float32)  6.97 us
    all_to_all x1, starting transfers between devices, on_device(): lax.all_to_all(pooled_second, 'feat', split_axis=2, concat_axis=1, tiled=...  5 us
  transfers between devices with their start and end apart: 4, of which 4 were waited for; matrix products, arithmetic and copies ran while one was open for 10% of the time, Pallas kernels for 0%

profile of v1, /device:TPU:0, one launch (start us, length us, event | category | flops | bytes accessed | tf_op | source)
XLA Modules:
  0.0 228.0 jit_solution(16493600487076962021)
XLA Ops:
  6.6 2.4 %fusion.35 = bf16[512,1024]{1,0:T(8,128)(2,1)} fusion(s32[]{:T(128)S(6)} %select_n.9, bf16[1024,256]{1,0:T(8,128)(2,1)} %bitcast.53, bf16[1024,256]{1,0:T(8,128)(2,1)} %bitcast.54, bf16[1024,512]{1,0:T(8,128)(2,1)} %bitcast.52), kind=kLoop, calls=%fused_computation.27 | loop fusion | flops 3145728 | bytes 3145732 | tf_op jit(solution)/shard_map/concatenate | solution.py:54
  9.0 8.6 %all-gather = bf16[4,62,1024]{2,1,0:T(8,128)(2,1)S(1)} all-gather(bf16[1,62,1024]{2,1,0:T(8,128)(2,1)S(1)} %bitcast.55), channel_id=1, replica_groups=mesh['groups'=2,'feat'=4,'tower'=4] {'tower'}, dimensions={0}, use_global_device_ids=true | all-gather | bytes 634880 | tf_op jit(solution)/shard_map/all_gather | solution.py:49
  17.6 1.0 reshape.38
  18.6 8.2 %copy.28 = bf16[1,4,1536,128]{3,1,0,2:T(4,128)(2,1)} copy(bf16[1,4,1536,128]{3,2,1,0:T(8,128)(2,1)S(1)} %copy-done.4) | data formatting | bytes 3145728 | tf_op jit(solution)/shard_map/optimization_barrier | solution.py:50
  26.8 5.0 %all-to-all-start.1 = ((bf16[1,4,1536,128]{3,1,0,2:T(4,128)(2,1)}), bf16[1,4,1536,128]{3,1,0,2:T(4,128)(2,1)S(1)}, u32[]{:S(2)}, u32[]{:S(2)}) async-start(bf16[1,4,1536,128]{3,1,0,2:T(4,128)(2,1)} %copy.28), calls=%async_computation.1 | async-start | bytes 3145728 | tf_op jit(solution)/shard_map/all_to_all | solution.py:65
  31.8 8.2 %copy.26 = bf16[1,4,1536,128]{3,1,0,2:T(4,128)(2,1)} copy(bf16[1,4,1536,128]{3,2,1,0:T(8,128)(2,1)S(1)} %copy-done.5) | data formatting | bytes 3145728 | tf_op jit(solution)/shard_map/optimization_barrier | solution.py:50
  40.0 52.6 %all-to-all-done.1 = bf16[1,4,1536,128]{3,1,0,2:T(4,128)(2,1)S(1)} async-done(((bf16[1,4,1536,128]{3,1,0,2:T(4,128)(2,1)}), bf16[1,4,1536,128]{3,1,0,2:T(4,128)(2,1)S(1)}, u32[]{:S(2)}, u32[]{:S(2)}) %all-to-all-start.1) | async-done | bytes 1572896 | tf_op jit(solution)/shard_map/all_to_all | solution.py:65
  92.5 3.7 %all-to-all-start = ((bf16[1,4,1536,128]{3,1,0,2:T(4,128)(2,1)}), bf16[1,4,1536,128]{3,1,0,2:T(4,128)(2,1)S(1)}, u32[]{:S(2)}, u32[]{:S(2)}) async-start(bf16[1,4,1536,128]{3,1,0,2:T(4,128)(2,1)} %copy.26), calls=%async_computation | async-start | bytes 3145728 | tf_op jit(solution)/shard_map/all_to_all | solution.py:64
  96.3 0.6 gather_fusion
  96.9 1.7 copy.29
  98.6 77.5 %all-to-all-done = bf16[1,4,1536,128]{3,1,0,2:T(4,128)(2,1)S(1)} async-done(((bf16[1,4,1536,128]{3,1,0,2:T(4,128)(2,1)}), bf16[1,4,1536,128]{3,1,0,2:T(4,128)(2,1)S(1)}, u32[]{:S(2)}, u32[]{:S(2)}) %all-to-all-start) | async-done | bytes 1572896 | tf_op jit(solution)/shard_map/all_to_all | solution.py:64
  176.1 0.5 copy.27
  176.7 2.7 %fusion.10 = bf16[384,128,32]{1,2,0:T(8,128)(2,1)} fusion(bf16[16,384,128]{2,0,1:T(8,128)(2,1)S(1)} %bitcast.46, bf16[16,384,128]{2,0,1:T(8,128)(2,1)S(1)} %bitcast.47, s32[32]{0:T(128)S(1)} %bitcast.58, s32[32]{0:T(128)S(1)} %copy-done.9), kind=kOutput, calls=%fused_computation.13 | convolution fusion | flops 108528640 | bytes 6291712 | tf_op jit(solution)/shard_map/fs,sre->rfe/dot_general | solution.py:72
  179.4 17.0 %all-gather.3.cloned.1.call-done = bf16[4096,1024]{1,0:T(8,128)(2,1)} async-done(((bf16[512,1024]{1,0:T(8,128)(2,1)}), bf16[4096,1024]{1,0:T(8,128)(2,1)}) %all-gather.3.cloned.1.call-update) | async-done | bytes 8388624 | tf_op jit(solution)/shard_map/all_gather | solution.py:58
  196.4 3.8 %fusion.29 = bf16[384,256]{1,0:T(8,128)(2,1)S(1)} fusion(bf16[4096,1024]{1,0:T(8,128)(2,1)} %all-gather.3.cloned.1.call-done, bf16[48,8,32,128]{3,2,1,0:T(8,128)(2,1)} %bitcast.48), kind=kOutput, calls=%fused_computation.25 | convolution fusion | flops 805404672 | bytes 5439488 | tf_op jit(solution)/shard_map/dot_general | solution.py:81
  200.3 7.0 %fusion.22 = bf16[384,512]{1,0:T(8,128)(2,1)} fusion(bf16[4096,1024]{1,0:T(8,128)(2,1)} %all-gather.3.cloned.1.call-done, bf16[384,256]{1,0:T(8,128)(2,1)S(1)} %fusion.29, f32[4096]{0:T(1024)S(1)} %bitcast.57, bf16[48,8,32,128]{3,2,1,0:T(8,128)(2,1)S(1)} %bitcast.49, f32[512]{0:T(512)S(1)} %bitcast.59), kind=kOutput, calls=%fused_computation.21 | convolution fusion | flops 2424176640 | bytes 10045440 | tf_op jit(solution)/shard_map/dot_general | solution.py:88
  207.2 3.6 %all-to-all-start.2 = ((bf16[4,96,512]{2,1,0:T(8,128)(2,1)}), bf16[4,96,512]{2,1,0:T(8,128)(2,1)S(1)}, u32[]{:S(2)}, u32[]{:S(2)}) async-start(bf16[4,96,512]{2,1,0:T(8,128)(2,1)} %bitcast.16), calls=%async_computation.2 | async-start | bytes 786432 | tf_op jit(solution)/shard_map/all_to_all | solution.py:90
  210.9 7.4 %all-to-all-done.2 = bf16[4,96,512]{2,1,0:T(8,128)(2,1)S(1)} async-done(((bf16[4,96,512]{2,1,0:T(8,128)(2,1)}), bf16[4,96,512]{2,1,0:T(8,128)(2,1)S(1)}, u32[]{:S(2)}, u32[]{:S(2)}) %all-to-all-start.2) | async-done | bytes 393248 | tf_op jit(solution)/shard_map/all_to_all | solution.py:90
  218.2 0.3 copy.30
  218.5 0.2 reshape.19
  218.7 0.3 convolution_multiply_fusion
  219.1 0.3 copy.31
  219.4 0.7 gather_fusion.1
  220.2 0.9 fusion.28
  (31 shorter events, 0.2 us)
Async XLA Ops:
  6.5 89.8 %copy-start = (f32[1,4096]{1,0:T(1,128)S(1)}, f32[1,4096]{1,0:T(1,128)}, u32[]{:S(2)}) copy-start(f32[1,4096]{1,0:T(1,128)} %param.20) | copy-start | bytes 49156
  6.5 2.5 %copy-start.6 = (bf16[62,1024]{1,0:T(8,128)(2,1)S(1)}, bf16[62,1024]{1,0:T(8,128)(2,1)}, u32[]{:S(2)}) copy-start(bf16[62,1024]{1,0:T(8,128)(2,1)} %param.24) | copy-start | bytes 380932
  6.5 12.1 %copy-start.4 = (bf16[1,4,1536,128]{3,2,1,0:T(8,128)(2,1)S(1)}, bf16[1,4,1536,128]{3,2,1,0:T(8,128)(2,1)}, u32[]{:S(2)}) copy-start(bf16[1,4,1536,128]{3,2,1,0:T(8,128)(2,1)} %param.16) | copy-start | bytes 4718596
  6.5 189.9 %all-gather.3.cloned.1.call-start = ((), (), s32[]{:S(2)}) async-start(), calls=%async_computation.3 | async-start | bytes 9437184 | tf_op jit(solution)/shard_map/all_gather | solution.py:58
  26.8 5.0 %copy-start.5 = (bf16[1,4,1536,128]{3,2,1,0:T(8,128)(2,1)S(1)}, bf16[1,4,1536,128]{3,2,1,0:T(8,128)(2,1)}, u32[]{:S(2)}) copy-start(bf16[1,4,1536,128]{3,2,1,0:T(8,128)(2,1)} %param.15) | copy-start | bytes 4718596
  26.8 65.7 %all-to-all-start.1 = ((bf16[1,4,1536,128]{3,1,0,2:T(4,128)(2,1)}), bf16[1,4,1536,128]{3,1,0,2:T(4,128)(2,1)S(1)}, u32[]{:S(2)}, u32[]{:S(2)}) async-start(bf16[1,4,1536,128]{3,1,0,2:T(4,128)(2,1)} %copy.28), calls=%async_computation.1 | async-start | bytes 3145728 | tf_op jit(solution)/shard_map/all_to_all | solution.py:65
  31.8 64.5 %copy-start.9 = (s32[32]{0:T(128)S(1)}, s32[32]{0:T(128)}, u32[]{:S(2)}) copy-start(s32[32]{0:T(128)} %constant.29.clone) | copy-start | bytes 388
  92.5 83.6 %all-to-all-start = ((bf16[1,4,1536,128]{3,1,0,2:T(4,128)(2,1)}), bf16[1,4,1536,128]{3,1,0,2:T(4,128)(2,1)S(1)}, u32[]{:S(2)}, u32[]{:S(2)}) async-start(bf16[1,4,1536,128]{3,1,0,2:T(4,128)(2,1)} %copy.26), calls=%async_computation | async-start | bytes 3145728 | tf_op jit(solution)/shard_map/all_to_all | solution.py:64
  96.9 79.8 %copy-start.11 = (s32[1,32]{1,0:T(1,128)S(1)}, s32[1,32]{1,0:T(1,128)}, u32[]{:S(2)}) copy-start(s32[1,32]{1,0:T(1,128)} %param.17) | copy-start | bytes 388
  98.6 78.1 %copy-start.1 = (bf16[1,4,4,384,128]{4,1,2,3,0:T(4,128)(2,1)S(1)}, bf16[1,4,4,384,128]{4,1,2,3,0:T(4,128)(2,1)}, u32[]{:S(2)}) copy-start(bf16[1,4,4,384,128]{4,1,2,3,0:T(4,128)(2,1)} %copy.29) | copy-start | bytes 4718596
  196.4 3.8 %copy-start.2 = (bf16[384,128,32]{1,2,0:T(8,128)(2,1)S(1)}, bf16[384,128,32]{1,2,0:T(8,128)(2,1)}, u32[]{:S(2)}) copy-start(bf16[384,128,32]{1,2,0:T(8,128)(2,1)} %fusion.10) | copy-start | bytes 9437188
  196.4 3.8 %copy-start.12 = (f32[1,512]{1,0:T(1,128)S(1)}, f32[1,512]{1,0:T(1,128)}, u32[]{:S(2)}) copy-start(f32[1,512]{1,0:T(1,128)} %param.22) | copy-start | bytes 6148
  200.2 10.6 %copy-start.10 = (s32[120]{0:T(128)S(1)}, s32[120]{0:T(128)}, u32[]{:S(2)}) copy-start(s32[120]{0:T(128)} %constant.44) | copy-start | bytes 1444
  207.2 13.0 %copy-start.3 = (bf16[248,1024]{1,0:T(8,128)(2,1)S(1)}, bf16[248,1024]{1,0:T(8,128)(2,1)}, u32[]{:S(2)}) copy-start(bf16[248,1024]{1,0:T(8,128)(2,1)} %reshape.38) | copy-start | bytes 1523716
  207.2 13.0 %copy-start.7 = (bf16[96,128]{1,0:T(8,128)(2,1)S(1)}, bf16[96,128]{1,0:T(8,128)(2,1)}, u32[]{:S(2)}) copy-start(bf16[96,128]{1,0:T(8,128)(2,1)} %param.23) | copy-start | bytes 73732
  207.2 13.0 %copy-start.8 = (f32[1024]{0:T(1024)S(1)}, f32[1024]{0:T(1024)}, u32[]{:S(2)}) copy-start(f32[1024]{0:T(1024)} %param.25) | copy-start | bytes 12292
  207.2 11.0 %all-to-all-start.2 = ((bf16[4,96,512]{2,1,0:T(8,128)(2,1)}), bf16[4,96,512]{2,1,0:T(8,128)(2,1)S(1)}, u32[]{:S(2)}, u32[]{:S(2)}) async-start(bf16[4,96,512]{2,1,0:T(8,128)(2,1)} %bitcast.16), calls=%async_computation.2 | async-start | bytes 786432 | tf_op jit(solution)/shard_map/all_to_all | solution.py:90
Sparse Core Ops, SparseCore 0:
  9.5 186.9 all-gather.2

commit v2 on v1

v2 whole, which is shorter than its diff:
```python
import functools
import math

import jax
import jax.numpy as jnp
import numpy as np
from jax import lax
from jax.sharding import PartitionSpec as P


def pair_positions(vector_count):
    upper_rows, upper_cols = np.triu_indices(vector_count, 1)
    return upper_rows * vector_count + upper_cols


def received_feature_table(rows_here, feat_count, group_count, entry_count):
    piece = rows_here // group_count
    table = np.zeros((group_count, group_count, feat_count * piece // entry_count), np.int32)
    for group in range(group_count):
        for shift in range(group_count):
            source = (group - shift) % group_count
            blocks = []
            for owner in range(feat_count):
                start = owner * rows_here + source * piece
                blocks.extend(range(start // entry_count, (start + piece) // entry_count))
            table[group, shift] = blocks
    return table


def gather_rows(part, group_count):
    own = lax.all_gather(part, "feat", axis=0, tiled=True)
    received = [own]
    for shift in range(1, group_count):
        pairs = [(source, (source + shift) % group_count) for source in range(group_count)]
        received.append(lax.ppermute(own, "groups", pairs))
    return received


def on_device(
    pooled_first,
    pooled_second,
    feature_order,
    cross_down,
    cross_up,
    cross_bias,
    compress_weight,
    compress_bias,
    dense_vector,
    mlp_weight,
    mlp_bias,
    *,
    feat_count,
    group_count,
):
    entry_count = pooled_first.shape[3]
    rows_here = cross_down.shape[1]
    rank = cross_down.shape[2]
    split = rows_here % group_count == 0 and (rows_here // group_count) % entry_count == 0
    share_count = group_count if split else 1
    piece = rows_here // share_count

    first_here = jnp.concatenate([cross_down[0], cross_up[0]], axis=1)
    second_here = compress_weight[0]
    if split:
        group_index = lax.axis_index("groups")
        first_here = lax.dynamic_slice_in_dim(first_here, group_index * piece, piece, axis=0)
        second_here = lax.dynamic_slice_in_dim(second_here, group_index * piece, piece, axis=0)
        table = jnp.asarray(received_feature_table(rows_here, feat_count, share_count, entry_count))
        position_feature = table[group_index]
    else:
        position_feature = jnp.asarray(
            received_feature_table(rows_here, feat_count, 1, entry_count)
        )[0]
    first_parts = gather_rows(first_here, share_count)
    second_parts = gather_rows(second_here, share_count)

    group_one, group_two = (
        lax.all_to_all(pooled_first, "feat", split_axis=2, concat_axis=1, tiled=True),
        lax.all_to_all(pooled_second, "feat", split_axis=2, concat_axis=1, tiled=True),
    )
    mlp_weight, group_one = lax.optimization_barrier((mlp_weight, group_one))
    hidden_weight = lax.all_gather(mlp_weight, "tower", axis=0, tiled=True)

    slot_data = jnp.concatenate([group_one[0], group_two[0]], 0)
    slot_count = slot_data.shape[0]
    row_count = slot_data.shape[1]
    orders = feature_order[0]
    position_count = position_feature.shape[1]
    one_hot = (orders[None, None, :] == position_feature[:, :, None]).astype(jnp.bfloat16)
    base_parts = jnp.einsum("kfs,sre->krfe", one_hot, slot_data, preferred_element_type=jnp.float32)
    base_parts = base_parts.astype(jnp.bfloat16).reshape(
        share_count, row_count, position_count * entry_count
    )
    bias_blocks = cross_bias[0].reshape(slot_count, entry_count)

    low_sum = None
    for shift in range(share_count):
        term = jnp.dot(
            base_parts[shift], first_parts[shift][:, :rank], preferred_element_type=jnp.float32
        )
        low_sum = term if low_sum is None else low_sum + term
    low_rank = low_sum.astype(jnp.bfloat16)

    squeezed = None
    for shift in range(share_count):
        lifted = lax.dot_general(
            low_rank,
            first_parts[shift][:, rank:],
            (((1,), (1,)), ((), ())),
            preferred_element_type=jnp.float32,
        )
        shift_row = bias_blocks[position_feature[shift]].reshape(position_count * entry_count)
        columns = base_parts[shift].astype(jnp.float32)
        crossed = (columns * (lifted + shift_row[None, :]) + columns).astype(jnp.bfloat16)
        term = jnp.dot(crossed, second_parts[shift], preferred_element_type=jnp.float32)
        squeezed = term if squeezed is None else squeezed + term
    compressed = (squeezed + compress_bias[0][None, :]).astype(jnp.bfloat16)
    gathered = lax.all_to_all(compressed, "tower", split_axis=0, concat_axis=1, tiled=True)
    local_rows = gathered.shape[0]
    vector_count = gathered.shape[1] // entry_count
    vectors = gathered.reshape(local_rows, vector_count, entry_count)
    gram_matrix = jnp.einsum(
        "bie,bje->bij", vectors, vectors, preferred_element_type=jnp.float32
    ) * (1.0 / math.sqrt(entry_count))
    pair_terms = gram_matrix.reshape(local_rows, vector_count * vector_count)[
        :, pair_positions(vector_count)
    ]
    joined = jnp.concatenate([dense_vector.astype(jnp.float32), pair_terms], 1).astype(jnp.bfloat16)
    hidden_units = mlp_weight.shape[1]
    width_here = hidden_weight.shape[0]
    columns = lax.slice_in_dim(joined, 0, width_here, axis=1)
    hidden_sum = jnp.zeros((local_rows, hidden_units), jnp.float32) + jnp.dot(
        columns, hidden_weight, preferred_element_type=jnp.float32
    )
    return jax.nn.relu(hidden_sum + mlp_bias[None, :]).astype(jnp.bfloat16)


def solution(mesh):
    in_specs = (
        P("tower", "feat", "groups", None),
        P("tower", "feat", "groups", None),
        P("tower", None),
        P("tower", "feat", None),
        P("tower", "feat", None),
        P("tower", None),
        P("tower", "feat", None),
        P("tower", None),
        P(("groups", "feat", "tower"), None),
        P("tower", None),
        P(),
    )
    out_specs = P(("groups", "feat", "tower"), None)
    body = functools.partial(
        on_device, feat_count=mesh.shape["feat"], group_count=mesh.shape["groups"]
    )
    return jax.shard_map(body, mesh=mesh, in_specs=in_specs, out_specs=out_specs, check_vma=False)
```

time: 228 us -> 244 us (1.070)
  starting transfers between devices: 12.3 us -> 17.4 us
  local copies, waits for them, and re-layouts: 21.8 us -> 26.1 us
  waiting for transfers between devices: 155 us -> 159 us
    all_gather x1 -> x2, waiting for transfers between devices: 17 us -> 69.6 us  [gather_rows(): own = lax.all_gather(part, 'feat', axis=0, tiled=True)]
    all_to_all x1, waiting for transfers between devices: 52.6 us -> 0.01 us  [on_device(): lax.all_to_all(pooled_second, 'feat', split_axis=2, concat_axis=1, tiled=...]
    ppermute x0 -> x2, waiting for transfers between devices: none -> 31.3 us  [gather_rows(): received.append(lax.ppermute(own, 'groups', pairs))]
    all_to_all x1, waiting for transfers between devices: 77.5 us -> 58.1 us  [on_device(): lax.all_to_all(pooled_first, 'feat', split_axis=2, concat_axis=1, tiled=T...]
    unnamed x26 -> x29, local copies, waits for them, and re-layouts: 0.05 us -> 18.1 us
    optimization_barrier x3 -> x0, local copies, waits for them, and re-layouts: 17.3 us -> none  [on_device(): lax.optimization_barrier((hidden_weight, pooled_first, pooled_second))]
    all_to_all x1, waiting for transfers between devices: 7.38 us -> 0.01 us  [on_device(): lax.all_to_all(compressed, 'tower', split_axis=0, concat_axis=1, tiled=True)]
    ppermute x0 -> x2, starting transfers between devices: none -> 3.03 us  [gather_rows(): received.append(lax.ppermute(own, 'groups', pairs))]
  transfers between devices with their start and end apart: 4 -> 7, of which waited for: 4 -> 3; matrix products, arithmetic and copies ran while one was open for 10% -> 13% of each run, Pallas kernels for 0% -> 0%
where the time goes in v2:
time: 244 us; the launch traced here: 243 us
  waiting for transfers between devices  159 us (65%)
  local copies, waits for them, and re-layouts  26.1 us (11%)
  starting transfers between devices  17.4 us (7%)
  matrix products  14.1 us (6%)
  between operations  13.6 us (6%)
  blocking collectives  11 us (5%)
    all_gather x2, waiting for transfers between devices, gather_rows(): own = lax.all_gather(part, 'feat', axis=0, tiled=True)  69.6 us
    all_to_all x1, waiting for transfers between devices, on_device(): lax.all_to_all(pooled_first, 'feat', split_axis=2, concat_axis=1, tiled=T...  58.1 us
    ppermute x2, waiting for transfers between devices, gather_rows(): received.append(lax.ppermute(own, 'groups', pairs))  31.3 us
    unnamed x29, local copies, waits for them, and re-layouts  18.1 us
    all_gather x1, blocking collectives, on_device(): hidden_weight = lax.all_gather(mlp_weight, 'tower', axis=0, tiled=True)  11 us
    dot_general x2, matrix products, on_device(): jnp.dot(crossed, second_parts[shift], preferred_element_type=jnp.float32)  9.42 us
    all_to_all x1, starting transfers between devices, on_device(): lax.all_to_all(pooled_first, 'feat', split_axis=2, concat_axis=1, tiled=T...  6.32 us
  transfers between devices with their start and end apart: 7, of which 3 were waited for; matrix products, arithmetic and copies ran while one was open for 13% of the time, Pallas kernels for 0%

profile of v2, /device:TPU:0, one launch (start us, length us, event | category | flops | bytes accessed | tf_op | source)
XLA Modules:
  0.0 243.4 jit_solution(15778819335520418898)
XLA Ops:
  6.5 2.0 fusion.30
  8.6 8.2 %copy.25 = bf16[1,4,1536,128]{3,1,0,2:T(4,128)(2,1)} copy(bf16[1,4,1536,128]{3,2,1,0:T(8,128)(2,1)S(1)} %copy-done.2) | data formatting | bytes 3145728 | tf_op args[0]
  16.8 6.3 %all-to-all-start = ((bf16[1,4,1536,128]{3,1,0,2:T(4,128)(2,1)}), bf16[1,4,1536,128]{3,1,0,2:T(4,128)(2,1)S(1)}, u32[]{:S(2)}, u32[]{:S(2)}) async-start(bf16[1,4,1536,128]{3,1,0,2:T(4,128)(2,1)} %copy.25), calls=%async_computation | async-start | bytes 3145728 | tf_op jit(solution)/shard_map/all_to_all | solution.py:78
  23.2 0.9 constant_dynamic-slice_fusion
  24.0 8.5 %copy.27 = bf16[1,4,1536,128]{3,1,0,2:T(4,128)(2,1)} copy(bf16[1,4,1536,128]{3,2,1,0:T(8,128)(2,1)} %param.15) | data formatting | bytes 3145728 | tf_op args[1]
  32.6 58.1 %all-to-all-done = bf16[1,4,1536,128]{3,1,0,2:T(4,128)(2,1)S(1)} async-done(((bf16[1,4,1536,128]{3,1,0,2:T(4,128)(2,1)}), bf16[1,4,1536,128]{3,1,0,2:T(4,128)(2,1)S(1)}, u32[]{:S(2)}, u32[]{:S(2)}) %all-to-all-start) | async-done | bytes 1572896 | tf_op jit(solution)/shard_map/all_to_all | solution.py:78
  90.7 4.6 %all-to-all-start.1 = ((bf16[1,4,1536,128]{3,1,0,2:T(4,128)(2,1)}), bf16[1,4,1536,128]{3,1,0,2:T(4,128)(2,1)}, u32[]{:S(2)}, u32[]{:S(2)}) async-start(bf16[1,4,1536,128]{3,1,0,2:T(4,128)(2,1)} %copy.27), calls=%async_computation.1 | async-start | bytes 3145728 | tf_op jit(solution)/shard_map/all_to_all | solution.py:79
  95.3 1.5 collective-permute-start
  96.9 69.6 %all-gather.7.cloned.1.call-done = bf16[1,2048,512]{2,1,0:T(8,128)(2,1)} async-done(((bf16[1,512,512]{2,1,0:T(8,128)(2,1)}), bf16[1,2048,512]{2,1,0:T(8,128)(2,1)}) %all-gather.7.cloned.1.call-update) | async-done | bytes 2097168 | tf_op jit(solution)/shard_map/all_gather | solution.py:31
  166.5 1.5 collective-permute-start.1
  168.0 0.6 gather_fusion
  169.1 1.8 copy.26
  170.9 2.1 copy.28
  173.0 1.0 convert_bitcast_fusion
  174.6 1.2 copy-done.11
  175.8 0.6 fusion.7
  176.4 1.8 fusion.18
  178.2 4.9 %fusion.28 = f32[384,512]{1,0:T(8,128)} fusion(bf16[384,256]{1,0:T(8,128)(2,1)S(1)} %fusion.18, f32[2048]{0:T(1024)S(1)} %bitcast.92, bf16[48,8,16,128]{3,2,1,0:T(8,128)(2,1)} %bitcast.83, bf16[2048,512]{1,0:T(8,128)(2,1)} %all-gather.5.cloned.1.call-done, bf16[1,2048,512]{2,1,0:T(8,128)(2,1)} %all-gather.7.cloned.1.call-done), kind=kOutput, calls=%fused_computation.33 | convolution fusion | flops 1211891712 | bytes 5709824 | tf_op jit(solution)/shard_map/dot_general | solution.py:115
  183.1 31.3 %collective-permute-done.1 = bf16[2048,512]{1,0:T(8,128)(2,1)} collective-permute-done((bf16[2048,512]{1,0:T(8,128)(2,1)}, bf16[2048,512]{1,0:T(8,128)(2,1)}, u32[]{:S(2)}, u32[]{:S(2)}) %collective-permute-start.1) | collective-permute-done | bytes 2097184 | tf_op jit(solution)/shard_map/ppermute | solution.py:35
  214.4 4.5 %fusion.12 = bf16[384,512]{1,0:T(8,128)(2,1)} fusion(f32[384,512]{1,0:T(8,128)} %fusion.28, bf16[2048,512]{1,0:T(8,128)(2,1)} %collective-permute-done.1, bf16[384,256]{1,0:T(8,128)(2,1)S(1)} %fusion.18, f32[2048]{0:T(1024)S(1)} %bitcast.91, bf16[48,8,16,128]{3,2,1,0:T(8,128)(2,1)S(1)} %bitcast.81, bf16[2048,512]{1,0:T(8,128)(2,1)} %collective-permute-done, ...), kind=kOutput, calls=%fused_computation.21 | convolution fusion | flops 1212481536 | bytes 6105088 | tf_op jit(solution)/shard_map/dot_general | solution.py:115
  218.9 3.5 %all-to-all-start.2 = ((bf16[4,96,512]{2,1,0:T(8,128)(2,1)}), bf16[4,96,512]{2,1,0:T(8,128)(2,1)S(1)}, u32[]{:S(2)}, u32[]{:S(2)}) async-start(bf16[4,96,512]{2,1,0:T(8,128)(2,1)} %bitcast.24), calls=%async_computation.2 | async-start | bytes 786432 | tf_op jit(solution)/shard_map/all_to_all | solution.py:118
  222.4 11.0 %all-gather.1 = bf16[4,62,1024]{2,1,0:T(8,128)(2,1)S(1)} all-gather(bf16[1,62,1024]{2,1,0:T(8,128)(2,1)S(1)} %bitcast.89), channel_id=1, replica_groups=mesh['groups'=2,'feat'=4,'tower'=4] {'tower'}, dimensions={0}, use_global_device_ids=true | all-gather | bytes 634880 | tf_op jit(solution)/shard_map/all_gather | solution.py:82
  234.8 0.7 gather_fusion.2
  235.6 0.9 fusion.17
  (45 shorter events, 2.6 us)
Async XLA Ops:
  6.5 16.6 %copy-start = (bf16[1,1024,512]{2,1,0:T(8,128)(2,1)S(1)}, bf16[1,1024,512]{2,1,0:T(8,128)(2,1)}, u32[]{:S(2)}) copy-start(bf16[1,1024,512]{2,1,0:T(8,128)(2,1)} %param.20) | copy-start | bytes 3145732
  6.5 2.1 copy-start.2
  6.5 88.8 %all-gather.5.cloned.1.call-start = ((), (), s32[]{:S(2)}) async-start(), calls=%async_computation.3 | async-start | bytes 2621440 | tf_op jit(solution)/shard_map/all_gather | solution.py:31
  16.8 73.9 %all-to-all-start = ((bf16[1,4,1536,128]{3,1,0,2:T(4,128)(2,1)}), bf16[1,4,1536,128]{3,1,0,2:T(4,128)(2,1)S(1)}, u32[]{:S(2)}, u32[]{:S(2)}) async-start(bf16[1,4,1536,128]{3,1,0,2:T(4,128)(2,1)} %copy.25), calls=%async_computation | async-start | bytes 3145728 | tf_op jit(solution)/shard_map/all_to_all | solution.py:78
  23.2 143.3 %all-gather.7.cloned.1.call-start = ((), (), s32[]{:S(2)}) async-start(), calls=%async_computation.4 | async-start | bytes 2621440 | tf_op jit(solution)/shard_map/all_gather | solution.py:31
  32.6 135.4 %copy-start.9 = (s32[2,2,16]{2,1,0:T(2,128)S(1)}, s32[2,2,16]{2,1,0:T(2,128)}, u32[]{:S(2)}) copy-start(s32[2,2,16]{2,1,0:T(2,128)} %constant.31.clone) | copy-start | bytes 772
  32.6 135.4 %copy-start.4 = (f32[1,4096]{1,0:T(1,128)S(1)}, f32[1,4096]{1,0:T(1,128)}, u32[]{:S(2)}) copy-start(f32[1,4096]{1,0:T(1,128)} %param.19) | copy-start | bytes 49156
  90.7 80.2 %all-to-all-start.1 = ((bf16[1,4,1536,128]{3,1,0,2:T(4,128)(2,1)}), bf16[1,4,1536,128]{3,1,0,2:T(4,128)(2,1)}, u32[]{:S(2)}, u32[]{:S(2)}) async-start(bf16[1,4,1536,128]{3,1,0,2:T(4,128)(2,1)} %copy.27), calls=%async_computation.1 | async-start | bytes 3145728 | tf_op jit(solution)/shard_map/all_to_all | solution.py:79
  95.3 81.0 %collective-permute-start = (bf16[2048,512]{1,0:T(8,128)(2,1)}, bf16[2048,512]{1,0:T(8,128)(2,1)}, u32[]{:S(2)}, u32[]{:S(2)}) collective-permute-start(bf16[2048,512]{1,0:T(8,128)(2,1)} %all-gather.5.cloned.1.call-done), channel_id=1, source_target_pairs={{0,16},{16,0},{1,17},{17,1},{2,18},{18,2},{3,19},{19,3},{4,20},{20... | collective-permute-start | bytes 6291464 | tf_op jit(solution)/shard_map/ppermute | solution.py:35
  166.5 47.9 %collective-permute-start.1 = (bf16[2048,512]{1,0:T(8,128)(2,1)}, bf16[2048,512]{1,0:T(8,128)(2,1)}, u32[]{:S(2)}, u32[]{:S(2)}) collective-permute-start(bf16[2048,512]{1,0:T(8,128)(2,1)} %bitcast.94), channel_id=1, source_target_pairs={{0,16},{16,0},{1,17},{17,1},{2,18},{18,2},{3,19},{19,3},{4,20},{20... | collective-permute-start | bytes 6291464 | tf_op jit(solution)/shard_map/ppermute | solution.py:35
  170.9 2.1 copy-start.1
  170.9 2.1 copy-start.8
  174.0 1.7 copy-start.11
  174.6 1.8 copy-start.3
  178.2 36.2 %copy-start.12 = (f32[1,512]{1,0:T(1,128)S(1)}, f32[1,512]{1,0:T(1,128)}, u32[]{:S(2)}) copy-start(f32[1,512]{1,0:T(1,128)} %param.21) | copy-start | bytes 6148
  214.4 8.0 %copy-start.10 = (s32[120]{0:T(128)S(1)}, s32[120]{0:T(128)}, u32[]{:S(2)}) copy-start(s32[120]{0:T(128)} %constant.44) | copy-start | bytes 1444
  214.4 8.0 %copy-start.5 = (bf16[62,1024]{1,0:T(8,128)(2,1)S(1)}, bf16[62,1024]{1,0:T(8,128)(2,1)}, u32[]{:S(2)}) copy-start(bf16[62,1024]{1,0:T(8,128)(2,1)} %param.23) | copy-start | bytes 380932
  218.9 14.7 %all-to-all-start.2 = ((bf16[4,96,512]{2,1,0:T(8,128)(2,1)}), bf16[4,96,512]{2,1,0:T(8,128)(2,1)S(1)}, u32[]{:S(2)}, u32[]{:S(2)}) async-start(bf16[4,96,512]{2,1,0:T(8,128)(2,1)} %bitcast.24), calls=%async_computation.2 | async-start | bytes 786432 | tf_op jit(solution)/shard_map/all_to_all | solution.py:118
  233.5 2.1 copy-start.6
  233.5 2.1 copy-start.7
Sparse Core Ops, SparseCore 0:
  8.9 80.4 all-gather.4
  91.0 75.4 all-gather.6

commit v3 on v2

v3 whole, which is shorter than its diff:
```python
import functools
import math

import jax
import jax.numpy as jnp
import numpy as np
from jax import lax
from jax.sharding import PartitionSpec as P


def pair_positions(vector_count):
    upper_rows, upper_cols = np.triu_indices(vector_count, 1)
    return upper_rows * vector_count + upper_cols


def weight_parts(weights_here, feat_count, group_count, share_count, entry_count):
    rows_here = weights_here.shape[0]
    piece = rows_here // share_count
    blocks_here = rows_here // entry_count
    blocks_piece = piece // entry_count
    owner = lax.axis_index("feat")
    group = lax.axis_index("groups") if share_count > 1 else 0
    block_range = jnp.arange(blocks_piece, dtype=jnp.int32)
    parts = [(weights_here, owner * blocks_here + jnp.arange(blocks_here, dtype=jnp.int32))]
    if share_count > 1:
        travelling = lax.dynamic_slice_in_dim(weights_here, group * piece, piece, axis=0)
    else:
        travelling = weights_here
    ring = [(source, (source + 1) % feat_count) for source in range(feat_count)]
    for step in range(1, feat_count):
        travelling = lax.ppermute(travelling, "feat", ring)
        source_block = (owner - step) % feat_count
        parts.append(
            (travelling, source_block * blocks_here + group * blocks_piece + block_range)
        )
        for shift in range(1, share_count):
            pairs = [(source, (source + shift) % group_count) for source in range(group_count)]
            forwarded = lax.ppermute(travelling, "groups", pairs)
            from_group = (group - shift) % group_count
            parts.append(
                (forwarded, source_block * blocks_here + from_group * blocks_piece + block_range)
            )
    return parts


def on_device(
    pooled_first,
    pooled_second,
    feature_order,
    cross_down,
    cross_up,
    cross_bias,
    compress_weight,
    compress_bias,
    dense_vector,
    mlp_weight,
    mlp_bias,
    *,
    feat_count,
    group_count,
):
    entry_count = pooled_first.shape[3]
    rows_here = cross_down.shape[1]
    rank = cross_down.shape[2]
    split = rows_here % group_count == 0 and (rows_here // group_count) % entry_count == 0
    share_count = group_count if split else 1

    weights_here = jnp.concatenate([cross_down[0], cross_up[0], compress_weight[0]], axis=1)
    parts = weight_parts(weights_here, feat_count, group_count, share_count, entry_count)

    group_one, group_two = (
        lax.all_to_all(pooled_first, "feat", split_axis=2, concat_axis=1, tiled=True),
        lax.all_to_all(pooled_second, "feat", split_axis=2, concat_axis=1, tiled=True),
    )
    mlp_weight, group_one = lax.optimization_barrier((mlp_weight, group_one))
    hidden_weight = lax.all_gather(mlp_weight, "tower", axis=0, tiled=True)

    slot_data = jnp.concatenate([group_one[0], group_two[0]], 0)
    slot_count = slot_data.shape[0]
    row_count = slot_data.shape[1]
    orders = feature_order[0]
    bias_blocks = cross_bias[0].reshape(slot_count, entry_count)

    bases = []
    low_sum = None
    for rows, features in parts:
        one_hot = (orders[None, :] == features[:, None]).astype(jnp.bfloat16)
        base = jnp.einsum("fs,sre->rfe", one_hot, slot_data, preferred_element_type=jnp.float32)
        base = base.astype(jnp.bfloat16).reshape(row_count, features.shape[0] * entry_count)
        bases.append(base)
        term = jnp.dot(base, rows[:, :rank], preferred_element_type=jnp.float32)
        low_sum = term if low_sum is None else low_sum + term
    low_rank = low_sum.astype(jnp.bfloat16)

    squeezed = None
    for (rows, features), base in zip(parts, bases):
        lifted = lax.dot_general(
            low_rank,
            rows[:, rank : 2 * rank],
            (((1,), (1,)), ((), ())),
            preferred_element_type=jnp.float32,
        )
        shift_row = bias_blocks[features].reshape(features.shape[0] * entry_count)
        columns = base.astype(jnp.float32)
        crossed = (columns * (lifted + shift_row[None, :]) + columns).astype(jnp.bfloat16)
        term = jnp.dot(crossed, rows[:, 2 * rank :], preferred_element_type=jnp.float32)
        squeezed = term if squeezed is None else squeezed + term
    compressed = (squeezed + compress_bias[0][None, :]).astype(jnp.bfloat16)
    gathered = lax.all_to_all(compressed, "tower", split_axis=0, concat_axis=1, tiled=True)
    local_rows = gathered.shape[0]
    vector_count = gathered.shape[1] // entry_count
    vectors = gathered.reshape(local_rows, vector_count, entry_count)
    gram_matrix = jnp.einsum(
        "bie,bje->bij", vectors, vectors, preferred_element_type=jnp.float32
    ) * (1.0 / math.sqrt(entry_count))
    pair_terms = gram_matrix.reshape(local_rows, vector_count * vector_count)[
        :, pair_positions(vector_count)
    ]
    joined = jnp.concatenate([dense_vector.astype(jnp.float32), pair_terms], 1).astype(jnp.bfloat16)
    hidden_units = mlp_weight.shape[1]
    width_here = hidden_weight.shape[0]
    columns = lax.slice_in_dim(joined, 0, width_here, axis=1)
    hidden_sum = jnp.zeros((local_rows, hidden_units), jnp.float32) + jnp.dot(
        columns, hidden_weight, preferred_element_type=jnp.float32
    )
    return jax.nn.relu(hidden_sum + mlp_bias[None, :]).astype(jnp.bfloat16)


def solution(mesh):
    in_specs = (
        P("tower", "feat", "groups", None),
        P("tower", "feat", "groups", None),
        P("tower", None),
        P("tower", "feat", None),
        P("tower", "feat", None),
        P("tower", None),
        P("tower", "feat", None),
        P("tower", None),
        P(("groups", "feat", "tower"), None),
        P("tower", None),
        P(),
    )
    out_specs = P(("groups", "feat", "tower"), None)
    body = functools.partial(
        on_device, feat_count=mesh.shape["feat"], group_count=mesh.shape["groups"]
    )
    return jax.shard_map(body, mesh=mesh, in_specs=in_specs, out_specs=out_specs, check_vma=False)
```

time: 244 us -> 225 us (0.922)
  waiting for transfers between devices: 159 us -> 123 us
  matrix products: 14.1 us -> 27.7 us
  between operations: 13.6 us -> 0.52 us
  starting transfers between devices: 17.4 us -> 28.5 us
  local copies, waits for them, and re-layouts: 26.1 us -> 30.3 us
    all_gather x2 -> x0, waiting for transfers between devices: 69.6 us -> none  [gather_rows(): own = lax.all_gather(part, 'feat', axis=0, tiled=True)]
    ppermute x2 -> x6, waiting for transfers between devices: 31.3 us -> 94.4 us  [the longest x3 70.5 us: weight_parts(): travelling = lax.ppermute(travelling, 'feat', ring)]
    all_to_all x1, waiting for transfers between devices: 58.1 us -> 28.8 us  [on_device(): lax.all_to_all(pooled_first, 'feat', split_axis=2, concat_axis=1, tiled=T...]
    dot_general x5 -> x21, matrix products: 12.8 us -> 26.4 us  [the longest x7 15.6 us: on_device(): jnp.dot(crossed, rows[:, 2 * rank:], preferred_element_type=jnp.float32)]
    ppermute x2 -> x6, starting transfers between devices: 3.03 us -> 15.1 us  [the longest x3 10.5 us: weight_parts(): travelling = lax.ppermute(travelling, 'feat', ring)]
    gather x2 -> x7, local copies, waits for them, and re-layouts: 1.12 us -> 7.92 us  [on_device(): shift_row = bias_blocks[features].reshape(features.shape[0] * entry_count)]
    unnamed x29 -> x51, local copies, waits for them, and re-layouts: 18.1 us -> 18.6 us
  transfers between devices with their start and end apart: 7 -> 9, of which waited for: 3 -> 6; matrix products, arithmetic and copies ran while one was open for 13% -> 14% of each run, Pallas kernels for 0% -> 0%
where the time goes in v3:
time: 225 us; the launch traced here: 224 us
  waiting for transfers between devices  123 us (55%)
  local copies, waits for them, and re-layouts  30.3 us (13%)
  starting transfers between devices  28.5 us (13%)
  matrix products  27.7 us (12%)
  blocking collectives  11 us (5%)
  other arithmetic  2.96 us (1%)
    ppermute x3, waiting for transfers between devices, weight_parts(): travelling = lax.ppermute(travelling, 'feat', ring)  70.5 us
    all_to_all x1, waiting for transfers between devices, on_device(): lax.all_to_all(pooled_first, 'feat', split_axis=2, concat_axis=1, tiled=T...  28.8 us
    ppermute x3, waiting for transfers between devices, weight_parts(): forwarded = lax.ppermute(travelling, 'groups', pairs)  23.9 us
    unnamed x51, local copies, waits for them, and re-layouts  18.6 us
    dot_general x7, matrix products, on_device(): jnp.dot(crossed, rows[:, 2 * rank:], preferred_element_type=jnp.float32)  15.6 us
    all_gather x1, blocking collectives, on_device(): hidden_weight = lax.all_gather(mlp_weight, 'tower', axis=0, tiled=True)  11 us
    ppermute x3, starting transfers between devices, weight_parts(): travelling = lax.ppermute(travelling, 'feat', ring)  10.5 us
    gather x7, local copies, waits for them, and re-layouts, on_device(): shift_row = bias_blocks[features].reshape(features.shape[0] * entry_count)  7.92 us
  transfers between devices with their start and end apart: 9, of which 6 were waited for; matrix products, arithmetic and copies ran while one was open for 14% of the time, Pallas kernels for 0%

profile of v3, /device:TPU:0, one launch (start us, length us, event | category | flops | bytes accessed | tf_op | source)
XLA Modules:
  0.0 224.2 jit_solution(1227638421198470508)
XLA Ops:
  0.0 8.5 %copy.24 = bf16[1,4,1536,128]{3,1,0,2:T(4,128)(2,1)} copy(bf16[1,4,1536,128]{3,2,1,0:T(8,128)(2,1)} %param.13) | data formatting | bytes 3145728 | tf_op args[0]
  8.5 6.4 %all-to-all-start = ((bf16[1,4,1536,128]{3,1,0,2:T(4,128)(2,1)}), bf16[1,4,1536,128]{3,1,0,2:T(4,128)(2,1)S(1)}, u32[]{:S(2)}, u32[]{:S(2)}) async-start(bf16[1,4,1536,128]{3,1,0,2:T(4,128)(2,1)} %copy.24), calls=%async_computation | async-start | bytes 3145728 | tf_op jit(solution)/shard_map/all_to_all | solution.py:72
  15.0 8.2 %copy.26 = bf16[1,4,1536,128]{3,1,0,2:T(4,128)(2,1)} copy(bf16[1,4,1536,128]{3,2,1,0:T(8,128)(2,1)S(1)} %copy-done.1) | data formatting | bytes 3145728 | tf_op args[1]
  23.2 28.8 %all-to-all-done = bf16[1,4,1536,128]{3,1,0,2:T(4,128)(2,1)S(1)} async-done(((bf16[1,4,1536,128]{3,1,0,2:T(4,128)(2,1)}), bf16[1,4,1536,128]{3,1,0,2:T(4,128)(2,1)S(1)}, u32[]{:S(2)}, u32[]{:S(2)}) %all-to-all-start) | async-done | bytes 1572896 | tf_op jit(solution)/shard_map/all_to_all | solution.py:72
  51.9 3.6 %all-to-all-start.1 = ((bf16[1,4,1536,128]{3,1,0,2:T(4,128)(2,1)}), bf16[1,4,1536,128]{3,1,0,2:T(4,128)(2,1)S(1)}, u32[]{:S(2)}, u32[]{:S(2)}) async-start(bf16[1,4,1536,128]{3,1,0,2:T(4,128)(2,1)} %copy.26), calls=%async_computation.1 | async-start | bytes 3145728 | tf_op jit(solution)/shard_map/all_to_all | solution.py:73
  55.5 2.3 %fusion.32 = bf16[512,1024]{1,0:T(8,128)(2,1)} fusion(s32[]{:T(128)S(6)} %select_n.100, bf16[1024,256]{1,0:T(8,128)(2,1)} %bitcast.176, bf16[1024,256]{1,0:T(8,128)(2,1)} %bitcast.177, bf16[1024,512]{1,0:T(8,128)(2,1)} %bitcast.175), kind=kLoop, calls=%fused_computation.68 | loop fusion | flops 3145728 | bytes 3145732 | tf_op jit(solution)/shard_map/concatenate | solution.py:68
  57.8 2.0 collective-permute-start
  59.9 47.2 %collective-permute-done = bf16[512,1024]{1,0:T(8,128)(2,1)} collective-permute-done((bf16[512,1024]{1,0:T(8,128)(2,1)}, bf16[512,1024]{1,0:T(8,128)(2,1)}, u32[]{:S(2)}, u32[]{:S(2)}) %collective-permute-start) | collective-permute-done | bytes 1048608 | tf_op jit(solution)/shard_map/ppermute | solution.py:31
  107.1 6.1 %collective-permute-start.2 = (bf16[512,1024]{1,0:T(8,128)(2,1)}, bf16[512,1024]{1,0:T(8,128)(2,1)}, u32[]{:S(2)}, u32[]{:S(2)}) collective-permute-start(bf16[512,1024]{1,0:T(8,128)(2,1)} %collective-permute-done), channel_id=1, source_target_pairs={{0,4},{4,8},{8,12},{12,0},{1,5},{5,9},{9,13},{13,1},{2,6},{6,10},{... | collective-permute-start | bytes 3145736 | tf_op jit(solution)/shard_map/ppermute | solution.py:31
  123.3 11.0 %collective-permute-done.2 = bf16[512,1024]{1,0:T(8,128)(2,1)} collective-permute-done((bf16[512,1024]{1,0:T(8,128)(2,1)}, bf16[512,1024]{1,0:T(8,128)(2,1)}, u32[]{:S(2)}, u32[]{:S(2)}) %collective-permute-start.2) | collective-permute-done | bytes 1048608 | tf_op jit(solution)/shard_map/ppermute | solution.py:31
  134.3 2.5 %collective-permute-start.4 = (bf16[512,1024]{1,0:T(8,128)(2,1)}, bf16[512,1024]{1,0:T(8,128)(2,1)}, u32[]{:S(2)}, u32[]{:S(2)}) collective-permute-start(bf16[512,1024]{1,0:T(8,128)(2,1)} %collective-permute-done.2), channel_id=1, source_target_pairs={{0,4},{4,8},{8,12},{12,0},{1,5},{5,9},{9,13},{13,1},{2,6},{6,10},{... | collective-permute-start | bytes 3145736 | tf_op jit(solution)/shard_map/ppermute | solution.py:31
  138.3 1.7 copy.25
  147.2 12.3 %collective-permute-done.4 = bf16[512,1024]{1,0:T(8,128)(2,1)} collective-permute-done((bf16[512,1024]{1,0:T(8,128)(2,1)}, bf16[512,1024]{1,0:T(8,128)(2,1)}, u32[]{:S(2)}, u32[]{:S(2)}) %collective-permute-start.4) | collective-permute-done | bytes 1048608 | tf_op jit(solution)/shard_map/ppermute | solution.py:31
  164.7 5.9 %collective-permute-done.3 = bf16[512,1024]{1,0:T(8,128)(2,1)} collective-permute-done((bf16[512,1024]{1,0:T(8,128)(2,1)}, bf16[512,1024]{1,0:T(8,128)(2,1)}, u32[]{:S(2)}, u32[]{:S(2)}) %collective-permute-start.3) | collective-permute-done | bytes 1048608 | tf_op jit(solution)/shard_map/ppermute | solution.py:38
  171.9 18.0 %collective-permute-done.5 = bf16[512,1024]{1,0:T(8,128)(2,1)S(1)} collective-permute-done((bf16[512,1024]{1,0:T(8,128)(2,1)}, bf16[512,1024]{1,0:T(8,128)(2,1)S(1)}, u32[]{:S(2)}, u32[]{:S(2)}) %collective-permute-start.5) | collective-permute-done | bytes 1048608 | tf_op jit(solution)/shard_map/ppermute | solution.py:38
  190.8 2.3 %fusion.1 = f32[384,512]{1,0:T(8,128)S(1)} fusion(bf16[384,256]{1,0:T(8,128)(2,1)S(1)} %fusion.30, f32[1024]{0:T(1024)S(1)} %bitcast.189, bf16[48,8,8,128]{3,2,1,0:T(8,128)(2,1)} %bitcast.202, bf16[1,1024,512]{2,1,0:T(8,128)(2,1)} %param.19, bf16[1,1024,256]{2,1,0:T(8,128)(2,1)S(1)} %copy-done.4), kind=kOutput, calls=%fused_computation.15 | convolution fusion | flops 605945856 | bytes 3346432 | tf_op jit(solution)/shard_map/dot_general | solution.py:106
  193.1 2.7 %fusion.25 = f32[384,512]{1,0:T(8,128)} fusion(bf16[384,256]{1,0:T(8,128)(2,1)S(1)} %fusion.30, bf16[512,1024]{1,0:T(8,128)(2,1)} %collective-permute-done.2, f32[512]{0:T(512)S(1)} %bitcast.191, bf16[48,8,4,128]{3,2,1,0:T(4,128)(2,1)} %bitcast.181), kind=kOutput, calls=%fused_computation.56 | convolution fusion | flops 302972928 | bytes 2164736 | tf_op jit(solution)/shard_map/dot_general | solution.py:106
  195.9 2.6 %fusion.24 = f32[384,512]{1,0:T(8,128)} fusion(bf16[384,256]{1,0:T(8,128)(2,1)S(1)} %fusion.30, bf16[512,1024]{1,0:T(8,128)(2,1)} %collective-permute-done.4, f32[512]{0:T(512)S(1)} %bitcast.192, bf16[48,8,4,128]{3,2,1,0:T(4,128)(2,1)S(1)} %bitcast.183), kind=kOutput, calls=%fused_computation.55 | convolution fusion | flops 302972928 | bytes 2164736 | tf_op jit(solution)/shard_map/dot_general | solution.py:106
  198.5 1.7 convolution_add_fusion.3
  200.2 1.9 fusion.2
  202.1 1.9 fusion.3
  204.1 2.5 %fusion.23 = bf16[384,512]{1,0:T(8,128)(2,1)} fusion(f32[384,512]{1,0:T(8,128)S(1)} %fusion.3, bf16[384,256]{1,0:T(8,128)(2,1)S(1)} %fusion.30, bf16[512,1024]{1,0:T(8,128)(2,1)} %copy-done.9, f32[512]{0:T(512)S(1)} %bitcast.193, f32[512]{0:T(512)S(1)} %bitcast.190, bf16[48,8,4,128]{3,2,1,0:T(4,128)(2,1)S(1)} %bitcast.179), kind=kOutput, calls=%fused_computation.48 | convolution fusion | flops 303562752 | bytes 2560000 | tf_op jit(solution)/shard_map/dot_general | solution.py:106
  206.6 3.5 %all-to-all-start.2 = ((bf16[4,96,512]{2,1,0:T(8,128)(2,1)}), bf16[4,96,512]{2,1,0:T(8,128)(2,1)S(1)}, u32[]{:S(2)}, u32[]{:S(2)}) async-start(bf16[4,96,512]{2,1,0:T(8,128)(2,1)} %bitcast.41), calls=%async_computation.2 | async-start | bytes 786432 | tf_op jit(solution)/shard_map/all_to_all | solution.py:109
  210.1 11.0 %all-gather = bf16[4,62,1024]{2,1,0:T(8,128)(2,1)S(1)} all-gather(bf16[1,62,1024]{2,1,0:T(8,128)(2,1)S(1)} %bitcast.184), channel_id=1, replica_groups=mesh['groups'=2,'feat'=4,'tower'=4] {'tower'}, dimensions={0}, use_global_device_ids=true | all-gather | bytes 634880 | tf_op jit(solution)/shard_map/all_gather | solution.py:76
  (103 shorter events, 29.2 us)
Async XLA Ops:
  0.0 113.2 %copy-start = (f32[1,4096]{1,0:T(1,128)S(1)}, f32[1,4096]{1,0:T(1,128)}, u32[]{:S(2)}) copy-start(f32[1,4096]{1,0:T(1,128)} %param.18) | copy-start | bytes 49156
  8.5 6.5 %copy-start.1 = (bf16[1,4,1536,128]{3,2,1,0:T(8,128)(2,1)S(1)}, bf16[1,4,1536,128]{3,2,1,0:T(8,128)(2,1)}, u32[]{:S(2)}) copy-start(bf16[1,4,1536,128]{3,2,1,0:T(8,128)(2,1)} %param.14) | copy-start | bytes 4718596
  8.5 43.4 %all-to-all-start = ((bf16[1,4,1536,128]{3,1,0,2:T(4,128)(2,1)}), bf16[1,4,1536,128]{3,1,0,2:T(4,128)(2,1)S(1)}, u32[]{:S(2)}, u32[]{:S(2)}) async-start(bf16[1,4,1536,128]{3,1,0,2:T(4,128)(2,1)} %copy.24), calls=%async_computation | async-start | bytes 3145728 | tf_op jit(solution)/shard_map/all_to_all | solution.py:72
  51.9 88.0 %all-to-all-start.1 = ((bf16[1,4,1536,128]{3,1,0,2:T(4,128)(2,1)}), bf16[1,4,1536,128]{3,1,0,2:T(4,128)(2,1)S(1)}, u32[]{:S(2)}, u32[]{:S(2)}) async-start(bf16[1,4,1536,128]{3,1,0,2:T(4,128)(2,1)} %copy.26), calls=%async_computation.1 | async-start | bytes 3145728 | tf_op jit(solution)/shard_map/all_to_all | solution.py:73
  57.8 49.3 %collective-permute-start = (bf16[512,1024]{1,0:T(8,128)(2,1)}, bf16[512,1024]{1,0:T(8,128)(2,1)}, u32[]{:S(2)}, u32[]{:S(2)}) collective-permute-start(bf16[512,1024]{1,0:T(8,128)(2,1)} %fusion.32), channel_id=1, source_target_pairs={{0,4},{4,8},{8,12},{12,0},{1,5},{5,9},{9,13},{13,1},{2,6},{6,10},{... | collective-permute-start | bytes 3145736 | tf_op jit(solution)/shard_map/ppermute | solution.py:31
  107.1 27.1 %collective-permute-start.2 = (bf16[512,1024]{1,0:T(8,128)(2,1)}, bf16[512,1024]{1,0:T(8,128)(2,1)}, u32[]{:S(2)}, u32[]{:S(2)}) collective-permute-start(bf16[512,1024]{1,0:T(8,128)(2,1)} %collective-permute-done), channel_id=1, source_target_pairs={{0,4},{4,8},{8,12},{12,0},{1,5},{5,9},{9,13},{13,1},{2,6},{6,10},{... | collective-permute-start | bytes 3145736 | tf_op jit(solution)/shard_map/ppermute | solution.py:31
  121.8 40.5 %collective-permute-start.1 = (bf16[512,1024]{1,0:T(8,128)(2,1)}, bf16[512,1024]{1,0:T(8,128)(2,1)}, u32[]{:S(2)}, u32[]{:S(2)}) collective-permute-start(bf16[512,1024]{1,0:T(8,128)(2,1)} %collective-permute-done), channel_id=1, source_target_pairs={{0,16},{16,0},{1,17},{17,1},{2,18},{18,2},{3,19},{19,3},{4,20},{20... | collective-permute-start | bytes 3145736 | tf_op jit(solution)/shard_map/ppermute | solution.py:38
  134.3 25.3 %collective-permute-start.4 = (bf16[512,1024]{1,0:T(8,128)(2,1)}, bf16[512,1024]{1,0:T(8,128)(2,1)}, u32[]{:S(2)}, u32[]{:S(2)}) collective-permute-start(bf16[512,1024]{1,0:T(8,128)(2,1)} %collective-permute-done.2), channel_id=1, source_target_pairs={{0,4},{4,8},{8,12},{12,0},{1,5},{5,9},{9,13},{13,1},{2,6},{6,10},{... | collective-permute-start | bytes 3145736 | tf_op jit(solution)/shard_map/ppermute | solution.py:31
  136.7 33.9 %collective-permute-start.3 = (bf16[512,1024]{1,0:T(8,128)(2,1)}, bf16[512,1024]{1,0:T(8,128)(2,1)}, u32[]{:S(2)}, u32[]{:S(2)}) collective-permute-start(bf16[512,1024]{1,0:T(8,128)(2,1)} %collective-permute-done.2), channel_id=1, source_target_pairs={{0,16},{16,0},{1,17},{17,1},{2,18},{18,2},{3,19},{19,3},{4,20},{20... | collective-permute-start | bytes 3145736 | tf_op jit(solution)/shard_map/ppermute | solution.py:38
  142.5 4.3 %copy-start.22 = (bf16[384,128,8]{1,2,0:T(8,128)(2,1)}, bf16[384,128,8]{1,2,0:T(8,128)(2,1)S(1)}, u32[]{:S(2)}) copy-start(bf16[384,128,8]{1,2,0:T(8,128)(2,1)S(1)} %convolution_convert_fusion) | copy-start | bytes 2359300
  143.1 2.4 %copy-start.5 = (bf16[384,128,4]{1,2,0:T(4,128)(2,1)}, bf16[384,128,4]{1,2,0:T(4,128)(2,1)S(1)}, u32[]{:S(2)}) copy-start(bf16[384,128,4]{1,2,0:T(4,128)(2,1)S(1)} %convolution_convert_fusion.4) | copy-start | bytes 1179652
  144.3 19.1 %copy-start.6 = (bf16[384,128,4]{1,2,0:T(4,128)(2,1)}, bf16[384,128,4]{1,2,0:T(4,128)(2,1)S(1)}, u32[]{:S(2)}) copy-start(bf16[384,128,4]{1,2,0:T(4,128)(2,1)S(1)} %convolution_convert_fusion.2) | copy-start | bytes 1179652
  159.5 30.3 %collective-permute-start.5 = (bf16[512,1024]{1,0:T(8,128)(2,1)}, bf16[512,1024]{1,0:T(8,128)(2,1)S(1)}, u32[]{:S(2)}, u32[]{:S(2)}) collective-permute-start(bf16[512,1024]{1,0:T(8,128)(2,1)} %collective-permute-done.4), channel_id=1, source_target_pairs={{0,16},{16,0},{1,17},{17,1},{2,18},{18,2},{3,19},{19,3},{4,20},{20... | collective-permute-start | bytes 3145736 | tf_op jit(solution)/shard_map/ppermute | solution.py:38
  164.7 26.1 %copy-start.4 = (bf16[1,1024,256]{2,1,0:T(8,128)(2,1)S(1)}, bf16[1,1024,256]{2,1,0:T(8,128)(2,1)}, u32[]{:S(2)}) copy-start(bf16[1,1024,256]{2,1,0:T(8,128)(2,1)} %param.17) | copy-start | bytes 1572868
  164.7 26.1 %copy-start.15 = (f32[8,128]{1,0:T(8,128)S(1)}, f32[8,128]{1,0:T(8,128)}, u32[]{:S(2)}) copy-start(f32[8,128]{1,0:T(8,128)} %gather_fusion) | copy-start | bytes 12292
  190.8 2.3 %copy-start.17 = (f32[4,128]{1,0:T(4,128)S(1)}, f32[4,128]{1,0:T(4,128)}, u32[]{:S(2)}) copy-start(f32[4,128]{1,0:T(4,128)} %gather_fusion.3) | copy-start | bytes 6148
  193.1 2.8 %copy-start.7 = (bf16[384,128,4]{1,2,0:T(4,128)(2,1)S(1)}, bf16[384,128,4]{1,2,0:T(4,128)(2,1)}, u32[]{:S(2)}) copy-start(bf16[384,128,4]{1,2,0:T(4,128)(2,1)} %copy-done.6) | copy-start | bytes 1179652
  193.1 2.8 %copy-start.18 = (f32[4,128]{1,0:T(4,128)S(1)}, f32[4,128]{1,0:T(4,128)}, u32[]{:S(2)}) copy-start(f32[4,128]{1,0:T(4,128)} %gather_fusion.5) | copy-start | bytes 6148
  195.9 2.6 %copy-start.11 = (f32[4,128]{1,0:T(4,128)S(1)}, f32[4,128]{1,0:T(4,128)}, u32[]{:S(2)}) copy-start(f32[4,128]{1,0:T(4,128)} %gather_fusion.1) | copy-start | bytes 6148
  204.1 6.0 %copy-start.19 = (s32[120]{0:T(128)S(1)}, s32[120]{0:T(128)}, u32[]{:S(2)}) copy-start(s32[120]{0:T(128)} %constant.90) | copy-start | bytes 1444
  204.1 6.0 %copy-start.8 = (bf16[62,1024]{1,0:T(8,128)(2,1)S(1)}, bf16[62,1024]{1,0:T(8,128)(2,1)}, u32[]{:S(2)}) copy-start(bf16[62,1024]{1,0:T(8,128)(2,1)} %param.22) | copy-start | bytes 380932
  206.6 14.7 %all-to-all-start.2 = ((bf16[4,96,512]{2,1,0:T(8,128)(2,1)}), bf16[4,96,512]{2,1,0:T(8,128)(2,1)S(1)}, u32[]{:S(2)}, u32[]{:S(2)}) async-start(bf16[4,96,512]{2,1,0:T(8,128)(2,1)} %bitcast.41), calls=%async_computation.2 | async-start | bytes 786432 | tf_op jit(solution)/shard_map/all_to_all | solution.py:109
  221.3 2.0 copy-start.10
  221.3 2.0 copy-start.14
  (9 other events, 13.8 us)

commit v4 on v3

--- a/solution.py
+++ b/solution.py
@@ -43,6 +43,33 @@
     return parts
 
 
+def exchange_rows(first, second, feat_count):
+    slots_here, row_count, _ = first.shape
+    share = row_count // feat_count
+    owner = lax.axis_index("feat")
+    pieces, ids = [], []
+    for shift in range(feat_count):
+        target = (owner + shift) % feat_count
+        piece = jnp.concatenate(
+            [
+                lax.dynamic_slice_in_dim(first, target * share, share, axis=1),
+                lax.dynamic_slice_in_dim(second, target * share, share, axis=1),
+            ],
+            0,
+        )
+        if shift:
+            piece = lax.ppermute(
+                piece, "feat", [(source, (source + shift) % feat_count) for source in range(feat_count)]
+            )
+        source = (owner - shift) % feat_count
+        local = jnp.arange(slots_here, dtype=jnp.int32)
+        ids.append(
+            jnp.concatenate([source * slots_here + local, (feat_count + source) * slots_here + local])
+        )
+        pieces.append(piece)
+    return jnp.concatenate(pieces, 0), jnp.concatenate(ids)
+
+
 def on_device(
     pooled_first,
     pooled_second,
@@ -58,6 +85,7 @@
     *,
     feat_count,
     group_count,
+    tower_count,
 ):
     entry_count = pooled_first.shape[3]
     rows_here = cross_down.shape[1]
@@ -65,20 +93,18 @@
     split = rows_here % group_count == 0 and (rows_here // group_count) % entry_count == 0
     share_count = group_count if split else 1
 
+    hidden_pieces = [mlp_weight]
+    for shift in range(1, tower_count):
+        pairs = [(source, (source + shift) % tower_count) for source in range(tower_count)]
+        hidden_pieces.append(lax.ppermute(mlp_weight, "tower", pairs))
+
     weights_here = jnp.concatenate([cross_down[0], cross_up[0], compress_weight[0]], axis=1)
     parts = weight_parts(weights_here, feat_count, group_count, share_count, entry_count)
 
-    group_one, group_two = (
-        lax.all_to_all(pooled_first, "feat", split_axis=2, concat_axis=1, tiled=True),
-        lax.all_to_all(pooled_second, "feat", split_axis=2, concat_axis=1, tiled=True),
-    )
-    mlp_weight, group_one = lax.optimization_barrier((mlp_weight, group_one))
-    hidden_weight = lax.all_gather(mlp_weight, "tower", axis=0, tiled=True)
-
-    slot_data = jnp.concatenate([group_one[0], group_two[0]], 0)
+    slot_data, slot_ids = exchange_rows(pooled_first[0], pooled_second[0], feat_count)
     slot_count = slot_data.shape[0]
     row_count = slot_data.shape[1]
-    orders = feature_order[0]
+    orders = feature_order[0][slot_ids]
     bias_blocks = cross_bias[0].reshape(slot_count, entry_count)
 
     bases = []
@@ -118,11 +144,13 @@
     ]
     joined = jnp.concatenate([dense_vector.astype(jnp.float32), pair_terms], 1).astype(jnp.bfloat16)
     hidden_units = mlp_weight.shape[1]
-    width_here = hidden_weight.shape[0]
-    columns = lax.slice_in_dim(joined, 0, width_here, axis=1)
-    hidden_sum = jnp.zeros((local_rows, hidden_units), jnp.float32) + jnp.dot(
-        columns, hidden_weight, preferred_element_type=jnp.float32
-    )
+    hidden_rows = mlp_weight.shape[0]
+    tower = lax.axis_index("tower")
+    hidden_sum = jnp.zeros((local_rows, hidden_units), jnp.float32)
+    for shift, rows in enumerate(hidden_pieces):
+        source = (tower - shift) % tower_count
+        columns = lax.dynamic_slice_in_dim(joined, source * hidden_rows, hidden_rows, axis=1)
+        hidden_sum = hidden_sum + jnp.dot(columns, rows, preferred_element_type=jnp.float32)
     return jax.nn.relu(hidden_sum + mlp_bias[None, :]).astype(jnp.bfloat16)
 
 
@@ -142,6 +170,8 @@
     )
     out_specs = P(("groups", "feat", "tower"), None)
     body = functools.partial(
-        on_device, feat_count=mesh.shape["feat"], group_count=mesh.shape["groups"]
+        on_device, feat_count=mesh.shape["feat"],
+        group_count=mesh.shape["groups"],
+        tower_count=mesh.shape["tower"],
     )
     return jax.shard_map(body, mesh=mesh, in_specs=in_specs, out_specs=out_specs, check_vma=False)

time: 225 us -> 244 us (1.084)
  waiting for transfers between devices: 123 us -> 156 us
  blocking collectives: 11 us -> 0 us
  starting transfers between devices: 28.5 us -> 19.6 us
  other arithmetic: 2.96 us -> 10 us
    ppermute x0 -> x6, waiting for transfers between devices: none -> 68.2 us  [the longest x3 65.8 us: exchange_rows(): lax.ppermute(piece, 'feat', [(source, (source + shift) % feat_count) for...]
    all_to_all x2 -> x0, waiting for transfers between devices: 28.8 us -> none  [the longest x1 28.8 us: on_device(): lax.all_to_all(pooled_first, 'feat', split_axis=2, concat_axis=1, tiled=T...]
    ppermute x3, waiting for transfers between devices: 70.5 us -> 43.3 us  [weight_parts(): travelling = lax.ppermute(travelling, 'feat', ring)]
    ppermute x3, waiting for transfers between devices: 23.9 us -> 40.7 us  [weight_parts(): forwarded = lax.ppermute(travelling, 'groups', pairs)]
    unnamed x51 -> x86, local copies, waits for them, and re-layouts: 18.6 us -> 1.88 us
    concatenate x0 -> x2, local copies, waits for them, and re-layouts: none -> 11.9 us  [exchange_rows(): return (jnp.concatenate(pieces, 0), jnp.concatenate(ids))]
    all_gather x1 -> x0, blocking collectives: 11 us -> none  [on_device(): hidden_weight = lax.all_gather(mlp_weight, 'tower', axis=0, tiled=True)]
    all_to_all x2 -> x0, starting transfers between devices: 10 us -> none  [the longest x1 6.45 us: on_device(): lax.all_to_all(pooled_first, 'feat', split_axis=2, concat_axis=1, tiled=T...]
  transfers between devices with their start and end apart: 9 -> 13, of which waited for: 6 -> 7; matrix products, arithmetic and copies ran while one was open for 14% -> 17% of each run, Pallas kernels for 0% -> 0%
where the time goes in v4:
time: 244 us; the launch traced here: 243 us
  waiting for transfers between devices  156 us (64%)
  local copies, waits for them, and re-layouts  29.7 us (12%)
  matrix products  26.3 us (11%)
  starting transfers between devices  19.6 us (8%)
  other arithmetic  10 us (4%)
    ppermute x3, waiting for transfers between devices, exchange_rows(): lax.ppermute(piece, 'feat', [(source, (source + shift) % feat_count) for...  65.8 us
    ppermute x3, waiting for transfers between devices, weight_parts(): travelling = lax.ppermute(travelling, 'feat', ring)  43.3 us
    ppermute x3, waiting for transfers between devices, weight_parts(): forwarded = lax.ppermute(travelling, 'groups', pairs)  40.7 us
    dot_general x7, matrix products, on_device(): jnp.dot(crossed, rows[:, 2 * rank:], preferred_element_type=jnp.float32)  16.6 us
    concatenate x2, local copies, waits for them, and re-layouts, exchange_rows(): return (jnp.concatenate(pieces, 0), jnp.concatenate(ids))  11.9 us
    gather x7, local copies, waits for them, and re-layouts, on_device(): shift_row = bias_blocks[features].reshape(features.shape[0] * entry_count)  7.79 us
    ppermute x3, starting transfers between devices, exchange_rows(): lax.ppermute(piece, 'feat', [(source, (source + shift) % feat_count) for...  6.07 us
  transfers between devices with their start and end apart: 13, of which 7 were waited for; matrix products, arithmetic and copies ran while one was open for 17% of the time, Pallas kernels for 0%

profile of v4, /device:TPU:0, one launch (start us, length us, event | category | flops | bytes accessed | tf_op | source)
XLA Modules:
  0.0 242.8 jit_solution(1313915244395497152)
XLA Ops:
  0.0 2.1 constant_dynamic-slice_fusion
  2.7 1.3 pad_maximum_fusion.2
  4.1 5.1 %collective-permute-start.2 = (bf16[8,384,128]{2,0,1:T(8,128)(2,1)}, bf16[8,384,128]{2,0,1:T(8,128)(2,1)}, u32[]{:S(2)}, u32[]{:S(2)}) collective-permute-start(bf16[8,384,128]{2,0,1:T(8,128)(2,1)} %pad_maximum_fusion.2), channel_id=1, source_target_pairs={{0,12},{4,0},{8,4},{12,8},{1,13},{5,1},{9,5},{13,9},{2,14},{6,2},{... | collective-permute-start | bytes 2359304 | tf_op jit(solution)/shard_map/ppermute | solution.py:61
  14.0 2.1 fusion.34
  16.1 2.5 %collective-permute-start.3 = (bf16[512,1024]{1,0:T(8,128)(2,1)}, bf16[512,1024]{1,0:T(8,128)(2,1)}, u32[]{:S(2)}, u32[]{:S(2)}) collective-permute-start(bf16[512,1024]{1,0:T(8,128)(2,1)} %fusion.34), channel_id=1, source_target_pairs={{0,4},{4,8},{8,12},{12,0},{1,5},{5,9},{9,13},{13,1},{2,6},{6,10},{... | collective-permute-start | bytes 3145736 | tf_op jit(solution)/shard_map/ppermute | solution.py:31
  33.2 65.8 %collective-permute-done.1 = bf16[8,384,128]{2,0,1:T(8,128)(2,1)S(1)} collective-permute-done((bf16[8,384,128]{2,0,1:T(8,128)(2,1)}, bf16[8,384,128]{2,0,1:T(8,128)(2,1)S(1)}, u32[]{:S(2)}, u32[]{:S(2)}) %collective-permute-start.1) | collective-permute-done | bytes 786464 | tf_op jit(solution)/shard_map/ppermute | solution.py:61
  100.0 11.8 %concatenate.60 = bf16[32,384,128]{2,0,1:T(8,128)(2,1)S(1)} concatenate(bf16[4,384,128]{2,0,1:T(4,128)(2,1)} %bitcast.202, bf16[4,384,128]{2,0,1:T(4,128)(2,1)S(1)} %bitcast.201, bf16[8,384,128]{2,0,1:T(8,128)(2,1)} %collective-permute-done, bf16[8,384,128]{2,0,1:T(8,128)(2,1)} %copy-done.16, bf16[8,384,128]{2,0,1:T(8,128)(2,1)} %collective-permute-done.2), dimensions={0} | concatenate | bytes 6291456 | tf_op jit(solution)/shard_map/concatenate | solution.py:70
  115.1 22.8 %collective-permute-done.5 = bf16[512,1024]{1,0:T(8,128)(2,1)S(1)} collective-permute-done((bf16[512,1024]{1,0:T(8,128)(2,1)}, bf16[512,1024]{1,0:T(8,128)(2,1)S(1)}, u32[]{:S(2)}, u32[]{:S(2)}) %collective-permute-start.5) | collective-permute-done | bytes 1048608 | tf_op jit(solution)/shard_map/ppermute | solution.py:31
  139.1 1.6 collective-permute-start.4
  142.3 20.5 %collective-permute-done.7 = bf16[512,1024]{1,0:T(8,128)(2,1)S(1)} collective-permute-done((bf16[512,1024]{1,0:T(8,128)(2,1)S(1)}, bf16[512,1024]{1,0:T(8,128)(2,1)S(1)}, u32[]{:S(2)}, u32[]{:S(2)}) %collective-permute-start.7) | collective-permute-done | bytes 1048608 | tf_op jit(solution)/shard_map/ppermute | solution.py:31
  162.8 1.5 collective-permute-start.8
  166.5 21.5 %collective-permute-done.6 = bf16[512,1024]{1,0:T(8,128)(2,1)S(1)} collective-permute-done((bf16[512,1024]{1,0:T(8,128)(2,1)S(1)}, bf16[512,1024]{1,0:T(8,128)(2,1)S(1)}, u32[]{:S(2)}, u32[]{:S(2)}) %collective-permute-start.6) | collective-permute-done | bytes 1048608 | tf_op jit(solution)/shard_map/ppermute | solution.py:38
  188.3 19.2 %collective-permute-done.8 = bf16[512,1024]{1,0:T(8,128)(2,1)S(1)} collective-permute-done((bf16[512,1024]{1,0:T(8,128)(2,1)S(1)}, bf16[512,1024]{1,0:T(8,128)(2,1)S(1)}, u32[]{:S(2)}, u32[]{:S(2)}) %collective-permute-start.8) | collective-permute-done | bytes 1048608 | tf_op jit(solution)/shard_map/ppermute | solution.py:38
  208.5 2.9 %fusion.1 = f32[384,512]{1,0:T(8,128)} fusion(bf16[384,256]{1,0:T(8,128)(2,1)S(1)} %fusion.32, f32[1024]{0:T(1024)S(1)} %bitcast.225, bf16[48,8,8,128]{3,2,1,0:T(8,128)(2,1)} %bitcast.218, bf16[1,1024,512]{2,1,0:T(8,128)(2,1)S(1)} %copy-done.13, bf16[1,1024,256]{2,1,0:T(8,128)(2,1)S(1)} %copy-done.20), kind=kOutput, calls=%fused_computation.15 | convolution fusion | flops 605945856 | bytes 3346432 | tf_op jit(solution)/shard_map/dot_general | solution.py:132
  211.4 2.7 %fusion.25 = f32[384,512]{1,0:T(8,128)} fusion(bf16[384,256]{1,0:T(8,128)(2,1)S(1)} %fusion.32, bf16[512,1024]{1,0:T(8,128)(2,1)} %copy-done.24, f32[512]{0:T(512)S(1)} %bitcast.227, bf16[48,8,4,128]{3,2,1,0:T(4,128)(2,1)S(1)} %bitcast.212), kind=kOutput, calls=%fused_computation.56 | convolution fusion | flops 302972928 | bytes 2164736 | tf_op jit(solution)/shard_map/dot_general | solution.py:132
  214.1 1.7 fusion.24
  215.8 1.9 convolution_add_fusion.3
  217.8 2.0 fusion.2
  219.8 2.6 %fusion.3 = f32[384,512]{1,0:T(8,128)} fusion(f32[384,512]{1,0:T(8,128)S(1)} %fusion.24, f32[384,512]{1,0:T(8,128)S(1)} %fusion.2, bf16[384,256]{1,0:T(8,128)(2,1)S(1)} %fusion.32, bf16[512,1024]{1,0:T(8,128)(2,1)} %copy-done.15, f32[512]{0:T(512)S(1)} %bitcast.222, bf16[48,8,4,128]{3,2,1,0:T(4,128)(2,1)S(1)} %bitcast.197), kind=kOutput, calls=%fused_computation.22 | convolution fusion | flops 303366144 | bytes 3737600 | tf_op jit(solution)/shard_map/dot_general | solution.py:132
  222.5 2.7 %fusion.23 = bf16[384,512]{1,0:T(8,128)(2,1)} fusion(f32[384,512]{1,0:T(8,128)} %fusion.3, bf16[384,256]{1,0:T(8,128)(2,1)S(1)} %fusion.32, bf16[512,1024]{1,0:T(8,128)(2,1)} %copy-done.23, f32[512]{0:T(512)S(1)} %bitcast.229, f32[512]{0:T(512)S(1)} %bitcast.226, bf16[48,8,4,128]{3,2,1,0:T(4,128)(2,1)S(1)} %bitcast.210), kind=kOutput, calls=%fused_computation.48 | convolution fusion | flops 303562752 | bytes 2560000 | tf_op jit(solution)/shard_map/dot_general | solution.py:132
  225.2 3.6 %all-to-all-start = ((bf16[4,96,512]{2,1,0:T(8,128)(2,1)}), bf16[4,96,512]{2,1,0:T(8,128)(2,1)S(1)}, u32[]{:S(2)}, u32[]{:S(2)}) async-start(bf16[4,96,512]{2,1,0:T(8,128)(2,1)} %bitcast.51), calls=%async_computation | async-start | bytes 786432 | tf_op jit(solution)/shard_map/all_to_all | solution.py:135
  230.6 1.9 collective-permute-start.10
  232.6 4.1 %all-to-all-done = bf16[4,96,512]{2,1,0:T(8,128)(2,1)S(1)} async-done(((bf16[4,96,512]{2,1,0:T(8,128)(2,1)}), bf16[4,96,512]{2,1,0:T(8,128)(2,1)S(1)}, u32[]{:S(2)}, u32[]{:S(2)}) %all-to-all-start) | async-done | bytes 393248 | tf_op jit(solution)/shard_map/all_to_all | solution.py:135
  239.5 2.3 collective-permute-done.10
  (167 shorter events, 35.7 us)
Async XLA Ops:
  4.1 29.1 %collective-permute-start.2 = (bf16[8,384,128]{2,0,1:T(8,128)(2,1)}, bf16[8,384,128]{2,0,1:T(8,128)(2,1)}, u32[]{:S(2)}, u32[]{:S(2)}) collective-permute-start(bf16[8,384,128]{2,0,1:T(8,128)(2,1)} %pad_maximum_fusion.2), channel_id=1, source_target_pairs={{0,12},{4,0},{8,4},{12,8},{1,13},{5,1},{9,5},{13,9},{2,14},{6,2},{... | collective-permute-start | bytes 2359304 | tf_op jit(solution)/shard_map/ppermute | solution.py:61
  11.1 88.0 %collective-permute-start.1 = (bf16[8,384,128]{2,0,1:T(8,128)(2,1)}, bf16[8,384,128]{2,0,1:T(8,128)(2,1)S(1)}, u32[]{:S(2)}, u32[]{:S(2)}) collective-permute-start(bf16[8,384,128]{2,0,1:T(8,128)(2,1)} %pad_maximum_fusion.1), channel_id=1, source_target_pairs={{0,8},{4,12},{8,0},{12,4},{1,9},{5,13},{9,1},{13,5},{2,10},{6,14},... | collective-permute-start | bytes 2359304 | tf_op jit(solution)/shard_map/ppermute | solution.py:61
  13.0 86.1 %collective-permute-start = (bf16[8,384,128]{2,0,1:T(8,128)(2,1)}, bf16[8,384,128]{2,0,1:T(8,128)(2,1)}, u32[]{:S(2)}, u32[]{:S(2)}) collective-permute-start(bf16[8,384,128]{2,0,1:T(8,128)(2,1)} %pad_maximum_fusion), channel_id=1, source_target_pairs={{0,4},{4,8},{8,12},{12,0},{1,5},{5,9},{9,13},{13,1},{2,6},{6,10},{... | collective-permute-start | bytes 2359304 | tf_op jit(solution)/shard_map/ppermute | solution.py:61
  16.1 95.7 %collective-permute-start.3 = (bf16[512,1024]{1,0:T(8,128)(2,1)}, bf16[512,1024]{1,0:T(8,128)(2,1)}, u32[]{:S(2)}, u32[]{:S(2)}) collective-permute-start(bf16[512,1024]{1,0:T(8,128)(2,1)} %fusion.34), channel_id=1, source_target_pairs={{0,4},{4,8},{8,12},{12,0},{1,5},{5,9},{9,13},{13,1},{2,6},{6,10},{... | collective-permute-start | bytes 3145736 | tf_op jit(solution)/shard_map/ppermute | solution.py:31
  111.8 26.1 %collective-permute-start.5 = (bf16[512,1024]{1,0:T(8,128)(2,1)}, bf16[512,1024]{1,0:T(8,128)(2,1)S(1)}, u32[]{:S(2)}, u32[]{:S(2)}) collective-permute-start(bf16[512,1024]{1,0:T(8,128)(2,1)} %collective-permute-done.3), channel_id=1, source_target_pairs={{0,4},{4,8},{8,12},{12,0},{1,5},{5,9},{9,13},{13,1},{2,6},{6,10},{... | collective-permute-start | bytes 3145736 | tf_op jit(solution)/shard_map/ppermute | solution.py:31
  113.1 51.2 %copy-start.4 = (bf16[384,128,4]{1,2,0:T(4,128)(2,1)}, bf16[384,128,4]{1,2,0:T(4,128)(2,1)S(1)}, u32[]{:S(2)}) copy-start(bf16[384,128,4]{1,2,0:T(4,128)(2,1)S(1)} %convolution_convert_fusion.6) | copy-start | bytes 1179652
  113.8 51.8 %copy-start.8 = (bf16[384,128,4]{1,2,0:T(4,128)(2,1)}, bf16[384,128,4]{1,2,0:T(4,128)(2,1)S(1)}, u32[]{:S(2)}) copy-start(bf16[384,128,4]{1,2,0:T(4,128)(2,1)S(1)} %convolution_convert_fusion.4) | copy-start | bytes 1179652
  114.4 23.5 %copy-start.37 = (s32[4]{0:T(128)S(1)}, s32[4]{0:T(128)}, u32[]{:S(2)}) copy-start(s32[4]{0:T(128)} %iota_add_fusion.2) | copy-start | bytes 52
  115.0 51.1 %copy-start.10 = (bf16[384,128,4]{1,2,0:T(4,128)(2,1)}, bf16[384,128,4]{1,2,0:T(4,128)(2,1)S(1)}, u32[]{:S(2)}) copy-start(bf16[384,128,4]{1,2,0:T(4,128)(2,1)S(1)} %convolution_convert_fusion.2) | copy-start | bytes 1179652
  137.9 27.7 %copy-start.24 = (bf16[512,1024]{1,0:T(8,128)(2,1)}, bf16[512,1024]{1,0:T(8,128)(2,1)S(1)}, u32[]{:S(2)}) copy-start(bf16[512,1024]{1,0:T(8,128)(2,1)S(1)} %collective-permute-done.5) | copy-start | bytes 3145732
  137.9 24.9 %collective-permute-start.7 = (bf16[512,1024]{1,0:T(8,128)(2,1)S(1)}, bf16[512,1024]{1,0:T(8,128)(2,1)S(1)}, u32[]{:S(2)}, u32[]{:S(2)}) collective-permute-start(bf16[512,1024]{1,0:T(8,128)(2,1)S(1)} %collective-permute-done.5), channel_id=1, source_target_pairs={{0,4},{4,8},{8,12},{12,0},{1,5},{5,9},{9,13},{13,1},{2,6},{6,10},{... | collective-permute-start | bytes 3145736 | tf_op jit(solution)/shard_map/ppermute | solution.py:31
  138.5 49.5 %copy-start.2 = (bf16[384,128,4]{1,2,0:T(4,128)(2,1)}, bf16[384,128,4]{1,2,0:T(4,128)(2,1)S(1)}, u32[]{:S(2)}) copy-start(bf16[384,128,4]{1,2,0:T(4,128)(2,1)S(1)} %convolution_convert_fusion.3) | copy-start | bytes 1179652
  139.1 26.7 %collective-permute-start.4 = (bf16[512,1024]{1,0:T(8,128)(2,1)}, bf16[512,1024]{1,0:T(8,128)(2,1)S(1)}, u32[]{:S(2)}, u32[]{:S(2)}) collective-permute-start(bf16[512,1024]{1,0:T(8,128)(2,1)} %collective-permute-done.3), channel_id=1, source_target_pairs={{0,16},{16,0},{1,17},{17,1},{2,18},{18,2},{3,19},{19,3},{4,20},{20... | collective-permute-start | bytes 3145736 | tf_op jit(solution)/shard_map/ppermute | solution.py:38
  141.3 66.1 %copy-start.6 = (bf16[384,128,4]{1,2,0:T(4,128)(2,1)}, bf16[384,128,4]{1,2,0:T(4,128)(2,1)S(1)}, u32[]{:S(2)}) copy-start(bf16[384,128,4]{1,2,0:T(4,128)(2,1)S(1)} %convolution_convert_fusion.1) | copy-start | bytes 1179652
  141.3 46.7 %collective-permute-start.6 = (bf16[512,1024]{1,0:T(8,128)(2,1)S(1)}, bf16[512,1024]{1,0:T(8,128)(2,1)S(1)}, u32[]{:S(2)}, u32[]{:S(2)}) collective-permute-start(bf16[512,1024]{1,0:T(8,128)(2,1)S(1)} %collective-permute-done.5), channel_id=1, source_target_pairs={{0,16},{16,0},{1,17},{17,1},{2,18},{18,2},{3,19},{19,3},{4,20},{20... | collective-permute-start | bytes 3145736 | tf_op jit(solution)/shard_map/ppermute | solution.py:38
  162.8 44.7 %collective-permute-start.8 = (bf16[512,1024]{1,0:T(8,128)(2,1)S(1)}, bf16[512,1024]{1,0:T(8,128)(2,1)S(1)}, u32[]{:S(2)}, u32[]{:S(2)}) collective-permute-start(bf16[512,1024]{1,0:T(8,128)(2,1)S(1)} %collective-permute-done.7), channel_id=1, source_target_pairs={{0,16},{16,0},{1,17},{17,1},{2,18},{18,2},{3,19},{19,3},{4,20},{20... | collective-permute-start | bytes 3145736 | tf_op jit(solution)/shard_map/ppermute | solution.py:38
  165.8 41.9 %copy-start.14 = (bf16[512,1024]{1,0:T(8,128)(2,1)}, bf16[512,1024]{1,0:T(8,128)(2,1)S(1)}, u32[]{:S(2)}) copy-start(bf16[512,1024]{1,0:T(8,128)(2,1)S(1)} %collective-permute-done.4) | copy-start | bytes 3145732
  166.1 42.3 %copy-start.13 = (bf16[1,1024,512]{2,1,0:T(8,128)(2,1)S(1)}, bf16[1,1024,512]{2,1,0:T(8,128)(2,1)}, u32[]{:S(2)}) copy-start(bf16[1,1024,512]{2,1,0:T(8,128)(2,1)} %param.19) | copy-start | bytes 3145732
  166.1 42.3 %copy-start.20 = (bf16[1,1024,256]{2,1,0:T(8,128)(2,1)S(1)}, bf16[1,1024,256]{2,1,0:T(8,128)(2,1)}, u32[]{:S(2)}) copy-start(bf16[1,1024,256]{2,1,0:T(8,128)(2,1)} %param.17) | copy-start | bytes 1572868
  166.2 42.3 %copy-start.31 = (f32[8,128]{1,0:T(8,128)S(1)}, f32[8,128]{1,0:T(8,128)}, u32[]{:S(2)}) copy-start(f32[8,128]{1,0:T(8,128)} %gather_fusion.1) | copy-start | bytes 12292
  225.2 11.5 %all-to-all-start = ((bf16[4,96,512]{2,1,0:T(8,128)(2,1)}), bf16[4,96,512]{2,1,0:T(8,128)(2,1)S(1)}, u32[]{:S(2)}, u32[]{:S(2)}) async-start(bf16[4,96,512]{2,1,0:T(8,128)(2,1)} %bitcast.51), calls=%async_computation | async-start | bytes 786432 | tf_op jit(solution)/shard_map/all_to_all | solution.py:135
  228.8 10.1 %collective-permute-start.9 = (bf16[62,1024]{1,0:T(8,128)(2,1)S(1)}, bf16[62,1024]{1,0:T(8,128)(2,1)S(1)}, u32[]{:S(2)}, u32[]{:S(2)}) collective-permute-start(bf16[62,1024]{1,0:T(8,128)(2,1)S(1)} %copy-done.22), channel_id=1, source_target_pairs={{0,1},{1,2},{2,3},{3,0},{4,5},{5,6},{6,7},{7,4},{8,9},{9,10},{10,1... | collective-permute-start | bytes 380936 | tf_op jit(solution)/shard_map/ppermute | solution.py:99
  229.3 9.9 %collective-permute-start.11 = (bf16[62,1024]{1,0:T(8,128)(2,1)S(1)}, bf16[62,1024]{1,0:T(8,128)(2,1)S(1)}, u32[]{:S(2)}, u32[]{:S(2)}) collective-permute-start(bf16[62,1024]{1,0:T(8,128)(2,1)S(1)} %copy-done.22), channel_id=1, source_target_pairs={{0,3},{1,0},{2,1},{3,2},{4,7},{5,4},{6,5},{7,6},{8,11},{9,8},{10,9... | collective-permute-start | bytes 380936 | tf_op jit(solution)/shard_map/ppermute | solution.py:99
  230.6 11.2 %collective-permute-start.10 = (bf16[62,1024]{1,0:T(8,128)(2,1)S(1)}, bf16[62,1024]{1,0:T(8,128)(2,1)S(1)}, u32[]{:S(2)}, u32[]{:S(2)}) collective-permute-start(bf16[62,1024]{1,0:T(8,128)(2,1)S(1)} %copy-done.22), channel_id=1, source_target_pairs={{0,2},{1,3},{2,0},{3,1},{4,6},{5,7},{6,4},{7,5},{8,10},{9,11},{10,... | collective-permute-start | bytes 380936 | tf_op jit(solution)/shard_map/ppermute | solution.py:99
  (32 other events, 172.5 us)

commit v5 on v4

--- a/solution.py
+++ b/solution.py
@@ -67,7 +67,7 @@
             jnp.concatenate([source * slots_here + local, (feat_count + source) * slots_here + local])
         )
         pieces.append(piece)
-    return jnp.concatenate(pieces, 0), jnp.concatenate(ids)
+    return pieces, ids
 
 
 def on_device(
@@ -101,18 +101,35 @@
     weights_here = jnp.concatenate([cross_down[0], cross_up[0], compress_weight[0]], axis=1)
     parts = weight_parts(weights_here, feat_count, group_count, share_count, entry_count)
 
-    slot_data, slot_ids = exchange_rows(pooled_first[0], pooled_second[0], feat_count)
-    slot_count = slot_data.shape[0]
-    row_count = slot_data.shape[1]
-    orders = feature_order[0][slot_ids]
+    last_rows = parts[-1][0]
+    first_rows, second_rows, last_rows = lax.optimization_barrier(
+        (pooled_first[0], pooled_second[0], last_rows)
+    )
+    parts[-1] = (last_rows, parts[-1][1])
+    pieces, slot_ids = exchange_rows(first_rows, second_rows, feat_count)
+    row_count = pieces[0].shape[1]
+    slot_count = sum(piece.shape[0] for piece in pieces)
     bias_blocks = cross_bias[0].reshape(slot_count, entry_count)
+    features = jnp.concatenate([part_features for _, part_features in parts])
+    position_count = features.shape[0]
+
+    if len(pieces) > 4:
+        pieces, slot_ids = [jnp.concatenate(pieces, 0)], [jnp.concatenate(slot_ids)]
+    base_sum = None
+    for piece, ids in zip(pieces, slot_ids):
+        orders = feature_order[0][ids]
+        one_hot = (orders[None, :] == features[:, None]).astype(jnp.bfloat16)
+        term = jnp.einsum("fs,sre->rfe", one_hot, piece, preferred_element_type=jnp.float32)
+        base_sum = term if base_sum is None else base_sum + term
+    base_all = base_sum.astype(jnp.bfloat16).reshape(row_count, position_count * entry_count)
 
     bases = []
     low_sum = None
-    for rows, features in parts:
-        one_hot = (orders[None, :] == features[:, None]).astype(jnp.bfloat16)
-        base = jnp.einsum("fs,sre->rfe", one_hot, slot_data, preferred_element_type=jnp.float32)
-        base = base.astype(jnp.bfloat16).reshape(row_count, features.shape[0] * entry_count)
+    offset = 0
+    for rows, part_features in parts:
+        width = part_features.shape[0] * entry_count
+        base = base_all[:, offset : offset + width]
+        offset += width
         bases.append(base)
         term = jnp.dot(base, rows[:, :rank], preferred_element_type=jnp.float32)
         low_sum = term if low_sum is None else low_sum + term

time: 244 us -> 222 us (0.910)
  the two profiles are of different devices: /device:TPU:0 before, /device:TPU:8 now
where the time goes in v5:
time: 222 us; the launch traced here: 221 us
  waiting for transfers between devices  142 us (64%)
  matrix products  37 us (17%)
  starting transfers between devices  20.2 us (9%)
  local copies, waits for them, and re-layouts  19 us (9%)
  other arithmetic  2.98 us (1%)
    ppermute x3, waiting for transfers between devices, weight_parts(): travelling = lax.ppermute(travelling, 'feat', ring)  71.6 us
    ppermute x3, waiting for transfers between devices, exchange_rows(): lax.ppermute(piece, 'feat', [(source, (source + shift) % feat_count) for...  49.9 us
    dot_general x7, matrix products, on_device(): jnp.dot(crossed, rows[:, 2 * rank:], preferred_element_type=jnp.float32)  20 us
    ppermute x3, waiting for transfers between devices, weight_parts(): forwarded = lax.ppermute(travelling, 'groups', pairs)  13.7 us
    squeeze x1, local copies, waits for them, and re-layouts, on_device(): pooled_second[0]  8.15 us
    dot_general x7, matrix products, on_device(): term = jnp.dot(base, rows[:, :rank], preferred_element_type=jnp.float32)  7.65 us
    dot_general x4, matrix products, on_device(): jnp.einsum('fs,sre->rfe', one_hot, piece, preferred_element_type=jnp.floa...  7.23 us
    ppermute x3, starting transfers between devices, exchange_rows(): lax.ppermute(piece, 'feat', [(source, (source + shift) % feat_count) for...  5.96 us
  transfers between devices with their start and end apart: 13, of which 9 were waited for; matrix products, arithmetic and copies ran while one was open for 15% of the time, Pallas kernels for 0%

profile of v5, /device:TPU:8, one launch (start us, length us, event | category | flops | bytes accessed | tf_op | source)
XLA Modules:
  0.0 221.4 jit_solution(7158471870390534212)
XLA Ops:
  1.5 1.6 collective-permute-start
  3.1 23.4 %collective-permute-done = bf16[512,1024]{1,0:T(8,128)(2,1)} collective-permute-done((bf16[512,1024]{1,0:T(8,128)(2,1)S(1)}, bf16[512,1024]{1,0:T(8,128)(2,1)}, u32[]{:S(2)}, u32[]{:S(2)}) %collective-permute-start) | collective-permute-done | bytes 1048608 | tf_op jit(solution)/shard_map/ppermute | solution.py:31
  28.2 23.6 %collective-permute-done.1 = bf16[512,1024]{1,0:T(8,128)(2,1)} collective-permute-done((bf16[512,1024]{1,0:T(8,128)(2,1)}, bf16[512,1024]{1,0:T(8,128)(2,1)}, u32[]{:S(2)}, u32[]{:S(2)}) %collective-permute-start.1) | collective-permute-done | bytes 1048608 | tf_op jit(solution)/shard_map/ppermute | solution.py:31
  52.7 24.6 %collective-permute-done.2 = bf16[512,1024]{1,0:T(8,128)(2,1)} collective-permute-done((bf16[512,1024]{1,0:T(8,128)(2,1)}, bf16[512,1024]{1,0:T(8,128)(2,1)}, u32[]{:S(2)}, u32[]{:S(2)}) %collective-permute-start.2) | collective-permute-done | bytes 1048608 | tf_op jit(solution)/shard_map/ppermute | solution.py:31
  78.4 8.1 %copy_bitcast_fusion.1 = (bf16[4,1536,128]{2,0,1:T(4,128)(2,1)S(1)}, bf16[4,1536,128]{2,0,1:T(4,128)(2,1)S(1)}) fusion(bf16[1,4,1536,128]{3,2,1,0:T(8,128)(2,1)S(1)} %copy-done.2, bf16[1,4,1536,128]{3,2,1,0:T(8,128)(2,1)S(1)} %copy-done.3), kind=kLoop, calls=%fused_computation.19 | loop fusion | bytes 6291456 | tf_op jit(solution)/shard_map/squeeze | solution.py:106
  86.6 13.7 %collective-permute-done.3 = bf16[512,1024]{1,0:T(8,128)(2,1)S(1)} collective-permute-done((bf16[512,1024]{1,0:T(8,128)(2,1)}, bf16[512,1024]{1,0:T(8,128)(2,1)S(1)}, u32[]{:S(2)}, u32[]{:S(2)}) %collective-permute-start.3) | collective-permute-done | bytes 1048608 | tf_op jit(solution)/shard_map/ppermute | solution.py:38
  102.4 5.7 %collective-permute-start.5 = (bf16[8,384,128]{2,0,1:T(8,128)(2,1)S(1)}, bf16[8,384,128]{2,0,1:T(8,128)(2,1)}, u32[]{:S(2)}, u32[]{:S(2)}) collective-permute-start(bf16[8,384,128]{2,0,1:T(8,128)(2,1)S(1)} %pad_maximum_fusion.1), channel_id=1, source_target_pairs={{0,8},{4,12},{8,0},{12,4},{1,9},{5,13},{9,1},{13,5},{2,10},{6,14},... | collective-permute-start | bytes 2359304 | tf_op jit(solution)/shard_map/ppermute | solution.py:61
  117.3 36.3 %collective-permute-done.4 = bf16[8,384,128]{2,0,1:T(8,128)(2,1)} collective-permute-done((bf16[8,384,128]{2,0,1:T(8,128)(2,1)S(1)}, bf16[8,384,128]{2,0,1:T(8,128)(2,1)}, u32[]{:S(2)}, u32[]{:S(2)}) %collective-permute-start.4) | collective-permute-done | bytes 786464 | tf_op jit(solution)/shard_map/ppermute | solution.py:61
  153.6 2.2 fusion.113
  155.8 10.7 %collective-permute-done.5 = bf16[8,384,128]{2,0,1:T(8,128)(2,1)} collective-permute-done((bf16[8,384,128]{2,0,1:T(8,128)(2,1)S(1)}, bf16[8,384,128]{2,0,1:T(8,128)(2,1)}, u32[]{:S(2)}, u32[]{:S(2)}) %collective-permute-start.5) | collective-permute-done | bytes 786464 | tf_op jit(solution)/shard_map/ppermute | solution.py:61
  166.5 2.2 fusion.111
  168.7 3.0 %collective-permute-done.6 = bf16[8,384,128]{2,0,1:T(8,128)(2,1)S(1)} collective-permute-done((bf16[8,384,128]{2,0,1:T(8,128)(2,1)S(1)}, bf16[8,384,128]{2,0,1:T(8,128)(2,1)S(1)}, u32[]{:S(2)}, u32[]{:S(2)}) %collective-permute-start.6) | collective-permute-done | bytes 786464 | tf_op jit(solution)/shard_map/ppermute | solution.py:61
  172.8 1.7 add_convert_fusion
  183.8 3.2 %fusion.1 = f32[384,512]{1,0:T(8,128)} fusion(bf16[384,256]{1,0:T(8,128)(2,1)S(1)} %fusion.32, f32[1024]{0:T(1024)S(1)} %bitcast.137, bf16[384,4096]{1,0:T(8,128)(2,1)S(1)} %bitcast.119, bf16[1,1024,512]{2,1,0:T(8,128)(2,1)} %param.19, bf16[1,1024,256]{2,1,0:T(8,128)(2,1)} %param.17), kind=kOutput, calls=%fused_computation.21 | convolution fusion | flops 605945856 | bytes 3346432 | tf_op jit(solution)/shard_map/dot_general | solution.py:149
  187.0 2.6 %fusion.25 = f32[384,512]{1,0:T(8,128)} fusion(bf16[384,256]{1,0:T(8,128)(2,1)S(1)} %fusion.32, bf16[512,1024]{1,0:T(8,128)(2,1)} %collective-permute-done.1, f32[512]{0:T(512)S(1)} %bitcast.139, bf16[384,4096]{1,0:T(8,128)(2,1)S(1)} %bitcast.120), kind=kOutput, calls=%fused_computation.56 | convolution fusion | flops 302972928 | bytes 2164736 | tf_op jit(solution)/shard_map/dot_general | solution.py:149
  189.5 2.6 %fusion.24 = f32[384,512]{1,0:T(8,128)} fusion(bf16[384,256]{1,0:T(8,128)(2,1)S(1)} %fusion.32, bf16[512,1024]{1,0:T(8,128)(2,1)} %collective-permute-done.2, f32[512]{0:T(512)S(1)} %bitcast.140, bf16[384,4096]{1,0:T(8,128)(2,1)S(1)} %bitcast.121), kind=kOutput, calls=%fused_computation.55 | convolution fusion | flops 302972928 | bytes 2164736 | tf_op jit(solution)/shard_map/dot_general | solution.py:149
  192.1 2.9 %convolution_add_fusion.3 = f32[384,512]{1,0:T(8,128)} fusion(f32[384,512]{1,0:T(8,128)} %fusion.1, bf16[384,256]{1,0:T(8,128)(2,1)S(1)} %fusion.32, bf16[512,1024]{1,0:T(8,128)(2,1)} %collective-permute-done, f32[512]{0:T(512)S(1)} %bitcast.134, bf16[384,4096]{1,0:T(8,128)(2,1)S(1)} %bitcast.122), kind=kOutput, calls=%fused_computation.26 | convolution fusion | flops 303169536 | bytes 2951168 | tf_op jit(solution)/shard_map/dot_general | solution.py:149
  195.0 3.1 %fusion.2 = f32[384,512]{1,0:T(8,128)} fusion(f32[384,512]{1,0:T(8,128)} %fusion.25, f32[384,512]{1,0:T(8,128)} %convolution_add_fusion.3, bf16[384,256]{1,0:T(8,128)(2,1)S(1)} %fusion.32, bf16[512,1024]{1,0:T(8,128)(2,1)} %collective-permute-done.7, f32[512]{0:T(512)S(1)} %bitcast.136, bf16[384,4096]{1,0:T(8,128)(2,1)S(1)} %bitcast.123), kind=kOutput, calls=%fused_computation.27 | convolution fusion | flops 303366144 | bytes 3737600 | tf_op jit(solution)/shard_map/dot_general | solution.py:149
  198.0 3.1 %fusion.3 = f32[384,512]{1,0:T(8,128)} fusion(f32[384,512]{1,0:T(8,128)} %fusion.24, f32[384,512]{1,0:T(8,128)} %fusion.2, bf16[384,256]{1,0:T(8,128)(2,1)S(1)} %fusion.32, bf16[512,1024]{1,0:T(8,128)(2,1)} %collective-permute-done.8, f32[512]{0:T(512)S(1)} %bitcast.135, bf16[384,4096]{1,0:T(8,128)(2,1)S(1)} %bitcast.124), kind=kOutput, calls=%fused_computation.28 | convolution fusion | flops 303366144 | bytes 3737600 | tf_op jit(solution)/shard_map/dot_general | solution.py:149
  201.1 2.7 %fusion.23 = bf16[384,512]{1,0:T(8,128)(2,1)} fusion(f32[384,512]{1,0:T(8,128)} %fusion.3, bf16[384,256]{1,0:T(8,128)(2,1)S(1)} %fusion.32, bf16[512,1024]{1,0:T(8,128)(2,1)} %copy-done.7, f32[512]{0:T(512)S(1)} %bitcast.141, f32[512]{0:T(512)S(1)} %bitcast.138, bf16[384,4096]{1,0:T(8,128)(2,1)S(1)} %bitcast.125), kind=kOutput, calls=%fused_computation.54 | convolution fusion | flops 303562752 | bytes 2560000 | tf_op jit(solution)/shard_map/dot_general | solution.py:149
  203.8 3.6 %all-to-all-start = ((bf16[4,96,512]{2,1,0:T(8,128)(2,1)}), bf16[4,96,512]{2,1,0:T(8,128)(2,1)S(1)}, u32[]{:S(2)}, u32[]{:S(2)}) async-start(bf16[4,96,512]{2,1,0:T(8,128)(2,1)} %bitcast.132), calls=%async_computation | async-start | bytes 786432 | tf_op jit(solution)/shard_map/all_to_all | solution.py:152
  209.2 1.9 collective-permute-start.10
  211.2 4.1 %all-to-all-done = bf16[4,96,512]{2,1,0:T(8,128)(2,1)S(1)} async-done(((bf16[4,96,512]{2,1,0:T(8,128)(2,1)}), bf16[4,96,512]{2,1,0:T(8,128)(2,1)S(1)}, u32[]{:S(2)}, u32[]{:S(2)}) %all-to-all-start) | async-done | bytes 393248 | tf_op jit(solution)/shard_map/all_to_all | solution.py:152
  218.1 2.3 %collective-permute-done.10 = bf16[62,1024]{1,0:T(8,128)(2,1)S(1)} collective-permute-done((bf16[62,1024]{1,0:T(8,128)(2,1)S(1)}, bf16[62,1024]{1,0:T(8,128)(2,1)S(1)}, u32[]{:S(2)}, u32[]{:S(2)}) %collective-permute-start.10) | collective-permute-done | bytes 127008 | tf_op jit(solution)/shard_map/ppermute | solution.py:99
  (102 shorter events, 32.1 us)
Async XLA Ops:
  0.0 110.6 %copy-start = (f32[1,4096]{1,0:T(1,128)S(1)}, f32[1,4096]{1,0:T(1,128)}, u32[]{:S(2)}) copy-start(f32[1,4096]{1,0:T(1,128)} %param.18) | copy-start | bytes 49156
  0.0 78.4 %copy-start.3 = (bf16[1,4,1536,128]{3,2,1,0:T(8,128)(2,1)S(1)}, bf16[1,4,1536,128]{3,2,1,0:T(8,128)(2,1)}, u32[]{:S(2)}) copy-start(bf16[1,4,1536,128]{3,2,1,0:T(8,128)(2,1)} %param.13) | copy-start | bytes 4718596
  0.0 78.4 %copy-start.2 = (bf16[1,4,1536,128]{3,2,1,0:T(8,128)(2,1)S(1)}, bf16[1,4,1536,128]{3,2,1,0:T(8,128)(2,1)}, u32[]{:S(2)}) copy-start(bf16[1,4,1536,128]{3,2,1,0:T(8,128)(2,1)} %param.14) | copy-start | bytes 4718596
  1.5 25.1 %collective-permute-start = (bf16[512,1024]{1,0:T(8,128)(2,1)S(1)}, bf16[512,1024]{1,0:T(8,128)(2,1)}, u32[]{:S(2)}, u32[]{:S(2)}) collective-permute-start(bf16[512,1024]{1,0:T(8,128)(2,1)S(1)} %fusion.34), channel_id=1, source_target_pairs={{0,4},{4,8},{8,12},{12,0},{1,5},{5,9},{9,13},{13,1},{2,6},{6,10},{... | collective-permute-start | bytes 3145736 | tf_op jit(solution)/shard_map/ppermute | solution.py:31
  26.5 25.2 %collective-permute-start.1 = (bf16[512,1024]{1,0:T(8,128)(2,1)}, bf16[512,1024]{1,0:T(8,128)(2,1)}, u32[]{:S(2)}, u32[]{:S(2)}) collective-permute-start(bf16[512,1024]{1,0:T(8,128)(2,1)} %collective-permute-done), channel_id=1, source_target_pairs={{0,4},{4,8},{8,12},{12,0},{1,5},{5,9},{9,13},{13,1},{2,6},{6,10},{... | collective-permute-start | bytes 3145736 | tf_op jit(solution)/shard_map/ppermute | solution.py:31
  51.8 25.5 %collective-permute-start.2 = (bf16[512,1024]{1,0:T(8,128)(2,1)}, bf16[512,1024]{1,0:T(8,128)(2,1)}, u32[]{:S(2)}, u32[]{:S(2)}) collective-permute-start(bf16[512,1024]{1,0:T(8,128)(2,1)} %collective-permute-done.1), channel_id=1, source_target_pairs={{0,4},{4,8},{8,12},{12,0},{1,5},{5,9},{9,13},{13,1},{2,6},{6,10},{... | collective-permute-start | bytes 3145736 | tf_op jit(solution)/shard_map/ppermute | solution.py:31
  77.3 23.0 %collective-permute-start.3 = (bf16[512,1024]{1,0:T(8,128)(2,1)}, bf16[512,1024]{1,0:T(8,128)(2,1)S(1)}, u32[]{:S(2)}, u32[]{:S(2)}) collective-permute-start(bf16[512,1024]{1,0:T(8,128)(2,1)} %collective-permute-done.2), channel_id=1, source_target_pairs={{0,16},{16,0},{1,17},{17,1},{2,18},{18,2},{3,19},{19,3},{4,20},{20... | collective-permute-start | bytes 3145736 | tf_op jit(solution)/shard_map/ppermute | solution.py:38
  100.3 1.1 copy-start.7
  100.8 7.2 %copy-start.1 = (s32[1,32]{1,0:T(1,128)S(1)}, s32[1,32]{1,0:T(1,128)}, u32[]{:S(2)}) copy-start(s32[1,32]{1,0:T(1,128)} %param.15) | copy-start | bytes 388
  101.8 51.8 %collective-permute-start.4 = (bf16[8,384,128]{2,0,1:T(8,128)(2,1)S(1)}, bf16[8,384,128]{2,0,1:T(8,128)(2,1)}, u32[]{:S(2)}, u32[]{:S(2)}) collective-permute-start(bf16[8,384,128]{2,0,1:T(8,128)(2,1)S(1)} %pad_maximum_fusion), channel_id=1, source_target_pairs={{0,4},{4,8},{8,12},{12,0},{1,5},{5,9},{9,13},{13,1},{2,6},{6,10},{... | collective-permute-start | bytes 2359304 | tf_op jit(solution)/shard_map/ppermute | solution.py:61
  102.4 64.2 %collective-permute-start.5 = (bf16[8,384,128]{2,0,1:T(8,128)(2,1)S(1)}, bf16[8,384,128]{2,0,1:T(8,128)(2,1)}, u32[]{:S(2)}, u32[]{:S(2)}) collective-permute-start(bf16[8,384,128]{2,0,1:T(8,128)(2,1)S(1)} %pad_maximum_fusion.1), channel_id=1, source_target_pairs={{0,8},{4,12},{8,0},{12,4},{1,9},{5,13},{9,1},{13,5},{2,10},{6,14},... | collective-permute-start | bytes 2359304 | tf_op jit(solution)/shard_map/ppermute | solution.py:61
  114.6 65.5 %collective-permute-start.7 = (bf16[512,1024]{1,0:T(8,128)(2,1)}, bf16[512,1024]{1,0:T(8,128)(2,1)}, u32[]{:S(2)}, u32[]{:S(2)}) collective-permute-start(bf16[512,1024]{1,0:T(8,128)(2,1)} %collective-permute-done), channel_id=1, source_target_pairs={{0,16},{16,0},{1,17},{17,1},{2,18},{18,2},{3,19},{19,3},{4,20},{20... | collective-permute-start | bytes 3145736 | tf_op jit(solution)/shard_map/ppermute | solution.py:38
  115.4 65.9 %collective-permute-start.8 = (bf16[512,1024]{1,0:T(8,128)(2,1)}, bf16[512,1024]{1,0:T(8,128)(2,1)}, u32[]{:S(2)}, u32[]{:S(2)}) collective-permute-start(bf16[512,1024]{1,0:T(8,128)(2,1)} %collective-permute-done.1), channel_id=1, source_target_pairs={{0,16},{16,0},{1,17},{17,1},{2,18},{18,2},{3,19},{19,3},{4,20},{20... | collective-permute-start | bytes 3145736 | tf_op jit(solution)/shard_map/ppermute | solution.py:38
  117.1 54.6 %collective-permute-start.6 = (bf16[8,384,128]{2,0,1:T(8,128)(2,1)S(1)}, bf16[8,384,128]{2,0,1:T(8,128)(2,1)S(1)}, u32[]{:S(2)}, u32[]{:S(2)}) collective-permute-start(bf16[8,384,128]{2,0,1:T(8,128)(2,1)S(1)} %pad_maximum_fusion.2), channel_id=1, source_target_pairs={{0,12},{4,0},{8,4},{12,8},{1,13},{5,1},{9,5},{13,9},{2,14},{6,2},{... | collective-permute-start | bytes 2359304 | tf_op jit(solution)/shard_map/ppermute | solution.py:61
  174.5 4.0 %copy-start.4 = (bf16[1,1024,256]{2,1,0:T(8,128)(2,1)S(1)}, bf16[1,1024,256]{2,1,0:T(8,128)(2,1)}, u32[]{:S(2)}) copy-start(bf16[1,1024,256]{2,1,0:T(8,128)(2,1)} %param.16) | copy-start | bytes 1572868
  195.0 6.2 %copy-start.10 = (f32[1,512]{1,0:T(1,128)S(1)}, f32[1,512]{1,0:T(1,128)}, u32[]{:S(2)}) copy-start(f32[1,512]{1,0:T(1,128)} %param.20) | copy-start | bytes 6148
  198.0 9.4 %copy-start.6 = (bf16[62,1024]{1,0:T(8,128)(2,1)S(1)}, bf16[62,1024]{1,0:T(8,128)(2,1)}, u32[]{:S(2)}) copy-start(bf16[62,1024]{1,0:T(8,128)(2,1)} %param.22) | copy-start | bytes 380932
  198.0 13.1 %copy-start.9 = (s32[120]{0:T(128)S(1)}, s32[120]{0:T(128)}, u32[]{:S(2)}) copy-start(s32[120]{0:T(128)} %constant.143) | copy-start | bytes 1444
  201.1 16.1 %copy-start.5 = (bf16[96,128]{1,0:T(8,128)(2,1)S(1)}, bf16[96,128]{1,0:T(8,128)(2,1)}, u32[]{:S(2)}) copy-start(bf16[96,128]{1,0:T(8,128)(2,1)} %param.21) | copy-start | bytes 73732
  203.8 16.6 %copy-start.8 = (f32[1024]{0:T(1024)S(1)}, f32[1024]{0:T(1024)}, u32[]{:S(2)}) copy-start(f32[1024]{0:T(1024)} %param.23) | copy-start | bytes 12292
  203.8 11.5 %all-to-all-start = ((bf16[4,96,512]{2,1,0:T(8,128)(2,1)}), bf16[4,96,512]{2,1,0:T(8,128)(2,1)S(1)}, u32[]{:S(2)}, u32[]{:S(2)}) async-start(bf16[4,96,512]{2,1,0:T(8,128)(2,1)} %bitcast.132), calls=%async_computation | async-start | bytes 786432 | tf_op jit(solution)/shard_map/all_to_all | solution.py:152
  207.4 10.1 %collective-permute-start.9 = (bf16[62,1024]{1,0:T(8,128)(2,1)S(1)}, bf16[62,1024]{1,0:T(8,128)(2,1)S(1)}, u32[]{:S(2)}, u32[]{:S(2)}) collective-permute-start(bf16[62,1024]{1,0:T(8,128)(2,1)S(1)} %copy-done.6), channel_id=1, source_target_pairs={{0,1},{1,2},{2,3},{3,0},{4,5},{5,6},{6,7},{7,4},{8,9},{9,10},{10,1... | collective-permute-start | bytes 380936 | tf_op jit(solution)/shard_map/ppermute | solution.py:99
  207.9 9.9 %collective-permute-start.11 = (bf16[62,1024]{1,0:T(8,128)(2,1)S(1)}, bf16[62,1024]{1,0:T(8,128)(2,1)S(1)}, u32[]{:S(2)}, u32[]{:S(2)}) collective-permute-start(bf16[62,1024]{1,0:T(8,128)(2,1)S(1)} %copy-done.6), channel_id=1, source_target_pairs={{0,3},{1,0},{2,1},{3,2},{4,7},{5,4},{6,5},{7,6},{8,11},{9,8},{10,9... | collective-permute-start | bytes 380936 | tf_op jit(solution)/shard_map/ppermute | solution.py:99
  209.2 11.2 %collective-permute-start.10 = (bf16[62,1024]{1,0:T(8,128)(2,1)S(1)}, bf16[62,1024]{1,0:T(8,128)(2,1)S(1)}, u32[]{:S(2)}, u32[]{:S(2)}) collective-permute-start(bf16[62,1024]{1,0:T(8,128)(2,1)S(1)} %copy-done.6), channel_id=1, source_target_pairs={{0,2},{1,3},{2,0},{3,1},{4,6},{5,7},{6,4},{7,5},{8,10},{9,11},{10,... | collective-permute-start | bytes 380936 | tf_op jit(solution)/shard_map/ppermute | solution.py:99

commit v6 on v5

--- a/solution.py
+++ b/solution.py
@@ -40,7 +40,7 @@
             parts.append(
                 (forwarded, source_block * blocks_here + from_group * blocks_piece + block_range)
             )
-    return parts
+    return parts, travelling
 
 
 def exchange_rows(first, second, feat_count):
@@ -99,13 +99,11 @@
         hidden_pieces.append(lax.ppermute(mlp_weight, "tower", pairs))
 
     weights_here = jnp.concatenate([cross_down[0], cross_up[0], compress_weight[0]], axis=1)
-    parts = weight_parts(weights_here, feat_count, group_count, share_count, entry_count)
+    parts, last_rows = weight_parts(weights_here, feat_count, group_count, share_count, entry_count)
 
-    last_rows = parts[-1][0]
-    first_rows, second_rows, last_rows = lax.optimization_barrier(
+    first_rows, second_rows, _ = lax.optimization_barrier(
         (pooled_first[0], pooled_second[0], last_rows)
     )
-    parts[-1] = (last_rows, parts[-1][1])
     pieces, slot_ids = exchange_rows(first_rows, second_rows, feat_count)
     row_count = pieces[0].shape[1]
     slot_count = sum(piece.shape[0] for piece in pieces)
@@ -123,31 +121,19 @@
         base_sum = term if base_sum is None else base_sum + term
     base_all = base_sum.astype(jnp.bfloat16).reshape(row_count, position_count * entry_count)
 
-    bases = []
-    low_sum = None
-    offset = 0
-    for rows, part_features in parts:
-        width = part_features.shape[0] * entry_count
-        base = base_all[:, offset : offset + width]
-        offset += width
-        bases.append(base)
-        term = jnp.dot(base, rows[:, :rank], preferred_element_type=jnp.float32)
-        low_sum = term if low_sum is None else low_sum + term
+    weights = jnp.concatenate([rows for rows, _ in parts], 0)
+    low_sum = jnp.dot(base_all, weights[:, :rank], preferred_element_type=jnp.float32)
     low_rank = low_sum.astype(jnp.bfloat16)
-
-    squeezed = None
-    for (rows, features), base in zip(parts, bases):
-        lifted = lax.dot_general(
-            low_rank,
-            rows[:, rank : 2 * rank],
-            (((1,), (1,)), ((), ())),
-            preferred_element_type=jnp.float32,
-        )
-        shift_row = bias_blocks[features].reshape(features.shape[0] * entry_count)
-        columns = base.astype(jnp.float32)
-        crossed = (columns * (lifted + shift_row[None, :]) + columns).astype(jnp.bfloat16)
-        term = jnp.dot(crossed, rows[:, 2 * rank :], preferred_element_type=jnp.float32)
-        squeezed = term if squeezed is None else squeezed + term
+    lifted = lax.dot_general(
+        low_rank,
+        weights[:, rank : 2 * rank],
+        (((1,), (1,)), ((), ())),
+        preferred_element_type=jnp.float32,
+    )
+    shift_row = bias_blocks[features].reshape(position_count * entry_count)
+    columns = base_all.astype(jnp.float32)
+    crossed = (columns * (lifted + shift_row[None, :]) + columns).astype(jnp.bfloat16)
+    squeezed = jnp.dot(crossed, weights[:, 2 * rank :], preferred_element_type=jnp.float32)
     compressed = (squeezed + compress_bias[0][None, :]).astype(jnp.bfloat16)
     gathered = lax.all_to_all(compressed, "tower", split_axis=0, concat_axis=1, tiled=True)
     local_rows = gathered.shape[0]

time: 222 us -> 185 us (0.83)
  the two profiles are of different devices: /device:TPU:8 before, /device:TPU:0 now
where the time goes in v6:
time: 185 us
  waiting for transfers between devices  119 us (64%)
  local copies, waits for them, and re-layouts  26.7 us (14%)
  starting transfers between devices  16.8 us (9%)
  matrix products  16.6 us (9%)
  other arithmetic  4.81 us (3%)
    ppermute x3, waiting for transfers between devices, weight_parts(): travelling = lax.ppermute(travelling, 'feat', ring)  61.5 us
    ppermute x3, waiting for transfers between devices, exchange_rows(): lax.ppermute(piece, 'feat', [(source, (source + shift) % feat_count) for...  39.2 us
    ppermute x3, waiting for transfers between devices, weight_parts(): forwarded = lax.ppermute(travelling, 'groups', pairs)  11 us
    unnamed x23, local copies, waits for them, and re-layouts  10.2 us
    squeeze x1, local copies, waits for them, and re-layouts, on_device(): pooled_second[0]  8.15 us
    dot_general x1, matrix products, on_device(): jnp.dot(crossed, weights[:, 2 * rank:], preferred_element_type=jnp.float32)  7.01 us
    all_to_all x1, waiting for transfers between devices, on_device(): lax.all_to_all(compressed, 'tower', split_axis=0, concat_axis=1, tiled=True)  5.37 us
    dot_general x4, matrix products, on_device(): jnp.einsum('fs,sre->rfe', one_hot, piece, preferred_element_type=jnp.floa...  4.87 us
  transfers between devices with their start and end apart: 13, of which 7 were waited for; matrix products, arithmetic and copies ran while one was open for 17% of the time, Pallas kernels for 0%

profile of v6, /device:TPU:0, one launch (start us, length us, event | category | flops | bytes accessed | tf_op | source)
XLA Modules:
  0.0 184.7 jit_solution(13426474628149961945)
XLA Ops:
  0.0 3.3 %pad_maximum_fusion = (bf16[1024,1024]{1,0:T(8,128)(2,1)S(1)}, bf16[4096,1024]{1,0:T(8,128)(2,1)}) fusion(bf16[1024,512]{1,0:T(8,128)(2,1)} %bitcast.102, bf16[1024,256]{1,0:T(8,128)(2,1)} %bitcast.103, bf16[1024,256]{1,0:T(8,128)(2,1)} %bitcast.104), kind=kLoop, calls=%fused_computation.16 | loop fusion | flops 6291455 | bytes 6291456 | tf_op jit(solution)/shard_map/concatenate | solution.py:101
  3.3 1.1 constant_dynamic-slice_fusion.8
  4.4 3.0 %collective-permute-start = (bf16[512,1024]{1,0:T(8,128)(2,1)}, bf16[512,1024]{1,0:T(8,128)(2,1)}, u32[]{:S(2)}, u32[]{:S(2)}) collective-permute-start(bf16[512,1024]{1,0:T(8,128)(2,1)} %constant_dynamic-slice_fusion.8), channel_id=1, source_target_pairs={{0,4},{4,8},{8,12},{12,0},{1,5},{5,9},{9,13},{13,1},{2,6},{6,10},{... | collective-permute-start | bytes 3145736 | tf_op jit(solution)/shard_map/ppermute | solution.py:31
  7.6 25.3 %collective-permute-done = bf16[512,1024]{1,0:T(8,128)(2,1)} collective-permute-done((bf16[512,1024]{1,0:T(8,128)(2,1)}, bf16[512,1024]{1,0:T(8,128)(2,1)}, u32[]{:S(2)}, u32[]{:S(2)}) %collective-permute-start) | collective-permute-done | bytes 1048608 | tf_op jit(solution)/shard_map/ppermute | solution.py:31
  35.8 23.6 %collective-permute-done.1 = bf16[512,1024]{1,0:T(8,128)(2,1)} collective-permute-done((bf16[512,1024]{1,0:T(8,128)(2,1)}, bf16[512,1024]{1,0:T(8,128)(2,1)}, u32[]{:S(2)}, u32[]{:S(2)}) %collective-permute-start.1) | collective-permute-done | bytes 1048608 | tf_op jit(solution)/shard_map/ppermute | solution.py:31
  60.0 1.3 collective-permute-start.6
  61.5 8.1 %copy_bitcast_fusion = (bf16[4,1536,128]{2,0,1:T(4,128)(2,1)S(1)}, bf16[4,1536,128]{2,0,1:T(4,128)(2,1)S(1)}) fusion(bf16[1,4,1536,128]{3,2,1,0:T(8,128)(2,1)S(1)} %copy-done.2, bf16[1,4,1536,128]{3,2,1,0:T(8,128)(2,1)S(1)} %copy-done.3), kind=kLoop, calls=%fused_computation.17 | loop fusion | bytes 6291456 | tf_op jit(solution)/shard_map/squeeze | solution.py:105
  70.4 2.3 %constant_dynamic-update-slice_fusion.5 = bf16[4096,1024]{1,0:T(8,128)(2,1)} fusion(bf16[4096,1024]{1,0:T(8,128)(2,1)} %get-tuple-element.10, bf16[512,1024]{1,0:T(8,128)(2,1)} %collective-permute-done), kind=kLoop, calls=%fused_computation.56 | loop fusion | bytes 2097152
  72.7 12.6 %collective-permute-done.2 = bf16[512,1024]{1,0:T(8,128)(2,1)} collective-permute-done((bf16[512,1024]{1,0:T(8,128)(2,1)}, bf16[512,1024]{1,0:T(8,128)(2,1)}, u32[]{:S(2)}, u32[]{:S(2)}) %collective-permute-start.2) | collective-permute-done | bytes 1048608 | tf_op jit(solution)/shard_map/ppermute | solution.py:31
  87.0 2.3 %constant_dynamic-update-slice_fusion.4 = bf16[4096,1024]{1,0:T(8,128)(2,1)} fusion(bf16[4096,1024]{1,0:T(8,128)(2,1)} %constant_dynamic-update-slice_fusion.5, bf16[512,1024]{1,0:T(8,128)(2,1)} %collective-permute-done.6), kind=kLoop, calls=%fused_computation.55 | loop fusion | bytes 2097152
  89.2 2.3 %constant_dynamic-update-slice_fusion.3 = bf16[4096,1024]{1,0:T(8,128)(2,1)} fusion(bf16[4096,1024]{1,0:T(8,128)(2,1)} %constant_dynamic-update-slice_fusion.4, bf16[512,1024]{1,0:T(8,128)(2,1)} %collective-permute-done.1), kind=kLoop, calls=%fused_computation.54 | loop fusion | bytes 2097152
  92.5 4.1 %collective-permute-start.3 = (bf16[8,384,128]{2,0,1:T(8,128)(2,1)S(1)}, bf16[8,384,128]{2,0,1:T(8,128)(2,1)S(1)}, u32[]{:S(2)}, u32[]{:S(2)}) collective-permute-start(bf16[8,384,128]{2,0,1:T(8,128)(2,1)S(1)} %pad_maximum_fusion.1), channel_id=1, source_target_pairs={{0,4},{4,8},{8,12},{12,0},{1,5},{5,9},{9,13},{13,1},{2,6},{6,10},{... | collective-permute-start | bytes 2359304 | tf_op jit(solution)/shard_map/ppermute | solution.py:61
  96.6 1.3 collective-permute-start.8
  97.9 11.0 %collective-permute-done.7 = bf16[512,1024]{1,0:T(8,128)(2,1)S(1)} collective-permute-done((bf16[512,1024]{1,0:T(8,128)(2,1)}, bf16[512,1024]{1,0:T(8,128)(2,1)S(1)}, u32[]{:S(2)}, u32[]{:S(2)}) %collective-permute-start.7) | collective-permute-done | bytes 1048608 | tf_op jit(solution)/shard_map/ppermute | solution.py:38
  110.0 2.2 %constant_dynamic-update-slice_fusion.1 = bf16[4096,1024]{1,0:T(8,128)(2,1)} fusion(bf16[4096,1024]{1,0:T(8,128)(2,1)} %constant_dynamic-update-slice_fusion.2, bf16[512,1024]{1,0:T(8,128)(2,1)} %collective-permute-done.2), kind=kLoop, calls=%fused_computation.52 | loop fusion | bytes 2097152
  113.3 39.1 %collective-permute-done.4 = bf16[8,384,128]{2,0,1:T(8,128)(2,1)S(1)} collective-permute-done((bf16[8,384,128]{2,0,1:T(8,128)(2,1)S(1)}, bf16[8,384,128]{2,0,1:T(8,128)(2,1)S(1)}, u32[]{:S(2)}, u32[]{:S(2)}) %collective-permute-start.4) | collective-permute-done | bytes 786464 | tf_op jit(solution)/shard_map/ppermute | solution.py:61
  154.6 1.6 add_convert_fusion
  156.3 1.1 constant_dynamic-update-slice_fusion
  157.4 2.7 %fusion.24 = bf16[384,256]{1,0:T(8,128)(2,1)S(1)} fusion(bf16[4096,1024]{1,0:T(8,128)(2,1)} %constant_dynamic-update-slice_fusion, bf16[48,8,32,128]{3,2,1,0:T(8,128)(2,1)S(1)} %bitcast.98), kind=kOutput, calls=%fused_computation.28 | convolution fusion | flops 805404672 | bytes 5439488 | tf_op jit(solution)/shard_map/dot_general | solution.py:125
  160.1 7.0 %fusion.15 = bf16[384,512]{1,0:T(8,128)(2,1)} fusion(bf16[4096,1024]{1,0:T(8,128)(2,1)} %constant_dynamic-update-slice_fusion, bf16[384,256]{1,0:T(8,128)(2,1)S(1)} %fusion.24, f32[4096]{0:T(1024)S(1)} %bitcast.106, bf16[48,8,32,128]{3,2,1,0:T(8,128)(2,1)S(1)} %bitcast.99, f32[512]{0:T(512)S(1)} %bitcast.107), kind=kOutput, calls=%fused_computation.21 | convolution fusion | flops 2424176640 | bytes 10045440 | tf_op jit(solution)/shard_map/dot_general | solution.py:136
  167.1 3.6 %all-to-all-start = ((bf16[4,96,512]{2,1,0:T(8,128)(2,1)}), bf16[4,96,512]{2,1,0:T(8,128)(2,1)S(1)}, u32[]{:S(2)}, u32[]{:S(2)}) async-start(bf16[4,96,512]{2,1,0:T(8,128)(2,1)} %bitcast.34), calls=%async_computation | async-start | bytes 786432 | tf_op jit(solution)/shard_map/all_to_all | solution.py:138
  170.7 1.7 collective-permute-start.11
  173.3 5.4 %all-to-all-done = bf16[4,96,512]{2,1,0:T(8,128)(2,1)S(1)} async-done(((bf16[4,96,512]{2,1,0:T(8,128)(2,1)}), bf16[4,96,512]{2,1,0:T(8,128)(2,1)S(1)}, u32[]{:S(2)}, u32[]{:S(2)}) %all-to-all-start) | async-done | bytes 393248 | tf_op jit(solution)/shard_map/all_to_all | solution.py:138
  181.4 2.3 %collective-permute-done.10 = bf16[62,1024]{1,0:T(8,128)(2,1)S(1)} collective-permute-done((bf16[62,1024]{1,0:T(8,128)(2,1)S(1)}, bf16[62,1024]{1,0:T(8,128)(2,1)S(1)}, u32[]{:S(2)}, u32[]{:S(2)}) %collective-permute-start.10) | collective-permute-done | bytes 127008 | tf_op jit(solution)/shard_map/ppermute | solution.py:99
  (82 shorter events, 15.7 us)
Async XLA Ops:
  0.0 59.4 %copy-start = (f32[1,4096]{1,0:T(1,128)S(1)}, f32[1,4096]{1,0:T(1,128)}, u32[]{:S(2)}) copy-start(f32[1,4096]{1,0:T(1,128)} %param.18) | copy-start | bytes 49156
  0.0 33.0 %copy-start.1 = (s32[1,32]{1,0:T(1,128)S(1)}, s32[1,32]{1,0:T(1,128)}, u32[]{:S(2)}) copy-start(s32[1,32]{1,0:T(1,128)} %param.15) | copy-start | bytes 388
  0.0 61.5 %copy-start.2 = (bf16[1,4,1536,128]{3,2,1,0:T(8,128)(2,1)S(1)}, bf16[1,4,1536,128]{3,2,1,0:T(8,128)(2,1)}, u32[]{:S(2)}) copy-start(bf16[1,4,1536,128]{3,2,1,0:T(8,128)(2,1)} %param.14) | copy-start | bytes 4718596
  0.0 61.5 %copy-start.3 = (bf16[1,4,1536,128]{3,2,1,0:T(8,128)(2,1)S(1)}, bf16[1,4,1536,128]{3,2,1,0:T(8,128)(2,1)}, u32[]{:S(2)}) copy-start(bf16[1,4,1536,128]{3,2,1,0:T(8,128)(2,1)} %param.13) | copy-start | bytes 4718596
  4.4 28.5 %collective-permute-start = (bf16[512,1024]{1,0:T(8,128)(2,1)}, bf16[512,1024]{1,0:T(8,128)(2,1)}, u32[]{:S(2)}, u32[]{:S(2)}) collective-permute-start(bf16[512,1024]{1,0:T(8,128)(2,1)} %constant_dynamic-slice_fusion.8), channel_id=1, source_target_pairs={{0,4},{4,8},{8,12},{12,0},{1,5},{5,9},{9,13},{13,1},{2,6},{6,10},{... | collective-permute-start | bytes 3145736 | tf_op jit(solution)/shard_map/ppermute | solution.py:31
  33.0 26.5 %collective-permute-start.1 = (bf16[512,1024]{1,0:T(8,128)(2,1)}, bf16[512,1024]{1,0:T(8,128)(2,1)}, u32[]{:S(2)}, u32[]{:S(2)}) collective-permute-start(bf16[512,1024]{1,0:T(8,128)(2,1)} %collective-permute-done), channel_id=1, source_target_pairs={{0,4},{4,8},{8,12},{12,0},{1,5},{5,9},{9,13},{13,1},{2,6},{6,10},{... | collective-permute-start | bytes 3145736 | tf_op jit(solution)/shard_map/ppermute | solution.py:31
  59.4 25.9 %collective-permute-start.2 = (bf16[512,1024]{1,0:T(8,128)(2,1)}, bf16[512,1024]{1,0:T(8,128)(2,1)}, u32[]{:S(2)}, u32[]{:S(2)}) collective-permute-start(bf16[512,1024]{1,0:T(8,128)(2,1)} %collective-permute-done.1), channel_id=1, source_target_pairs={{0,4},{4,8},{8,12},{12,0},{1,5},{5,9},{9,13},{13,1},{2,6},{6,10},{... | collective-permute-start | bytes 3145736 | tf_op jit(solution)/shard_map/ppermute | solution.py:31
  60.0 26.9 %collective-permute-start.6 = (bf16[512,1024]{1,0:T(8,128)(2,1)}, bf16[512,1024]{1,0:T(8,128)(2,1)}, u32[]{:S(2)}, u32[]{:S(2)}) collective-permute-start(bf16[512,1024]{1,0:T(8,128)(2,1)} %collective-permute-done), channel_id=1, source_target_pairs={{0,16},{16,0},{1,17},{17,1},{2,18},{18,2},{3,19},{19,3},{4,20},{20... | collective-permute-start | bytes 3145736 | tf_op jit(solution)/shard_map/ppermute | solution.py:38
  69.6 39.3 %collective-permute-start.7 = (bf16[512,1024]{1,0:T(8,128)(2,1)}, bf16[512,1024]{1,0:T(8,128)(2,1)S(1)}, u32[]{:S(2)}, u32[]{:S(2)}) collective-permute-start(bf16[512,1024]{1,0:T(8,128)(2,1)} %collective-permute-done.1), channel_id=1, source_target_pairs={{0,16},{16,0},{1,17},{17,1},{2,18},{18,2},{3,19},{19,3},{4,20},{20... | collective-permute-start | bytes 3145736 | tf_op jit(solution)/shard_map/ppermute | solution.py:38
  86.9 25.3 %collective-permute-start.5 = (bf16[8,384,128]{2,0,1:T(8,128)(2,1)S(1)}, bf16[8,384,128]{2,0,1:T(8,128)(2,1)S(1)}, u32[]{:S(2)}, u32[]{:S(2)}) collective-permute-start(bf16[8,384,128]{2,0,1:T(8,128)(2,1)S(1)} %pad_maximum_fusion.3), channel_id=1, source_target_pairs={{0,12},{4,0},{8,4},{12,8},{1,13},{5,1},{9,5},{13,9},{2,14},{6,2},{... | collective-permute-start | bytes 2359304 | tf_op jit(solution)/shard_map/ppermute | solution.py:61
  92.0 60.4 %collective-permute-start.4 = (bf16[8,384,128]{2,0,1:T(8,128)(2,1)S(1)}, bf16[8,384,128]{2,0,1:T(8,128)(2,1)S(1)}, u32[]{:S(2)}, u32[]{:S(2)}) collective-permute-start(bf16[8,384,128]{2,0,1:T(8,128)(2,1)S(1)} %pad_maximum_fusion.2), channel_id=1, source_target_pairs={{0,8},{4,12},{8,0},{12,4},{1,9},{5,13},{9,1},{13,5},{2,10},{6,14},... | collective-permute-start | bytes 2359304 | tf_op jit(solution)/shard_map/ppermute | solution.py:61
  92.5 61.0 %collective-permute-start.3 = (bf16[8,384,128]{2,0,1:T(8,128)(2,1)S(1)}, bf16[8,384,128]{2,0,1:T(8,128)(2,1)S(1)}, u32[]{:S(2)}, u32[]{:S(2)}) collective-permute-start(bf16[8,384,128]{2,0,1:T(8,128)(2,1)S(1)} %pad_maximum_fusion.1), channel_id=1, source_target_pairs={{0,4},{4,8},{8,12},{12,0},{1,5},{5,9},{9,13},{13,1},{2,6},{6,10},{... | collective-permute-start | bytes 2359304 | tf_op jit(solution)/shard_map/ppermute | solution.py:61
  96.6 59.6 %collective-permute-start.8 = (bf16[512,1024]{1,0:T(8,128)(2,1)}, bf16[512,1024]{1,0:T(8,128)(2,1)S(1)}, u32[]{:S(2)}, u32[]{:S(2)}) collective-permute-start(bf16[512,1024]{1,0:T(8,128)(2,1)} %collective-permute-done.2), channel_id=1, source_target_pairs={{0,16},{16,0},{1,17},{17,1},{2,18},{18,2},{3,19},{19,3},{4,20},{20... | collective-permute-start | bytes 3145736 | tf_op jit(solution)/shard_map/ppermute | solution.py:38
  157.4 2.7 %copy-start.8 = (f32[1,512]{1,0:T(1,128)S(1)}, f32[1,512]{1,0:T(1,128)}, u32[]{:S(2)}) copy-start(f32[1,512]{1,0:T(1,128)} %param.20) | copy-start | bytes 6148
  160.1 10.6 %copy-start.5 = (bf16[62,1024]{1,0:T(8,128)(2,1)S(1)}, bf16[62,1024]{1,0:T(8,128)(2,1)}, u32[]{:S(2)}) copy-start(bf16[62,1024]{1,0:T(8,128)(2,1)} %param.22) | copy-start | bytes 380932
  160.1 13.1 %copy-start.7 = (s32[120]{0:T(128)S(1)}, s32[120]{0:T(128)}, u32[]{:S(2)}) copy-start(s32[120]{0:T(128)} %constant.143) | copy-start | bytes 1444
  167.1 13.5 %copy-start.4 = (bf16[96,128]{1,0:T(8,128)(2,1)S(1)}, bf16[96,128]{1,0:T(8,128)(2,1)}, u32[]{:S(2)}) copy-start(bf16[96,128]{1,0:T(8,128)(2,1)} %param.21) | copy-start | bytes 73732
  167.1 16.6 %copy-start.6 = (f32[1024]{0:T(1024)S(1)}, f32[1024]{0:T(1024)}, u32[]{:S(2)}) copy-start(f32[1024]{0:T(1024)} %param.23) | copy-start | bytes 12292
  167.1 11.5 %all-to-all-start = ((bf16[4,96,512]{2,1,0:T(8,128)(2,1)}), bf16[4,96,512]{2,1,0:T(8,128)(2,1)S(1)}, u32[]{:S(2)}, u32[]{:S(2)}) async-start(bf16[4,96,512]{2,1,0:T(8,128)(2,1)} %bitcast.34), calls=%async_computation | async-start | bytes 786432 | tf_op jit(solution)/shard_map/all_to_all | solution.py:138
  170.7 10.4 %collective-permute-start.11 = (bf16[62,1024]{1,0:T(8,128)(2,1)S(1)}, bf16[62,1024]{1,0:T(8,128)(2,1)S(1)}, u32[]{:S(2)}, u32[]{:S(2)}) collective-permute-start(bf16[62,1024]{1,0:T(8,128)(2,1)S(1)} %copy-done.5), channel_id=1, source_target_pairs={{0,3},{1,0},{2,1},{3,2},{4,7},{5,4},{6,5},{7,6},{8,11},{9,8},{10,9... | collective-permute-start | bytes 380936 | tf_op jit(solution)/shard_map/ppermute | solution.py:99
  172.5 8.4 %collective-permute-start.9 = (bf16[62,1024]{1,0:T(8,128)(2,1)S(1)}, bf16[62,1024]{1,0:T(8,128)(2,1)S(1)}, u32[]{:S(2)}, u32[]{:S(2)}) collective-permute-start(bf16[62,1024]{1,0:T(8,128)(2,1)S(1)} %copy-done.5), channel_id=1, source_target_pairs={{0,1},{1,2},{2,3},{3,0},{4,5},{5,6},{6,7},{7,4},{8,9},{9,10},{10,1... | collective-permute-start | bytes 380936 | tf_op jit(solution)/shard_map/ppermute | solution.py:99
  172.5 11.3 %collective-permute-start.10 = (bf16[62,1024]{1,0:T(8,128)(2,1)S(1)}, bf16[62,1024]{1,0:T(8,128)(2,1)S(1)}, u32[]{:S(2)}, u32[]{:S(2)}) collective-permute-start(bf16[62,1024]{1,0:T(8,128)(2,1)S(1)} %copy-done.5), channel_id=1, source_target_pairs={{0,2},{1,3},{2,0},{3,1},{4,6},{5,7},{6,4},{7,5},{8,10},{9,11},{10,... | collective-permute-start | bytes 380936 | tf_op jit(solution)/shard_map/ppermute | solution.py:99

commit v7 on v6

--- a/solution.py
+++ b/solution.py
@@ -27,7 +27,10 @@
     else:
         travelling = weights_here
     ring = [(source, (source + 1) % feat_count) for source in range(feat_count)]
+    released = travelling
     for step in range(1, feat_count):
+        if step == feat_count - 1:
+            released = travelling
         travelling = lax.ppermute(travelling, "feat", ring)
         source_block = (owner - step) % feat_count
         parts.append(
@@ -40,7 +43,7 @@
             parts.append(
                 (forwarded, source_block * blocks_here + from_group * blocks_piece + block_range)
             )
-    return parts, travelling
+    return parts, released
 
 
 def exchange_rows(first, second, feat_count):

time: 185 us -> 207 us (1.12)
  waiting for transfers between devices: 119 us -> 137 us
    ppermute x3, waiting for transfers between devices: 39.2 us -> 75.6 us  [exchange_rows(): lax.ppermute(piece, 'feat', [(source, (source + shift) % feat_count) for...]
    ppermute x3, waiting for transfers between devices: 61.5 us -> 37.4 us  [weight_parts(): travelling = lax.ppermute(travelling, 'feat', ring)]
    ppermute x3, waiting for transfers between devices: 11 us -> 17.5 us  [weight_parts(): forwarded = lax.ppermute(travelling, 'groups', pairs)]
    unnamed x23 -> x29, local copies, waits for them, and re-layouts: 10.2 us -> 7.8 us
    ppermute x3, starting transfers between devices: 4.27 us -> 2.15 us  [exchange_rows(): lax.ppermute(piece, 'feat', [(source, (source + shift) % feat_count) for...]
where the time goes in v7:
time: 207 us
  waiting for transfers between devices  137 us (66%)
  local copies, waits for them, and re-layouts  27.3 us (13%)
  matrix products  18.4 us (9%)
  starting transfers between devices  16.7 us (8%)
  other arithmetic  6.35 us (3%)
    ppermute x3, waiting for transfers between devices, exchange_rows(): lax.ppermute(piece, 'feat', [(source, (source + shift) % feat_count) for...  75.6 us
    ppermute x3, waiting for transfers between devices, weight_parts(): travelling = lax.ppermute(travelling, 'feat', ring)  37.4 us
    ppermute x3, waiting for transfers between devices, weight_parts(): forwarded = lax.ppermute(travelling, 'groups', pairs)  17.5 us
    squeeze x1, local copies, waits for them, and re-layouts, on_device(): pooled_second[0]  8.15 us
    unnamed x29, local copies, waits for them, and re-layouts  7.8 us
    dot_general x1, matrix products, on_device(): jnp.dot(crossed, weights[:, 2 * rank:], preferred_element_type=jnp.float32)  6.97 us
    dot_general x4, matrix products, on_device(): jnp.einsum('fs,sre->rfe', one_hot, piece, preferred_element_type=jnp.floa...  6.67 us
    all_to_all x1, waiting for transfers between devices, on_device(): lax.all_to_all(compressed, 'tower', split_axis=0, concat_axis=1, tiled=True)  4.72 us
  transfers between devices with their start and end apart: 13, of which 7 were waited for; matrix products, arithmetic and copies ran while one was open for 17% of the time, Pallas kernels for 0%

profile of v7, /device:TPU:0, one launch (start us, length us, event | category | flops | bytes accessed | tf_op | source)
XLA Modules:
  0.0 206.7 jit_solution(3738450878819571503)
XLA Ops:
  0.0 3.3 %pad_maximum_fusion = (bf16[1024,1024]{1,0:T(8,128)(2,1)S(1)}, bf16[4096,1024]{1,0:T(8,128)(2,1)}) fusion(bf16[1024,512]{1,0:T(8,128)(2,1)} %bitcast.102, bf16[1024,256]{1,0:T(8,128)(2,1)} %bitcast.103, bf16[1024,256]{1,0:T(8,128)(2,1)} %bitcast.104), kind=kLoop, calls=%fused_computation.16 | loop fusion | flops 6291455 | bytes 6291456 | tf_op jit(solution)/shard_map/concatenate | solution.py:104
  4.4 3.0 %collective-permute-start = (bf16[512,1024]{1,0:T(8,128)(2,1)}, bf16[512,1024]{1,0:T(8,128)(2,1)}, u32[]{:S(2)}, u32[]{:S(2)}) collective-permute-start(bf16[512,1024]{1,0:T(8,128)(2,1)} %constant_dynamic-slice_fusion.8), channel_id=1, source_target_pairs={{0,4},{4,8},{8,12},{12,0},{1,5},{5,9},{9,13},{13,1},{2,6},{6,10},{... | collective-permute-start | bytes 3145736 | tf_op jit(solution)/shard_map/ppermute | solution.py:34
  11.0 21.9 %collective-permute-done = bf16[512,1024]{1,0:T(8,128)(2,1)} collective-permute-done((bf16[512,1024]{1,0:T(8,128)(2,1)}, bf16[512,1024]{1,0:T(8,128)(2,1)}, u32[]{:S(2)}, u32[]{:S(2)}) %collective-permute-start) | collective-permute-done | bytes 1048608 | tf_op jit(solution)/shard_map/ppermute | solution.py:34
  34.2 8.1 %copy_bitcast_fusion = (bf16[4,1536,128]{2,0,1:T(4,128)(2,1)S(1)}, bf16[4,1536,128]{2,0,1:T(4,128)(2,1)S(1)}) fusion(bf16[1,4,1536,128]{3,2,1,0:T(8,128)(2,1)S(1)} %copy-done.2, bf16[1,4,1536,128]{3,2,1,0:T(8,128)(2,1)S(1)} %copy-done.3), kind=kLoop, calls=%fused_computation.17 | loop fusion | bytes 6291456 | tf_op jit(solution)/shard_map/squeeze | solution.py:108
  42.3 1.6 collective-permute-start.5
  43.9 15.5 %collective-permute-done.1 = bf16[512,1024]{1,0:T(8,128)(2,1)} collective-permute-done((bf16[512,1024]{1,0:T(8,128)(2,1)}, bf16[512,1024]{1,0:T(8,128)(2,1)}, u32[]{:S(2)}, u32[]{:S(2)}) %collective-permute-start.1) | collective-permute-done | bytes 1048608 | tf_op jit(solution)/shard_map/ppermute | solution.py:34
  59.9 1.3 constant_dynamic-slice_fusion.7
  61.3 1.3 pad_maximum_fusion.3
  62.6 2.3 %constant_dynamic-update-slice_fusion.5 = bf16[4096,1024]{1,0:T(8,128)(2,1)} fusion(bf16[4096,1024]{1,0:T(8,128)(2,1)} %get-tuple-element.10, bf16[512,1024]{1,0:T(8,128)(2,1)} %collective-permute-done), kind=kLoop, calls=%fused_computation.56 | loop fusion | bytes 2097152
  65.8 2.1 %collective-permute-start.2 = (bf16[8,384,128]{2,0,1:T(8,128)(2,1)S(1)}, bf16[8,384,128]{2,0,1:T(8,128)(2,1)S(1)}, u32[]{:S(2)}, u32[]{:S(2)}) collective-permute-start(bf16[8,384,128]{2,0,1:T(8,128)(2,1)S(1)} %pad_maximum_fusion.1), channel_id=1, source_target_pairs={{0,4},{4,8},{8,12},{12,0},{1,5},{5,9},{9,13},{13,1},{2,6},{6,10},{... | collective-permute-start | bytes 2359304 | tf_op jit(solution)/shard_map/ppermute | solution.py:64
  69.2 1.4 collective-permute-start.7
  71.7 2.3 %constant_dynamic-update-slice_fusion.3 = bf16[4096,1024]{1,0:T(8,128)(2,1)} fusion(bf16[4096,1024]{1,0:T(8,128)(2,1)} %constant_dynamic-update-slice_fusion.4, bf16[512,1024]{1,0:T(8,128)(2,1)} %collective-permute-done.1), kind=kLoop, calls=%fused_computation.54 | loop fusion | bytes 2097152
  74.0 7.7 %collective-permute-done.4 = bf16[8,384,128]{2,0,1:T(8,128)(2,1)} collective-permute-done((bf16[8,384,128]{2,0,1:T(8,128)(2,1)}, bf16[8,384,128]{2,0,1:T(8,128)(2,1)}, u32[]{:S(2)}, u32[]{:S(2)}) %collective-permute-start.4) | collective-permute-done | bytes 786464 | tf_op jit(solution)/shard_map/ppermute | solution.py:64
  81.7 2.2 %fusion.49 = f32[384,128,32]{1,2,0:T(8,128)S(1)} fusion(bf16[8,384,128]{2,0,1:T(8,128)(2,1)} %collective-permute-done.4, s32[32]{0:T(128)S(1)} %concatenate.169, s32[8]{0:T(128)S(1)} %gather_fusion.3), kind=kOutput, calls=%fused_computation.77 | convolution fusion | flops 25166080 | bytes 7078048 | tf_op jit(solution)/shard_map/fs,sre->rfe/dot_general | solution.py:123
  83.9 67.9 %collective-permute-done.3 = bf16[8,384,128]{2,0,1:T(8,128)(2,1)S(1)} collective-permute-done((bf16[8,384,128]{2,0,1:T(8,128)(2,1)S(1)}, bf16[8,384,128]{2,0,1:T(8,128)(2,1)S(1)}, u32[]{:S(2)}, u32[]{:S(2)}) %collective-permute-start.3) | collective-permute-done | bytes 786464 | tf_op jit(solution)/shard_map/ppermute | solution.py:64
  155.1 2.3 %add_convert_fusion = bf16[384,128,32]{1,2,0:T(8,128)(2,1)S(1)} fusion(f32[384,128,32]{1,2,0:T(8,128)S(1)} %fusion.49, f32[384,128,32]{1,2,0:T(8,128)S(1)} %fusion.51, f32[384,128,32]{1,2,0:T(8,128)S(1)} %fusion.53, bf16[4,384,128]{2,0,1:T(4,128)(2,1)S(1)} %get-tuple-element.15, bf16[4,384,128]{2,0,1:T(4,128)(2,1)S(1)} %copy-done.4, s32[32]{0:T(128)} %copy-done.8, ...), kind=kOutput, calls=%fused_computation.8 | convolution fusion | flops 33030400 | bytes 22806688 | tf_op jit(solution)/shard_map/fs,sre->rfe/dot_general | solution.py:123
  159.6 17.4 %collective-permute-done.8 = bf16[512,1024]{1,0:T(8,128)(2,1)} collective-permute-done((bf16[512,1024]{1,0:T(8,128)(2,1)S(1)}, bf16[512,1024]{1,0:T(8,128)(2,1)}, u32[]{:S(2)}, u32[]{:S(2)}) %collective-permute-start.8) | collective-permute-done | bytes 1048608 | tf_op jit(solution)/shard_map/ppermute | solution.py:41
  177.0 2.4 %constant_dynamic-update-slice_fusion = bf16[4096,1024]{1,0:T(8,128)(2,1)} fusion(bf16[4096,1024]{1,0:T(8,128)(2,1)} %constant_dynamic-update-slice_fusion.1, bf16[512,1024]{1,0:T(8,128)(2,1)} %collective-permute-done.8), kind=kLoop, calls=%fused_computation.51 | loop fusion | bytes 2097152 | tf_op jit(solution)/shard_map/concatenate | solution.py:127
  179.4 2.7 %fusion.24 = bf16[384,256]{1,0:T(8,128)(2,1)S(1)} fusion(bf16[4096,1024]{1,0:T(8,128)(2,1)} %constant_dynamic-update-slice_fusion, bf16[48,8,32,128]{3,2,1,0:T(8,128)(2,1)S(1)} %bitcast.98), kind=kOutput, calls=%fused_computation.28 | convolution fusion | flops 805404672 | bytes 5439488 | tf_op jit(solution)/shard_map/dot_general | solution.py:128
  182.1 7.0 %fusion.15 = bf16[384,512]{1,0:T(8,128)(2,1)} fusion(bf16[4096,1024]{1,0:T(8,128)(2,1)} %constant_dynamic-update-slice_fusion, bf16[384,256]{1,0:T(8,128)(2,1)S(1)} %fusion.24, f32[4096]{0:T(1024)S(1)} %bitcast.107, bf16[48,8,32,128]{3,2,1,0:T(8,128)(2,1)S(1)} %bitcast.99, f32[512]{0:T(512)S(1)} %bitcast.108), kind=kOutput, calls=%fused_computation.21 | convolution fusion | flops 2424176640 | bytes 10045440 | tf_op jit(solution)/shard_map/dot_general | solution.py:139
  189.1 3.6 %all-to-all-start = ((bf16[4,96,512]{2,1,0:T(8,128)(2,1)}), bf16[4,96,512]{2,1,0:T(8,128)(2,1)S(1)}, u32[]{:S(2)}, u32[]{:S(2)}) async-start(bf16[4,96,512]{2,1,0:T(8,128)(2,1)} %bitcast.105), calls=%async_computation | async-start | bytes 786432 | tf_op jit(solution)/shard_map/all_to_all | solution.py:141
  192.7 1.7 collective-permute-start.11
  195.8 4.7 %all-to-all-done = bf16[4,96,512]{2,1,0:T(8,128)(2,1)S(1)} async-done(((bf16[4,96,512]{2,1,0:T(8,128)(2,1)}), bf16[4,96,512]{2,1,0:T(8,128)(2,1)S(1)}, u32[]{:S(2)}, u32[]{:S(2)}) %all-to-all-start) | async-done | bytes 393248 | tf_op jit(solution)/shard_map/all_to_all | solution.py:141
  203.4 2.3 %collective-permute-done.10 = bf16[62,1024]{1,0:T(8,128)(2,1)S(1)} collective-permute-done((bf16[62,1024]{1,0:T(8,128)(2,1)}, bf16[62,1024]{1,0:T(8,128)(2,1)S(1)}, u32[]{:S(2)}, u32[]{:S(2)}) %collective-permute-start.10) | collective-permute-done | bytes 127008 | tf_op jit(solution)/shard_map/ppermute | solution.py:102
  (88 shorter events, 20.0 us)
Async XLA Ops:
  0.0 33.0 %copy-start = (f32[1,4096]{1,0:T(1,128)S(1)}, f32[1,4096]{1,0:T(1,128)}, u32[]{:S(2)}) copy-start(f32[1,4096]{1,0:T(1,128)} %param.18) | copy-start | bytes 49156
  0.0 7.7 %copy-start.1 = (s32[1,32]{1,0:T(1,128)S(1)}, s32[1,32]{1,0:T(1,128)}, u32[]{:S(2)}) copy-start(s32[1,32]{1,0:T(1,128)} %param.15) | copy-start | bytes 388
  0.0 34.1 %copy-start.2 = (bf16[1,4,1536,128]{3,2,1,0:T(8,128)(2,1)S(1)}, bf16[1,4,1536,128]{3,2,1,0:T(8,128)(2,1)}, u32[]{:S(2)}) copy-start(bf16[1,4,1536,128]{3,2,1,0:T(8,128)(2,1)} %param.14) | copy-start | bytes 4718596
  0.0 34.1 %copy-start.3 = (bf16[1,4,1536,128]{3,2,1,0:T(8,128)(2,1)S(1)}, bf16[1,4,1536,128]{3,2,1,0:T(8,128)(2,1)}, u32[]{:S(2)}) copy-start(bf16[1,4,1536,128]{3,2,1,0:T(8,128)(2,1)} %param.13) | copy-start | bytes 4718596
  4.4 28.5 %collective-permute-start = (bf16[512,1024]{1,0:T(8,128)(2,1)}, bf16[512,1024]{1,0:T(8,128)(2,1)}, u32[]{:S(2)}, u32[]{:S(2)}) collective-permute-start(bf16[512,1024]{1,0:T(8,128)(2,1)} %constant_dynamic-slice_fusion.8), channel_id=1, source_target_pairs={{0,4},{4,8},{8,12},{12,0},{1,5},{5,9},{9,13},{13,1},{2,6},{6,10},{... | collective-permute-start | bytes 3145736 | tf_op jit(solution)/shard_map/ppermute | solution.py:34
  32.9 26.5 %collective-permute-start.1 = (bf16[512,1024]{1,0:T(8,128)(2,1)}, bf16[512,1024]{1,0:T(8,128)(2,1)}, u32[]{:S(2)}, u32[]{:S(2)}) collective-permute-start(bf16[512,1024]{1,0:T(8,128)(2,1)} %collective-permute-done), channel_id=1, source_target_pairs={{0,4},{4,8},{8,12},{12,0},{1,5},{5,9},{9,13},{13,1},{2,6},{6,10},{... | collective-permute-start | bytes 3145736 | tf_op jit(solution)/shard_map/ppermute | solution.py:34
  42.3 26.9 %collective-permute-start.5 = (bf16[512,1024]{1,0:T(8,128)(2,1)}, bf16[512,1024]{1,0:T(8,128)(2,1)S(1)}, u32[]{:S(2)}, u32[]{:S(2)}) collective-permute-start(bf16[512,1024]{1,0:T(8,128)(2,1)} %collective-permute-done), channel_id=1, source_target_pairs={{0,16},{16,0},{1,17},{17,1},{2,18},{18,2},{3,19},{19,3},{4,20},{20... | collective-permute-start | bytes 3145736 | tf_op jit(solution)/shard_map/ppermute | solution.py:41
  62.6 19.2 %collective-permute-start.4 = (bf16[8,384,128]{2,0,1:T(8,128)(2,1)}, bf16[8,384,128]{2,0,1:T(8,128)(2,1)}, u32[]{:S(2)}, u32[]{:S(2)}) collective-permute-start(bf16[8,384,128]{2,0,1:T(8,128)(2,1)} %pad_maximum_fusion.3), channel_id=1, source_target_pairs={{0,12},{4,0},{8,4},{12,8},{1,13},{5,1},{9,5},{13,9},{2,14},{6,2},{... | collective-permute-start | bytes 2359304 | tf_op jit(solution)/shard_map/ppermute | solution.py:64
  62.6 90.3 %copy-start.8 = (s32[32]{0:T(128)}, s32[32]{0:T(128)S(1)}, u32[]{:S(2)}) copy-start(s32[32]{0:T(128)S(1)} %concatenate.169) | copy-start | bytes 388
  65.4 86.5 %collective-permute-start.3 = (bf16[8,384,128]{2,0,1:T(8,128)(2,1)S(1)}, bf16[8,384,128]{2,0,1:T(8,128)(2,1)S(1)}, u32[]{:S(2)}, u32[]{:S(2)}) collective-permute-start(bf16[8,384,128]{2,0,1:T(8,128)(2,1)S(1)} %pad_maximum_fusion.2), channel_id=1, source_target_pairs={{0,8},{4,12},{8,0},{12,4},{1,9},{5,13},{9,1},{13,5},{2,10},{6,14},... | collective-permute-start | bytes 2359304 | tf_op jit(solution)/shard_map/ppermute | solution.py:64
  65.8 87.1 %collective-permute-start.2 = (bf16[8,384,128]{2,0,1:T(8,128)(2,1)S(1)}, bf16[8,384,128]{2,0,1:T(8,128)(2,1)S(1)}, u32[]{:S(2)}, u32[]{:S(2)}) collective-permute-start(bf16[8,384,128]{2,0,1:T(8,128)(2,1)S(1)} %pad_maximum_fusion.1), channel_id=1, source_target_pairs={{0,4},{4,8},{8,12},{12,0},{1,5},{5,9},{9,13},{13,1},{2,6},{6,10},{... | collective-permute-start | bytes 2359304 | tf_op jit(solution)/shard_map/ppermute | solution.py:64
  67.9 89.5 %collective-permute-start.6 = (bf16[512,1024]{1,0:T(8,128)(2,1)}, bf16[512,1024]{1,0:T(8,128)(2,1)S(1)}, u32[]{:S(2)}, u32[]{:S(2)}) collective-permute-start(bf16[512,1024]{1,0:T(8,128)(2,1)} %collective-permute-done.1), channel_id=1, source_target_pairs={{0,16},{16,0},{1,17},{17,1},{2,18},{18,2},{3,19},{19,3},{4,20},{20... | collective-permute-start | bytes 3145736 | tf_op jit(solution)/shard_map/ppermute | solution.py:41
  69.2 84.8 %collective-permute-start.7 = (bf16[512,1024]{1,0:T(8,128)(2,1)}, bf16[512,1024]{1,0:T(8,128)(2,1)S(1)}, u32[]{:S(2)}, u32[]{:S(2)}) collective-permute-start(bf16[512,1024]{1,0:T(8,128)(2,1)} %collective-permute-done.1), channel_id=1, source_target_pairs={{0,4},{4,8},{8,12},{12,0},{1,5},{5,9},{9,13},{13,1},{2,6},{6,10},{... | collective-permute-start | bytes 3145736 | tf_op jit(solution)/shard_map/ppermute | solution.py:34
  152.9 2.2 %copy-start.4 = (bf16[4,384,128]{2,0,1:T(4,128)(2,1)S(1)}, bf16[4,384,128]{2,0,1:T(4,128)(2,1)}, u32[]{:S(2)}) copy-start(bf16[4,384,128]{2,0,1:T(4,128)(2,1)} %get-tuple-element.11) | copy-start | bytes 1179652
  154.0 23.0 %collective-permute-start.8 = (bf16[512,1024]{1,0:T(8,128)(2,1)S(1)}, bf16[512,1024]{1,0:T(8,128)(2,1)}, u32[]{:S(2)}, u32[]{:S(2)}) collective-permute-start(bf16[512,1024]{1,0:T(8,128)(2,1)S(1)} %collective-permute-done.7), channel_id=1, source_target_pairs={{0,16},{16,0},{1,17},{17,1},{2,18},{18,2},{3,19},{19,3},{4,20},{20... | collective-permute-start | bytes 3145736 | tf_op jit(solution)/shard_map/ppermute | solution.py:41
  179.4 2.7 %copy-start.7 = (f32[32,128]{1,0:T(8,128)S(1)}, f32[32,128]{1,0:T(8,128)}, u32[]{:S(2)}) copy-start(f32[32,128]{1,0:T(8,128)} %gather_fusion.4) | copy-start | bytes 49156
  179.4 2.7 %copy-start.11 = (f32[1,512]{1,0:T(1,128)S(1)}, f32[1,512]{1,0:T(1,128)}, u32[]{:S(2)}) copy-start(f32[1,512]{1,0:T(1,128)} %param.20) | copy-start | bytes 6148
  189.1 13.5 %copy-start.5 = (bf16[96,128]{1,0:T(8,128)(2,1)S(1)}, bf16[96,128]{1,0:T(8,128)(2,1)}, u32[]{:S(2)}) copy-start(bf16[96,128]{1,0:T(8,128)(2,1)} %param.21) | copy-start | bytes 73732
  189.1 13.5 %copy-start.6 = (bf16[62,1024]{1,0:T(8,128)(2,1)S(1)}, bf16[62,1024]{1,0:T(8,128)(2,1)}, u32[]{:S(2)}) copy-start(bf16[62,1024]{1,0:T(8,128)(2,1)} %param.22) | copy-start | bytes 380932
  189.1 16.6 %copy-start.9 = (f32[1024]{0:T(1024)S(1)}, f32[1024]{0:T(1024)}, u32[]{:S(2)}) copy-start(f32[1024]{0:T(1024)} %param.23) | copy-start | bytes 12292
  189.1 11.5 %all-to-all-start = ((bf16[4,96,512]{2,1,0:T(8,128)(2,1)}), bf16[4,96,512]{2,1,0:T(8,128)(2,1)S(1)}, u32[]{:S(2)}, u32[]{:S(2)}) async-start(bf16[4,96,512]{2,1,0:T(8,128)(2,1)} %bitcast.105), calls=%async_computation | async-start | bytes 786432 | tf_op jit(solution)/shard_map/all_to_all | solution.py:141
  192.7 10.4 %collective-permute-start.11 = (bf16[62,1024]{1,0:T(8,128)(2,1)}, bf16[62,1024]{1,0:T(8,128)(2,1)S(1)}, u32[]{:S(2)}, u32[]{:S(2)}) collective-permute-start(bf16[62,1024]{1,0:T(8,128)(2,1)} %param.22), channel_id=1, source_target_pairs={{0,3},{1,0},{2,1},{3,2},{4,7},{5,4},{6,5},{7,6},{8,11},{9,8},{10,9... | collective-permute-start | bytes 380936 | tf_op jit(solution)/shard_map/ppermute | solution.py:102
  194.4 8.4 %collective-permute-start.9 = (bf16[62,1024]{1,0:T(8,128)(2,1)}, bf16[62,1024]{1,0:T(8,128)(2,1)S(1)}, u32[]{:S(2)}, u32[]{:S(2)}) collective-permute-start(bf16[62,1024]{1,0:T(8,128)(2,1)} %param.22), channel_id=1, source_target_pairs={{0,1},{1,2},{2,3},{3,0},{4,5},{5,6},{6,7},{7,4},{8,9},{9,10},{10,1... | collective-permute-start | bytes 380936 | tf_op jit(solution)/shard_map/ppermute | solution.py:102
  194.4 11.3 %collective-permute-start.10 = (bf16[62,1024]{1,0:T(8,128)(2,1)}, bf16[62,1024]{1,0:T(8,128)(2,1)S(1)}, u32[]{:S(2)}, u32[]{:S(2)}) collective-permute-start(bf16[62,1024]{1,0:T(8,128)(2,1)} %param.22), channel_id=1, source_target_pairs={{0,2},{1,3},{2,0},{3,1},{4,6},{5,7},{6,4},{7,5},{8,10},{9,11},{10,... | collective-permute-start | bytes 380936 | tf_op jit(solution)/shard_map/ppermute | solution.py:102
  (1 other events, 2.2 us)

commit v8 on v6

--- a/solution.py
+++ b/solution.py
@@ -43,30 +43,35 @@
     return parts, travelling
 
 
-def exchange_rows(first, second, feat_count):
+def exchange_rows(first, second, feat_count, gate):
     slots_here, row_count, _ = first.shape
     share = row_count // feat_count
     owner = lax.axis_index("feat")
     pieces, ids = [], []
     for shift in range(feat_count):
         target = (owner + shift) % feat_count
-        piece = jnp.concatenate(
-            [
-                lax.dynamic_slice_in_dim(first, target * share, share, axis=1),
-                lax.dynamic_slice_in_dim(second, target * share, share, axis=1),
-            ],
-            0,
+        pieces.append(
+            jnp.concatenate(
+                [
+                    lax.dynamic_slice_in_dim(first, target * share, share, axis=1),
+                    lax.dynamic_slice_in_dim(second, target * share, share, axis=1),
+                ],
+                0,
+            )
         )
+    pieces, _ = lax.optimization_barrier((pieces, gate))
+    for shift in range(feat_count):
         if shift:
-            piece = lax.ppermute(
-                piece, "feat", [(source, (source + shift) % feat_count) for source in range(feat_count)]
+            pieces[shift] = lax.ppermute(
+                pieces[shift],
+                "feat",
+                [(source, (source + shift) % feat_count) for source in range(feat_count)],
             )
         source = (owner - shift) % feat_count
         local = jnp.arange(slots_here, dtype=jnp.int32)
         ids.append(
             jnp.concatenate([source * slots_here + local, (feat_count + source) * slots_here + local])
         )
-        pieces.append(piece)
     return pieces, ids
 
 
@@ -101,10 +106,7 @@
     weights_here = jnp.concatenate([cross_down[0], cross_up[0], compress_weight[0]], axis=1)
     parts, last_rows = weight_parts(weights_here, feat_count, group_count, share_count, entry_count)
 
-    first_rows, second_rows, _ = lax.optimization_barrier(
-        (pooled_first[0], pooled_second[0], last_rows)
-    )
-    pieces, slot_ids = exchange_rows(first_rows, second_rows, feat_count)
+    pieces, slot_ids = exchange_rows(pooled_first[0], pooled_second[0], feat_count, last_rows)
     row_count = pieces[0].shape[1]
     slot_count = sum(piece.shape[0] for piece in pieces)
     bias_blocks = cross_bias[0].reshape(slot_count, entry_count)

time: 185 us -> 186 us (level)
  local copies, waits for them, and re-layouts: 26.7 us -> 23.8 us
  other arithmetic: 4.81 us -> 7.59 us
    squeeze x1 -> x0, local copies, waits for them, and re-layouts: 8.15 us -> none  [on_device(): pooled_second[0]]
    dynamic_slice x1 -> x4, local copies, waits for them, and re-layouts: 0.54 us -> 3.75 us  [exchange_rows(): lax.dynamic_slice_in_dim(second, target * share, share, axis=1)]
    concatenate x3 -> x4, other arithmetic: 1.23 us -> 4.17 us  [exchange_rows(): jnp.concatenate([lax.dynamic_slice_in_dim(first, target * share, share, a...]
    ppermute x3, waiting for transfers between devices: 39.2 us -> 36.3 us  [exchange_rows(): lax.ppermute(pieces[shift], 'feat', [(source, (source + shift) % feat_cou...]
    ppermute x3, waiting for transfers between devices: 61.5 us -> 63.8 us  [weight_parts(): travelling = lax.ppermute(travelling, 'feat', ring)]
    unnamed x23 -> x21, local copies, waits for them, and re-layouts: 10.2 us -> 12.2 us
  transfers between devices with their start and end apart: 13 -> 13, of which waited for: 7 -> 7; matrix products, arithmetic and copies ran while one was open for 17% -> 18% of each run, Pallas kernels for 0% -> 0%
where the time goes in v8:
time: 186 us; the launch traced here: 185 us
  waiting for transfers between devices  120 us (65%)
  local copies, waits for them, and re-layouts  23.8 us (13%)
  matrix products  17.8 us (10%)
  starting transfers between devices  15.6 us (8%)
  other arithmetic  7.59 us (4%)
    ppermute x3, waiting for transfers between devices, weight_parts(): travelling = lax.ppermute(travelling, 'feat', ring)  63.8 us
    ppermute x3, waiting for transfers between devices, exchange_rows(): lax.ppermute(pieces[shift], 'feat', [(source, (source + shift) % feat_cou...  36.3 us
    ppermute x3, waiting for transfers between devices, weight_parts(): forwarded = lax.ppermute(travelling, 'groups', pairs)  12.3 us
    unnamed x21, local copies, waits for them, and re-layouts  12.2 us
    dot_general x1, matrix products, on_device(): jnp.dot(crossed, weights[:, 2 * rank:], preferred_element_type=jnp.float32)  7.92 us
    all_to_all x1, waiting for transfers between devices, on_device(): lax.all_to_all(compressed, 'tower', split_axis=0, concat_axis=1, tiled=True)  5.37 us
    dot_general x4, matrix products, on_device(): jnp.einsum('fs,sre->rfe', one_hot, piece, preferred_element_type=jnp.floa...  5.11 us
    concatenate x4, other arithmetic, exchange_rows(): jnp.concatenate([lax.dynamic_slice_in_dim(first, target * share, share, a...  4.17 us
  transfers between devices with their start and end apart: 13, of which 7 were waited for; matrix products, arithmetic and copies ran while one was open for 18% of the time, Pallas kernels for 0%

profile of v8, /device:TPU:0, one launch (start us, length us, event | category | flops | bytes accessed | tf_op | source)
XLA Modules:
  0.0 185.3 jit_solution(1952010134511852757)
XLA Ops:
  0.0 3.2 %pad_maximum_fusion = (bf16[1024,1024]{1,0:T(8,128)(2,1)S(1)}, bf16[4096,1024]{1,0:T(8,128)(2,1)}) fusion(bf16[1024,512]{1,0:T(8,128)(2,1)} %bitcast.126, bf16[1024,256]{1,0:T(8,128)(2,1)} %bitcast.127, bf16[1024,256]{1,0:T(8,128)(2,1)} %bitcast.128), kind=kLoop, calls=%fused_computation.16 | loop fusion | flops 6291455 | bytes 6291456 | tf_op jit(solution)/shard_map/concatenate | solution.py:106
  3.2 3.1 %collective-permute-start = (bf16[512,1024]{1,0:T(8,128)(2,1)S(1)}, bf16[512,1024]{1,0:T(8,128)(2,1)}, u32[]{:S(2)}, u32[]{:S(2)}) collective-permute-start(bf16[512,1024]{1,0:T(8,128)(2,1)S(1)} %constant_dynamic-slice_fusion), channel_id=1, source_target_pairs={{0,4},{4,8},{8,12},{12,0},{1,5},{5,9},{9,13},{13,1},{2,6},{6,10},{... | collective-permute-start | bytes 3145736 | tf_op jit(solution)/shard_map/ppermute | solution.py:31
  6.4 25.2 %collective-permute-done = bf16[512,1024]{1,0:T(8,128)(2,1)} collective-permute-done((bf16[512,1024]{1,0:T(8,128)(2,1)S(1)}, bf16[512,1024]{1,0:T(8,128)(2,1)}, u32[]{:S(2)}, u32[]{:S(2)}) %collective-permute-start) | collective-permute-done | bytes 1048608 | tf_op jit(solution)/shard_map/ppermute | solution.py:31
  31.9 26.1 %collective-permute-done.1 = bf16[512,1024]{1,0:T(8,128)(2,1)} collective-permute-done((bf16[512,1024]{1,0:T(8,128)(2,1)}, bf16[512,1024]{1,0:T(8,128)(2,1)}, u32[]{:S(2)}, u32[]{:S(2)}) %collective-permute-start.1) | collective-permute-done | bytes 1048608 | tf_op jit(solution)/shard_map/ppermute | solution.py:31
  58.1 2.1 %constant_dynamic-slice_fusion.1 = (bf16[1,4,384,128]{3,2,1,0:T(8,128)(2,1)S(1)}, bf16[1,4,384,128]{3,2,1,0:T(8,128)(2,1)S(1)}, bf16[4,384,128]{2,1,0:T(8,128)(2...) fusion(bf16[1,4,1536,128]{3,2,1,0:T(8,128)(2,1)} %param.14, ...), kind=kLoop, calls=%fused_computation.67 | loop fusion | bytes 6291472 | tf_op jit(solution)/shard_map/dynamic_slice | solution.py:57
  60.2 1.3 collective-permute-start.6
  70.3 1.3 pad_maximum_fusion.3
  71.6 1.5 pad_maximum_fusion.4
  73.1 12.5 %collective-permute-done.2 = bf16[512,1024]{1,0:T(8,128)(2,1)} collective-permute-done((bf16[512,1024]{1,0:T(8,128)(2,1)}, bf16[512,1024]{1,0:T(8,128)(2,1)}, u32[]{:S(2)}, u32[]{:S(2)}) %collective-permute-start.2) | collective-permute-done | bytes 1048608 | tf_op jit(solution)/shard_map/ppermute | solution.py:31
  85.7 2.3 %constant_dynamic-update-slice_fusion.5 = bf16[4096,1024]{1,0:T(8,128)(2,1)} fusion(bf16[4096,1024]{1,0:T(8,128)(2,1)} %get-tuple-element.14, bf16[512,1024]{1,0:T(8,128)(2,1)} %collective-permute-done), kind=kLoop, calls=%fused_computation.60 | loop fusion | bytes 2097152
  88.0 2.3 %constant_dynamic-update-slice_fusion.4 = bf16[4096,1024]{1,0:T(8,128)(2,1)} fusion(bf16[4096,1024]{1,0:T(8,128)(2,1)} %constant_dynamic-update-slice_fusion.5, bf16[512,1024]{1,0:T(8,128)(2,1)} %collective-permute-done.6), kind=kLoop, calls=%fused_computation.59 | loop fusion | bytes 2097152
  90.2 2.3 %constant_dynamic-update-slice_fusion.3 = bf16[4096,1024]{1,0:T(8,128)(2,1)} fusion(bf16[4096,1024]{1,0:T(8,128)(2,1)} %constant_dynamic-update-slice_fusion.4, bf16[512,1024]{1,0:T(8,128)(2,1)} %collective-permute-done.1), kind=kLoop, calls=%fused_computation.58 | loop fusion | bytes 2097152
  92.5 3.0 %collective-permute-start.3 = (bf16[8,384,128]{2,0,1:T(8,128)(2,1)}, bf16[8,384,128]{2,0,1:T(8,128)(2,1)S(1)}, u32[]{:S(2)}, u32[]{:S(2)}) collective-permute-start(bf16[8,384,128]{2,0,1:T(8,128)(2,1)} %pad_maximum_fusion.2), channel_id=1, source_target_pairs={{0,4},{4,8},{8,12},{12,0},{1,5},{5,9},{9,13},{13,1},{2,6},{6,10},{... | collective-permute-start | bytes 2359304 | tf_op jit(solution)/shard_map/ppermute | solution.py:65
  96.8 12.3 %collective-permute-done.7 = bf16[512,1024]{1,0:T(8,128)(2,1)} collective-permute-done((bf16[512,1024]{1,0:T(8,128)(2,1)}, bf16[512,1024]{1,0:T(8,128)(2,1)}, u32[]{:S(2)}, u32[]{:S(2)}) %collective-permute-start.7) | collective-permute-done | bytes 1048608 | tf_op jit(solution)/shard_map/ppermute | solution.py:38
  109.2 2.3 %constant_dynamic-update-slice_fusion.2 = bf16[4096,1024]{1,0:T(8,128)(2,1)} fusion(bf16[4096,1024]{1,0:T(8,128)(2,1)} %constant_dynamic-update-slice_fusion.3, bf16[512,1024]{1,0:T(8,128)(2,1)} %collective-permute-done.7), kind=kLoop, calls=%fused_computation.57 | loop fusion | bytes 2097152
  111.4 2.3 %constant_dynamic-update-slice_fusion.1 = bf16[4096,1024]{1,0:T(8,128)(2,1)} fusion(bf16[4096,1024]{1,0:T(8,128)(2,1)} %constant_dynamic-update-slice_fusion.2, bf16[512,1024]{1,0:T(8,128)(2,1)} %collective-permute-done.2), kind=kLoop, calls=%fused_computation.56 | loop fusion | bytes 2097152
  114.8 36.3 %collective-permute-done.4 = bf16[8,384,128]{2,0,1:T(8,128)(2,1)S(1)} collective-permute-done((bf16[8,384,128]{2,0,1:T(8,128)(2,1)}, bf16[8,384,128]{2,0,1:T(8,128)(2,1)S(1)}, u32[]{:S(2)}, u32[]{:S(2)}) %collective-permute-start.4) | collective-permute-done | bytes 786464 | tf_op jit(solution)/shard_map/ppermute | solution.py:65
  153.3 1.9 %add_convert_fusion = bf16[384,128,32]{1,2,0:T(8,128)(2,1)S(1)} fusion(f32[384,128,32]{1,2,0:T(8,128)S(1)} %fusion.44, f32[384,128,32]{1,2,0:T(8,128)S(1)} %fusion.46, f32[384,128,32]{1,2,0:T(8,128)S(1)} %fusion.48, bf16[8,384,128]{2,1,0:T(8,128)(2,1)S(1)} %pad_maximum_fusion.1, s32[32]{0:T(128)S(1)} %concatenate.172, s32[8]{0:T(128)S(1)} %gather_fusion), kind=kOutput, calls=%fused_computation.8 | convolution fusion | flops 31457536 | bytes 22806688 | tf_op jit(solution)/shard_map/fs,sre->rfe/dot_general | solution.py:122
  157.1 2.7 %fusion.24 = bf16[384,256]{1,0:T(8,128)(2,1)S(1)} fusion(bf16[4096,1024]{1,0:T(8,128)(2,1)} %constant_dynamic-update-slice_fusion, bf16[48,8,32,128]{3,2,1,0:T(8,128)(2,1)S(1)} %bitcast.116), kind=kOutput, calls=%fused_computation.26 | convolution fusion | flops 805404672 | bytes 5439488 | tf_op jit(solution)/shard_map/dot_general | solution.py:127
  159.8 7.9 %fusion.15 = bf16[384,512]{1,0:T(8,128)(2,1)} fusion(bf16[4096,1024]{1,0:T(8,128)(2,1)} %constant_dynamic-update-slice_fusion, bf16[384,256]{1,0:T(8,128)(2,1)S(1)} %fusion.24, f32[4096]{0:T(1024)S(1)} %bitcast.130, bf16[48,8,32,128]{3,2,1,0:T(8,128)(2,1)} %bitcast.117, f32[512]{0:T(512)S(1)} %bitcast.131), kind=kOutput, calls=%fused_computation.19 | convolution fusion | flops 2424176640 | bytes 10045440 | tf_op jit(solution)/shard_map/dot_general | solution.py:138
  167.8 3.6 %all-to-all-start = ((bf16[4,96,512]{2,1,0:T(8,128)(2,1)}), bf16[4,96,512]{2,1,0:T(8,128)(2,1)S(1)}, u32[]{:S(2)}, u32[]{:S(2)}) async-start(bf16[4,96,512]{2,1,0:T(8,128)(2,1)} %bitcast.40), calls=%async_computation | async-start | bytes 786432 | tf_op jit(solution)/shard_map/all_to_all | solution.py:140
  171.4 1.7 collective-permute-start.11
  173.9 5.4 %all-to-all-done = bf16[4,96,512]{2,1,0:T(8,128)(2,1)S(1)} async-done(((bf16[4,96,512]{2,1,0:T(8,128)(2,1)}), bf16[4,96,512]{2,1,0:T(8,128)(2,1)S(1)}, u32[]{:S(2)}, u32[]{:S(2)}) %all-to-all-start) | async-done | bytes 393248 | tf_op jit(solution)/shard_map/all_to_all | solution.py:140
  182.0 2.3 %collective-permute-done.10 = bf16[62,1024]{1,0:T(8,128)(2,1)S(1)} collective-permute-done((bf16[62,1024]{1,0:T(8,128)(2,1)S(1)}, bf16[62,1024]{1,0:T(8,128)(2,1)S(1)}, u32[]{:S(2)}, u32[]{:S(2)}) %collective-permute-start.10) | collective-permute-done | bytes 127008 | tf_op jit(solution)/shard_map/ppermute | solution.py:104
  (85 shorter events, 20.1 us)
Async XLA Ops:
  0.0 67.5 %copy-start = (f32[1,4096]{1,0:T(1,128)S(1)}, f32[1,4096]{1,0:T(1,128)}, u32[]{:S(2)}) copy-start(f32[1,4096]{1,0:T(1,128)} %param.18) | copy-start | bytes 49156
  3.2 61.8 %copy-start.1 = (s32[1,32]{1,0:T(1,128)S(1)}, s32[1,32]{1,0:T(1,128)}, u32[]{:S(2)}) copy-start(s32[1,32]{1,0:T(1,128)} %param.15) | copy-start | bytes 388
  3.2 28.4 %collective-permute-start = (bf16[512,1024]{1,0:T(8,128)(2,1)S(1)}, bf16[512,1024]{1,0:T(8,128)(2,1)}, u32[]{:S(2)}, u32[]{:S(2)}) collective-permute-start(bf16[512,1024]{1,0:T(8,128)(2,1)S(1)} %constant_dynamic-slice_fusion), channel_id=1, source_target_pairs={{0,4},{4,8},{8,12},{12,0},{1,5},{5,9},{9,13},{13,1},{2,6},{6,10},{... | collective-permute-start | bytes 3145736 | tf_op jit(solution)/shard_map/ppermute | solution.py:31
  31.6 26.5 %collective-permute-start.1 = (bf16[512,1024]{1,0:T(8,128)(2,1)}, bf16[512,1024]{1,0:T(8,128)(2,1)}, u32[]{:S(2)}, u32[]{:S(2)}) collective-permute-start(bf16[512,1024]{1,0:T(8,128)(2,1)} %collective-permute-done), channel_id=1, source_target_pairs={{0,4},{4,8},{8,12},{12,0},{1,5},{5,9},{9,13},{13,1},{2,6},{6,10},{... | collective-permute-start | bytes 3145736 | tf_op jit(solution)/shard_map/ppermute | solution.py:31
  58.1 27.5 %collective-permute-start.2 = (bf16[512,1024]{1,0:T(8,128)(2,1)}, bf16[512,1024]{1,0:T(8,128)(2,1)}, u32[]{:S(2)}, u32[]{:S(2)}) collective-permute-start(bf16[512,1024]{1,0:T(8,128)(2,1)} %collective-permute-done.1), channel_id=1, source_target_pairs={{0,4},{4,8},{8,12},{12,0},{1,5},{5,9},{9,13},{13,1},{2,6},{6,10},{... | collective-permute-start | bytes 3145736 | tf_op jit(solution)/shard_map/ppermute | solution.py:31
  60.2 27.8 %collective-permute-start.6 = (bf16[512,1024]{1,0:T(8,128)(2,1)}, bf16[512,1024]{1,0:T(8,128)(2,1)}, u32[]{:S(2)}, u32[]{:S(2)}) collective-permute-start(bf16[512,1024]{1,0:T(8,128)(2,1)} %collective-permute-done), channel_id=1, source_target_pairs={{0,16},{16,0},{1,17},{17,1},{2,18},{18,2},{3,19},{19,3},{4,20},{20... | collective-permute-start | bytes 3145736 | tf_op jit(solution)/shard_map/ppermute | solution.py:38
  68.1 41.0 %collective-permute-start.7 = (bf16[512,1024]{1,0:T(8,128)(2,1)}, bf16[512,1024]{1,0:T(8,128)(2,1)}, u32[]{:S(2)}, u32[]{:S(2)}) collective-permute-start(bf16[512,1024]{1,0:T(8,128)(2,1)} %collective-permute-done.1), channel_id=1, source_target_pairs={{0,16},{16,0},{1,17},{17,1},{2,18},{18,2},{3,19},{19,3},{4,20},{20... | collective-permute-start | bytes 3145736 | tf_op jit(solution)/shard_map/ppermute | solution.py:38
  85.6 28.1 %collective-permute-start.5 = (bf16[8,384,128]{2,0,1:T(8,128)(2,1)S(1)}, bf16[8,384,128]{2,0,1:T(8,128)(2,1)S(1)}, u32[]{:S(2)}, u32[]{:S(2)}) collective-permute-start(bf16[8,384,128]{2,0,1:T(8,128)(2,1)S(1)} %pad_maximum_fusion.4), channel_id=1, source_target_pairs={{0,12},{4,0},{8,4},{12,8},{1,13},{5,1},{9,5},{13,9},{2,14},{6,2},{... | collective-permute-start | bytes 2359304 | tf_op jit(solution)/shard_map/ppermute | solution.py:65
  90.2 60.8 %collective-permute-start.4 = (bf16[8,384,128]{2,0,1:T(8,128)(2,1)}, bf16[8,384,128]{2,0,1:T(8,128)(2,1)S(1)}, u32[]{:S(2)}, u32[]{:S(2)}) collective-permute-start(bf16[8,384,128]{2,0,1:T(8,128)(2,1)} %pad_maximum_fusion.3), channel_id=1, source_target_pairs={{0,8},{4,12},{8,0},{12,4},{1,9},{5,13},{9,1},{13,5},{2,10},{6,14},... | collective-permute-start | bytes 2359304 | tf_op jit(solution)/shard_map/ppermute | solution.py:65
  92.5 59.6 %collective-permute-start.3 = (bf16[8,384,128]{2,0,1:T(8,128)(2,1)}, bf16[8,384,128]{2,0,1:T(8,128)(2,1)S(1)}, u32[]{:S(2)}, u32[]{:S(2)}) collective-permute-start(bf16[8,384,128]{2,0,1:T(8,128)(2,1)} %pad_maximum_fusion.2), channel_id=1, source_target_pairs={{0,4},{4,8},{8,12},{12,0},{1,5},{5,9},{9,13},{13,1},{2,6},{6,10},{... | collective-permute-start | bytes 2359304 | tf_op jit(solution)/shard_map/ppermute | solution.py:65
  95.6 59.6 %collective-permute-start.8 = (bf16[512,1024]{1,0:T(8,128)(2,1)}, bf16[512,1024]{1,0:T(8,128)(2,1)S(1)}, u32[]{:S(2)}, u32[]{:S(2)}) collective-permute-start(bf16[512,1024]{1,0:T(8,128)(2,1)} %collective-permute-done.2), channel_id=1, source_target_pairs={{0,16},{16,0},{1,17},{17,1},{2,18},{18,2},{3,19},{19,3},{4,20},{20... | collective-permute-start | bytes 3145736 | tf_op jit(solution)/shard_map/ppermute | solution.py:38
  155.1 2.0 %copy-start.2 = (bf16[384,128,32]{1,2,0:T(8,128)(2,1)}, bf16[384,128,32]{1,2,0:T(8,128)(2,1)S(1)}, u32[]{:S(2)}) copy-start(bf16[384,128,32]{1,2,0:T(8,128)(2,1)S(1)} %add_convert_fusion) | copy-start | bytes 9437188
  155.2 4.6 %copy-start.7 = (f32[1,512]{1,0:T(1,128)S(1)}, f32[1,512]{1,0:T(1,128)}, u32[]{:S(2)}) copy-start(f32[1,512]{1,0:T(1,128)} %param.20) | copy-start | bytes 6148
  159.8 11.6 %copy-start.4 = (bf16[62,1024]{1,0:T(8,128)(2,1)S(1)}, bf16[62,1024]{1,0:T(8,128)(2,1)}, u32[]{:S(2)}) copy-start(bf16[62,1024]{1,0:T(8,128)(2,1)} %param.22) | copy-start | bytes 380932
  159.8 14.1 %copy-start.6 = (s32[120]{0:T(128)S(1)}, s32[120]{0:T(128)}, u32[]{:S(2)}) copy-start(s32[120]{0:T(128)} %constant.151) | copy-start | bytes 1444
  159.8 21.4 %copy-start.3 = (bf16[96,128]{1,0:T(8,128)(2,1)S(1)}, bf16[96,128]{1,0:T(8,128)(2,1)}, u32[]{:S(2)}) copy-start(bf16[96,128]{1,0:T(8,128)(2,1)} %param.21) | copy-start | bytes 73732
  167.8 16.6 %copy-start.5 = (f32[1024]{0:T(1024)S(1)}, f32[1024]{0:T(1024)}, u32[]{:S(2)}) copy-start(f32[1024]{0:T(1024)} %param.23) | copy-start | bytes 12292
  167.8 11.5 %all-to-all-start = ((bf16[4,96,512]{2,1,0:T(8,128)(2,1)}), bf16[4,96,512]{2,1,0:T(8,128)(2,1)S(1)}, u32[]{:S(2)}, u32[]{:S(2)}) async-start(bf16[4,96,512]{2,1,0:T(8,128)(2,1)} %bitcast.40), calls=%async_computation | async-start | bytes 786432 | tf_op jit(solution)/shard_map/all_to_all | solution.py:140
  171.4 10.4 %collective-permute-start.11 = (bf16[62,1024]{1,0:T(8,128)(2,1)S(1)}, bf16[62,1024]{1,0:T(8,128)(2,1)S(1)}, u32[]{:S(2)}, u32[]{:S(2)}) collective-permute-start(bf16[62,1024]{1,0:T(8,128)(2,1)S(1)} %copy-done.4), channel_id=1, source_target_pairs={{0,3},{1,0},{2,1},{3,2},{4,7},{5,4},{6,5},{7,6},{8,11},{9,8},{10,9... | collective-permute-start | bytes 380936 | tf_op jit(solution)/shard_map/ppermute | solution.py:104
  173.1 8.4 %collective-permute-start.9 = (bf16[62,1024]{1,0:T(8,128)(2,1)S(1)}, bf16[62,1024]{1,0:T(8,128)(2,1)S(1)}, u32[]{:S(2)}, u32[]{:S(2)}) collective-permute-start(bf16[62,1024]{1,0:T(8,128)(2,1)S(1)} %copy-done.4), channel_id=1, source_target_pairs={{0,1},{1,2},{2,3},{3,0},{4,5},{5,6},{6,7},{7,4},{8,9},{9,10},{10,1... | collective-permute-start | bytes 380936 | tf_op jit(solution)/shard_map/ppermute | solution.py:104
  173.1 11.3 %collective-permute-start.10 = (bf16[62,1024]{1,0:T(8,128)(2,1)S(1)}, bf16[62,1024]{1,0:T(8,128)(2,1)S(1)}, u32[]{:S(2)}, u32[]{:S(2)}) collective-permute-start(bf16[62,1024]{1,0:T(8,128)(2,1)S(1)} %copy-done.4), channel_id=1, source_target_pairs={{0,2},{1,3},{2,0},{3,1},{4,6},{5,7},{6,4},{7,5},{8,10},{9,11},{10,... | collective-permute-start | bytes 380936 | tf_op jit(solution)/shard_map/ppermute | solution.py:104

commit v9 on v6

--- a/solution.py
+++ b/solution.py
@@ -26,20 +26,27 @@
         travelling = lax.dynamic_slice_in_dim(weights_here, group * piece, piece, axis=0)
     else:
         travelling = weights_here
+    chunk_count = 2 if blocks_piece % 2 == 0 else 1
+    chunk_blocks = blocks_piece // chunk_count
+    chunk_rows = chunk_blocks * entry_count
+    chunk_range = jnp.arange(chunk_blocks, dtype=jnp.int32)
+    rings = [
+        lax.slice_in_dim(travelling, chunk * chunk_rows, (chunk + 1) * chunk_rows, axis=0)
+        for chunk in range(chunk_count)
+    ]
     ring = [(source, (source + 1) % feat_count) for source in range(feat_count)]
     for step in range(1, feat_count):
-        travelling = lax.ppermute(travelling, "feat", ring)
         source_block = (owner - step) % feat_count
-        parts.append(
-            (travelling, source_block * blocks_here + group * blocks_piece + block_range)
-        )
-        for shift in range(1, share_count):
-            pairs = [(source, (source + shift) % group_count) for source in range(group_count)]
-            forwarded = lax.ppermute(travelling, "groups", pairs)
-            from_group = (group - shift) % group_count
-            parts.append(
-                (forwarded, source_block * blocks_here + from_group * blocks_piece + block_range)
-            )
+        for chunk in range(chunk_count):
+            rings[chunk] = lax.ppermute(rings[chunk], "feat", ring)
+            first_block = source_block * blocks_here + chunk * chunk_blocks
+            parts.append((rings[chunk], first_block + group * blocks_piece + chunk_range))
+            for shift in range(1, share_count):
+                pairs = [(source, (source + shift) % group_count) for source in range(group_count)]
+                forwarded = lax.ppermute(rings[chunk], "groups", pairs)
+                from_group = (group - shift) % group_count
+                parts.append((forwarded, first_block + from_group * blocks_piece + chunk_range))
+    travelling = rings
     return parts, travelling
 
 

time: 185 us -> 179 us (0.968)
  waiting for transfers between devices: 119 us -> 101 us
  local copies, waits for them, and re-layouts: 26.7 us -> 35.4 us
  starting transfers between devices: 16.8 us -> 20.5 us
    ppermute x6 -> x12, waiting for transfers between devices: 72.5 us -> 52.8 us  [the longest x6 38.6 us: weight_parts(): rings[chunk] = lax.ppermute(rings[chunk], 'feat', ring)]
    unnamed x23 -> x25, local copies, waits for them, and re-layouts: 10.2 us -> 15.5 us
    ppermute x6 -> x12, starting transfers between devices: 6.47 us -> 11.7 us  [the longest x6 6.27 us: weight_parts(): forwarded = lax.ppermute(rings[chunk], 'groups', pairs)]
    squeeze x1, local copies, waits for them, and re-layouts: 8.15 us -> 12 us  [on_device(): pooled_second[0]]
  transfers between devices with their start and end apart: 13 -> 19, of which waited for: 7 -> 10; matrix products, arithmetic and copies ran while one was open for 17% -> 22% of each run, Pallas kernels for 0% -> 0%
where the time goes in v9:
time: 179 us; the launch traced here: 178 us
  waiting for transfers between devices  101 us (56%)
  local copies, waits for them, and re-layouts  35.4 us (20%)
  starting transfers between devices  20.5 us (11%)
  matrix products  16.6 us (9%)
  other arithmetic  4.75 us (3%)
    ppermute x3, waiting for transfers between devices, exchange_rows(): lax.ppermute(piece, 'feat', [(source, (source + shift) % feat_count) for...  40.1 us
    ppermute x6, waiting for transfers between devices, weight_parts(): rings[chunk] = lax.ppermute(rings[chunk], 'feat', ring)  38.6 us
    unnamed x25, local copies, waits for them, and re-layouts  15.5 us
    ppermute x6, waiting for transfers between devices, weight_parts(): forwarded = lax.ppermute(rings[chunk], 'groups', pairs)  14.2 us
    squeeze x1, local copies, waits for them, and re-layouts, on_device(): pooled_second[0]  12 us
    dot_general x1, matrix products, on_device(): jnp.dot(crossed, weights[:, 2 * rank:], preferred_element_type=jnp.float32)  6.99 us
    ppermute x6, starting transfers between devices, weight_parts(): forwarded = lax.ppermute(rings[chunk], 'groups', pairs)  6.27 us
    ppermute x6, starting transfers between devices, weight_parts(): rings[chunk] = lax.ppermute(rings[chunk], 'feat', ring)  5.39 us
  transfers between devices with their start and end apart: 19, of which 10 were waited for; matrix products, arithmetic and copies ran while one was open for 22% of the time, Pallas kernels for 0%

profile of v9, /device:TPU:0, one launch (start us, length us, event | category | flops | bytes accessed | tf_op | source)
XLA Modules:
  0.0 178.4 jit_solution(8262448125429391541)
XLA Ops:
  0.0 3.2 %pad_maximum_fusion = (bf16[1024,1024]{1,0:T(8,128)(2,1)S(1)}, bf16[4096,1024]{1,0:T(8,128)(2,1)}) fusion(bf16[1024,512]{1,0:T(8,128)(2,1)} %bitcast.114, bf16[1024,256]{1,0:T(8,128)(2,1)} %bitcast.115, bf16[1024,256]{1,0:T(8,128)(2,1)} %bitcast.116), kind=kLoop, calls=%fused_computation.16 | loop fusion | flops 6291455 | bytes 6291456 | tf_op jit(solution)/shard_map/concatenate | solution.py:108
  4.3 3.0 %collective-permute-start = (bf16[256,1024]{1,0:T(8,128)(2,1)}, bf16[256,1024]{1,0:T(8,128)(2,1)}, u32[]{:S(2)}, u32[]{:S(2)}) collective-permute-start(bf16[256,1024]{1,0:T(8,128)(2,1)} %get-tuple-element.10), channel_id=1, source_target_pairs={{0,4},{4,8},{8,12},{12,0},{1,5},{5,9},{9,13},{13,1},{2,6},{6,10},{... | collective-permute-start | bytes 1572872 | tf_op jit(solution)/shard_map/ppermute | solution.py:41
  9.5 12.0 %copy_bitcast_fusion = (bf16[4,1536,128]{2,0,1:T(4,128)(2,1)S(1)}, bf16[4,1536,128]{2,0,1:T(4,128)(2,1)S(1)}) fusion(bf16[1,4,1536,128]{3,2,1,0:T(8,128)(2,1)} %param.14, bf16[1,4,1536,128]{3,2,1,0:T(8,128)(2,1)} %param.13), kind=kLoop, calls=%fused_computation.17 | loop fusion | bytes 6291456 | tf_op jit(solution)/shard_map/squeeze | solution.py:112
  23.1 10.5 %collective-permute-done.3 = bf16[256,1024]{1,0:T(8,128)(2,1)} collective-permute-done((bf16[256,1024]{1,0:T(8,128)(2,1)}, bf16[256,1024]{1,0:T(8,128)(2,1)}, u32[]{:S(2)}, u32[]{:S(2)}) %collective-permute-start.3) | collective-permute-done | bytes 524320 | tf_op jit(solution)/shard_map/ppermute | solution.py:41
  33.7 1.7 collective-permute-start.9
  39.1 5.8 %collective-permute-done.1 = bf16[256,1024]{1,0:T(8,128)(2,1)} collective-permute-done((bf16[256,1024]{1,0:T(8,128)(2,1)}, bf16[256,1024]{1,0:T(8,128)(2,1)}, u32[]{:S(2)}, u32[]{:S(2)}) %collective-permute-start.1) | collective-permute-done | bytes 524320 | tf_op jit(solution)/shard_map/ppermute | solution.py:41
  44.9 11.2 %collective-permute-done.4 = bf16[256,1024]{1,0:T(8,128)(2,1)} collective-permute-done((bf16[256,1024]{1,0:T(8,128)(2,1)}, bf16[256,1024]{1,0:T(8,128)(2,1)}, u32[]{:S(2)}, u32[]{:S(2)}) %collective-permute-start.4) | collective-permute-done | bytes 524320 | tf_op jit(solution)/shard_map/ppermute | solution.py:41
  56.1 1.9 %constant_dynamic-update-slice_fusion.11 = bf16[4096,1024]{1,0:T(8,128)(2,1)} fusion(bf16[4096,1024]{1,0:T(8,128)(2,1)} %get-tuple-element.12, bf16[256,1024]{1,0:T(8,128)(2,1)} %collective-permute-done), kind=kLoop, calls=%fused_computation.56 | loop fusion | bytes 1048576
  60.0 1.9 %constant_dynamic-update-slice_fusion.10 = bf16[4096,1024]{1,0:T(8,128)(2,1)} fusion(bf16[4096,1024]{1,0:T(8,128)(2,1)} %constant_dynamic-update-slice_fusion.11, bf16[256,1024]{1,0:T(8,128)(2,1)} %collective-permute-done.9), kind=kLoop, calls=%fused_computation.55 | loop fusion | bytes 1048576
  61.9 1.9 %constant_dynamic-update-slice_fusion.9 = bf16[4096,1024]{1,0:T(8,128)(2,1)} fusion(bf16[4096,1024]{1,0:T(8,128)(2,1)} %constant_dynamic-update-slice_fusion.10, bf16[256,1024]{1,0:T(8,128)(2,1)} %collective-permute-done.3), kind=kLoop, calls=%fused_computation.54 | loop fusion | bytes 1048576
  63.8 1.9 %constant_dynamic-update-slice_fusion.8 = bf16[4096,1024]{1,0:T(8,128)(2,1)} fusion(bf16[4096,1024]{1,0:T(8,128)(2,1)} %constant_dynamic-update-slice_fusion.9, bf16[256,1024]{1,0:T(8,128)(2,1)} %collective-permute-done.10), kind=kLoop, calls=%fused_computation.53 | loop fusion | bytes 1048576
  65.7 1.9 %constant_dynamic-update-slice_fusion.7 = bf16[4096,1024]{1,0:T(8,128)(2,1)} fusion(bf16[4096,1024]{1,0:T(8,128)(2,1)} %constant_dynamic-update-slice_fusion.8, bf16[256,1024]{1,0:T(8,128)(2,1)} %collective-permute-done.1), kind=kLoop, calls=%fused_computation.52 | loop fusion | bytes 1048576
  67.5 10.1 %collective-permute-done.5 = bf16[256,1024]{1,0:T(8,128)(2,1)S(1)} collective-permute-done((bf16[256,1024]{1,0:T(8,128)(2,1)}, bf16[256,1024]{1,0:T(8,128)(2,1)S(1)}, u32[]{:S(2)}, u32[]{:S(2)}) %collective-permute-start.5) | collective-permute-done | bytes 524320 | tf_op jit(solution)/shard_map/ppermute | solution.py:41
  79.2 1.8 %collective-permute-start.8 = (bf16[8,384,128]{2,0,1:T(8,128)(2,1)S(1)}, bf16[8,384,128]{2,0,1:T(8,128)(2,1)S(1)}, u32[]{:S(2)}, u32[]{:S(2)}) collective-permute-start(bf16[8,384,128]{2,0,1:T(8,128)(2,1)S(1)} %pad_maximum_fusion.3), channel_id=1, source_target_pairs={{0,12},{4,0},{8,4},{12,8},{1,13},{5,1},{9,5},{13,9},{2,14},{6,2},{... | collective-permute-start | bytes 2359304 | tf_op jit(solution)/shard_map/ppermute | solution.py:68
  84.9 1.9 %constant_dynamic-update-slice_fusion.5 = bf16[4096,1024]{1,0:T(8,128)(2,1)} fusion(bf16[4096,1024]{1,0:T(8,128)(2,1)} %constant_dynamic-update-slice_fusion.6, bf16[256,1024]{1,0:T(8,128)(2,1)} %collective-permute-done.4), kind=kLoop, calls=%fused_computation.50 | loop fusion | bytes 1048576
  89.4 7.0 %collective-permute-done.13 = bf16[256,1024]{1,0:T(8,128)(2,1)S(1)} collective-permute-done((bf16[256,1024]{1,0:T(8,128)(2,1)S(1)}, bf16[256,1024]{1,0:T(8,128)(2,1)S(1)}, u32[]{:S(2)}, u32[]{:S(2)}) %collective-permute-start.13) | collective-permute-done | bytes 524320 | tf_op jit(solution)/shard_map/ppermute | solution.py:46
  98.1 7.2 %collective-permute-done.14 = bf16[256,1024]{1,0:T(8,128)(2,1)S(1)} collective-permute-done((bf16[256,1024]{1,0:T(8,128)(2,1)S(1)}, bf16[256,1024]{1,0:T(8,128)(2,1)S(1)}, u32[]{:S(2)}, u32[]{:S(2)}) %collective-permute-start.14) | collective-permute-done | bytes 524320 | tf_op jit(solution)/shard_map/ppermute | solution.py:46
  107.2 40.1 %collective-permute-done.7 = bf16[8,384,128]{2,0,1:T(8,128)(2,1)S(1)} collective-permute-done((bf16[8,384,128]{2,0,1:T(8,128)(2,1)S(1)}, bf16[8,384,128]{2,0,1:T(8,128)(2,1)S(1)}, u32[]{:S(2)}, u32[]{:S(2)}) %collective-permute-start.7) | collective-permute-done | bytes 786464 | tf_op jit(solution)/shard_map/ppermute | solution.py:68
  151.2 2.7 %fusion.24 = bf16[384,256]{1,0:T(8,128)(2,1)S(1)} fusion(bf16[4096,1024]{1,0:T(8,128)(2,1)} %constant_dynamic-update-slice_fusion, bf16[48,8,32,128]{3,2,1,0:T(8,128)(2,1)S(1)} %bitcast.110), kind=kOutput, calls=%fused_computation.28 | convolution fusion | flops 805404672 | bytes 5439488 | tf_op jit(solution)/shard_map/dot_general | solution.py:132
  153.9 7.0 %fusion.15 = bf16[384,512]{1,0:T(8,128)(2,1)} fusion(bf16[4096,1024]{1,0:T(8,128)(2,1)} %constant_dynamic-update-slice_fusion, bf16[384,256]{1,0:T(8,128)(2,1)S(1)} %fusion.24, f32[4096]{0:T(1024)S(1)} %bitcast.118, bf16[48,8,32,128]{3,2,1,0:T(8,128)(2,1)S(1)} %bitcast.111, f32[512]{0:T(512)S(1)} %bitcast.119), kind=kOutput, calls=%fused_computation.21 | convolution fusion | flops 2424176640 | bytes 10045440 | tf_op jit(solution)/shard_map/dot_general | solution.py:143
  160.9 3.6 %all-to-all-start = ((bf16[4,96,512]{2,1,0:T(8,128)(2,1)}), bf16[4,96,512]{2,1,0:T(8,128)(2,1)S(1)}, u32[]{:S(2)}, u32[]{:S(2)}) async-start(bf16[4,96,512]{2,1,0:T(8,128)(2,1)} %bitcast.40), calls=%async_computation | async-start | bytes 786432 | tf_op jit(solution)/shard_map/all_to_all | solution.py:145
  164.5 1.7 collective-permute-start.17
  167.0 5.4 %all-to-all-done = bf16[4,96,512]{2,1,0:T(8,128)(2,1)S(1)} async-done(((bf16[4,96,512]{2,1,0:T(8,128)(2,1)}), bf16[4,96,512]{2,1,0:T(8,128)(2,1)S(1)}, u32[]{:S(2)}, u32[]{:S(2)}) %all-to-all-start) | async-done | bytes 393248 | tf_op jit(solution)/shard_map/all_to_all | solution.py:145
  175.1 2.3 %collective-permute-done.16 = bf16[62,1024]{1,0:T(8,128)(2,1)S(1)} collective-permute-done((bf16[62,1024]{1,0:T(8,128)(2,1)S(1)}, bf16[62,1024]{1,0:T(8,128)(2,1)S(1)}, u32[]{:S(2)}, u32[]{:S(2)}) %collective-permute-start.16) | collective-permute-done | bytes 127008 | tf_op jit(solution)/shard_map/ppermute | solution.py:106
  (107 shorter events, 30.4 us)
Async XLA Ops:
  0.0 38.4 %copy-start = (f32[1,4096]{1,0:T(1,128)S(1)}, f32[1,4096]{1,0:T(1,128)}, u32[]{:S(2)}) copy-start(f32[1,4096]{1,0:T(1,128)} %param.18) | copy-start | bytes 49156
  0.0 35.4 %copy-start.5 = (s32[120]{0:T(128)S(1)}, s32[120]{0:T(128)}, u32[]{:S(2)}) copy-start(s32[120]{0:T(128)} %constant.149) | copy-start | bytes 1444
  0.0 35.8 %copy-start.1 = (s32[1,32]{1,0:T(1,128)S(1)}, s32[1,32]{1,0:T(1,128)}, u32[]{:S(2)}) copy-start(s32[1,32]{1,0:T(1,128)} %param.15) | copy-start | bytes 388
  4.3 18.1 %collective-permute-start = (bf16[256,1024]{1,0:T(8,128)(2,1)}, bf16[256,1024]{1,0:T(8,128)(2,1)}, u32[]{:S(2)}, u32[]{:S(2)}) collective-permute-start(bf16[256,1024]{1,0:T(8,128)(2,1)} %get-tuple-element.10), channel_id=1, source_target_pairs={{0,4},{4,8},{8,12},{12,0},{1,5},{5,9},{9,13},{13,1},{2,6},{6,10},{... | collective-permute-start | bytes 1572872 | tf_op jit(solution)/shard_map/ppermute | solution.py:41
  7.3 26.3 %collective-permute-start.3 = (bf16[256,1024]{1,0:T(8,128)(2,1)}, bf16[256,1024]{1,0:T(8,128)(2,1)}, u32[]{:S(2)}, u32[]{:S(2)}) collective-permute-start(bf16[256,1024]{1,0:T(8,128)(2,1)} %get-tuple-element.9), channel_id=1, source_target_pairs={{0,4},{4,8},{8,12},{12,0},{1,5},{5,9},{9,13},{13,1},{2,6},{6,10},{... | collective-permute-start | bytes 1572872 | tf_op jit(solution)/shard_map/ppermute | solution.py:41
  22.4 22.5 %collective-permute-start.1 = (bf16[256,1024]{1,0:T(8,128)(2,1)}, bf16[256,1024]{1,0:T(8,128)(2,1)}, u32[]{:S(2)}, u32[]{:S(2)}) collective-permute-start(bf16[256,1024]{1,0:T(8,128)(2,1)} %collective-permute-done), channel_id=1, source_target_pairs={{0,4},{4,8},{8,12},{12,0},{1,5},{5,9},{9,13},{13,1},{2,6},{6,10},{... | collective-permute-start | bytes 1572872 | tf_op jit(solution)/shard_map/ppermute | solution.py:41
  33.6 22.5 %collective-permute-start.4 = (bf16[256,1024]{1,0:T(8,128)(2,1)}, bf16[256,1024]{1,0:T(8,128)(2,1)}, u32[]{:S(2)}, u32[]{:S(2)}) collective-permute-start(bf16[256,1024]{1,0:T(8,128)(2,1)} %collective-permute-done.3), channel_id=1, source_target_pairs={{0,4},{4,8},{8,12},{12,0},{1,5},{5,9},{9,13},{13,1},{2,6},{6,10},{... | collective-permute-start | bytes 1572872 | tf_op jit(solution)/shard_map/ppermute | solution.py:41
  33.7 26.1 %collective-permute-start.9 = (bf16[256,1024]{1,0:T(8,128)(2,1)}, bf16[256,1024]{1,0:T(8,128)(2,1)}, u32[]{:S(2)}, u32[]{:S(2)}) collective-permute-start(bf16[256,1024]{1,0:T(8,128)(2,1)} %collective-permute-done), channel_id=1, source_target_pairs={{0,16},{16,0},{1,17},{17,1},{2,18},{18,2},{3,19},{19,3},{4,20},{20... | collective-permute-start | bytes 1572872 | tf_op jit(solution)/shard_map/ppermute | solution.py:46
  35.4 28.4 %collective-permute-start.10 = (bf16[256,1024]{1,0:T(8,128)(2,1)}, bf16[256,1024]{1,0:T(8,128)(2,1)}, u32[]{:S(2)}, u32[]{:S(2)}) collective-permute-start(bf16[256,1024]{1,0:T(8,128)(2,1)} %collective-permute-done.3), channel_id=1, source_target_pairs={{0,16},{16,0},{1,17},{17,1},{2,18},{18,2},{3,19},{19,3},{4,20},{20... | collective-permute-start | bytes 1572872 | tf_op jit(solution)/shard_map/ppermute | solution.py:46
  44.9 22.7 %collective-permute-start.2 = (bf16[256,1024]{1,0:T(8,128)(2,1)}, bf16[256,1024]{1,0:T(8,128)(2,1)S(1)}, u32[]{:S(2)}, u32[]{:S(2)}) collective-permute-start(bf16[256,1024]{1,0:T(8,128)(2,1)} %collective-permute-done.1), channel_id=1, source_target_pairs={{0,4},{4,8},{8,12},{12,0},{1,5},{5,9},{9,13},{13,1},{2,6},{6,10},{... | collective-permute-start | bytes 1572872 | tf_op jit(solution)/shard_map/ppermute | solution.py:41
  56.1 21.5 %collective-permute-start.5 = (bf16[256,1024]{1,0:T(8,128)(2,1)}, bf16[256,1024]{1,0:T(8,128)(2,1)S(1)}, u32[]{:S(2)}, u32[]{:S(2)}) collective-permute-start(bf16[256,1024]{1,0:T(8,128)(2,1)} %collective-permute-done.4), channel_id=1, source_target_pairs={{0,4},{4,8},{8,12},{12,0},{1,5},{5,9},{9,13},{13,1},{2,6},{6,10},{... | collective-permute-start | bytes 1572872 | tf_op jit(solution)/shard_map/ppermute | solution.py:41
  58.0 25.4 %collective-permute-start.11 = (bf16[256,1024]{1,0:T(8,128)(2,1)}, bf16[256,1024]{1,0:T(8,128)(2,1)S(1)}, u32[]{:S(2)}, u32[]{:S(2)}) collective-permute-start(bf16[256,1024]{1,0:T(8,128)(2,1)} %collective-permute-done.1), channel_id=1, source_target_pairs={{0,16},{16,0},{1,17},{17,1},{2,18},{18,2},{3,19},{19,3},{4,20},{20... | collective-permute-start | bytes 1572872 | tf_op jit(solution)/shard_map/ppermute | solution.py:46
  59.7 27.0 %collective-permute-start.12 = (bf16[256,1024]{1,0:T(8,128)(2,1)}, bf16[256,1024]{1,0:T(8,128)(2,1)S(1)}, u32[]{:S(2)}, u32[]{:S(2)}) collective-permute-start(bf16[256,1024]{1,0:T(8,128)(2,1)} %collective-permute-done.4), channel_id=1, source_target_pairs={{0,16},{16,0},{1,17},{17,1},{2,18},{18,2},{3,19},{19,3},{4,20},{20... | collective-permute-start | bytes 1572872 | tf_op jit(solution)/shard_map/ppermute | solution.py:46
  79.2 27.0 %collective-permute-start.8 = (bf16[8,384,128]{2,0,1:T(8,128)(2,1)S(1)}, bf16[8,384,128]{2,0,1:T(8,128)(2,1)S(1)}, u32[]{:S(2)}, u32[]{:S(2)}) collective-permute-start(bf16[8,384,128]{2,0,1:T(8,128)(2,1)S(1)} %pad_maximum_fusion.3), channel_id=1, source_target_pairs={{0,12},{4,0},{8,4},{12,8},{1,13},{5,1},{9,5},{13,9},{2,14},{6,2},{... | collective-permute-start | bytes 2359304 | tf_op jit(solution)/shard_map/ppermute | solution.py:68
  81.4 66.0 %collective-permute-start.7 = (bf16[8,384,128]{2,0,1:T(8,128)(2,1)S(1)}, bf16[8,384,128]{2,0,1:T(8,128)(2,1)S(1)}, u32[]{:S(2)}, u32[]{:S(2)}) collective-permute-start(bf16[8,384,128]{2,0,1:T(8,128)(2,1)S(1)} %pad_maximum_fusion.2), channel_id=1, source_target_pairs={{0,8},{4,12},{8,0},{12,4},{1,9},{5,13},{9,1},{13,5},{2,10},{6,14},... | collective-permute-start | bytes 2359304 | tf_op jit(solution)/shard_map/ppermute | solution.py:68
  81.4 14.9 %collective-permute-start.13 = (bf16[256,1024]{1,0:T(8,128)(2,1)S(1)}, bf16[256,1024]{1,0:T(8,128)(2,1)S(1)}, u32[]{:S(2)}, u32[]{:S(2)}) collective-permute-start(bf16[256,1024]{1,0:T(8,128)(2,1)S(1)} %collective-permute-done.2), channel_id=1, source_target_pairs={{0,16},{16,0},{1,17},{17,1},{2,18},{18,2},{3,19},{19,3},{4,20},{20... | collective-permute-start | bytes 1572872 | tf_op jit(solution)/shard_map/ppermute | solution.py:46
  83.4 21.8 %collective-permute-start.14 = (bf16[256,1024]{1,0:T(8,128)(2,1)S(1)}, bf16[256,1024]{1,0:T(8,128)(2,1)S(1)}, u32[]{:S(2)}, u32[]{:S(2)}) collective-permute-start(bf16[256,1024]{1,0:T(8,128)(2,1)S(1)} %collective-permute-done.5), channel_id=1, source_target_pairs={{0,16},{16,0},{1,17},{17,1},{2,18},{18,2},{3,19},{19,3},{4,20},{20... | collective-permute-start | bytes 1572872 | tf_op jit(solution)/shard_map/ppermute | solution.py:46
  86.7 61.7 %collective-permute-start.6 = (bf16[8,384,128]{2,0,1:T(8,128)(2,1)S(1)}, bf16[8,384,128]{2,0,1:T(8,128)(2,1)S(1)}, u32[]{:S(2)}, u32[]{:S(2)}) collective-permute-start(bf16[8,384,128]{2,0,1:T(8,128)(2,1)S(1)} %pad_maximum_fusion.1), channel_id=1, source_target_pairs={{0,4},{4,8},{8,12},{12,0},{1,5},{5,9},{9,13},{13,1},{2,6},{6,10},{... | collective-permute-start | bytes 2359304 | tf_op jit(solution)/shard_map/ppermute | solution.py:68
  153.9 20.4 %copy-start.2 = (bf16[96,128]{1,0:T(8,128)(2,1)S(1)}, bf16[96,128]{1,0:T(8,128)(2,1)}, u32[]{:S(2)}) copy-start(bf16[96,128]{1,0:T(8,128)(2,1)} %param.21) | copy-start | bytes 73732
  160.9 16.6 %copy-start.4 = (f32[1024]{0:T(1024)S(1)}, f32[1024]{0:T(1024)}, u32[]{:S(2)}) copy-start(f32[1024]{0:T(1024)} %param.23) | copy-start | bytes 12292
  160.9 11.5 %all-to-all-start = ((bf16[4,96,512]{2,1,0:T(8,128)(2,1)}), bf16[4,96,512]{2,1,0:T(8,128)(2,1)S(1)}, u32[]{:S(2)}, u32[]{:S(2)}) async-start(bf16[4,96,512]{2,1,0:T(8,128)(2,1)} %bitcast.40), calls=%async_computation | async-start | bytes 786432 | tf_op jit(solution)/shard_map/all_to_all | solution.py:145
  164.5 10.4 %collective-permute-start.17 = (bf16[62,1024]{1,0:T(8,128)(2,1)S(1)}, bf16[62,1024]{1,0:T(8,128)(2,1)S(1)}, u32[]{:S(2)}, u32[]{:S(2)}) collective-permute-start(bf16[62,1024]{1,0:T(8,128)(2,1)S(1)} %copy-done.3), channel_id=1, source_target_pairs={{0,3},{1,0},{2,1},{3,2},{4,7},{5,4},{6,5},{7,6},{8,11},{9,8},{10,9... | collective-permute-start | bytes 380936 | tf_op jit(solution)/shard_map/ppermute | solution.py:106
  166.2 8.4 %collective-permute-start.15 = (bf16[62,1024]{1,0:T(8,128)(2,1)S(1)}, bf16[62,1024]{1,0:T(8,128)(2,1)S(1)}, u32[]{:S(2)}, u32[]{:S(2)}) collective-permute-start(bf16[62,1024]{1,0:T(8,128)(2,1)S(1)} %copy-done.3), channel_id=1, source_target_pairs={{0,1},{1,2},{2,3},{3,0},{4,5},{5,6},{6,7},{7,4},{8,9},{9,10},{10,1... | collective-permute-start | bytes 380936 | tf_op jit(solution)/shard_map/ppermute | solution.py:106
  166.2 11.3 %collective-permute-start.16 = (bf16[62,1024]{1,0:T(8,128)(2,1)S(1)}, bf16[62,1024]{1,0:T(8,128)(2,1)S(1)}, u32[]{:S(2)}, u32[]{:S(2)}) collective-permute-start(bf16[62,1024]{1,0:T(8,128)(2,1)S(1)} %copy-done.3), channel_id=1, source_target_pairs={{0,2},{1,3},{2,0},{3,1},{4,6},{5,7},{6,4},{7,5},{8,10},{9,11},{10,... | collective-permute-start | bytes 380936 | tf_op jit(solution)/shard_map/ppermute | solution.py:106
  (2 other events, 13.3 us)

commit v10 on v9

--- a/solution.py
+++ b/solution.py
@@ -26,7 +26,7 @@
         travelling = lax.dynamic_slice_in_dim(weights_here, group * piece, piece, axis=0)
     else:
         travelling = weights_here
-    chunk_count = 2 if blocks_piece % 2 == 0 else 1
+    chunk_count = next(count for count in (4, 2, 1) if blocks_piece % count == 0)
     chunk_blocks = blocks_piece // chunk_count
     chunk_rows = chunk_blocks * entry_count
     chunk_range = jnp.arange(chunk_blocks, dtype=jnp.int32)

time: 179 us -> 179 us (level)
  waiting for transfers between devices: 101 us -> 71.9 us
  starting transfers between devices: 20.5 us -> 41.8 us
  local copies, waits for them, and re-layouts: 35.4 us -> 42.2 us
    ppermute x6 -> x12, waiting for transfers between devices: 38.6 us -> 17.3 us  [weight_parts(): rings[chunk] = lax.ppermute(rings[chunk], 'feat', ring)]
    ppermute x6 -> x12, starting transfers between devices: 6.27 us -> 17 us  [weight_parts(): forwarded = lax.ppermute(rings[chunk], 'groups', pairs)]
    ppermute x6 -> x12, starting transfers between devices: 5.39 us -> 16 us  [weight_parts(): rings[chunk] = lax.ppermute(rings[chunk], 'feat', ring)]
    unnamed x25 -> x37, local copies, waits for them, and re-layouts: 15.5 us -> 22.5 us
    ppermute x6 -> x12, waiting for transfers between devices: 14.2 us -> 10.3 us  [weight_parts(): forwarded = lax.ppermute(rings[chunk], 'groups', pairs)]
    ppermute x3, waiting for transfers between devices: 40.1 us -> 36.5 us  [exchange_rows(): lax.ppermute(piece, 'feat', [(source, (source + shift) % feat_count) for...]
  transfers between devices with their start and end apart: 19 -> 31, of which waited for: 10 -> 13; matrix products, arithmetic and copies ran while one was open for 22% -> 26% of each run, Pallas kernels for 0% -> 0%
where the time goes in v10:
time: 179 us
  waiting for transfers between devices  71.9 us (40%)
  local copies, waits for them, and re-layouts  42.2 us (24%)
  starting transfers between devices  41.8 us (23%)
  matrix products  17.7 us (10%)
  other arithmetic  4.67 us (3%)
    ppermute x3, waiting for transfers between devices, exchange_rows(): lax.ppermute(piece, 'feat', [(source, (source + shift) % feat_count) for...  36.5 us
    unnamed x37, local copies, waits for them, and re-layouts  22.5 us
    ppermute x12, waiting for transfers between devices, weight_parts(): rings[chunk] = lax.ppermute(rings[chunk], 'feat', ring)  17.3 us
    ppermute x12, starting transfers between devices, weight_parts(): forwarded = lax.ppermute(rings[chunk], 'groups', pairs)  17 us
    ppermute x12, starting transfers between devices, weight_parts(): rings[chunk] = lax.ppermute(rings[chunk], 'feat', ring)  16 us
    squeeze x1, local copies, waits for them, and re-layouts, on_device(): pooled_second[0]  12 us
    ppermute x12, waiting for transfers between devices, weight_parts(): forwarded = lax.ppermute(rings[chunk], 'groups', pairs)  10.3 us
    dot_general x1, matrix products, on_device(): jnp.dot(crossed, weights[:, 2 * rank:], preferred_element_type=jnp.float32)  7.28 us
  transfers between devices with their start and end apart: 31, of which 13 were waited for; matrix products, arithmetic and copies ran while one was open for 26% of the time, Pallas kernels for 0%

profile of v10, /device:TPU:0, one launch (start us, length us, event | category | flops | bytes accessed | tf_op | source)
XLA Modules:
  0.0 178.7 jit_solution(11782700645112761163)
XLA Ops:
  0.0 3.2 %pad_maximum_fusion = (bf16[1024,1024]{1,0:T(8,128)(2,1)S(1)}, bf16[4096,1024]{1,0:T(8,128)(2,1)}) fusion(bf16[1024,512]{1,0:T(8,128)(2,1)} %bitcast.138, bf16[1024,256]{1,0:T(8,128)(2,1)} %bitcast.139, bf16[1024,256]{1,0:T(8,128)(2,1)} %bitcast.140), kind=kLoop, calls=%fused_computation.16 | loop fusion | flops 6291455 | bytes 6291456 | tf_op jit(solution)/shard_map/concatenate | solution.py:108
  4.1 3.0 %collective-permute-start = (bf16[128,1024]{1,0:T(8,128)(2,1)}, bf16[128,1024]{1,0:T(8,128)(2,1)}, u32[]{:S(2)}, u32[]{:S(2)}) collective-permute-start(bf16[128,1024]{1,0:T(8,128)(2,1)} %get-tuple-element.11), channel_id=1, source_target_pairs={{0,4},{4,8},{8,12},{12,0},{1,5},{5,9},{9,13},{13,1},{2,6},{6,10},{... | collective-permute-start | bytes 786440 | tf_op jit(solution)/shard_map/ppermute | solution.py:41
  10.7 12.0 %copy_bitcast_fusion = (bf16[4,1536,128]{2,0,1:T(4,128)(2,1)S(1)}, bf16[4,1536,128]{2,0,1:T(4,128)(2,1)S(1)}) fusion(bf16[1,4,1536,128]{3,2,1,0:T(8,128)(2,1)} %param.14, bf16[1,4,1536,128]{3,2,1,0:T(8,128)(2,1)} %param.13), kind=kLoop, calls=%fused_computation.17 | loop fusion | bytes 6291456 | tf_op jit(solution)/shard_map/squeeze | solution.py:112
  22.8 1.8 collective-permute-start.15
  28.2 1.8 %collective-permute-start.1 = (bf16[128,1024]{1,0:T(8,128)(2,1)}, bf16[128,1024]{1,0:T(8,128)(2,1)S(1)}, u32[]{:S(2)}, u32[]{:S(2)}) collective-permute-start(bf16[128,1024]{1,0:T(8,128)(2,1)} %collective-permute-done), channel_id=1, source_target_pairs={{0,4},{4,8},{8,12},{12,0},{1,5},{5,9},{9,13},{13,1},{2,6},{6,10},{... | collective-permute-start | bytes 786440 | tf_op jit(solution)/shard_map/ppermute | solution.py:41
  30.0 1.7 constant_dynamic-update-slice_fusion.23
  44.3 1.7 constant_dynamic-update-slice_fusion.19
  46.0 1.9 %collective-permute-start.2 = (bf16[128,1024]{1,0:T(8,128)(2,1)S(1)}, bf16[128,1024]{1,0:T(8,128)(2,1)S(1)}, u32[]{:S(2)}, u32[]{:S(2)}) collective-permute-start(bf16[128,1024]{1,0:T(8,128)(2,1)S(1)} %collective-permute-done.1), channel_id=1, source_target_pairs={{0,4},{4,8},{8,12},{12,0},{1,5},{5,9},{9,13},{13,1},{2,6},{6,10},{... | collective-permute-start | bytes 786440 | tf_op jit(solution)/shard_map/ppermute | solution.py:41
  50.8 5.6 %collective-permute-done.10 = bf16[128,1024]{1,0:T(8,128)(2,1)S(1)} collective-permute-done((bf16[128,1024]{1,0:T(8,128)(2,1)}, bf16[128,1024]{1,0:T(8,128)(2,1)S(1)}, u32[]{:S(2)}, u32[]{:S(2)}) %collective-permute-start.10) | collective-permute-done | bytes 262176 | tf_op jit(solution)/shard_map/ppermute | solution.py:41
  63.7 3.9 %collective-permute-done.5 = bf16[128,1024]{1,0:T(8,128)(2,1)S(1)} collective-permute-done((bf16[128,1024]{1,0:T(8,128)(2,1)S(1)}, bf16[128,1024]{1,0:T(8,128)(2,1)S(1)}, u32[]{:S(2)}, u32[]{:S(2)}) %collective-permute-start.5) | collective-permute-done | bytes 262176 | tf_op jit(solution)/shard_map/ppermute | solution.py:41
  69.3 3.9 %collective-permute-done.8 = bf16[128,1024]{1,0:T(8,128)(2,1)S(1)} collective-permute-done((bf16[128,1024]{1,0:T(8,128)(2,1)S(1)}, bf16[128,1024]{1,0:T(8,128)(2,1)S(1)}, u32[]{:S(2)}, u32[]{:S(2)}) %collective-permute-start.8) | collective-permute-done | bytes 262176 | tf_op jit(solution)/shard_map/ppermute | solution.py:41
  74.9 2.5 %collective-permute-done.11 = bf16[128,1024]{1,0:T(8,128)(2,1)S(1)} collective-permute-done((bf16[128,1024]{1,0:T(8,128)(2,1)S(1)}, bf16[128,1024]{1,0:T(8,128)(2,1)S(1)}, u32[]{:S(2)}, u32[]{:S(2)}) %collective-permute-start.11) | collective-permute-done | bytes 262176 | tf_op jit(solution)/shard_map/ppermute | solution.py:41
  79.0 1.8 %collective-permute-start.14 = (bf16[8,384,128]{2,0,1:T(8,128)(2,1)S(1)}, bf16[8,384,128]{2,0,1:T(8,128)(2,1)S(1)}, u32[]{:S(2)}, u32[]{:S(2)}) collective-permute-start(bf16[8,384,128]{2,0,1:T(8,128)(2,1)S(1)} %pad_maximum_fusion.3), channel_id=1, source_target_pairs={{0,12},{4,0},{8,4},{12,8},{1,13},{5,1},{9,5},{13,9},{2,14},{6,2},{... | collective-permute-start | bytes 2359304 | tf_op jit(solution)/shard_map/ppermute | solution.py:68
  90.6 4.3 %collective-permute-done.23 = bf16[128,1024]{1,0:T(8,128)(2,1)S(1)} collective-permute-done((bf16[128,1024]{1,0:T(8,128)(2,1)S(1)}, bf16[128,1024]{1,0:T(8,128)(2,1)S(1)}, u32[]{:S(2)}, u32[]{:S(2)}) %collective-permute-start.23) | collective-permute-done | bytes 262176 | tf_op jit(solution)/shard_map/ppermute | solution.py:46
  97.9 2.6 %collective-permute-done.24 = bf16[128,1024]{1,0:T(8,128)(2,1)S(1)} collective-permute-done((bf16[128,1024]{1,0:T(8,128)(2,1)S(1)}, bf16[128,1024]{1,0:T(8,128)(2,1)S(1)}, u32[]{:S(2)}, u32[]{:S(2)}) %collective-permute-start.24) | collective-permute-done | bytes 262176 | tf_op jit(solution)/shard_map/ppermute | solution.py:46
  103.5 2.1 %collective-permute-done.25 = bf16[128,1024]{1,0:T(8,128)(2,1)S(1)} collective-permute-done((bf16[128,1024]{1,0:T(8,128)(2,1)S(1)}, bf16[128,1024]{1,0:T(8,128)(2,1)S(1)}, u32[]{:S(2)}, u32[]{:S(2)}) %collective-permute-start.25) | collective-permute-done | bytes 262176 | tf_op jit(solution)/shard_map/ppermute | solution.py:46
  110.2 36.5 %collective-permute-done.13 = bf16[8,384,128]{2,0,1:T(8,128)(2,1)S(1)} collective-permute-done((bf16[8,384,128]{2,0,1:T(8,128)(2,1)S(1)}, bf16[8,384,128]{2,0,1:T(8,128)(2,1)S(1)}, u32[]{:S(2)}, u32[]{:S(2)}) %collective-permute-start.13) | collective-permute-done | bytes 786464 | tf_op jit(solution)/shard_map/ppermute | solution.py:68
  148.9 1.8 add_convert_fusion
  150.6 3.4 %fusion.24 = bf16[384,256]{1,0:T(8,128)(2,1)} fusion(bf16[4096,1024]{1,0:T(8,128)(2,1)} %constant_dynamic-update-slice_fusion, bf16[48,8,32,128]{3,2,1,0:T(8,128)(2,1)S(1)} %bitcast.134), kind=kOutput, calls=%fused_computation.28 | convolution fusion | flops 805404672 | bytes 5439488 | tf_op jit(solution)/shard_map/dot_general | solution.py:132
  154.0 7.3 %fusion.15 = bf16[384,512]{1,0:T(8,128)(2,1)} fusion(bf16[4096,1024]{1,0:T(8,128)(2,1)} %constant_dynamic-update-slice_fusion, bf16[384,256]{1,0:T(8,128)(2,1)} %fusion.24, f32[4096]{0:T(1024)S(1)} %bitcast.143, bf16[48,8,32,128]{3,2,1,0:T(8,128)(2,1)S(1)} %bitcast.135, f32[512]{0:T(512)S(1)} %bitcast.144), kind=kOutput, calls=%fused_computation.21 | convolution fusion | flops 2424176640 | bytes 10045440 | tf_op jit(solution)/shard_map/dot_general | solution.py:143
  161.3 3.5 %all-to-all-start = ((bf16[4,96,512]{2,1,0:T(8,128)(2,1)}), bf16[4,96,512]{2,1,0:T(8,128)(2,1)S(1)}, u32[]{:S(2)}, u32[]{:S(2)}) async-start(bf16[4,96,512]{2,1,0:T(8,128)(2,1)} %bitcast.141), calls=%async_computation | async-start | bytes 786432 | tf_op jit(solution)/shard_map/all_to_all | solution.py:145
  164.8 1.7 collective-permute-start.29
  167.3 5.4 %all-to-all-done = bf16[4,96,512]{2,1,0:T(8,128)(2,1)S(1)} async-done(((bf16[4,96,512]{2,1,0:T(8,128)(2,1)}), bf16[4,96,512]{2,1,0:T(8,128)(2,1)S(1)}, u32[]{:S(2)}, u32[]{:S(2)}) %all-to-all-start) | async-done | bytes 393248 | tf_op jit(solution)/shard_map/all_to_all | solution.py:145
  175.4 2.3 %collective-permute-done.28 = bf16[62,1024]{1,0:T(8,128)(2,1)S(1)} collective-permute-done((bf16[62,1024]{1,0:T(8,128)(2,1)S(1)}, bf16[62,1024]{1,0:T(8,128)(2,1)S(1)}, u32[]{:S(2)}, u32[]{:S(2)}) %collective-permute-start.28) | collective-permute-done | bytes 127008 | tf_op jit(solution)/shard_map/ppermute | solution.py:106
  (125 shorter events, 62.7 us)
Async XLA Ops:
  4.1 18.6 %collective-permute-start = (bf16[128,1024]{1,0:T(8,128)(2,1)}, bf16[128,1024]{1,0:T(8,128)(2,1)}, u32[]{:S(2)}, u32[]{:S(2)}) collective-permute-start(bf16[128,1024]{1,0:T(8,128)(2,1)} %get-tuple-element.11), channel_id=1, source_target_pairs={{0,4},{4,8},{8,12},{12,0},{1,5},{5,9},{9,13},{13,1},{2,6},{6,10},{... | collective-permute-start | bytes 786440 | tf_op jit(solution)/shard_map/ppermute | solution.py:41
  7.1 17.4 %collective-permute-start.3 = (bf16[128,1024]{1,0:T(8,128)(2,1)}, bf16[128,1024]{1,0:T(8,128)(2,1)}, u32[]{:S(2)}, u32[]{:S(2)}) collective-permute-start(bf16[128,1024]{1,0:T(8,128)(2,1)} %get-tuple-element.10), channel_id=1, source_target_pairs={{0,4},{4,8},{8,12},{12,0},{1,5},{5,9},{9,13},{13,1},{2,6},{6,10},{... | collective-permute-start | bytes 786440 | tf_op jit(solution)/shard_map/ppermute | solution.py:41
  8.7 23.0 %collective-permute-start.6 = (bf16[128,1024]{1,0:T(8,128)(2,1)}, bf16[128,1024]{1,0:T(8,128)(2,1)}, u32[]{:S(2)}, u32[]{:S(2)}) collective-permute-start(bf16[128,1024]{1,0:T(8,128)(2,1)} %get-tuple-element.12), channel_id=1, source_target_pairs={{0,4},{4,8},{8,12},{12,0},{1,5},{5,9},{9,13},{13,1},{2,6},{6,10},{... | collective-permute-start | bytes 786440 | tf_op jit(solution)/shard_map/ppermute | solution.py:41
  10.3 26.2 %collective-permute-start.9 = (bf16[128,1024]{1,0:T(8,128)(2,1)S(1)}, bf16[128,1024]{1,0:T(8,128)(2,1)}, u32[]{:S(2)}, u32[]{:S(2)}) collective-permute-start(bf16[128,1024]{1,0:T(8,128)(2,1)S(1)} %get-tuple-element.9), channel_id=1, source_target_pairs={{0,4},{4,8},{8,12},{12,0},{1,5},{5,9},{9,13},{13,1},{2,6},{6,10},{... | collective-permute-start | bytes 786440 | tf_op jit(solution)/shard_map/ppermute | solution.py:41
  24.5 13.6 %collective-permute-start.16 = (bf16[128,1024]{1,0:T(8,128)(2,1)}, bf16[128,1024]{1,0:T(8,128)(2,1)}, u32[]{:S(2)}, u32[]{:S(2)}) collective-permute-start(bf16[128,1024]{1,0:T(8,128)(2,1)} %collective-permute-done.3), channel_id=1, source_target_pairs={{0,16},{16,0},{1,17},{17,1},{2,18},{18,2},{3,19},{19,3},{4,20},{20... | collective-permute-start | bytes 786440 | tf_op jit(solution)/shard_map/ppermute | solution.py:46
  28.2 17.7 %collective-permute-start.1 = (bf16[128,1024]{1,0:T(8,128)(2,1)}, bf16[128,1024]{1,0:T(8,128)(2,1)S(1)}, u32[]{:S(2)}, u32[]{:S(2)}) collective-permute-start(bf16[128,1024]{1,0:T(8,128)(2,1)} %collective-permute-done), channel_id=1, source_target_pairs={{0,4},{4,8},{8,12},{12,0},{1,5},{5,9},{9,13},{13,1},{2,6},{6,10},{... | collective-permute-start | bytes 786440 | tf_op jit(solution)/shard_map/ppermute | solution.py:41
  31.8 16.2 %collective-permute-start.4 = (bf16[128,1024]{1,0:T(8,128)(2,1)}, bf16[128,1024]{1,0:T(8,128)(2,1)S(1)}, u32[]{:S(2)}, u32[]{:S(2)}) collective-permute-start(bf16[128,1024]{1,0:T(8,128)(2,1)} %collective-permute-done.3), channel_id=1, source_target_pairs={{0,4},{4,8},{8,12},{12,0},{1,5},{5,9},{9,13},{13,1},{2,6},{6,10},{... | collective-permute-start | bytes 786440 | tf_op jit(solution)/shard_map/ppermute | solution.py:41
  36.5 14.2 %collective-permute-start.7 = (bf16[128,1024]{1,0:T(8,128)(2,1)}, bf16[128,1024]{1,0:T(8,128)(2,1)S(1)}, u32[]{:S(2)}, u32[]{:S(2)}) collective-permute-start(bf16[128,1024]{1,0:T(8,128)(2,1)} %collective-permute-done.6), channel_id=1, source_target_pairs={{0,4},{4,8},{8,12},{12,0},{1,5},{5,9},{9,13},{13,1},{2,6},{6,10},{... | collective-permute-start | bytes 786440 | tf_op jit(solution)/shard_map/ppermute | solution.py:41
  38.1 18.3 %collective-permute-start.10 = (bf16[128,1024]{1,0:T(8,128)(2,1)}, bf16[128,1024]{1,0:T(8,128)(2,1)S(1)}, u32[]{:S(2)}, u32[]{:S(2)}) collective-permute-start(bf16[128,1024]{1,0:T(8,128)(2,1)} %collective-permute-done.9), channel_id=1, source_target_pairs={{0,4},{4,8},{8,12},{12,0},{1,5},{5,9},{9,13},{13,1},{2,6},{6,10},{... | collective-permute-start | bytes 786440 | tf_op jit(solution)/shard_map/ppermute | solution.py:41
  42.7 16.1 %collective-permute-start.18 = (bf16[128,1024]{1,0:T(8,128)(2,1)}, bf16[128,1024]{1,0:T(8,128)(2,1)S(1)}, u32[]{:S(2)}, u32[]{:S(2)}) collective-permute-start(bf16[128,1024]{1,0:T(8,128)(2,1)} %collective-permute-done.9), channel_id=1, source_target_pairs={{0,16},{16,0},{1,17},{17,1},{2,18},{18,2},{3,19},{19,3},{4,20},{20... | collective-permute-start | bytes 786440 | tf_op jit(solution)/shard_map/ppermute | solution.py:46
  46.0 16.1 %collective-permute-start.2 = (bf16[128,1024]{1,0:T(8,128)(2,1)S(1)}, bf16[128,1024]{1,0:T(8,128)(2,1)S(1)}, u32[]{:S(2)}, u32[]{:S(2)}) collective-permute-start(bf16[128,1024]{1,0:T(8,128)(2,1)S(1)} %collective-permute-done.1), channel_id=1, source_target_pairs={{0,4},{4,8},{8,12},{12,0},{1,5},{5,9},{9,13},{13,1},{2,6},{6,10},{... | collective-permute-start | bytes 786440 | tf_op jit(solution)/shard_map/ppermute | solution.py:41
  47.9 19.7 %collective-permute-start.5 = (bf16[128,1024]{1,0:T(8,128)(2,1)S(1)}, bf16[128,1024]{1,0:T(8,128)(2,1)S(1)}, u32[]{:S(2)}, u32[]{:S(2)}) collective-permute-start(bf16[128,1024]{1,0:T(8,128)(2,1)S(1)} %collective-permute-done.4), channel_id=1, source_target_pairs={{0,4},{4,8},{8,12},{12,0},{1,5},{5,9},{9,13},{13,1},{2,6},{6,10},{... | collective-permute-start | bytes 786440 | tf_op jit(solution)/shard_map/ppermute | solution.py:41
  50.8 22.5 %collective-permute-start.8 = (bf16[128,1024]{1,0:T(8,128)(2,1)S(1)}, bf16[128,1024]{1,0:T(8,128)(2,1)S(1)}, u32[]{:S(2)}, u32[]{:S(2)}) collective-permute-start(bf16[128,1024]{1,0:T(8,128)(2,1)S(1)} %collective-permute-done.7), channel_id=1, source_target_pairs={{0,4},{4,8},{8,12},{12,0},{1,5},{5,9},{9,13},{13,1},{2,6},{6,10},{... | collective-permute-start | bytes 786440 | tf_op jit(solution)/shard_map/ppermute | solution.py:41
  56.4 21.1 %collective-permute-start.11 = (bf16[128,1024]{1,0:T(8,128)(2,1)S(1)}, bf16[128,1024]{1,0:T(8,128)(2,1)S(1)}, u32[]{:S(2)}, u32[]{:S(2)}) collective-permute-start(bf16[128,1024]{1,0:T(8,128)(2,1)S(1)} %collective-permute-done.10), channel_id=1, source_target_pairs={{0,4},{4,8},{8,12},{12,0},{1,5},{5,9},{9,13},{13,1},{2,6},{6,10},{... | collective-permute-start | bytes 786440 | tf_op jit(solution)/shard_map/ppermute | solution.py:41
  58.8 22.4 %collective-permute-start.19 = (bf16[128,1024]{1,0:T(8,128)(2,1)S(1)}, bf16[128,1024]{1,0:T(8,128)(2,1)S(1)}, u32[]{:S(2)}, u32[]{:S(2)}) collective-permute-start(bf16[128,1024]{1,0:T(8,128)(2,1)S(1)} %collective-permute-done.1), channel_id=1, source_target_pairs={{0,16},{16,0},{1,17},{17,1},{2,18},{18,2},{3,19},{19,3},{4,20},{20... | collective-permute-start | bytes 786440 | tf_op jit(solution)/shard_map/ppermute | solution.py:46
  62.0 21.2 %collective-permute-start.20 = (bf16[128,1024]{1,0:T(8,128)(2,1)S(1)}, bf16[128,1024]{1,0:T(8,128)(2,1)S(1)}, u32[]{:S(2)}, u32[]{:S(2)}) collective-permute-start(bf16[128,1024]{1,0:T(8,128)(2,1)S(1)} %collective-permute-done.4), channel_id=1, source_target_pairs={{0,16},{16,0},{1,17},{17,1},{2,18},{18,2},{3,19},{19,3},{4,20},{20... | collective-permute-start | bytes 786440 | tf_op jit(solution)/shard_map/ppermute | solution.py:46
  67.6 18.0 %collective-permute-start.21 = (bf16[128,1024]{1,0:T(8,128)(2,1)S(1)}, bf16[128,1024]{1,0:T(8,128)(2,1)S(1)}, u32[]{:S(2)}, u32[]{:S(2)}) collective-permute-start(bf16[128,1024]{1,0:T(8,128)(2,1)S(1)} %collective-permute-done.7), channel_id=1, source_target_pairs={{0,16},{16,0},{1,17},{17,1},{2,18},{18,2},{3,19},{19,3},{4,20},{20... | collective-permute-start | bytes 786440 | tf_op jit(solution)/shard_map/ppermute | solution.py:46
  73.2 15.4 %collective-permute-start.22 = (bf16[128,1024]{1,0:T(8,128)(2,1)S(1)}, bf16[128,1024]{1,0:T(8,128)(2,1)S(1)}, u32[]{:S(2)}, u32[]{:S(2)}) collective-permute-start(bf16[128,1024]{1,0:T(8,128)(2,1)S(1)} %collective-permute-done.10), channel_id=1, source_target_pairs={{0,16},{16,0},{1,17},{17,1},{2,18},{18,2},{3,19},{19,3},{4,20},{20... | collective-permute-start | bytes 786440 | tf_op jit(solution)/shard_map/ppermute | solution.py:46
  79.0 30.1 %collective-permute-start.14 = (bf16[8,384,128]{2,0,1:T(8,128)(2,1)S(1)}, bf16[8,384,128]{2,0,1:T(8,128)(2,1)S(1)}, u32[]{:S(2)}, u32[]{:S(2)}) collective-permute-start(bf16[8,384,128]{2,0,1:T(8,128)(2,1)S(1)} %pad_maximum_fusion.3), channel_id=1, source_target_pairs={{0,12},{4,0},{8,4},{12,8},{1,13},{5,1},{9,5},{13,9},{2,14},{6,2},{... | collective-permute-start | bytes 2359304 | tf_op jit(solution)/shard_map/ppermute | solution.py:68
  81.2 65.5 %collective-permute-start.13 = (bf16[8,384,128]{2,0,1:T(8,128)(2,1)S(1)}, bf16[8,384,128]{2,0,1:T(8,128)(2,1)S(1)}, u32[]{:S(2)}, u32[]{:S(2)}) collective-permute-start(bf16[8,384,128]{2,0,1:T(8,128)(2,1)S(1)} %pad_maximum_fusion.2), channel_id=1, source_target_pairs={{0,8},{4,12},{8,0},{12,4},{1,9},{5,13},{9,1},{13,5},{2,10},{6,14},... | collective-permute-start | bytes 2359304 | tf_op jit(solution)/shard_map/ppermute | solution.py:68
  83.2 64.6 %collective-permute-start.12 = (bf16[8,384,128]{2,0,1:T(8,128)(2,1)S(1)}, bf16[8,384,128]{2,0,1:T(8,128)(2,1)S(1)}, u32[]{:S(2)}, u32[]{:S(2)}) collective-permute-start(bf16[8,384,128]{2,0,1:T(8,128)(2,1)S(1)} %pad_maximum_fusion.1), channel_id=1, source_target_pairs={{0,4},{4,8},{8,12},{12,0},{1,5},{5,9},{9,13},{13,1},{2,6},{6,10},{... | collective-permute-start | bytes 2359304 | tf_op jit(solution)/shard_map/ppermute | solution.py:68
  88.6 11.9 %collective-permute-start.24 = (bf16[128,1024]{1,0:T(8,128)(2,1)S(1)}, bf16[128,1024]{1,0:T(8,128)(2,1)S(1)}, u32[]{:S(2)}, u32[]{:S(2)}) collective-permute-start(bf16[128,1024]{1,0:T(8,128)(2,1)S(1)} %collective-permute-done.5), channel_id=1, source_target_pairs={{0,16},{16,0},{1,17},{17,1},{2,18},{18,2},{3,19},{19,3},{4,20},{20... | collective-permute-start | bytes 786440 | tf_op jit(solution)/shard_map/ppermute | solution.py:46
  161.3 11.3 %all-to-all-start = ((bf16[4,96,512]{2,1,0:T(8,128)(2,1)}), bf16[4,96,512]{2,1,0:T(8,128)(2,1)S(1)}, u32[]{:S(2)}, u32[]{:S(2)}) async-start(bf16[4,96,512]{2,1,0:T(8,128)(2,1)} %bitcast.141), calls=%async_computation | async-start | bytes 786432 | tf_op jit(solution)/shard_map/all_to_all | solution.py:145
  166.5 11.3 %collective-permute-start.28 = (bf16[62,1024]{1,0:T(8,128)(2,1)S(1)}, bf16[62,1024]{1,0:T(8,128)(2,1)S(1)}, u32[]{:S(2)}, u32[]{:S(2)}) collective-permute-start(bf16[62,1024]{1,0:T(8,128)(2,1)S(1)} %copy-done.3), channel_id=1, source_target_pairs={{0,2},{1,3},{2,0},{3,1},{4,6},{5,7},{6,4},{7,5},{8,10},{9,11},{10,... | collective-permute-start | bytes 380936 | tf_op jit(solution)/shard_map/ppermute | solution.py:106
  (14 other events, 200.2 us)

commit v11 on v10

--- a/solution.py
+++ b/solution.py
@@ -50,7 +50,7 @@
     return parts, travelling
 
 
-def exchange_rows(first, second, feat_count):
+def exchange_rows(first, second, feat_count, tower_count, half, half_count, gate):
     slots_here, row_count, _ = first.shape
     share = row_count // feat_count
     owner = lax.axis_index("feat")
@@ -64,6 +64,13 @@
             ],
             0,
         )
+        block = share // (tower_count * half_count)
+        piece = piece.reshape(piece.shape[0], tower_count, half_count, block, piece.shape[2])
+        piece = piece[:, :, half].reshape(piece.shape[0], tower_count * block, piece.shape[4])
+        pieces.append(piece)
+    pieces, _ = lax.optimization_barrier((pieces, gate))
+    for shift in range(feat_count):
+        piece = pieces[shift]
         if shift:
             piece = lax.ppermute(
                 piece, "feat", [(source, (source + shift) % feat_count) for source in range(feat_count)]
@@ -73,7 +80,7 @@
         ids.append(
             jnp.concatenate([source * slots_here + local, (feat_count + source) * slots_here + local])
         )
-        pieces.append(piece)
+        pieces[shift] = piece
     return pieces, ids
 
 
@@ -108,60 +115,70 @@
     weights_here = jnp.concatenate([cross_down[0], cross_up[0], compress_weight[0]], axis=1)
     parts, last_rows = weight_parts(weights_here, feat_count, group_count, share_count, entry_count)
 
-    first_rows, second_rows, _ = lax.optimization_barrier(
-        (pooled_first[0], pooled_second[0], last_rows)
-    )
-    pieces, slot_ids = exchange_rows(first_rows, second_rows, feat_count)
-    row_count = pieces[0].shape[1]
-    slot_count = sum(piece.shape[0] for piece in pieces)
-    bias_blocks = cross_bias[0].reshape(slot_count, entry_count)
     features = jnp.concatenate([part_features for _, part_features in parts])
     position_count = features.shape[0]
-
-    if len(pieces) > 4:
-        pieces, slot_ids = [jnp.concatenate(pieces, 0)], [jnp.concatenate(slot_ids)]
-    base_sum = None
-    for piece, ids in zip(pieces, slot_ids):
-        orders = feature_order[0][ids]
-        one_hot = (orders[None, :] == features[:, None]).astype(jnp.bfloat16)
-        term = jnp.einsum("fs,sre->rfe", one_hot, piece, preferred_element_type=jnp.float32)
-        base_sum = term if base_sum is None else base_sum + term
-    base_all = base_sum.astype(jnp.bfloat16).reshape(row_count, position_count * entry_count)
-
+    width = cross_bias.shape[1]
+    bias_blocks = cross_bias[0].reshape(width // entry_count, entry_count)
+    shift_row = bias_blocks[features].reshape(position_count * entry_count)
     weights = jnp.concatenate([rows for rows, _ in parts], 0)
-    low_sum = jnp.dot(base_all, weights[:, :rank], preferred_element_type=jnp.float32)
-    low_rank = low_sum.astype(jnp.bfloat16)
-    lifted = lax.dot_general(
-        low_rank,
-        weights[:, rank : 2 * rank],
-        (((1,), (1,)), ((), ())),
-        preferred_element_type=jnp.float32,
-    )
-    shift_row = bias_blocks[features].reshape(position_count * entry_count)
-    columns = base_all.astype(jnp.float32)
-    crossed = (columns * (lifted + shift_row[None, :]) + columns).astype(jnp.bfloat16)
-    squeezed = jnp.dot(crossed, weights[:, 2 * rank :], preferred_element_type=jnp.float32)
-    compressed = (squeezed + compress_bias[0][None, :]).astype(jnp.bfloat16)
-    gathered = lax.all_to_all(compressed, "tower", split_axis=0, concat_axis=1, tiled=True)
-    local_rows = gathered.shape[0]
-    vector_count = gathered.shape[1] // entry_count
-    vectors = gathered.reshape(local_rows, vector_count, entry_count)
-    gram_matrix = jnp.einsum(
-        "bie,bje->bij", vectors, vectors, preferred_element_type=jnp.float32
-    ) * (1.0 / math.sqrt(entry_count))
-    pair_terms = gram_matrix.reshape(local_rows, vector_count * vector_count)[
-        :, pair_positions(vector_count)
-    ]
-    joined = jnp.concatenate([dense_vector.astype(jnp.float32), pair_terms], 1).astype(jnp.bfloat16)
+    share = pooled_first.shape[2] // feat_count
+    half_count = 2 if share % (2 * tower_count) == 0 else 1
+    local_block = dense_vector.shape[0] // half_count
     hidden_units = mlp_weight.shape[1]
     hidden_rows = mlp_weight.shape[0]
     tower = lax.axis_index("tower")
-    hidden_sum = jnp.zeros((local_rows, hidden_units), jnp.float32)
-    for shift, rows in enumerate(hidden_pieces):
-        source = (tower - shift) % tower_count
-        columns = lax.dynamic_slice_in_dim(joined, source * hidden_rows, hidden_rows, axis=1)
-        hidden_sum = hidden_sum + jnp.dot(columns, rows, preferred_element_type=jnp.float32)
-    return jax.nn.relu(hidden_sum + mlp_bias[None, :]).astype(jnp.bfloat16)
+
+    gate = last_rows
+    outputs = []
+    for half in range(half_count):
+        pieces, slot_ids = exchange_rows(
+            pooled_first[0], pooled_second[0], feat_count, tower_count, half, half_count, gate
+        )
+        gate = pieces
+        row_count = pieces[0].shape[1]
+        if len(pieces) > 4:
+            pieces, slot_ids = [jnp.concatenate(pieces, 0)], [jnp.concatenate(slot_ids)]
+        base_sum = None
+        for piece, ids in zip(pieces, slot_ids):
+            orders = feature_order[0][ids]
+            one_hot = (orders[None, :] == features[:, None]).astype(jnp.bfloat16)
+            term = jnp.einsum("fs,sre->rfe", one_hot, piece, preferred_element_type=jnp.float32)
+            base_sum = term if base_sum is None else base_sum + term
+        base_all = base_sum.astype(jnp.bfloat16).reshape(row_count, position_count * entry_count)
+
+        low_sum = jnp.dot(base_all, weights[:, :rank], preferred_element_type=jnp.float32)
+        low_rank = low_sum.astype(jnp.bfloat16)
+        lifted = lax.dot_general(
+            low_rank,
+            weights[:, rank : 2 * rank],
+            (((1,), (1,)), ((), ())),
+            preferred_element_type=jnp.float32,
+        )
+        columns = base_all.astype(jnp.float32)
+        crossed = (columns * (lifted + shift_row[None, :]) + columns).astype(jnp.bfloat16)
+        squeezed = jnp.dot(crossed, weights[:, 2 * rank :], preferred_element_type=jnp.float32)
+        compressed = (squeezed + compress_bias[0][None, :]).astype(jnp.bfloat16)
+        gathered = lax.all_to_all(compressed, "tower", split_axis=0, concat_axis=1, tiled=True)
+        local_rows = gathered.shape[0]
+        vector_count = gathered.shape[1] // entry_count
+        vectors = gathered.reshape(local_rows, vector_count, entry_count)
+        gram_matrix = jnp.einsum(
+            "bie,bje->bij", vectors, vectors, preferred_element_type=jnp.float32
+        ) * (1.0 / math.sqrt(entry_count))
+        pair_terms = gram_matrix.reshape(local_rows, vector_count * vector_count)[
+            :, pair_positions(vector_count)
+        ]
+        dense_rows = lax.slice_in_dim(dense_vector, half * local_block, (half + 1) * local_block)
+        joined = jnp.concatenate([dense_rows.astype(jnp.float32), pair_terms], 1).astype(
+            jnp.bfloat16
+        )
+        hidden_sum = jnp.zeros((local_rows, hidden_units), jnp.float32)
+        for shift, rows in enumerate(hidden_pieces):
+            source = (tower - shift) % tower_count
+            columns = lax.dynamic_slice_in_dim(joined, source * hidden_rows, hidden_rows, axis=1)
+            hidden_sum = hidden_sum + jnp.dot(columns, rows, preferred_element_type=jnp.float32)
+        outputs.append(jax.nn.relu(hidden_sum + mlp_bias[None, :]).astype(jnp.bfloat16))
+    return jnp.concatenate(outputs, 0)
 
 
 def solution(mesh):

time: 179 us -> 180 us (level)
  waiting for transfers between devices: 71.9 us -> 50.7 us
  matrix products: 17.7 us -> 35.7 us
  starting transfers between devices: 41.8 us -> 49.1 us
  local copies, waits for them, and re-layouts: 42.2 us -> 37.5 us
    ppermute x3 -> x6, waiting for transfers between devices: 36.5 us -> 4.61 us  [exchange_rows(): lax.ppermute(piece, 'feat', [(source, (source + shift) % feat_count) for...]
    squeeze x1 -> x0, local copies, waits for them, and re-layouts: 12 us -> none  [on_device(): pooled_second[0]]
    ppermute x3 -> x6, starting transfers between devices: 2.87 us -> 12.3 us  [exchange_rows(): lax.ppermute(piece, 'feat', [(source, (source + shift) % feat_count) for...]
    ppermute x12, waiting for transfers between devices: 17.3 us -> 25.4 us  [weight_parts(): rings[chunk] = lax.ppermute(rings[chunk], 'feat', ring)]
    dot_general x4 -> x8, matrix products: 1.75 us -> 9.84 us  [on_device(): jnp.dot(columns, rows, preferred_element_type=jnp.float32)]
    slice x0 -> x7, local copies, waits for them, and re-layouts: none -> 4.43 us  [the longest x6 3.81 us: exchange_rows(): piece[:, :, half]]
    dot_general x4 -> x8, matrix products: 5 us -> 9.37 us  [on_device(): jnp.einsum('fs,sre->rfe', one_hot, piece, preferred_element_type=jnp.floa...]
    dot_general x1 -> x2, matrix products: 7.28 us -> 11.5 us  [on_device(): jnp.dot(crossed, weights[:, 2 * rank:], preferred_element_type=jnp.float32)]
  transfers between devices with their start and end apart: 31 -> 35, of which waited for: 13 -> 16; matrix products, arithmetic and copies ran while one was open for 26% -> 37% of each run, Pallas kernels for 0% -> 0%
where the time goes in v11:
time: 180 us; the launch traced here: 179 us
  waiting for transfers between devices  50.7 us (28%)
  starting transfers between devices  49.1 us (27%)
  local copies, waits for them, and re-layouts  37.5 us (21%)
  matrix products  35.7 us (20%)
  other arithmetic  5.07 us (3%)
    ppermute x12, waiting for transfers between devices, weight_parts(): rings[chunk] = lax.ppermute(rings[chunk], 'feat', ring)  25.4 us
    unnamed x61, local copies, waits for them, and re-layouts  22.7 us
    ppermute x12, starting transfers between devices, weight_parts(): forwarded = lax.ppermute(rings[chunk], 'groups', pairs)  16 us
    ppermute x12, waiting for transfers between devices, weight_parts(): forwarded = lax.ppermute(rings[chunk], 'groups', pairs)  14.1 us
    ppermute x6, starting transfers between devices, exchange_rows(): lax.ppermute(piece, 'feat', [(source, (source + shift) % feat_count) for...  12.3 us
    ppermute x12, starting transfers between devices, weight_parts(): rings[chunk] = lax.ppermute(rings[chunk], 'feat', ring)  12.2 us
    dot_general x2, matrix products, on_device(): jnp.dot(crossed, weights[:, 2 * rank:], preferred_element_type=jnp.float32)  11.5 us
    dot_general x8, matrix products, on_device(): jnp.dot(columns, rows, preferred_element_type=jnp.float32)  9.84 us
  transfers between devices with their start and end apart: 35, of which 16 were waited for; matrix products, arithmetic and copies ran while one was open for 37% of the time, Pallas kernels for 0%

profile of v11, /device:TPU:0, one launch (start us, length us, event | category | flops | bytes accessed | tf_op | source)
XLA Modules:
  0.0 178.7 jit_solution(554622015920576842)
XLA Ops:
  0.0 3.3 %pad_maximum_fusion = (bf16[1024,1024]{1,0:T(8,128)(2,1)S(1)}, bf16[4096,1024]{1,0:T(8,128)(2,1)}) fusion(bf16[1024,512]{1,0:T(8,128)(2,1)} %bitcast.200, bf16[1024,256]{1,0:T(8,128)(2,1)} %bitcast.202, bf16[1024,256]{1,0:T(8,128)(2,1)} %bitcast.203), kind=kLoop, calls=%fused_computation.21 | loop fusion | flops 6291455 | bytes 6291456 | tf_op jit(solution)/shard_map/concatenate | solution.py:115
  4.2 3.0 %collective-permute-start = (bf16[128,1024]{1,0:T(8,128)(2,1)}, bf16[128,1024]{1,0:T(8,128)(2,1)}, u32[]{:S(2)}, u32[]{:S(2)}) collective-permute-start(bf16[128,1024]{1,0:T(8,128)(2,1)} %get-tuple-element.23), channel_id=1, source_target_pairs={{0,4},{4,8},{8,12},{12,0},{1,5},{5,9},{9,13},{13,1},{2,6},{6,10},{... | collective-permute-start | bytes 786440 | tf_op jit(solution)/shard_map/ppermute | solution.py:41
  14.0 2.7 %collective-permute-done = bf16[128,1024]{1,0:T(8,128)(2,1)} collective-permute-done((bf16[128,1024]{1,0:T(8,128)(2,1)}, bf16[128,1024]{1,0:T(8,128)(2,1)}, u32[]{:S(2)}, u32[]{:S(2)}) %collective-permute-start) | collective-permute-done | bytes 262176 | tf_op jit(solution)/shard_map/ppermute | solution.py:41
  36.6 2.7 %collective-permute-done.17 = bf16[128,1024]{1,0:T(8,128)(2,1)S(1)} collective-permute-done((bf16[128,1024]{1,0:T(8,128)(2,1)}, bf16[128,1024]{1,0:T(8,128)(2,1)S(1)}, u32[]{:S(2)}, u32[]{:S(2)}) %collective-permute-start.17) | collective-permute-done | bytes 262176 | tf_op jit(solution)/shard_map/ppermute | solution.py:46
  44.8 3.3 %collective-permute-start.5 = (bf16[128,1024]{1,0:T(8,128)(2,1)S(1)}, bf16[128,1024]{1,0:T(8,128)(2,1)S(1)}, u32[]{:S(2)}, u32[]{:S(2)}) collective-permute-start(bf16[128,1024]{1,0:T(8,128)(2,1)S(1)} %collective-permute-done.4), channel_id=1, source_target_pairs={{0,4},{4,8},{8,12},{12,0},{1,5},{5,9},{9,13},{13,1},{2,6},{6,10},{... | collective-permute-start | bytes 786440 | tf_op jit(solution)/shard_map/ppermute | solution.py:41
  50.3 5.6 %collective-permute-done.10 = bf16[128,1024]{1,0:T(8,128)(2,1)S(1)} collective-permute-done((bf16[128,1024]{1,0:T(8,128)(2,1)}, bf16[128,1024]{1,0:T(8,128)(2,1)S(1)}, u32[]{:S(2)}, u32[]{:S(2)}) %collective-permute-start.10) | collective-permute-done | bytes 262176 | tf_op jit(solution)/shard_map/ppermute | solution.py:41
  58.3 3.2 %collective-permute-done.2 = bf16[128,1024]{1,0:T(8,128)(2,1)S(1)} collective-permute-done((bf16[128,1024]{1,0:T(8,128)(2,1)S(1)}, bf16[128,1024]{1,0:T(8,128)(2,1)S(1)}, u32[]{:S(2)}, u32[]{:S(2)}) %collective-permute-start.2) | collective-permute-done | bytes 262176 | tf_op jit(solution)/shard_map/ppermute | solution.py:41
  64.0 3.1 %collective-permute-done.5 = bf16[128,1024]{1,0:T(8,128)(2,1)S(1)} collective-permute-done((bf16[128,1024]{1,0:T(8,128)(2,1)S(1)}, bf16[128,1024]{1,0:T(8,128)(2,1)S(1)}, u32[]{:S(2)}, u32[]{:S(2)}) %collective-permute-start.5) | collective-permute-done | bytes 262176 | tf_op jit(solution)/shard_map/ppermute | solution.py:41
  68.9 3.9 %collective-permute-done.8 = bf16[128,1024]{1,0:T(8,128)(2,1)S(1)} collective-permute-done((bf16[128,1024]{1,0:T(8,128)(2,1)S(1)}, bf16[128,1024]{1,0:T(8,128)(2,1)S(1)}, u32[]{:S(2)}, u32[]{:S(2)}) %collective-permute-start.8) | collective-permute-done | bytes 262176 | tf_op jit(solution)/shard_map/ppermute | solution.py:41
  74.5 3.0 %collective-permute-done.11 = bf16[128,1024]{1,0:T(8,128)(2,1)S(1)} collective-permute-done((bf16[128,1024]{1,0:T(8,128)(2,1)S(1)}, bf16[128,1024]{1,0:T(8,128)(2,1)S(1)}, u32[]{:S(2)}, u32[]{:S(2)}) %collective-permute-start.11) | collective-permute-done | bytes 262176 | tf_op jit(solution)/shard_map/ppermute | solution.py:41
  77.6 2.3 %collective-permute-start.13 = (bf16[8,192,128]{2,0,1:T(8,128)(2,1)S(1)}, bf16[8,192,128]{2,0,1:T(8,128)(2,1)S(1)}, u32[]{:S(2)}, u32[]{:S(2)}) collective-permute-start(bf16[8,192,128]{2,0,1:T(8,128)(2,1)S(1)} %bitcast.209), channel_id=1, source_target_pairs={{0,8},{4,12},{8,0},{12,4},{1,9},{5,13},{9,1},{13,5},{2,10},{6,14},... | collective-permute-start | bytes 1179656 | tf_op jit(solution)/shard_map/ppermute | solution.py:75
  89.3 4.3 %collective-permute-done.23 = bf16[128,1024]{1,0:T(8,128)(2,1)S(1)} collective-permute-done((bf16[128,1024]{1,0:T(8,128)(2,1)S(1)}, bf16[128,1024]{1,0:T(8,128)(2,1)S(1)}, u32[]{:S(2)}, u32[]{:S(2)}) %collective-permute-start.23) | collective-permute-done | bytes 262176 | tf_op jit(solution)/shard_map/ppermute | solution.py:46
  96.5 2.7 %collective-permute-done.24 = bf16[128,1024]{1,0:T(8,128)(2,1)S(1)} collective-permute-done((bf16[128,1024]{1,0:T(8,128)(2,1)S(1)}, bf16[128,1024]{1,0:T(8,128)(2,1)S(1)}, u32[]{:S(2)}, u32[]{:S(2)}) %collective-permute-start.24) | collective-permute-done | bytes 262176 | tf_op jit(solution)/shard_map/ppermute | solution.py:46
  102.2 2.6 %collective-permute-done.25 = bf16[128,1024]{1,0:T(8,128)(2,1)S(1)} collective-permute-done((bf16[128,1024]{1,0:T(8,128)(2,1)S(1)}, bf16[128,1024]{1,0:T(8,128)(2,1)S(1)}, u32[]{:S(2)}, u32[]{:S(2)}) %collective-permute-start.25) | collective-permute-done | bytes 262176 | tf_op jit(solution)/shard_map/ppermute | solution.py:46
  110.1 3.5 %collective-permute-start.31 = (bf16[8,192,128]{2,0,1:T(8,128)(2,1)}, bf16[8,192,128]{2,0,1:T(8,128)(2,1)}, u32[]{:S(2)}, u32[]{:S(2)}) collective-permute-start(bf16[8,192,128]{2,0,1:T(8,128)(2,1)} %bitcast.92), channel_id=1, source_target_pairs={{0,8},{4,12},{8,0},{12,4},{1,9},{5,13},{9,1},{13,5},{2,10},{6,14},... | collective-permute-start | bytes 1179656 | tf_op jit(solution)/shard_map/ppermute | solution.py:75
  116.7 2.3 %fusion.54 = bf16[192,256]{1,0:T(8,128)(2,1)S(1)} fusion(bf16[4096,1024]{1,0:T(8,128)(2,1)} %constant_dynamic-update-slice_fusion, bf16[24,8,32,128]{3,2,1,0:T(8,128)(2,1)S(1)} %bitcast.198), kind=kOutput, calls=%fused_computation.52 | convolution fusion | flops 402702336 | bytes 3768320 | tf_op jit(solution)/shard_map/dot_general | solution.py:149
  119.0 5.5 %fusion.41 = bf16[192,512]{1,0:T(8,128)(2,1)} fusion(bf16[4096,1024]{1,0:T(8,128)(2,1)} %constant_dynamic-update-slice_fusion, bf16[192,256]{1,0:T(8,128)(2,1)S(1)} %fusion.54, f32[4096]{0:T(1024)S(1)} %bitcast.213, bf16[24,8,32,128]{3,2,1,0:T(8,128)(2,1)S(1)} %bitcast.199, f32[512]{0:T(512)S(1)} %bitcast.216), kind=kOutput, calls=%fused_computation.39 | convolution fusion | flops 1212088320 | bytes 8177664 | tf_op jit(solution)/shard_map/dot_general | solution.py:159
  124.5 4.0 %all-to-all-start = ((bf16[4,48,512]{2,1,0:T(8,128)(2,1)}), bf16[4,48,512]{2,1,0:T(8,128)(2,1)}, u32[]{:S(2)}, u32[]{:S(2)}) async-start(bf16[4,48,512]{2,1,0:T(8,128)(2,1)} %bitcast.86), calls=%async_computation | async-start | bytes 393216 | tf_op jit(solution)/shard_map/all_to_all | solution.py:161
  131.4 2.4 %all-to-all-done = bf16[4,48,512]{2,1,0:T(8,128)(2,1)} async-done(((bf16[4,48,512]{2,1,0:T(8,128)(2,1)}), bf16[4,48,512]{2,1,0:T(8,128)(2,1)}, u32[]{:S(2)}, u32[]{:S(2)}) %all-to-all-start) | async-done | bytes 196640 | tf_op jit(solution)/shard_map/all_to_all | solution.py:161
  137.6 3.4 %collective-permute-start.32 = (bf16[8,192,128]{2,0,1:T(8,128)(2,1)}, bf16[8,192,128]{2,0,1:T(8,128)(2,1)S(1)}, u32[]{:S(2)}, u32[]{:S(2)}) collective-permute-start(bf16[8,192,128]{2,0,1:T(8,128)(2,1)} %bitcast.206), channel_id=1, source_target_pairs={{0,12},{4,0},{8,4},{12,8},{1,13},{5,1},{9,5},{13,9},{2,14},{6,2},{... | collective-permute-start | bytes 1179656 | tf_op jit(solution)/shard_map/ppermute | solution.py:75
  147.4 4.6 %collective-permute-done.32 = bf16[8,192,128]{2,0,1:T(8,128)(2,1)S(1)} collective-permute-done((bf16[8,192,128]{2,0,1:T(8,128)(2,1)}, bf16[8,192,128]{2,0,1:T(8,128)(2,1)S(1)}, u32[]{:S(2)}, u32[]{:S(2)}) %collective-permute-start.32) | collective-permute-done | bytes 393248 | tf_op jit(solution)/shard_map/ppermute | solution.py:75
  157.1 6.0 %fusion.36 = bf16[192,512]{1,0:T(8,128)(2,1)} fusion(bf16[4096,1024]{1,0:T(8,128)(2,1)} %constant_dynamic-update-slice_fusion, bf16[192,256]{1,0:T(8,128)(2,1)S(1)} %fusion.59, f32[4096]{0:T(1024)} %bitcast.214, bf16[24,8,32,128]{3,2,1,0:T(8,128)(2,1)} %bitcast.197, f32[512]{0:T(512)} %bitcast.215), kind=kOutput, calls=%fused_computation.38 | convolution fusion | flops 1212088320 | bytes 8177664 | tf_op jit(solution)/shard_map/dot_general | solution.py:159
  163.1 3.4 %all-to-all-start.1 = ((bf16[4,48,512]{2,1,0:T(8,128)(2,1)}), bf16[4,48,512]{2,1,0:T(8,128)(2,1)S(1)}, u32[]{:S(2)}, u32[]{:S(2)}) async-start(bf16[4,48,512]{2,1,0:T(8,128)(2,1)} %bitcast.95), calls=%async_computation.1 | async-start | bytes 393216 | tf_op jit(solution)/shard_map/all_to_all | solution.py:161
  167.7 4.1 %all-to-all-done.1 = bf16[4,48,512]{2,1,0:T(8,128)(2,1)S(1)} async-done(((bf16[4,48,512]{2,1,0:T(8,128)(2,1)}), bf16[4,48,512]{2,1,0:T(8,128)(2,1)S(1)}, u32[]{:S(2)}, u32[]{:S(2)}) %all-to-all-start.1) | async-done | bytes 196640 | tf_op jit(solution)/shard_map/all_to_all | solution.py:161
  (180 shorter events, 93.3 us)
Async XLA Ops:
  7.2 18.6 %collective-permute-start.3 = (bf16[128,1024]{1,0:T(8,128)(2,1)}, bf16[128,1024]{1,0:T(8,128)(2,1)}, u32[]{:S(2)}, u32[]{:S(2)}) collective-permute-start(bf16[128,1024]{1,0:T(8,128)(2,1)} %get-tuple-element.22), channel_id=1, source_target_pairs={{0,4},{4,8},{8,12},{12,0},{1,5},{5,9},{9,13},{13,1},{2,6},{6,10},{... | collective-permute-start | bytes 786440 | tf_op jit(solution)/shard_map/ppermute | solution.py:41
  8.8 19.1 %collective-permute-start.6 = (bf16[128,1024]{1,0:T(8,128)(2,1)}, bf16[128,1024]{1,0:T(8,128)(2,1)}, u32[]{:S(2)}, u32[]{:S(2)}) collective-permute-start(bf16[128,1024]{1,0:T(8,128)(2,1)} %get-tuple-element.24), channel_id=1, source_target_pairs={{0,4},{4,8},{8,12},{12,0},{1,5},{5,9},{9,13},{13,1},{2,6},{6,10},{... | collective-permute-start | bytes 786440 | tf_op jit(solution)/shard_map/ppermute | solution.py:41
  10.4 24.3 %collective-permute-start.9 = (bf16[128,1024]{1,0:T(8,128)(2,1)S(1)}, bf16[128,1024]{1,0:T(8,128)(2,1)}, u32[]{:S(2)}, u32[]{:S(2)}) collective-permute-start(bf16[128,1024]{1,0:T(8,128)(2,1)S(1)} %get-tuple-element.21), channel_id=1, source_target_pairs={{0,4},{4,8},{8,12},{12,0},{1,5},{5,9},{9,13},{13,1},{2,6},{6,10},{... | collective-permute-start | bytes 786440 | tf_op jit(solution)/shard_map/ppermute | solution.py:41
  16.7 14.7 %collective-permute-start.15 = (bf16[128,1024]{1,0:T(8,128)(2,1)}, bf16[128,1024]{1,0:T(8,128)(2,1)}, u32[]{:S(2)}, u32[]{:S(2)}) collective-permute-start(bf16[128,1024]{1,0:T(8,128)(2,1)} %collective-permute-done), channel_id=1, source_target_pairs={{0,16},{16,0},{1,17},{17,1},{2,18},{18,2},{3,19},{19,3},{4,20},{20... | collective-permute-start | bytes 786440 | tf_op jit(solution)/shard_map/ppermute | solution.py:46
  25.7 16.0 %collective-permute-start.1 = (bf16[128,1024]{1,0:T(8,128)(2,1)}, bf16[128,1024]{1,0:T(8,128)(2,1)S(1)}, u32[]{:S(2)}, u32[]{:S(2)}) collective-permute-start(bf16[128,1024]{1,0:T(8,128)(2,1)} %collective-permute-done), channel_id=1, source_target_pairs={{0,4},{4,8},{8,12},{12,0},{1,5},{5,9},{9,13},{13,1},{2,6},{6,10},{... | collective-permute-start | bytes 786440 | tf_op jit(solution)/shard_map/ppermute | solution.py:41
  34.7 15.6 %collective-permute-start.7 = (bf16[128,1024]{1,0:T(8,128)(2,1)}, bf16[128,1024]{1,0:T(8,128)(2,1)S(1)}, u32[]{:S(2)}, u32[]{:S(2)}) collective-permute-start(bf16[128,1024]{1,0:T(8,128)(2,1)} %collective-permute-done.6), channel_id=1, source_target_pairs={{0,4},{4,8},{8,12},{12,0},{1,5},{5,9},{9,13},{13,1},{2,6},{6,10},{... | collective-permute-start | bytes 786440 | tf_op jit(solution)/shard_map/ppermute | solution.py:41
  39.3 16.6 %collective-permute-start.10 = (bf16[128,1024]{1,0:T(8,128)(2,1)}, bf16[128,1024]{1,0:T(8,128)(2,1)S(1)}, u32[]{:S(2)}, u32[]{:S(2)}) collective-permute-start(bf16[128,1024]{1,0:T(8,128)(2,1)} %collective-permute-done.9), channel_id=1, source_target_pairs={{0,4},{4,8},{8,12},{12,0},{1,5},{5,9},{9,13},{13,1},{2,6},{6,10},{... | collective-permute-start | bytes 786440 | tf_op jit(solution)/shard_map/ppermute | solution.py:41
  41.7 19.8 %collective-permute-start.2 = (bf16[128,1024]{1,0:T(8,128)(2,1)S(1)}, bf16[128,1024]{1,0:T(8,128)(2,1)S(1)}, u32[]{:S(2)}, u32[]{:S(2)}) collective-permute-start(bf16[128,1024]{1,0:T(8,128)(2,1)S(1)} %collective-permute-done.1), channel_id=1, source_target_pairs={{0,4},{4,8},{8,12},{12,0},{1,5},{5,9},{9,13},{13,1},{2,6},{6,10},{... | collective-permute-start | bytes 786440 | tf_op jit(solution)/shard_map/ppermute | solution.py:41
  43.5 34.0 %collective-permute-start.19 = (bf16[128,1024]{1,0:T(8,128)(2,1)S(1)}, bf16[128,1024]{1,0:T(8,128)(2,1)S(1)}, u32[]{:S(2)}, u32[]{:S(2)}) collective-permute-start(bf16[128,1024]{1,0:T(8,128)(2,1)S(1)} %collective-permute-done.1), channel_id=1, source_target_pairs={{0,16},{16,0},{1,17},{17,1},{2,18},{18,2},{3,19},{19,3},{4,20},{20... | collective-permute-start | bytes 786440 | tf_op jit(solution)/shard_map/ppermute | solution.py:46
  44.8 22.3 %collective-permute-start.5 = (bf16[128,1024]{1,0:T(8,128)(2,1)S(1)}, bf16[128,1024]{1,0:T(8,128)(2,1)S(1)}, u32[]{:S(2)}, u32[]{:S(2)}) collective-permute-start(bf16[128,1024]{1,0:T(8,128)(2,1)S(1)} %collective-permute-done.4), channel_id=1, source_target_pairs={{0,4},{4,8},{8,12},{12,0},{1,5},{5,9},{9,13},{13,1},{2,6},{6,10},{... | collective-permute-start | bytes 786440 | tf_op jit(solution)/shard_map/ppermute | solution.py:41
  50.3 22.5 %collective-permute-start.8 = (bf16[128,1024]{1,0:T(8,128)(2,1)S(1)}, bf16[128,1024]{1,0:T(8,128)(2,1)S(1)}, u32[]{:S(2)}, u32[]{:S(2)}) collective-permute-start(bf16[128,1024]{1,0:T(8,128)(2,1)S(1)} %collective-permute-done.7), channel_id=1, source_target_pairs={{0,4},{4,8},{8,12},{12,0},{1,5},{5,9},{9,13},{13,1},{2,6},{6,10},{... | collective-permute-start | bytes 786440 | tf_op jit(solution)/shard_map/ppermute | solution.py:41
  55.9 21.6 %collective-permute-start.11 = (bf16[128,1024]{1,0:T(8,128)(2,1)S(1)}, bf16[128,1024]{1,0:T(8,128)(2,1)S(1)}, u32[]{:S(2)}, u32[]{:S(2)}) collective-permute-start(bf16[128,1024]{1,0:T(8,128)(2,1)S(1)} %collective-permute-done.10), channel_id=1, source_target_pairs={{0,4},{4,8},{8,12},{12,0},{1,5},{5,9},{9,13},{13,1},{2,6},{6,10},{... | collective-permute-start | bytes 786440 | tf_op jit(solution)/shard_map/ppermute | solution.py:41
  61.5 19.8 %collective-permute-start.20 = (bf16[128,1024]{1,0:T(8,128)(2,1)S(1)}, bf16[128,1024]{1,0:T(8,128)(2,1)S(1)}, u32[]{:S(2)}, u32[]{:S(2)}) collective-permute-start(bf16[128,1024]{1,0:T(8,128)(2,1)S(1)} %collective-permute-done.4), channel_id=1, source_target_pairs={{0,16},{16,0},{1,17},{17,1},{2,18},{18,2},{3,19},{19,3},{4,20},{20... | collective-permute-start | bytes 786440 | tf_op jit(solution)/shard_map/ppermute | solution.py:46
  67.1 17.2 %collective-permute-start.21 = (bf16[128,1024]{1,0:T(8,128)(2,1)S(1)}, bf16[128,1024]{1,0:T(8,128)(2,1)S(1)}, u32[]{:S(2)}, u32[]{:S(2)}) collective-permute-start(bf16[128,1024]{1,0:T(8,128)(2,1)S(1)} %collective-permute-done.7), channel_id=1, source_target_pairs={{0,16},{16,0},{1,17},{17,1},{2,18},{18,2},{3,19},{19,3},{4,20},{20... | collective-permute-start | bytes 786440 | tf_op jit(solution)/shard_map/ppermute | solution.py:46
  72.8 14.6 %collective-permute-start.22 = (bf16[128,1024]{1,0:T(8,128)(2,1)S(1)}, bf16[128,1024]{1,0:T(8,128)(2,1)S(1)}, u32[]{:S(2)}, u32[]{:S(2)}) collective-permute-start(bf16[128,1024]{1,0:T(8,128)(2,1)S(1)} %collective-permute-done.10), channel_id=1, source_target_pairs={{0,16},{16,0},{1,17},{17,1},{2,18},{18,2},{3,19},{19,3},{4,20},{20... | collective-permute-start | bytes 786440 | tf_op jit(solution)/shard_map/ppermute | solution.py:46
  77.5 31.3 %collective-permute-start.12 = (bf16[8,192,128]{2,0,1:T(8,128)(2,1)S(1)}, bf16[8,192,128]{2,0,1:T(8,128)(2,1)S(1)}, u32[]{:S(2)}, u32[]{:S(2)}) collective-permute-start(bf16[8,192,128]{2,0,1:T(8,128)(2,1)S(1)} %bitcast.210), channel_id=1, source_target_pairs={{0,4},{4,8},{8,12},{12,0},{1,5},{5,9},{9,13},{13,1},{2,6},{6,10},{... | collective-permute-start | bytes 1179656 | tf_op jit(solution)/shard_map/ppermute | solution.py:75
  77.6 32.6 %collective-permute-start.13 = (bf16[8,192,128]{2,0,1:T(8,128)(2,1)S(1)}, bf16[8,192,128]{2,0,1:T(8,128)(2,1)S(1)}, u32[]{:S(2)}, u32[]{:S(2)}) collective-permute-start(bf16[8,192,128]{2,0,1:T(8,128)(2,1)S(1)} %bitcast.209), channel_id=1, source_target_pairs={{0,8},{4,12},{8,0},{12,4},{1,9},{5,13},{9,1},{13,5},{2,10},{6,14},... | collective-permute-start | bytes 1179656 | tf_op jit(solution)/shard_map/ppermute | solution.py:75
  81.3 28.8 %collective-permute-start.14 = (bf16[8,192,128]{2,0,1:T(8,128)(2,1)S(1)}, bf16[8,192,128]{2,0,1:T(8,128)(2,1)S(1)}, u32[]{:S(2)}, u32[]{:S(2)}) collective-permute-start(bf16[8,192,128]{2,0,1:T(8,128)(2,1)S(1)} %bitcast.208), channel_id=1, source_target_pairs={{0,12},{4,0},{8,4},{12,8},{1,13},{5,1},{9,5},{13,9},{2,14},{6,2},{... | collective-permute-start | bytes 1179656 | tf_op jit(solution)/shard_map/ppermute | solution.py:75
  104.8 37.3 %collective-permute-start.29 = (bf16[62,1024]{1,0:T(8,128)(2,1)}, bf16[62,1024]{1,0:T(8,128)(2,1)}, u32[]{:S(2)}, u32[]{:S(2)}) collective-permute-start(bf16[62,1024]{1,0:T(8,128)(2,1)} %param.24), channel_id=1, source_target_pairs={{0,3},{1,0},{2,1},{3,2},{4,7},{5,4},{6,5},{7,6},{8,11},{9,8},{10,9... | collective-permute-start | bytes 380936 | tf_op jit(solution)/shard_map/ppermute | solution.py:113
  108.1 29.4 %collective-permute-start.27 = (bf16[62,1024]{1,0:T(8,128)(2,1)}, bf16[62,1024]{1,0:T(8,128)(2,1)}, u32[]{:S(2)}, u32[]{:S(2)}) collective-permute-start(bf16[62,1024]{1,0:T(8,128)(2,1)} %param.24), channel_id=1, source_target_pairs={{0,1},{1,2},{2,3},{3,0},{4,5},{5,6},{6,7},{7,4},{8,9},{9,10},{10,1... | collective-permute-start | bytes 380936 | tf_op jit(solution)/shard_map/ppermute | solution.py:113
  108.9 57.6 %collective-permute-start.28 = (bf16[62,1024]{1,0:T(8,128)(2,1)}, bf16[62,1024]{1,0:T(8,128)(2,1)}, u32[]{:S(2)}, u32[]{:S(2)}) collective-permute-start(bf16[62,1024]{1,0:T(8,128)(2,1)} %param.24), channel_id=1, source_target_pairs={{0,2},{1,3},{2,0},{3,1},{4,6},{5,7},{6,4},{7,5},{8,10},{9,11},{10,... | collective-permute-start | bytes 380936 | tf_op jit(solution)/shard_map/ppermute | solution.py:113
  110.1 33.9 %collective-permute-start.31 = (bf16[8,192,128]{2,0,1:T(8,128)(2,1)}, bf16[8,192,128]{2,0,1:T(8,128)(2,1)}, u32[]{:S(2)}, u32[]{:S(2)}) collective-permute-start(bf16[8,192,128]{2,0,1:T(8,128)(2,1)} %bitcast.92), channel_id=1, source_target_pairs={{0,8},{4,12},{8,0},{12,4},{1,9},{5,13},{9,1},{13,5},{2,10},{6,14},... | collective-permute-start | bytes 1179656 | tf_op jit(solution)/shard_map/ppermute | solution.py:75
  129.8 15.9 %collective-permute-start.30 = (bf16[8,192,128]{2,0,1:T(8,128)(2,1)}, bf16[8,192,128]{2,0,1:T(8,128)(2,1)}, u32[]{:S(2)}, u32[]{:S(2)}) collective-permute-start(bf16[8,192,128]{2,0,1:T(8,128)(2,1)} %bitcast.207), channel_id=1, source_target_pairs={{0,4},{4,8},{8,12},{12,0},{1,5},{5,9},{9,13},{13,1},{2,6},{6,10},{... | collective-permute-start | bytes 1179656 | tf_op jit(solution)/shard_map/ppermute | solution.py:75
  137.6 14.4 %collective-permute-start.32 = (bf16[8,192,128]{2,0,1:T(8,128)(2,1)}, bf16[8,192,128]{2,0,1:T(8,128)(2,1)S(1)}, u32[]{:S(2)}, u32[]{:S(2)}) collective-permute-start(bf16[8,192,128]{2,0,1:T(8,128)(2,1)} %bitcast.206), channel_id=1, source_target_pairs={{0,12},{4,0},{8,4},{12,8},{1,13},{5,1},{9,5},{13,9},{2,14},{6,2},{... | collective-permute-start | bytes 1179656 | tf_op jit(solution)/shard_map/ppermute | solution.py:75
  (30 other events, 799.6 us)

commit v12 on v11

--- a/solution.py
+++ b/solution.py
@@ -128,7 +128,7 @@
     hidden_rows = mlp_weight.shape[0]
     tower = lax.axis_index("tower")
 
-    gate = last_rows
+    gate = (last_rows, hidden_pieces)
     outputs = []
     for half in range(half_count):
         pieces, slot_ids = exchange_rows(

time: 180 us -> 182 us (1.011)
  waiting for transfers between devices: 50.7 us -> 63 us
  starting transfers between devices: 49.1 us -> 42.3 us
  matrix products: 35.7 us -> 32.4 us
    ppermute x12, waiting for transfers between devices: 25.4 us -> 38.4 us  [weight_parts(): rings[chunk] = lax.ppermute(rings[chunk], 'feat', ring)]
    ppermute x12, starting transfers between devices: 16 us -> 9.18 us  [weight_parts(): forwarded = lax.ppermute(rings[chunk], 'groups', pairs)]
    dot_general x8, matrix products: 9.84 us -> 6.22 us  [on_device(): jnp.dot(columns, rows, preferred_element_type=jnp.float32)]
    ppermute x12, starting transfers between devices: 12.2 us -> 9.29 us  [weight_parts(): rings[chunk] = lax.ppermute(rings[chunk], 'feat', ring)]
    ppermute x3, starting transfers between devices: 1.25 us -> 3.51 us  [on_device(): hidden_pieces.append(lax.ppermute(mlp_weight, 'tower', pairs))]
    unnamed x61 -> x75, local copies, waits for them, and re-layouts: 22.7 us -> 22.3 us
  transfers between devices with their start and end apart: 35 -> 35, of which waited for: 16 -> 19; matrix products, arithmetic and copies ran while one was open for 37% -> 32% of each run, Pallas kernels for 0% -> 0%
where the time goes in v12:
time: 182 us; the launch traced here: 181 us
  waiting for transfers between devices  63 us (35%)
  starting transfers between devices  42.3 us (23%)
  local copies, waits for them, and re-layouts  37.9 us (21%)
  matrix products  32.4 us (18%)
  other arithmetic  4.95 us (3%)
    ppermute x12, waiting for transfers between devices, weight_parts(): rings[chunk] = lax.ppermute(rings[chunk], 'feat', ring)  38.4 us
    unnamed x75, local copies, waits for them, and re-layouts  22.3 us
    ppermute x12, waiting for transfers between devices, weight_parts(): forwarded = lax.ppermute(rings[chunk], 'groups', pairs)  13 us
    ppermute x6, starting transfers between devices, exchange_rows(): lax.ppermute(piece, 'feat', [(source, (source + shift) % feat_count) for...  12.8 us
    dot_general x2, matrix products, on_device(): jnp.dot(crossed, weights[:, 2 * rank:], preferred_element_type=jnp.float32)  11.5 us
    dot_general x8, matrix products, on_device(): jnp.einsum('fs,sre->rfe', one_hot, piece, preferred_element_type=jnp.floa...  9.69 us
    ppermute x12, starting transfers between devices, weight_parts(): rings[chunk] = lax.ppermute(rings[chunk], 'feat', ring)  9.29 us
    ppermute x12, starting transfers between devices, weight_parts(): forwarded = lax.ppermute(rings[chunk], 'groups', pairs)  9.18 us
  transfers between devices with their start and end apart: 35, of which 19 were waited for; matrix products, arithmetic and copies ran while one was open for 32% of the time, Pallas kernels for 0%

profile of v12, /device:TPU:0, one launch (start us, length us, event | category | flops | bytes accessed | tf_op | source)
XLA Modules:
  0.0 181.3 jit_solution(5127836731849282839)
XLA Ops:
  0.0 2.4 %collective-permute-start.14 = (bf16[62,1024]{1,0:T(8,128)(2,1)}, bf16[62,1024]{1,0:T(8,128)(2,1)}, u32[]{:S(2)}, u32[]{:S(2)}) collective-permute-start(bf16[62,1024]{1,0:T(8,128)(2,1)} %param.24), channel_id=1, source_target_pairs={{0,3},{1,0},{2,1},{3,2},{4,7},{5,4},{6,5},{7,6},{8,11},{9,8},{10,9... | collective-permute-start | bytes 380936 | tf_op jit(solution)/shard_map/ppermute | solution.py:113
  2.4 3.1 %pad_maximum_fusion = (bf16[1024,1024]{1,0:T(8,128)(2,1)S(1)}, bf16[4096,1024]{1,0:T(8,128)(2,1)}) fusion(bf16[1024,512]{1,0:T(8,128)(2,1)} %bitcast.200, bf16[1024,256]{1,0:T(8,128)(2,1)} %bitcast.202, bf16[1024,256]{1,0:T(8,128)(2,1)} %bitcast.203), kind=kLoop, calls=%fused_computation.21 | loop fusion | flops 6291455 | bytes 6291456 | tf_op jit(solution)/shard_map/concatenate | solution.py:115
  14.9 3.0 %collective-permute-done = bf16[128,1024]{1,0:T(8,128)(2,1)} collective-permute-done((bf16[128,1024]{1,0:T(8,128)(2,1)}, bf16[128,1024]{1,0:T(8,128)(2,1)}, u32[]{:S(2)}, u32[]{:S(2)}) %collective-permute-start) | collective-permute-done | bytes 262176 | tf_op jit(solution)/shard_map/ppermute | solution.py:41
  47.5 4.3 %collective-permute-done.4 = bf16[128,1024]{1,0:T(8,128)(2,1)S(1)} collective-permute-done((bf16[128,1024]{1,0:T(8,128)(2,1)}, bf16[128,1024]{1,0:T(8,128)(2,1)S(1)}, u32[]{:S(2)}, u32[]{:S(2)}) %collective-permute-start.4) | collective-permute-done | bytes 262176 | tf_op jit(solution)/shard_map/ppermute | solution.py:41
  51.7 5.6 %collective-permute-done.7 = bf16[128,1024]{1,0:T(8,128)(2,1)S(1)} collective-permute-done((bf16[128,1024]{1,0:T(8,128)(2,1)}, bf16[128,1024]{1,0:T(8,128)(2,1)S(1)}, u32[]{:S(2)}, u32[]{:S(2)}) %collective-permute-start.7) | collective-permute-done | bytes 262176 | tf_op jit(solution)/shard_map/ppermute | solution.py:41
  57.3 5.6 %collective-permute-done.10 = bf16[128,1024]{1,0:T(8,128)(2,1)S(1)} collective-permute-done((bf16[128,1024]{1,0:T(8,128)(2,1)S(1)}, bf16[128,1024]{1,0:T(8,128)(2,1)S(1)}, u32[]{:S(2)}, u32[]{:S(2)}) %collective-permute-start.10) | collective-permute-done | bytes 262176 | tf_op jit(solution)/shard_map/ppermute | solution.py:41
  64.4 4.2 %collective-permute-done.2 = bf16[128,1024]{1,0:T(8,128)(2,1)S(1)} collective-permute-done((bf16[128,1024]{1,0:T(8,128)(2,1)S(1)}, bf16[128,1024]{1,0:T(8,128)(2,1)S(1)}, u32[]{:S(2)}, u32[]{:S(2)}) %collective-permute-start.2) | collective-permute-done | bytes 262176 | tf_op jit(solution)/shard_map/ppermute | solution.py:41
  69.8 4.4 %collective-permute-done.5 = bf16[128,1024]{1,0:T(8,128)(2,1)S(1)} collective-permute-done((bf16[128,1024]{1,0:T(8,128)(2,1)S(1)}, bf16[128,1024]{1,0:T(8,128)(2,1)S(1)}, u32[]{:S(2)}, u32[]{:S(2)}) %collective-permute-start.5) | collective-permute-done | bytes 262176 | tf_op jit(solution)/shard_map/ppermute | solution.py:41
  74.7 5.1 %collective-permute-done.8 = bf16[128,1024]{1,0:T(8,128)(2,1)S(1)} collective-permute-done((bf16[128,1024]{1,0:T(8,128)(2,1)S(1)}, bf16[128,1024]{1,0:T(8,128)(2,1)S(1)}, u32[]{:S(2)}, u32[]{:S(2)}) %collective-permute-start.8) | collective-permute-done | bytes 262176 | tf_op jit(solution)/shard_map/ppermute | solution.py:41
  80.3 3.6 %collective-permute-done.11 = bf16[128,1024]{1,0:T(8,128)(2,1)S(1)} collective-permute-done((bf16[128,1024]{1,0:T(8,128)(2,1)S(1)}, bf16[128,1024]{1,0:T(8,128)(2,1)S(1)}, u32[]{:S(2)}, u32[]{:S(2)}) %collective-permute-start.11) | collective-permute-done | bytes 262176 | tf_op jit(solution)/shard_map/ppermute | solution.py:41
  86.4 2.9 %collective-permute-start.17 = (bf16[8,192,128]{2,0,1:T(8,128)(2,1)S(1)}, bf16[8,192,128]{2,0,1:T(8,128)(2,1)S(1)}, u32[]{:S(2)}, u32[]{:S(2)}) collective-permute-start(bf16[8,192,128]{2,0,1:T(8,128)(2,1)S(1)} %bitcast.208), channel_id=1, source_target_pairs={{0,12},{4,0},{8,4},{12,8},{1,13},{5,1},{9,5},{13,9},{2,14},{6,2},{... | collective-permute-start | bytes 1179656 | tf_op jit(solution)/shard_map/ppermute | solution.py:75
  95.6 4.3 %collective-permute-done.26 = bf16[128,1024]{1,0:T(8,128)(2,1)S(1)} collective-permute-done((bf16[128,1024]{1,0:T(8,128)(2,1)S(1)}, bf16[128,1024]{1,0:T(8,128)(2,1)S(1)}, u32[]{:S(2)}, u32[]{:S(2)}) %collective-permute-start.26) | collective-permute-done | bytes 262176 | tf_op jit(solution)/shard_map/ppermute | solution.py:46
  101.9 3.7 %collective-permute-done.27 = bf16[128,1024]{1,0:T(8,128)(2,1)S(1)} collective-permute-done((bf16[128,1024]{1,0:T(8,128)(2,1)S(1)}, bf16[128,1024]{1,0:T(8,128)(2,1)S(1)}, u32[]{:S(2)}, u32[]{:S(2)}) %collective-permute-start.27) | collective-permute-done | bytes 262176 | tf_op jit(solution)/shard_map/ppermute | solution.py:46
  107.6 3.5 %collective-permute-done.28 = bf16[128,1024]{1,0:T(8,128)(2,1)S(1)} collective-permute-done((bf16[128,1024]{1,0:T(8,128)(2,1)S(1)}, bf16[128,1024]{1,0:T(8,128)(2,1)S(1)}, u32[]{:S(2)}, u32[]{:S(2)}) %collective-permute-start.28) | collective-permute-done | bytes 262176 | tf_op jit(solution)/shard_map/ppermute | solution.py:46
  114.6 5.1 %collective-permute-start.31 = (bf16[8,192,128]{2,0,1:T(8,128)(2,1)}, bf16[8,192,128]{2,0,1:T(8,128)(2,1)}, u32[]{:S(2)}, u32[]{:S(2)}) collective-permute-start(bf16[8,192,128]{2,0,1:T(8,128)(2,1)} %bitcast.92), channel_id=1, source_target_pairs={{0,8},{4,12},{8,0},{12,4},{1,9},{5,13},{9,1},{13,5},{2,10},{6,14},... | collective-permute-start | bytes 1179656 | tf_op jit(solution)/shard_map/ppermute | solution.py:75
  122.8 2.2 %fusion.54 = bf16[192,256]{1,0:T(8,128)(2,1)S(1)} fusion(bf16[4096,1024]{1,0:T(8,128)(2,1)} %constant_dynamic-update-slice_fusion, bf16[24,8,32,128]{3,2,1,0:T(8,128)(2,1)S(1)} %bitcast.198), kind=kOutput, calls=%fused_computation.52 | convolution fusion | flops 402702336 | bytes 3768320 | tf_op jit(solution)/shard_map/dot_general | solution.py:149
  125.1 5.5 %fusion.41 = bf16[192,512]{1,0:T(8,128)(2,1)} fusion(bf16[4096,1024]{1,0:T(8,128)(2,1)} %constant_dynamic-update-slice_fusion, bf16[192,256]{1,0:T(8,128)(2,1)S(1)} %fusion.54, f32[4096]{0:T(1024)S(1)} %bitcast.213, bf16[24,8,32,128]{3,2,1,0:T(8,128)(2,1)S(1)} %bitcast.199, f32[512]{0:T(512)S(1)} %bitcast.216), kind=kOutput, calls=%fused_computation.39 | convolution fusion | flops 1212088320 | bytes 8177664 | tf_op jit(solution)/shard_map/dot_general | solution.py:159
  130.5 4.2 %all-to-all-start = ((bf16[4,48,512]{2,1,0:T(8,128)(2,1)}), bf16[4,48,512]{2,1,0:T(8,128)(2,1)}, u32[]{:S(2)}, u32[]{:S(2)}) async-start(bf16[4,48,512]{2,1,0:T(8,128)(2,1)} %bitcast.86), calls=%async_computation | async-start | bytes 393216 | tf_op jit(solution)/shard_map/all_to_all | solution.py:161
  137.1 2.8 %collective-permute-start.32 = (bf16[8,192,128]{2,0,1:T(8,128)(2,1)}, bf16[8,192,128]{2,0,1:T(8,128)(2,1)}, u32[]{:S(2)}, u32[]{:S(2)}) collective-permute-start(bf16[8,192,128]{2,0,1:T(8,128)(2,1)} %bitcast.206), channel_id=1, source_target_pairs={{0,12},{4,0},{8,4},{12,8},{1,13},{5,1},{9,5},{13,9},{2,14},{6,2},{... | collective-permute-start | bytes 1179656 | tf_op jit(solution)/shard_map/ppermute | solution.py:75
  151.9 5.0 %collective-permute-done.32 = bf16[8,192,128]{2,0,1:T(8,128)(2,1)} collective-permute-done((bf16[8,192,128]{2,0,1:T(8,128)(2,1)}, bf16[8,192,128]{2,0,1:T(8,128)(2,1)}, u32[]{:S(2)}, u32[]{:S(2)}) %collective-permute-start.32) | collective-permute-done | bytes 393248 | tf_op jit(solution)/shard_map/ppermute | solution.py:75
  160.0 2.3 %fusion.59 = bf16[192,256]{1,0:T(8,128)(2,1)S(1)} fusion(bf16[4096,1024]{1,0:T(8,128)(2,1)} %constant_dynamic-update-slice_fusion, bf16[24,8,32,128]{3,2,1,0:T(8,128)(2,1)S(1)} %bitcast.196), kind=kOutput, calls=%fused_computation.53 | convolution fusion | flops 402702336 | bytes 3768320 | tf_op jit(solution)/shard_map/dot_general | solution.py:149
  162.4 6.1 %fusion.36 = bf16[192,512]{1,0:T(8,128)(2,1)} fusion(bf16[4096,1024]{1,0:T(8,128)(2,1)} %constant_dynamic-update-slice_fusion, bf16[192,256]{1,0:T(8,128)(2,1)S(1)} %fusion.59, f32[4096]{0:T(1024)} %bitcast.214, bf16[24,8,32,128]{3,2,1,0:T(8,128)(2,1)} %bitcast.197, f32[512]{0:T(512)} %bitcast.215), kind=kOutput, calls=%fused_computation.38 | convolution fusion | flops 1212088320 | bytes 8177664 | tf_op jit(solution)/shard_map/dot_general | solution.py:159
  168.4 3.4 %all-to-all-start.1 = ((bf16[4,48,512]{2,1,0:T(8,128)(2,1)}), bf16[4,48,512]{2,1,0:T(8,128)(2,1)S(1)}, u32[]{:S(2)}, u32[]{:S(2)}) async-start(bf16[4,48,512]{2,1,0:T(8,128)(2,1)} %bitcast.95), calls=%async_computation.1 | async-start | bytes 393216 | tf_op jit(solution)/shard_map/all_to_all | solution.py:161
  172.1 5.0 %all-to-all-done.1 = bf16[4,48,512]{2,1,0:T(8,128)(2,1)S(1)} async-done(((bf16[4,48,512]{2,1,0:T(8,128)(2,1)}), bf16[4,48,512]{2,1,0:T(8,128)(2,1)S(1)}, u32[]{:S(2)}, u32[]{:S(2)}) %all-to-all-start.1) | async-done | bytes 196640 | tf_op jit(solution)/shard_map/all_to_all | solution.py:161
  (194 shorter events, 83.5 us)
Async XLA Ops:
  0.0 27.4 %collective-permute-start.14 = (bf16[62,1024]{1,0:T(8,128)(2,1)}, bf16[62,1024]{1,0:T(8,128)(2,1)}, u32[]{:S(2)}, u32[]{:S(2)}) collective-permute-start(bf16[62,1024]{1,0:T(8,128)(2,1)} %param.24), channel_id=1, source_target_pairs={{0,3},{1,0},{2,1},{3,2},{4,7},{5,4},{6,5},{7,6},{8,11},{9,8},{10,9... | collective-permute-start | bytes 380936 | tf_op jit(solution)/shard_map/ppermute | solution.py:113
  2.4 32.4 %collective-permute-start.12 = (bf16[62,1024]{1,0:T(8,128)(2,1)}, bf16[62,1024]{1,0:T(8,128)(2,1)S(1)}, u32[]{:S(2)}, u32[]{:S(2)}) collective-permute-start(bf16[62,1024]{1,0:T(8,128)(2,1)} %param.24), channel_id=1, source_target_pairs={{0,1},{1,2},{2,3},{3,0},{4,5},{5,6},{6,7},{7,4},{8,9},{9,10},{10,1... | collective-permute-start | bytes 380936 | tf_op jit(solution)/shard_map/ppermute | solution.py:113
  8.1 19.3 %collective-permute-start.3 = (bf16[128,1024]{1,0:T(8,128)(2,1)}, bf16[128,1024]{1,0:T(8,128)(2,1)}, u32[]{:S(2)}, u32[]{:S(2)}) collective-permute-start(bf16[128,1024]{1,0:T(8,128)(2,1)} %get-tuple-element.22), channel_id=1, source_target_pairs={{0,4},{4,8},{8,12},{12,0},{1,5},{5,9},{9,13},{13,1},{2,6},{6,10},{... | collective-permute-start | bytes 786440 | tf_op jit(solution)/shard_map/ppermute | solution.py:41
  9.7 19.2 %collective-permute-start.6 = (bf16[128,1024]{1,0:T(8,128)(2,1)}, bf16[128,1024]{1,0:T(8,128)(2,1)}, u32[]{:S(2)}, u32[]{:S(2)}) collective-permute-start(bf16[128,1024]{1,0:T(8,128)(2,1)} %get-tuple-element.24), channel_id=1, source_target_pairs={{0,4},{4,8},{8,12},{12,0},{1,5},{5,9},{9,13},{13,1},{2,6},{6,10},{... | collective-permute-start | bytes 786440 | tf_op jit(solution)/shard_map/ppermute | solution.py:41
  17.9 14.3 %collective-permute-start.18 = (bf16[128,1024]{1,0:T(8,128)(2,1)}, bf16[128,1024]{1,0:T(8,128)(2,1)}, u32[]{:S(2)}, u32[]{:S(2)}) collective-permute-start(bf16[128,1024]{1,0:T(8,128)(2,1)} %collective-permute-done), channel_id=1, source_target_pairs={{0,16},{16,0},{1,17},{17,1},{2,18},{18,2},{3,19},{19,3},{4,20},{20... | collective-permute-start | bytes 786440 | tf_op jit(solution)/shard_map/ppermute | solution.py:46
  27.5 12.9 %collective-permute-start.19 = (bf16[128,1024]{1,0:T(8,128)(2,1)}, bf16[128,1024]{1,0:T(8,128)(2,1)S(1)}, u32[]{:S(2)}, u32[]{:S(2)}) collective-permute-start(bf16[128,1024]{1,0:T(8,128)(2,1)} %collective-permute-done.3), channel_id=1, source_target_pairs={{0,16},{16,0},{1,17},{17,1},{2,18},{18,2},{3,19},{19,3},{4,20},{20... | collective-permute-start | bytes 786440 | tf_op jit(solution)/shard_map/ppermute | solution.py:46
  37.2 14.5 %collective-permute-start.4 = (bf16[128,1024]{1,0:T(8,128)(2,1)}, bf16[128,1024]{1,0:T(8,128)(2,1)S(1)}, u32[]{:S(2)}, u32[]{:S(2)}) collective-permute-start(bf16[128,1024]{1,0:T(8,128)(2,1)} %collective-permute-done.3), channel_id=1, source_target_pairs={{0,4},{4,8},{8,12},{12,0},{1,5},{5,9},{9,13},{13,1},{2,6},{6,10},{... | collective-permute-start | bytes 786440 | tf_op jit(solution)/shard_map/ppermute | solution.py:41
  38.4 18.9 %collective-permute-start.7 = (bf16[128,1024]{1,0:T(8,128)(2,1)}, bf16[128,1024]{1,0:T(8,128)(2,1)S(1)}, u32[]{:S(2)}, u32[]{:S(2)}) collective-permute-start(bf16[128,1024]{1,0:T(8,128)(2,1)} %collective-permute-done.6), channel_id=1, source_target_pairs={{0,4},{4,8},{8,12},{12,0},{1,5},{5,9},{9,13},{13,1},{2,6},{6,10},{... | collective-permute-start | bytes 786440 | tf_op jit(solution)/shard_map/ppermute | solution.py:41
  41.1 21.9 %collective-permute-start.10 = (bf16[128,1024]{1,0:T(8,128)(2,1)S(1)}, bf16[128,1024]{1,0:T(8,128)(2,1)S(1)}, u32[]{:S(2)}, u32[]{:S(2)}) collective-permute-start(bf16[128,1024]{1,0:T(8,128)(2,1)S(1)} %collective-permute-done.9), channel_id=1, source_target_pairs={{0,4},{4,8},{8,12},{12,0},{1,5},{5,9},{9,13},{13,1},{2,6},{6,10},{... | collective-permute-start | bytes 786440 | tf_op jit(solution)/shard_map/ppermute | solution.py:41
  46.1 22.5 %collective-permute-start.2 = (bf16[128,1024]{1,0:T(8,128)(2,1)S(1)}, bf16[128,1024]{1,0:T(8,128)(2,1)S(1)}, u32[]{:S(2)}, u32[]{:S(2)}) collective-permute-start(bf16[128,1024]{1,0:T(8,128)(2,1)S(1)} %collective-permute-done.1), channel_id=1, source_target_pairs={{0,4},{4,8},{8,12},{12,0},{1,5},{5,9},{9,13},{13,1},{2,6},{6,10},{... | collective-permute-start | bytes 786440 | tf_op jit(solution)/shard_map/ppermute | solution.py:41
  47.0 37.0 %collective-permute-start.22 = (bf16[128,1024]{1,0:T(8,128)(2,1)S(1)}, bf16[128,1024]{1,0:T(8,128)(2,1)S(1)}, u32[]{:S(2)}, u32[]{:S(2)}) collective-permute-start(bf16[128,1024]{1,0:T(8,128)(2,1)S(1)} %collective-permute-done.1), channel_id=1, source_target_pairs={{0,16},{16,0},{1,17},{17,1},{2,18},{18,2},{3,19},{19,3},{4,20},{20... | collective-permute-start | bytes 786440 | tf_op jit(solution)/shard_map/ppermute | solution.py:46
  51.7 22.5 %collective-permute-start.5 = (bf16[128,1024]{1,0:T(8,128)(2,1)S(1)}, bf16[128,1024]{1,0:T(8,128)(2,1)S(1)}, u32[]{:S(2)}, u32[]{:S(2)}) collective-permute-start(bf16[128,1024]{1,0:T(8,128)(2,1)S(1)} %collective-permute-done.4), channel_id=1, source_target_pairs={{0,4},{4,8},{8,12},{12,0},{1,5},{5,9},{9,13},{13,1},{2,6},{6,10},{... | collective-permute-start | bytes 786440 | tf_op jit(solution)/shard_map/ppermute | solution.py:41
  57.3 22.5 %collective-permute-start.8 = (bf16[128,1024]{1,0:T(8,128)(2,1)S(1)}, bf16[128,1024]{1,0:T(8,128)(2,1)S(1)}, u32[]{:S(2)}, u32[]{:S(2)}) collective-permute-start(bf16[128,1024]{1,0:T(8,128)(2,1)S(1)} %collective-permute-done.7), channel_id=1, source_target_pairs={{0,4},{4,8},{8,12},{12,0},{1,5},{5,9},{9,13},{13,1},{2,6},{6,10},{... | collective-permute-start | bytes 786440 | tf_op jit(solution)/shard_map/ppermute | solution.py:41
  63.0 21.0 %collective-permute-start.11 = (bf16[128,1024]{1,0:T(8,128)(2,1)S(1)}, bf16[128,1024]{1,0:T(8,128)(2,1)S(1)}, u32[]{:S(2)}, u32[]{:S(2)}) collective-permute-start(bf16[128,1024]{1,0:T(8,128)(2,1)S(1)} %collective-permute-done.10), channel_id=1, source_target_pairs={{0,4},{4,8},{8,12},{12,0},{1,5},{5,9},{9,13},{13,1},{2,6},{6,10},{... | collective-permute-start | bytes 786440 | tf_op jit(solution)/shard_map/ppermute | solution.py:41
  68.6 17.8 %collective-permute-start.23 = (bf16[128,1024]{1,0:T(8,128)(2,1)S(1)}, bf16[128,1024]{1,0:T(8,128)(2,1)S(1)}, u32[]{:S(2)}, u32[]{:S(2)}) collective-permute-start(bf16[128,1024]{1,0:T(8,128)(2,1)S(1)} %collective-permute-done.4), channel_id=1, source_target_pairs={{0,16},{16,0},{1,17},{17,1},{2,18},{18,2},{3,19},{19,3},{4,20},{20... | collective-permute-start | bytes 786440 | tf_op jit(solution)/shard_map/ppermute | solution.py:46
  74.2 16.5 %collective-permute-start.24 = (bf16[128,1024]{1,0:T(8,128)(2,1)S(1)}, bf16[128,1024]{1,0:T(8,128)(2,1)S(1)}, u32[]{:S(2)}, u32[]{:S(2)}) collective-permute-start(bf16[128,1024]{1,0:T(8,128)(2,1)S(1)} %collective-permute-done.7), channel_id=1, source_target_pairs={{0,16},{16,0},{1,17},{17,1},{2,18},{18,2},{3,19},{19,3},{4,20},{20... | collective-permute-start | bytes 786440 | tf_op jit(solution)/shard_map/ppermute | solution.py:46
  79.8 12.8 %collective-permute-start.25 = (bf16[128,1024]{1,0:T(8,128)(2,1)S(1)}, bf16[128,1024]{1,0:T(8,128)(2,1)S(1)}, u32[]{:S(2)}, u32[]{:S(2)}) collective-permute-start(bf16[128,1024]{1,0:T(8,128)(2,1)S(1)} %collective-permute-done.10), channel_id=1, source_target_pairs={{0,16},{16,0},{1,17},{17,1},{2,18},{18,2},{3,19},{19,3},{4,20},{20... | collective-permute-start | bytes 786440 | tf_op jit(solution)/shard_map/ppermute | solution.py:46
  84.0 30.6 %collective-permute-start.15 = (bf16[8,192,128]{2,0,1:T(8,128)(2,1)S(1)}, bf16[8,192,128]{2,0,1:T(8,128)(2,1)S(1)}, u32[]{:S(2)}, u32[]{:S(2)}) collective-permute-start(bf16[8,192,128]{2,0,1:T(8,128)(2,1)S(1)} %bitcast.210), channel_id=1, source_target_pairs={{0,4},{4,8},{8,12},{12,0},{1,5},{5,9},{9,13},{13,1},{2,6},{6,10},{... | collective-permute-start | bytes 1179656 | tf_op jit(solution)/shard_map/ppermute | solution.py:75
  84.0 30.6 %collective-permute-start.16 = (bf16[8,192,128]{2,0,1:T(8,128)(2,1)S(1)}, bf16[8,192,128]{2,0,1:T(8,128)(2,1)S(1)}, u32[]{:S(2)}, u32[]{:S(2)}) collective-permute-start(bf16[8,192,128]{2,0,1:T(8,128)(2,1)S(1)} %bitcast.209), channel_id=1, source_target_pairs={{0,8},{4,12},{8,0},{12,4},{1,9},{5,13},{9,1},{13,5},{2,10},{6,14},... | collective-permute-start | bytes 1179656 | tf_op jit(solution)/shard_map/ppermute | solution.py:75
  86.4 28.2 %collective-permute-start.17 = (bf16[8,192,128]{2,0,1:T(8,128)(2,1)S(1)}, bf16[8,192,128]{2,0,1:T(8,128)(2,1)S(1)}, u32[]{:S(2)}, u32[]{:S(2)}) collective-permute-start(bf16[8,192,128]{2,0,1:T(8,128)(2,1)S(1)} %bitcast.208), channel_id=1, source_target_pairs={{0,12},{4,0},{8,4},{12,8},{1,13},{5,1},{9,5},{13,9},{2,14},{6,2},{... | collective-permute-start | bytes 1179656 | tf_op jit(solution)/shard_map/ppermute | solution.py:75
  92.6 12.9 %collective-permute-start.27 = (bf16[128,1024]{1,0:T(8,128)(2,1)S(1)}, bf16[128,1024]{1,0:T(8,128)(2,1)S(1)}, u32[]{:S(2)}, u32[]{:S(2)}) collective-permute-start(bf16[128,1024]{1,0:T(8,128)(2,1)S(1)} %collective-permute-done.5), channel_id=1, source_target_pairs={{0,16},{16,0},{1,17},{17,1},{2,18},{18,2},{3,19},{19,3},{4,20},{20... | collective-permute-start | bytes 786440 | tf_op jit(solution)/shard_map/ppermute | solution.py:46
  114.6 32.7 %collective-permute-start.31 = (bf16[8,192,128]{2,0,1:T(8,128)(2,1)}, bf16[8,192,128]{2,0,1:T(8,128)(2,1)}, u32[]{:S(2)}, u32[]{:S(2)}) collective-permute-start(bf16[8,192,128]{2,0,1:T(8,128)(2,1)} %bitcast.92), channel_id=1, source_target_pairs={{0,8},{4,12},{8,0},{12,4},{1,9},{5,13},{9,1},{13,5},{2,10},{6,14},... | collective-permute-start | bytes 1179656 | tf_op jit(solution)/shard_map/ppermute | solution.py:75
  136.0 14.2 %collective-permute-start.30 = (bf16[8,192,128]{2,0,1:T(8,128)(2,1)}, bf16[8,192,128]{2,0,1:T(8,128)(2,1)}, u32[]{:S(2)}, u32[]{:S(2)}) collective-permute-start(bf16[8,192,128]{2,0,1:T(8,128)(2,1)} %bitcast.207), channel_id=1, source_target_pairs={{0,4},{4,8},{8,12},{12,0},{1,5},{5,9},{9,13},{13,1},{2,6},{6,10},{... | collective-permute-start | bytes 1179656 | tf_op jit(solution)/shard_map/ppermute | solution.py:75
  137.1 19.8 %collective-permute-start.32 = (bf16[8,192,128]{2,0,1:T(8,128)(2,1)}, bf16[8,192,128]{2,0,1:T(8,128)(2,1)}, u32[]{:S(2)}, u32[]{:S(2)}) collective-permute-start(bf16[8,192,128]{2,0,1:T(8,128)(2,1)} %bitcast.206), channel_id=1, source_target_pairs={{0,12},{4,0},{8,4},{12,8},{1,13},{5,1},{9,5},{13,9},{2,14},{6,2},{... | collective-permute-start | bytes 1179656 | tf_op jit(solution)/shard_map/ppermute | solution.py:75
  (37 other events, 1108.2 us)

commit v13 on v10

--- a/solution.py
+++ b/solution.py
@@ -13,27 +13,32 @@
     return upper_rows * vector_count + upper_cols
 
 
-def weight_parts(weights_here, feat_count, group_count, share_count, entry_count):
-    rows_here = weights_here.shape[0]
+def weight_parts(weight_list, feat_count, group_count, share_count, entry_count):
+    rows_here = weight_list[0].shape[0]
     piece = rows_here // share_count
     blocks_here = rows_here // entry_count
     blocks_piece = piece // entry_count
     owner = lax.axis_index("feat")
     group = lax.axis_index("groups") if share_count > 1 else 0
     block_range = jnp.arange(blocks_piece, dtype=jnp.int32)
-    parts = [(weights_here, owner * blocks_here + jnp.arange(blocks_here, dtype=jnp.int32))]
-    if share_count > 1:
-        travelling = lax.dynamic_slice_in_dim(weights_here, group * piece, piece, axis=0)
-    else:
-        travelling = weights_here
     chunk_count = next(count for count in (4, 2, 1) if blocks_piece % count == 0)
     chunk_blocks = blocks_piece // chunk_count
     chunk_rows = chunk_blocks * entry_count
     chunk_range = jnp.arange(chunk_blocks, dtype=jnp.int32)
     rings = [
-        lax.slice_in_dim(travelling, chunk * chunk_rows, (chunk + 1) * chunk_rows, axis=0)
+        jnp.concatenate(
+            [
+                lax.dynamic_slice_in_dim(
+                    weight, group * piece + chunk * chunk_rows, chunk_rows, axis=0
+                )
+                for weight in weight_list
+            ],
+            axis=1,
+        )
         for chunk in range(chunk_count)
     ]
+    weights_here = jnp.concatenate(weight_list, axis=1)
+    parts = [(weights_here, owner * blocks_here + jnp.arange(blocks_here, dtype=jnp.int32))]
     ring = [(source, (source + 1) % feat_count) for source in range(feat_count)]
     for step in range(1, feat_count):
         source_block = (owner - step) % feat_count
@@ -105,11 +110,11 @@
         pairs = [(source, (source + shift) % tower_count) for source in range(tower_count)]
         hidden_pieces.append(lax.ppermute(mlp_weight, "tower", pairs))
 
-    weights_here = jnp.concatenate([cross_down[0], cross_up[0], compress_weight[0]], axis=1)
-    parts, last_rows = weight_parts(weights_here, feat_count, group_count, share_count, entry_count)
+    weight_list = [cross_down[0], cross_up[0], compress_weight[0]]
+    parts, last_rows = weight_parts(weight_list, feat_count, group_count, share_count, entry_count)
 
     first_rows, second_rows, _ = lax.optimization_barrier(
-        (pooled_first[0], pooled_second[0], last_rows)
+        (pooled_first[0], pooled_second[0], (last_rows, hidden_pieces))
     )
     pieces, slot_ids = exchange_rows(first_rows, second_rows, feat_count)
     row_count = pieces[0].shape[1]

time: 179 us -> 184 us (1.028)
  the two profiles are of different devices: /device:TPU:0 before, /device:TPU:8 now
where the time goes in v13:
time: 184 us
  waiting for transfers between devices  94.8 us (52%)
  starting transfers between devices  38.8 us (21%)
  local copies, waits for them, and re-layouts  23.6 us (13%)
  matrix products  19.5 us (11%)
  other arithmetic  6.19 us (3%)
    ppermute x3, waiting for transfers between devices, exchange_rows(): lax.ppermute(piece, 'feat', [(source, (source + shift) % feat_count) for...  32.3 us
    ppermute x12, waiting for transfers between devices, weight_parts(): forwarded = lax.ppermute(rings[chunk], 'groups', pairs)  29.5 us
    ppermute x12, waiting for transfers between devices, weight_parts(): rings[chunk] = lax.ppermute(rings[chunk], 'feat', ring)  21 us
    ppermute x12, starting transfers between devices, weight_parts(): rings[chunk] = lax.ppermute(rings[chunk], 'feat', ring)  16.3 us
    squeeze x1, local copies, waits for them, and re-layouts, on_device(): pooled_second[0]  12 us
    ppermute x12, starting transfers between devices, weight_parts(): forwarded = lax.ppermute(rings[chunk], 'groups', pairs)  10.2 us
    all_to_all x1, waiting for transfers between devices, on_device(): lax.all_to_all(compressed, 'tower', split_axis=0, concat_axis=1, tiled=True)  7.44 us
    dot_general x1, matrix products, on_device(): jnp.dot(crossed, weights[:, 2 * rank:], preferred_element_type=jnp.float32)  7.26 us
  transfers between devices with their start and end apart: 31, of which 18 were waited for; matrix products, arithmetic and copies ran while one was open for 17% of the time, Pallas kernels for 0%

profile of v13, /device:TPU:8, one launch (start us, length us, event | category | flops | bytes accessed | tf_op | source)
XLA Modules:
  0.0 183.5 jit_solution(14364792257297336313)
XLA Ops:
  11.6 12.0 %copy_bitcast_fusion = (bf16[4,1536,128]{2,0,1:T(4,128)(2,1)S(1)}, bf16[4,1536,128]{2,0,1:T(4,128)(2,1)S(1)}) fusion(bf16[1,4,1536,128]{3,2,1,0:T(8,128)(2,1)} %param.14, bf16[1,4,1536,128]{3,2,1,0:T(8,128)(2,1)} %param.13), kind=kLoop, calls=%fused_computation.17 | loop fusion | bytes 6291456 | tf_op jit(solution)/shard_map/squeeze | solution.py:117
  28.6 1.8 maximum_dynamic-update-slice_fusion
  32.5 3.9 %collective-permute-done.18 = bf16[128,1024]{1,0:T(8,128)(2,1)S(1)} collective-permute-done((bf16[128,1024]{1,0:T(8,128)(2,1)}, bf16[128,1024]{1,0:T(8,128)(2,1)S(1)}, u32[]{:S(2)}, u32[]{:S(2)}) %collective-permute-start.18) | collective-permute-done | bytes 262176 | tf_op jit(solution)/shard_map/ppermute | solution.py:51
  50.1 4.0 %collective-permute-done.4 = bf16[128,1024]{1,0:T(8,128)(2,1)S(1)} collective-permute-done((bf16[128,1024]{1,0:T(8,128)(2,1)}, bf16[128,1024]{1,0:T(8,128)(2,1)S(1)}, u32[]{:S(2)}, u32[]{:S(2)}) %collective-permute-start.4) | collective-permute-done | bytes 262176 | tf_op jit(solution)/shard_map/ppermute | solution.py:46
  55.7 4.0 %collective-permute-done.7 = bf16[128,1024]{1,0:T(8,128)(2,1)S(1)} collective-permute-done((bf16[128,1024]{1,0:T(8,128)(2,1)}, bf16[128,1024]{1,0:T(8,128)(2,1)S(1)}, u32[]{:S(2)}, u32[]{:S(2)}) %collective-permute-start.7) | collective-permute-done | bytes 262176 | tf_op jit(solution)/shard_map/ppermute | solution.py:46
  61.3 4.0 %collective-permute-done.10 = bf16[128,1024]{1,0:T(8,128)(2,1)S(1)} collective-permute-done((bf16[128,1024]{1,0:T(8,128)(2,1)S(1)}, bf16[128,1024]{1,0:T(8,128)(2,1)S(1)}, u32[]{:S(2)}, u32[]{:S(2)}) %collective-permute-start.10) | collective-permute-done | bytes 262176 | tf_op jit(solution)/shard_map/ppermute | solution.py:46
  67.1 4.5 %collective-permute-done.12 = bf16[62,1024]{1,0:T(8,128)(2,1)S(1)} collective-permute-done((bf16[62,1024]{1,0:T(8,128)(2,1)}, bf16[62,1024]{1,0:T(8,128)(2,1)S(1)}, u32[]{:S(2)}, u32[]{:S(2)}) %collective-permute-start.12) | collective-permute-done | bytes 127008 | tf_op jit(solution)/shard_map/ppermute | solution.py:111
  73.7 2.2 %collective-permute-done.5 = bf16[128,1024]{1,0:T(8,128)(2,1)S(1)} collective-permute-done((bf16[128,1024]{1,0:T(8,128)(2,1)S(1)}, bf16[128,1024]{1,0:T(8,128)(2,1)S(1)}, u32[]{:S(2)}, u32[]{:S(2)}) %collective-permute-start.5) | collective-permute-done | bytes 262176 | tf_op jit(solution)/shard_map/ppermute | solution.py:46
  76.4 2.3 %collective-permute-done.8 = bf16[128,1024]{1,0:T(8,128)(2,1)S(1)} collective-permute-done((bf16[128,1024]{1,0:T(8,128)(2,1)S(1)}, bf16[128,1024]{1,0:T(8,128)(2,1)S(1)}, u32[]{:S(2)}, u32[]{:S(2)}) %collective-permute-start.8) | collective-permute-done | bytes 262176 | tf_op jit(solution)/shard_map/ppermute | solution.py:46
  79.2 3.5 %collective-permute-done.11 = bf16[128,1024]{1,0:T(8,128)(2,1)S(1)} collective-permute-done((bf16[128,1024]{1,0:T(8,128)(2,1)S(1)}, bf16[128,1024]{1,0:T(8,128)(2,1)S(1)}, u32[]{:S(2)}, u32[]{:S(2)}) %collective-permute-start.11) | collective-permute-done | bytes 262176 | tf_op jit(solution)/shard_map/ppermute | solution.py:46
  84.2 2.4 %collective-permute-start.15 = (bf16[8,384,128]{2,0,1:T(8,128)(2,1)S(1)}, bf16[8,384,128]{2,0,1:T(8,128)(2,1)S(1)}, u32[]{:S(2)}, u32[]{:S(2)}) collective-permute-start(bf16[8,384,128]{2,0,1:T(8,128)(2,1)S(1)} %pad_maximum_fusion), channel_id=1, source_target_pairs={{0,4},{4,8},{8,12},{12,0},{1,5},{5,9},{9,13},{13,1},{2,6},{6,10},{... | collective-permute-start | bytes 2359304 | tf_op jit(solution)/shard_map/ppermute | solution.py:73
  88.9 2.0 %collective-permute-start.17 = (bf16[8,384,128]{2,0,1:T(8,128)(2,1)S(1)}, bf16[8,384,128]{2,0,1:T(8,128)(2,1)S(1)}, u32[]{:S(2)}, u32[]{:S(2)}) collective-permute-start(bf16[8,384,128]{2,0,1:T(8,128)(2,1)S(1)} %pad_maximum_fusion.2), channel_id=1, source_target_pairs={{0,12},{4,0},{8,4},{12,8},{1,13},{5,1},{9,5},{13,9},{2,14},{6,2},{... | collective-permute-start | bytes 2359304 | tf_op jit(solution)/shard_map/ppermute | solution.py:73
  92.6 5.1 %collective-permute-done.25 = bf16[128,1024]{1,0:T(8,128)(2,1)S(1)} collective-permute-done((bf16[128,1024]{1,0:T(8,128)(2,1)S(1)}, bf16[128,1024]{1,0:T(8,128)(2,1)S(1)}, u32[]{:S(2)}, u32[]{:S(2)}) %collective-permute-start.25) | collective-permute-done | bytes 262176 | tf_op jit(solution)/shard_map/ppermute | solution.py:51
  98.3 5.1 %collective-permute-done.26 = bf16[128,1024]{1,0:T(8,128)(2,1)S(1)} collective-permute-done((bf16[128,1024]{1,0:T(8,128)(2,1)S(1)}, bf16[128,1024]{1,0:T(8,128)(2,1)S(1)}, u32[]{:S(2)}, u32[]{:S(2)}) %collective-permute-start.26) | collective-permute-done | bytes 262176 | tf_op jit(solution)/shard_map/ppermute | solution.py:51
  103.9 5.1 %collective-permute-done.27 = bf16[128,1024]{1,0:T(8,128)(2,1)S(1)} collective-permute-done((bf16[128,1024]{1,0:T(8,128)(2,1)S(1)}, bf16[128,1024]{1,0:T(8,128)(2,1)S(1)}, u32[]{:S(2)}, u32[]{:S(2)}) %collective-permute-start.27) | collective-permute-done | bytes 262176 | tf_op jit(solution)/shard_map/ppermute | solution.py:51
  109.5 5.1 %collective-permute-done.28 = bf16[128,1024]{1,0:T(8,128)(2,1)S(1)} collective-permute-done((bf16[128,1024]{1,0:T(8,128)(2,1)S(1)}, bf16[128,1024]{1,0:T(8,128)(2,1)S(1)}, u32[]{:S(2)}, u32[]{:S(2)}) %collective-permute-start.28) | collective-permute-done | bytes 262176 | tf_op jit(solution)/shard_map/ppermute | solution.py:51
  114.6 2.9 %collective-permute-done.29 = bf16[128,1024]{1,0:T(8,128)(2,1)S(1)} collective-permute-done((bf16[128,1024]{1,0:T(8,128)(2,1)S(1)}, bf16[128,1024]{1,0:T(8,128)(2,1)S(1)}, u32[]{:S(2)}, u32[]{:S(2)}) %collective-permute-start.29) | collective-permute-done | bytes 262176 | tf_op jit(solution)/shard_map/ppermute | solution.py:51
  117.6 32.3 %collective-permute-done.17 = bf16[8,384,128]{2,0,1:T(8,128)(2,1)S(1)} collective-permute-done((bf16[8,384,128]{2,0,1:T(8,128)(2,1)S(1)}, bf16[8,384,128]{2,0,1:T(8,128)(2,1)S(1)}, u32[]{:S(2)}, u32[]{:S(2)}) %collective-permute-start.17) | collective-permute-done | bytes 786464 | tf_op jit(solution)/shard_map/ppermute | solution.py:73
  153.2 1.8 add_convert_fusion
  155.0 3.3 %fusion.24 = bf16[384,256]{1,0:T(8,128)(2,1)} fusion(bf16[4096,1024]{1,0:T(8,128)(2,1)} %copy-done.2, bf16[48,8,32,128]{3,2,1,0:T(8,128)(2,1)S(1)} %bitcast.158), kind=kOutput, calls=%fused_computation.28 | convolution fusion | flops 805404672 | bytes 5439488 | tf_op jit(solution)/shard_map/dot_general | solution.py:137
  158.3 7.3 %fusion.15 = bf16[384,512]{1,0:T(8,128)(2,1)} fusion(bf16[4096,1024]{1,0:T(8,128)(2,1)} %copy-done.2, bf16[384,256]{1,0:T(8,128)(2,1)} %fusion.24, f32[4096]{0:T(1024)S(1)} %bitcast.167, bf16[48,8,32,128]{3,2,1,0:T(8,128)(2,1)S(1)} %bitcast.159, f32[512]{0:T(512)S(1)} %bitcast.168), kind=kOutput, calls=%fused_computation.21 | convolution fusion | flops 2424176640 | bytes 10045440 | tf_op jit(solution)/shard_map/dot_general | solution.py:148
  165.6 4.9 %all-to-all-start = ((bf16[4,96,512]{2,1,0:T(8,128)(2,1)}), bf16[4,96,512]{2,1,0:T(8,128)(2,1)S(1)}, u32[]{:S(2)}, u32[]{:S(2)}) async-start(bf16[4,96,512]{2,1,0:T(8,128)(2,1)} %bitcast.165), calls=%async_computation | async-start | bytes 786432 | tf_op jit(solution)/shard_map/all_to_all | solution.py:150
  170.5 7.4 %all-to-all-done = bf16[4,96,512]{2,1,0:T(8,128)(2,1)S(1)} async-done(((bf16[4,96,512]{2,1,0:T(8,128)(2,1)}), bf16[4,96,512]{2,1,0:T(8,128)(2,1)S(1)}, u32[]{:S(2)}, u32[]{:S(2)}) %all-to-all-start) | async-done | bytes 393248 | tf_op jit(solution)/shard_map/all_to_all | solution.py:150
  181.6 1.9 %fusion.23 = bf16[96,1024]{1,0:T(8,128)(2,1)} fusion(f32[96,1024]{1,0:T(8,128)S(1)} %fusion.36, f32[96,1024]{1,0:T(8,128)S(1)} %convolution_add_fusion.1, bf16[62,1024]{1,0:T(8,128)(2,1)} %copy-done.5, f32[1024]{0:T(1024)S(1)} %copy-done.6, s32[]{:T(128)S(6)} %select_n.209, bf16[96,128]{1,0:T(8,128)(2,1)S(1)} %copy-done.3, bf16[96,120]{1,0:T(8,128)(2,1)S(1)} %copy.23), kind=kOutput, calls=%fused_computation.27 | convolution fusion | flops 12705024 | bytes 1161732 | tf_op jit(solution)/shard_map/dot_general | solution.py:168
  (134 shorter events, 54.0 us)
Async XLA Ops:
  0.0 39.0 %collective-permute-start.14 = (bf16[62,1024]{1,0:T(8,128)(2,1)}, bf16[62,1024]{1,0:T(8,128)(2,1)}, u32[]{:S(2)}, u32[]{:S(2)}) collective-permute-start(bf16[62,1024]{1,0:T(8,128)(2,1)} %param.22), channel_id=1, source_target_pairs={{0,3},{1,0},{2,1},{3,2},{4,7},{5,4},{6,5},{7,6},{8,11},{9,8},{10,9... | collective-permute-start | bytes 380936 | tf_op jit(solution)/shard_map/ppermute | solution.py:111
  4.0 23.0 %collective-permute-start = (bf16[128,1024]{1,0:T(8,128)(2,1)}, bf16[128,1024]{1,0:T(8,128)(2,1)}, u32[]{:S(2)}, u32[]{:S(2)}) collective-permute-start(bf16[128,1024]{1,0:T(8,128)(2,1)} %pad_maximum_fusion.3), channel_id=1, source_target_pairs={{0,4},{4,8},{8,12},{12,0},{1,5},{5,9},{9,13},{13,1},{2,6},{6,10},{... | collective-permute-start | bytes 786440 | tf_op jit(solution)/shard_map/ppermute | solution.py:46
  6.3 24.0 %collective-permute-start.3 = (bf16[128,1024]{1,0:T(8,128)(2,1)}, bf16[128,1024]{1,0:T(8,128)(2,1)}, u32[]{:S(2)}, u32[]{:S(2)}) collective-permute-start(bf16[128,1024]{1,0:T(8,128)(2,1)} %pad_maximum_fusion.4), channel_id=1, source_target_pairs={{0,4},{4,8},{8,12},{12,0},{1,5},{5,9},{9,13},{13,1},{2,6},{6,10},{... | collective-permute-start | bytes 786440 | tf_op jit(solution)/shard_map/ppermute | solution.py:46
  8.6 23.2 %collective-permute-start.6 = (bf16[128,1024]{1,0:T(8,128)(2,1)}, bf16[128,1024]{1,0:T(8,128)(2,1)}, u32[]{:S(2)}, u32[]{:S(2)}) collective-permute-start(bf16[128,1024]{1,0:T(8,128)(2,1)} %pad_maximum_fusion.5), channel_id=1, source_target_pairs={{0,4},{4,8},{8,12},{12,0},{1,5},{5,9},{9,13},{13,1},{2,6},{6,10},{... | collective-permute-start | bytes 786440 | tf_op jit(solution)/shard_map/ppermute | solution.py:46
  9.6 32.6 %collective-permute-start.9 = (bf16[128,1024]{1,0:T(8,128)(2,1)}, bf16[128,1024]{1,0:T(8,128)(2,1)S(1)}, u32[]{:S(2)}, u32[]{:S(2)}) collective-permute-start(bf16[128,1024]{1,0:T(8,128)(2,1)} %pad_maximum_fusion.6), channel_id=1, source_target_pairs={{0,4},{4,8},{8,12},{12,0},{1,5},{5,9},{9,13},{13,1},{2,6},{6,10},{... | collective-permute-start | bytes 786440 | tf_op jit(solution)/shard_map/ppermute | solution.py:46
  30.3 12.6 %collective-permute-start.19 = (bf16[128,1024]{1,0:T(8,128)(2,1)}, bf16[128,1024]{1,0:T(8,128)(2,1)S(1)}, u32[]{:S(2)}, u32[]{:S(2)}) collective-permute-start(bf16[128,1024]{1,0:T(8,128)(2,1)} %collective-permute-done.3), channel_id=1, source_target_pairs={{0,16},{16,0},{1,17},{17,1},{2,18},{18,2},{3,19},{19,3},{4,20},{20... | collective-permute-start | bytes 786440 | tf_op jit(solution)/shard_map/ppermute | solution.py:51
  40.6 13.5 %collective-permute-start.4 = (bf16[128,1024]{1,0:T(8,128)(2,1)}, bf16[128,1024]{1,0:T(8,128)(2,1)S(1)}, u32[]{:S(2)}, u32[]{:S(2)}) collective-permute-start(bf16[128,1024]{1,0:T(8,128)(2,1)} %collective-permute-done.3), channel_id=1, source_target_pairs={{0,4},{4,8},{8,12},{12,0},{1,5},{5,9},{9,13},{13,1},{2,6},{6,10},{... | collective-permute-start | bytes 786440 | tf_op jit(solution)/shard_map/ppermute | solution.py:46
  42.2 17.5 %collective-permute-start.7 = (bf16[128,1024]{1,0:T(8,128)(2,1)}, bf16[128,1024]{1,0:T(8,128)(2,1)S(1)}, u32[]{:S(2)}, u32[]{:S(2)}) collective-permute-start(bf16[128,1024]{1,0:T(8,128)(2,1)} %collective-permute-done.6), channel_id=1, source_target_pairs={{0,4},{4,8},{8,12},{12,0},{1,5},{5,9},{9,13},{13,1},{2,6},{6,10},{... | collective-permute-start | bytes 786440 | tf_op jit(solution)/shard_map/ppermute | solution.py:46
  42.9 22.5 %collective-permute-start.10 = (bf16[128,1024]{1,0:T(8,128)(2,1)S(1)}, bf16[128,1024]{1,0:T(8,128)(2,1)S(1)}, u32[]{:S(2)}, u32[]{:S(2)}) collective-permute-start(bf16[128,1024]{1,0:T(8,128)(2,1)S(1)} %collective-permute-done.9), channel_id=1, source_target_pairs={{0,4},{4,8},{8,12},{12,0},{1,5},{5,9},{9,13},{13,1},{2,6},{6,10},{... | collective-permute-start | bytes 786440 | tf_op jit(solution)/shard_map/ppermute | solution.py:46
  45.2 21.8 %collective-permute-start.21 = (bf16[128,1024]{1,0:T(8,128)(2,1)S(1)}, bf16[128,1024]{1,0:T(8,128)(2,1)S(1)}, u32[]{:S(2)}, u32[]{:S(2)}) collective-permute-start(bf16[128,1024]{1,0:T(8,128)(2,1)S(1)} %collective-permute-done.9), channel_id=1, source_target_pairs={{0,16},{16,0},{1,17},{17,1},{2,18},{18,2},{3,19},{19,3},{4,20},{20... | collective-permute-start | bytes 786440 | tf_op jit(solution)/shard_map/ppermute | solution.py:51
  48.5 23.6 %collective-permute-start.2 = (bf16[128,1024]{1,0:T(8,128)(2,1)S(1)}, bf16[128,1024]{1,0:T(8,128)(2,1)S(1)}, u32[]{:S(2)}, u32[]{:S(2)}) collective-permute-start(bf16[128,1024]{1,0:T(8,128)(2,1)S(1)} %collective-permute-done.1), channel_id=1, source_target_pairs={{0,4},{4,8},{8,12},{12,0},{1,5},{5,9},{9,13},{13,1},{2,6},{6,10},{... | collective-permute-start | bytes 786440 | tf_op jit(solution)/shard_map/ppermute | solution.py:46
  54.1 21.7 %collective-permute-start.5 = (bf16[128,1024]{1,0:T(8,128)(2,1)S(1)}, bf16[128,1024]{1,0:T(8,128)(2,1)S(1)}, u32[]{:S(2)}, u32[]{:S(2)}) collective-permute-start(bf16[128,1024]{1,0:T(8,128)(2,1)S(1)} %collective-permute-done.4), channel_id=1, source_target_pairs={{0,4},{4,8},{8,12},{12,0},{1,5},{5,9},{9,13},{13,1},{2,6},{6,10},{... | collective-permute-start | bytes 786440 | tf_op jit(solution)/shard_map/ppermute | solution.py:46
  59.8 18.9 %collective-permute-start.8 = (bf16[128,1024]{1,0:T(8,128)(2,1)S(1)}, bf16[128,1024]{1,0:T(8,128)(2,1)S(1)}, u32[]{:S(2)}, u32[]{:S(2)}) collective-permute-start(bf16[128,1024]{1,0:T(8,128)(2,1)S(1)} %collective-permute-done.7), channel_id=1, source_target_pairs={{0,4},{4,8},{8,12},{12,0},{1,5},{5,9},{9,13},{13,1},{2,6},{6,10},{... | collective-permute-start | bytes 786440 | tf_op jit(solution)/shard_map/ppermute | solution.py:46
  65.4 17.3 %collective-permute-start.11 = (bf16[128,1024]{1,0:T(8,128)(2,1)S(1)}, bf16[128,1024]{1,0:T(8,128)(2,1)S(1)}, u32[]{:S(2)}, u32[]{:S(2)}) collective-permute-start(bf16[128,1024]{1,0:T(8,128)(2,1)S(1)} %collective-permute-done.10), channel_id=1, source_target_pairs={{0,4},{4,8},{8,12},{12,0},{1,5},{5,9},{9,13},{13,1},{2,6},{6,10},{... | collective-permute-start | bytes 786440 | tf_op jit(solution)/shard_map/ppermute | solution.py:46
  71.6 15.4 %collective-permute-start.22 = (bf16[128,1024]{1,0:T(8,128)(2,1)S(1)}, bf16[128,1024]{1,0:T(8,128)(2,1)S(1)}, u32[]{:S(2)}, u32[]{:S(2)}) collective-permute-start(bf16[128,1024]{1,0:T(8,128)(2,1)S(1)} %collective-permute-done.1), channel_id=1, source_target_pairs={{0,16},{16,0},{1,17},{17,1},{2,18},{18,2},{3,19},{19,3},{4,20},{20... | collective-permute-start | bytes 786440 | tf_op jit(solution)/shard_map/ppermute | solution.py:51
  72.1 16.8 %collective-permute-start.23 = (bf16[128,1024]{1,0:T(8,128)(2,1)S(1)}, bf16[128,1024]{1,0:T(8,128)(2,1)S(1)}, u32[]{:S(2)}, u32[]{:S(2)}) collective-permute-start(bf16[128,1024]{1,0:T(8,128)(2,1)S(1)} %collective-permute-done.4), channel_id=1, source_target_pairs={{0,16},{16,0},{1,17},{17,1},{2,18},{18,2},{3,19},{19,3},{4,20},{20... | collective-permute-start | bytes 786440 | tf_op jit(solution)/shard_map/ppermute | solution.py:51
  75.9 16.2 %collective-permute-start.24 = (bf16[128,1024]{1,0:T(8,128)(2,1)S(1)}, bf16[128,1024]{1,0:T(8,128)(2,1)S(1)}, u32[]{:S(2)}, u32[]{:S(2)}) collective-permute-start(bf16[128,1024]{1,0:T(8,128)(2,1)S(1)} %collective-permute-done.7), channel_id=1, source_target_pairs={{0,16},{16,0},{1,17},{17,1},{2,18},{18,2},{3,19},{19,3},{4,20},{20... | collective-permute-start | bytes 786440 | tf_op jit(solution)/shard_map/ppermute | solution.py:51
  78.7 19.0 %collective-permute-start.25 = (bf16[128,1024]{1,0:T(8,128)(2,1)S(1)}, bf16[128,1024]{1,0:T(8,128)(2,1)S(1)}, u32[]{:S(2)}, u32[]{:S(2)}) collective-permute-start(bf16[128,1024]{1,0:T(8,128)(2,1)S(1)} %collective-permute-done.10), channel_id=1, source_target_pairs={{0,16},{16,0},{1,17},{17,1},{2,18},{18,2},{3,19},{19,3},{4,20},{20... | collective-permute-start | bytes 786440 | tf_op jit(solution)/shard_map/ppermute | solution.py:51
  84.2 67.8 %collective-permute-start.15 = (bf16[8,384,128]{2,0,1:T(8,128)(2,1)S(1)}, bf16[8,384,128]{2,0,1:T(8,128)(2,1)S(1)}, u32[]{:S(2)}, u32[]{:S(2)}) collective-permute-start(bf16[8,384,128]{2,0,1:T(8,128)(2,1)S(1)} %pad_maximum_fusion), channel_id=1, source_target_pairs={{0,4},{4,8},{8,12},{12,0},{1,5},{5,9},{9,13},{13,1},{2,6},{6,10},{... | collective-permute-start | bytes 2359304 | tf_op jit(solution)/shard_map/ppermute | solution.py:73
  87.1 63.9 %collective-permute-start.16 = (bf16[8,384,128]{2,0,1:T(8,128)(2,1)S(1)}, bf16[8,384,128]{2,0,1:T(8,128)(2,1)S(1)}, u32[]{:S(2)}, u32[]{:S(2)}) collective-permute-start(bf16[8,384,128]{2,0,1:T(8,128)(2,1)S(1)} %pad_maximum_fusion.1), channel_id=1, source_target_pairs={{0,8},{4,12},{8,0},{12,4},{1,9},{5,13},{9,1},{13,5},{2,10},{6,14},... | collective-permute-start | bytes 2359304 | tf_op jit(solution)/shard_map/ppermute | solution.py:73
  88.9 61.0 %collective-permute-start.17 = (bf16[8,384,128]{2,0,1:T(8,128)(2,1)S(1)}, bf16[8,384,128]{2,0,1:T(8,128)(2,1)S(1)}, u32[]{:S(2)}, u32[]{:S(2)}) collective-permute-start(bf16[8,384,128]{2,0,1:T(8,128)(2,1)S(1)} %pad_maximum_fusion.2), channel_id=1, source_target_pairs={{0,12},{4,0},{8,4},{12,8},{1,13},{5,1},{9,5},{13,9},{2,14},{6,2},{... | collective-permute-start | bytes 2359304 | tf_op jit(solution)/shard_map/ppermute | solution.py:73
  92.1 11.2 %collective-permute-start.26 = (bf16[128,1024]{1,0:T(8,128)(2,1)S(1)}, bf16[128,1024]{1,0:T(8,128)(2,1)S(1)}, u32[]{:S(2)}, u32[]{:S(2)}) collective-permute-start(bf16[128,1024]{1,0:T(8,128)(2,1)S(1)} %collective-permute-done.2), channel_id=1, source_target_pairs={{0,16},{16,0},{1,17},{17,1},{2,18},{18,2},{3,19},{19,3},{4,20},{20... | collective-permute-start | bytes 786440 | tf_op jit(solution)/shard_map/ppermute | solution.py:51
  97.7 11.2 %collective-permute-start.27 = (bf16[128,1024]{1,0:T(8,128)(2,1)S(1)}, bf16[128,1024]{1,0:T(8,128)(2,1)S(1)}, u32[]{:S(2)}, u32[]{:S(2)}) collective-permute-start(bf16[128,1024]{1,0:T(8,128)(2,1)S(1)} %collective-permute-done.5), channel_id=1, source_target_pairs={{0,16},{16,0},{1,17},{17,1},{2,18},{18,2},{3,19},{19,3},{4,20},{20... | collective-permute-start | bytes 786440 | tf_op jit(solution)/shard_map/ppermute | solution.py:51
  165.6 12.4 %all-to-all-start = ((bf16[4,96,512]{2,1,0:T(8,128)(2,1)}), bf16[4,96,512]{2,1,0:T(8,128)(2,1)S(1)}, u32[]{:S(2)}, u32[]{:S(2)}) async-start(bf16[4,96,512]{2,1,0:T(8,128)(2,1)} %bitcast.165), calls=%async_computation | async-start | bytes 786432 | tf_op jit(solution)/shard_map/all_to_all | solution.py:150
  (16 other events, 244.1 us)

commit v14 on v10

--- a/solution.py
+++ b/solution.py
@@ -120,16 +120,17 @@
 
     if len(pieces) > 4:
         pieces, slot_ids = [jnp.concatenate(pieces, 0)], [jnp.concatenate(slot_ids)]
-    base_sum = None
+    weights = jnp.concatenate([rows for rows, _ in parts], 0)
+    base_all = None
+    low_sum = None
     for piece, ids in zip(pieces, slot_ids):
         orders = feature_order[0][ids]
         one_hot = (orders[None, :] == features[:, None]).astype(jnp.bfloat16)
-        term = jnp.einsum("fs,sre->rfe", one_hot, piece, preferred_element_type=jnp.float32)
-        base_sum = term if base_sum is None else base_sum + term
-    base_all = base_sum.astype(jnp.bfloat16).reshape(row_count, position_count * entry_count)
-
-    weights = jnp.concatenate([rows for rows, _ in parts], 0)
-    low_sum = jnp.dot(base_all, weights[:, :rank], preferred_element_type=jnp.float32)
+        term = jnp.einsum("fs,sre->rfe", one_hot, piece, preferred_element_type=jnp.bfloat16)
+        term = term.reshape(row_count, position_count * entry_count)
+        base_all = term if base_all is None else base_all + term
+        partial = jnp.dot(term, weights[:, :rank], preferred_element_type=jnp.float32)
+        low_sum = partial if low_sum is None else low_sum + partial
     low_rank = low_sum.astype(jnp.bfloat16)
     lifted = lax.dot_general(
         low_rank,

time: 179 us -> 183 us (1.022)
  the two profiles are of different devices: /device:TPU:0 before, /device:TPU:8 now
where the time goes in v14:
time: 183 us
  waiting for transfers between devices  76.7 us (42%)
  starting transfers between devices  43.5 us (24%)
  local copies, waits for them, and re-layouts  31.5 us (17%)
  matrix products  25.8 us (14%)
  other arithmetic  4.65 us (3%)
    ppermute x3, waiting for transfers between devices, exchange_rows(): lax.ppermute(piece, 'feat', [(source, (source + shift) % feat_count) for...  36.3 us
    ppermute x12, waiting for transfers between devices, weight_parts(): forwarded = lax.ppermute(rings[chunk], 'groups', pairs)  18.3 us
    ppermute x12, starting transfers between devices, weight_parts(): rings[chunk] = lax.ppermute(rings[chunk], 'feat', ring)  15.7 us
    ppermute x12, waiting for transfers between devices, weight_parts(): rings[chunk] = lax.ppermute(rings[chunk], 'feat', ring)  15.6 us
    ppermute x12, starting transfers between devices, weight_parts(): forwarded = lax.ppermute(rings[chunk], 'groups', pairs)  15.4 us
    dot_general x1, matrix products, on_device(): jnp.dot(crossed, weights[:, 2 * rank:], preferred_element_type=jnp.float32)  13.7 us
    unnamed x47, local copies, waits for them, and re-layouts  12.5 us
    squeeze x1, local copies, waits for them, and re-layouts, on_device(): pooled_second[0]  12 us
  transfers between devices with their start and end apart: 31, of which 15 were waited for; matrix products, arithmetic and copies ran while one was open for 21% of the time, Pallas kernels for 0%

profile of v14, /device:TPU:8, one launch (start us, length us, event | category | flops | bytes accessed | tf_op | source)
XLA Modules:
  0.0 182.7 jit_solution(10600454161040130196)
XLA Ops:
  0.0 3.2 %pad_maximum_fusion = (bf16[1024,1024]{1,0:T(8,128)(2,1)S(1)}, bf16[4096,1024]{1,0:T(8,128)(2,1)}) fusion(bf16[1024,512]{1,0:T(8,128)(2,1)} %bitcast.192, bf16[1024,256]{1,0:T(8,128)(2,1)} %bitcast.193, bf16[1024,256]{1,0:T(8,128)(2,1)} %bitcast.194), kind=kLoop, calls=%fused_computation.26 | loop fusion | flops 6291455 | bytes 6291456 | tf_op jit(solution)/shard_map/concatenate | solution.py:108
  7.3 1.8 collective-permute-start.9
  9.4 12.0 %copy_bitcast_fusion = (bf16[4,1536,128]{2,0,1:T(4,128)(2,1)S(1)}, bf16[4,1536,128]{2,0,1:T(4,128)(2,1)S(1)}) fusion(bf16[1,4,1536,128]{3,2,1,0:T(8,128)(2,1)} %param.14, bf16[1,4,1536,128]{3,2,1,0:T(8,128)(2,1)} %param.13), kind=kLoop, calls=%fused_computation.27 | loop fusion | bytes 6291456 | tf_op jit(solution)/shard_map/squeeze | solution.py:112
  28.6 1.7 constant_dynamic-update-slice_fusion.23
  36.3 2.0 %collective-permute-start.10 = (bf16[128,1024]{1,0:T(8,128)(2,1)}, bf16[128,1024]{1,0:T(8,128)(2,1)S(1)}, u32[]{:S(2)}, u32[]{:S(2)}) collective-permute-start(bf16[128,1024]{1,0:T(8,128)(2,1)} %collective-permute-done.9), channel_id=1, source_target_pairs={{0,4},{4,8},{8,12},{12,0},{1,5},{5,9},{9,13},{13,1},{2,6},{6,10},{... | collective-permute-start | bytes 786440 | tf_op jit(solution)/shard_map/ppermute | solution.py:41
  43.2 1.7 constant_dynamic-update-slice_fusion.19
  49.3 4.0 %collective-permute-done.10 = bf16[128,1024]{1,0:T(8,128)(2,1)S(1)} collective-permute-done((bf16[128,1024]{1,0:T(8,128)(2,1)}, bf16[128,1024]{1,0:T(8,128)(2,1)S(1)}, u32[]{:S(2)}, u32[]{:S(2)}) %collective-permute-start.10) | collective-permute-done | bytes 262176 | tf_op jit(solution)/shard_map/ppermute | solution.py:41
  55.6 1.7 constant_dynamic-update-slice_fusion.17
  60.8 3.8 %collective-permute-done.5 = bf16[128,1024]{1,0:T(8,128)(2,1)S(1)} collective-permute-done((bf16[128,1024]{1,0:T(8,128)(2,1)S(1)}, bf16[128,1024]{1,0:T(8,128)(2,1)S(1)}, u32[]{:S(2)}, u32[]{:S(2)}) %collective-permute-start.5) | collective-permute-done | bytes 262176 | tf_op jit(solution)/shard_map/ppermute | solution.py:41
  66.1 4.1 %collective-permute-done.8 = bf16[128,1024]{1,0:T(8,128)(2,1)S(1)} collective-permute-done((bf16[128,1024]{1,0:T(8,128)(2,1)S(1)}, bf16[128,1024]{1,0:T(8,128)(2,1)S(1)}, u32[]{:S(2)}, u32[]{:S(2)}) %collective-permute-start.8) | collective-permute-done | bytes 262176 | tf_op jit(solution)/shard_map/ppermute | solution.py:41
  71.7 2.5 %collective-permute-done.11 = bf16[128,1024]{1,0:T(8,128)(2,1)S(1)} collective-permute-done((bf16[128,1024]{1,0:T(8,128)(2,1)S(1)}, bf16[128,1024]{1,0:T(8,128)(2,1)S(1)}, u32[]{:S(2)}, u32[]{:S(2)}) %collective-permute-start.11) | collective-permute-done | bytes 262176 | tf_op jit(solution)/shard_map/ppermute | solution.py:41
  78.8 3.2 %collective-permute-start.13 = (bf16[8,384,128]{2,0,1:T(8,128)(2,1)S(1)}, bf16[8,384,128]{2,0,1:T(8,128)(2,1)S(1)}, u32[]{:S(2)}, u32[]{:S(2)}) collective-permute-start(bf16[8,384,128]{2,0,1:T(8,128)(2,1)S(1)} %pad_maximum_fusion.2), channel_id=1, source_target_pairs={{0,8},{4,12},{8,0},{12,4},{1,9},{5,13},{9,1},{13,5},{2,10},{6,14},... | collective-permute-start | bytes 2359304 | tf_op jit(solution)/shard_map/ppermute | solution.py:68
  85.0 7.0 %collective-permute-done.23 = bf16[128,1024]{1,0:T(8,128)(2,1)S(1)} collective-permute-done((bf16[128,1024]{1,0:T(8,128)(2,1)S(1)}, bf16[128,1024]{1,0:T(8,128)(2,1)S(1)}, u32[]{:S(2)}, u32[]{:S(2)}) %collective-permute-start.23) | collective-permute-done | bytes 262176 | tf_op jit(solution)/shard_map/ppermute | solution.py:46
  93.7 4.1 %collective-permute-done.24 = bf16[128,1024]{1,0:T(8,128)(2,1)S(1)} collective-permute-done((bf16[128,1024]{1,0:T(8,128)(2,1)S(1)}, bf16[128,1024]{1,0:T(8,128)(2,1)S(1)}, u32[]{:S(2)}, u32[]{:S(2)}) %collective-permute-start.24) | collective-permute-done | bytes 262176 | tf_op jit(solution)/shard_map/ppermute | solution.py:46
  99.3 4.0 %collective-permute-done.25 = bf16[128,1024]{1,0:T(8,128)(2,1)S(1)} collective-permute-done((bf16[128,1024]{1,0:T(8,128)(2,1)S(1)}, bf16[128,1024]{1,0:T(8,128)(2,1)S(1)}, u32[]{:S(2)}, u32[]{:S(2)}) %collective-permute-start.25) | collective-permute-done | bytes 262176 | tf_op jit(solution)/shard_map/ppermute | solution.py:46
  103.3 2.8 %collective-permute-done.26 = bf16[128,1024]{1,0:T(8,128)(2,1)S(1)} collective-permute-done((bf16[128,1024]{1,0:T(8,128)(2,1)S(1)}, bf16[128,1024]{1,0:T(8,128)(2,1)S(1)}, u32[]{:S(2)}, u32[]{:S(2)}) %collective-permute-start.26) | collective-permute-done | bytes 262176 | tf_op jit(solution)/shard_map/ppermute | solution.py:46
  106.1 22.9 %collective-permute-done.12 = bf16[8,384,128]{2,0,1:T(8,128)(2,1)S(1)} collective-permute-done((bf16[8,384,128]{2,0,1:T(8,128)(2,1)S(1)}, bf16[8,384,128]{2,0,1:T(8,128)(2,1)S(1)}, u32[]{:S(2)}, u32[]{:S(2)}) %collective-permute-start.12) | collective-permute-done | bytes 786464 | tf_op jit(solution)/shard_map/ppermute | solution.py:68
  131.4 11.9 %collective-permute-done.13 = bf16[8,384,128]{2,0,1:T(8,128)(2,1)S(1)} collective-permute-done((bf16[8,384,128]{2,0,1:T(8,128)(2,1)S(1)}, bf16[8,384,128]{2,0,1:T(8,128)(2,1)S(1)}, u32[]{:S(2)}, u32[]{:S(2)}) %collective-permute-start.13) | collective-permute-done | bytes 786464 | tf_op jit(solution)/shard_map/ppermute | solution.py:68
  149.5 1.9 %fusion.50 = bf16[384,256]{1,0:T(8,128)(2,1)} fusion(f32[384,256]{1,0:T(8,128)S(1)} %fusion.3, f32[384,256]{1,0:T(8,128)S(1)} %fusion.5, f32[384,256]{1,0:T(8,128)S(1)} %fusion.7, bf16[4096,1024]{1,0:T(8,128)(2,1)S(1)} %constant_dynamic-update-slice_fusion, bf16[48,8,32,128]{3,2,1,0:T(8,128)(2,1)S(1)} %bitcast.182), kind=kOutput, calls=%fused_computation.44 | convolution fusion | flops 805699584 | bytes 6619136 | tf_op jit(solution)/shard_map/dot_general | solution.py:132
  151.5 13.7 %fusion.27 = bf16[384,512]{1,0:T(8,128)(2,1)} fusion(bf16[4096,1024]{1,0:T(8,128)(2,1)} %copy-done.6, bf16[384,256]{1,0:T(8,128)(2,1)} %fusion.50, f32[4096]{0:T(1024)S(1)} %bitcast.196, bf16[48,8,32,128]{3,2,1,0:T(8,128)(2,1)} %bitcast.189, bf16[48,8,32,128]{3,2,1,0:T(8,128)(2,1)} %bitcast.187, bf16[48,8,32,128]{3,2,1,0:T(8,128)(2,1)} %bitcast.185, ...), kind=kOutput, calls=%fused_computation.35 | convolution fusion | flops 2428895232 | bytes 19482624 | tf_op jit(solution)/shard_map/dot_general | solution.py:144
  165.1 3.6 %all-to-all-start = ((bf16[4,96,512]{2,1,0:T(8,128)(2,1)}), bf16[4,96,512]{2,1,0:T(8,128)(2,1)S(1)}, u32[]{:S(2)}, u32[]{:S(2)}) async-start(bf16[4,96,512]{2,1,0:T(8,128)(2,1)} %bitcast.79), calls=%async_computation | async-start | bytes 786432 | tf_op jit(solution)/shard_map/all_to_all | solution.py:146
  170.5 1.9 %collective-permute-start.28 = (bf16[62,1024]{1,0:T(8,128)(2,1)S(1)}, bf16[62,1024]{1,0:T(8,128)(2,1)S(1)}, u32[]{:S(2)}, u32[]{:S(2)}) collective-permute-start(bf16[62,1024]{1,0:T(8,128)(2,1)S(1)} %copy-done.8), channel_id=1, source_target_pairs={{0,2},{1,3},{2,0},{3,1},{4,6},{5,7},{6,4},{7,5},{8,10},{9,11},{10,... | collective-permute-start | bytes 380936 | tf_op jit(solution)/shard_map/ppermute | solution.py:106
  172.5 4.1 %all-to-all-done = bf16[4,96,512]{2,1,0:T(8,128)(2,1)S(1)} async-done(((bf16[4,96,512]{2,1,0:T(8,128)(2,1)}), bf16[4,96,512]{2,1,0:T(8,128)(2,1)S(1)}, u32[]{:S(2)}, u32[]{:S(2)}) %all-to-all-start) | async-done | bytes 393248 | tf_op jit(solution)/shard_map/all_to_all | solution.py:146
  179.4 2.3 %collective-permute-done.28 = bf16[62,1024]{1,0:T(8,128)(2,1)S(1)} collective-permute-done((bf16[62,1024]{1,0:T(8,128)(2,1)S(1)}, bf16[62,1024]{1,0:T(8,128)(2,1)S(1)}, u32[]{:S(2)}, u32[]{:S(2)}) %collective-permute-start.28) | collective-permute-done | bytes 127008 | tf_op jit(solution)/shard_map/ppermute | solution.py:106
  (138 shorter events, 60.5 us)
Async XLA Ops:
  4.1 17.4 %collective-permute-start = (bf16[128,1024]{1,0:T(8,128)(2,1)}, bf16[128,1024]{1,0:T(8,128)(2,1)}, u32[]{:S(2)}, u32[]{:S(2)}) collective-permute-start(bf16[128,1024]{1,0:T(8,128)(2,1)} %get-tuple-element.11), channel_id=1, source_target_pairs={{0,4},{4,8},{8,12},{12,0},{1,5},{5,9},{9,13},{13,1},{2,6},{6,10},{... | collective-permute-start | bytes 786440 | tf_op jit(solution)/shard_map/ppermute | solution.py:41
  5.7 17.4 %collective-permute-start.3 = (bf16[128,1024]{1,0:T(8,128)(2,1)}, bf16[128,1024]{1,0:T(8,128)(2,1)}, u32[]{:S(2)}, u32[]{:S(2)}) collective-permute-start(bf16[128,1024]{1,0:T(8,128)(2,1)} %get-tuple-element.10), channel_id=1, source_target_pairs={{0,4},{4,8},{8,12},{12,0},{1,5},{5,9},{9,13},{13,1},{2,6},{6,10},{... | collective-permute-start | bytes 786440 | tf_op jit(solution)/shard_map/ppermute | solution.py:41
  7.3 23.1 %collective-permute-start.6 = (bf16[128,1024]{1,0:T(8,128)(2,1)}, bf16[128,1024]{1,0:T(8,128)(2,1)}, u32[]{:S(2)}, u32[]{:S(2)}) collective-permute-start(bf16[128,1024]{1,0:T(8,128)(2,1)} %get-tuple-element.12), channel_id=1, source_target_pairs={{0,4},{4,8},{8,12},{12,0},{1,5},{5,9},{9,13},{13,1},{2,6},{6,10},{... | collective-permute-start | bytes 786440 | tf_op jit(solution)/shard_map/ppermute | solution.py:41
  7.3 27.8 %collective-permute-start.9 = (bf16[128,1024]{1,0:T(8,128)(2,1)S(1)}, bf16[128,1024]{1,0:T(8,128)(2,1)}, u32[]{:S(2)}, u32[]{:S(2)}) collective-permute-start(bf16[128,1024]{1,0:T(8,128)(2,1)S(1)} %get-tuple-element.9), channel_id=1, source_target_pairs={{0,4},{4,8},{8,12},{12,0},{1,5},{5,9},{9,13},{13,1},{2,6},{6,10},{... | collective-permute-start | bytes 786440 | tf_op jit(solution)/shard_map/ppermute | solution.py:41
  23.1 13.3 %collective-permute-start.16 = (bf16[128,1024]{1,0:T(8,128)(2,1)}, bf16[128,1024]{1,0:T(8,128)(2,1)}, u32[]{:S(2)}, u32[]{:S(2)}) collective-permute-start(bf16[128,1024]{1,0:T(8,128)(2,1)} %collective-permute-done.3), channel_id=1, source_target_pairs={{0,16},{16,0},{1,17},{17,1},{2,18},{18,2},{3,19},{19,3},{4,20},{20... | collective-permute-start | bytes 786440 | tf_op jit(solution)/shard_map/ppermute | solution.py:46
  27.0 17.9 %collective-permute-start.1 = (bf16[128,1024]{1,0:T(8,128)(2,1)}, bf16[128,1024]{1,0:T(8,128)(2,1)S(1)}, u32[]{:S(2)}, u32[]{:S(2)}) collective-permute-start(bf16[128,1024]{1,0:T(8,128)(2,1)} %collective-permute-done), channel_id=1, source_target_pairs={{0,4},{4,8},{8,12},{12,0},{1,5},{5,9},{9,13},{13,1},{2,6},{6,10},{... | collective-permute-start | bytes 786440 | tf_op jit(solution)/shard_map/ppermute | solution.py:41
  30.3 16.1 %collective-permute-start.4 = (bf16[128,1024]{1,0:T(8,128)(2,1)}, bf16[128,1024]{1,0:T(8,128)(2,1)S(1)}, u32[]{:S(2)}, u32[]{:S(2)}) collective-permute-start(bf16[128,1024]{1,0:T(8,128)(2,1)} %collective-permute-done.3), channel_id=1, source_target_pairs={{0,4},{4,8},{8,12},{12,0},{1,5},{5,9},{9,13},{13,1},{2,6},{6,10},{... | collective-permute-start | bytes 786440 | tf_op jit(solution)/shard_map/ppermute | solution.py:41
  35.1 12.6 %collective-permute-start.7 = (bf16[128,1024]{1,0:T(8,128)(2,1)}, bf16[128,1024]{1,0:T(8,128)(2,1)S(1)}, u32[]{:S(2)}, u32[]{:S(2)}) collective-permute-start(bf16[128,1024]{1,0:T(8,128)(2,1)} %collective-permute-done.6), channel_id=1, source_target_pairs={{0,4},{4,8},{8,12},{12,0},{1,5},{5,9},{9,13},{13,1},{2,6},{6,10},{... | collective-permute-start | bytes 786440 | tf_op jit(solution)/shard_map/ppermute | solution.py:41
  36.3 17.0 %collective-permute-start.10 = (bf16[128,1024]{1,0:T(8,128)(2,1)}, bf16[128,1024]{1,0:T(8,128)(2,1)S(1)}, u32[]{:S(2)}, u32[]{:S(2)}) collective-permute-start(bf16[128,1024]{1,0:T(8,128)(2,1)} %collective-permute-done.9), channel_id=1, source_target_pairs={{0,4},{4,8},{8,12},{12,0},{1,5},{5,9},{9,13},{13,1},{2,6},{6,10},{... | collective-permute-start | bytes 786440 | tf_op jit(solution)/shard_map/ppermute | solution.py:41
  41.6 15.7 %collective-permute-start.18 = (bf16[128,1024]{1,0:T(8,128)(2,1)}, bf16[128,1024]{1,0:T(8,128)(2,1)S(1)}, u32[]{:S(2)}, u32[]{:S(2)}) collective-permute-start(bf16[128,1024]{1,0:T(8,128)(2,1)} %collective-permute-done.9), channel_id=1, source_target_pairs={{0,16},{16,0},{1,17},{17,1},{2,18},{18,2},{3,19},{19,3},{4,20},{20... | collective-permute-start | bytes 786440 | tf_op jit(solution)/shard_map/ppermute | solution.py:46
  44.8 15.4 %collective-permute-start.2 = (bf16[128,1024]{1,0:T(8,128)(2,1)S(1)}, bf16[128,1024]{1,0:T(8,128)(2,1)S(1)}, u32[]{:S(2)}, u32[]{:S(2)}) collective-permute-start(bf16[128,1024]{1,0:T(8,128)(2,1)S(1)} %collective-permute-done.1), channel_id=1, source_target_pairs={{0,4},{4,8},{8,12},{12,0},{1,5},{5,9},{9,13},{13,1},{2,6},{6,10},{... | collective-permute-start | bytes 786440 | tf_op jit(solution)/shard_map/ppermute | solution.py:41
  46.4 18.1 %collective-permute-start.5 = (bf16[128,1024]{1,0:T(8,128)(2,1)S(1)}, bf16[128,1024]{1,0:T(8,128)(2,1)S(1)}, u32[]{:S(2)}, u32[]{:S(2)}) collective-permute-start(bf16[128,1024]{1,0:T(8,128)(2,1)S(1)} %collective-permute-done.4), channel_id=1, source_target_pairs={{0,4},{4,8},{8,12},{12,0},{1,5},{5,9},{9,13},{13,1},{2,6},{6,10},{... | collective-permute-start | bytes 786440 | tf_op jit(solution)/shard_map/ppermute | solution.py:41
  47.7 22.5 %collective-permute-start.8 = (bf16[128,1024]{1,0:T(8,128)(2,1)S(1)}, bf16[128,1024]{1,0:T(8,128)(2,1)S(1)}, u32[]{:S(2)}, u32[]{:S(2)}) collective-permute-start(bf16[128,1024]{1,0:T(8,128)(2,1)S(1)} %collective-permute-done.7), channel_id=1, source_target_pairs={{0,4},{4,8},{8,12},{12,0},{1,5},{5,9},{9,13},{13,1},{2,6},{6,10},{... | collective-permute-start | bytes 786440 | tf_op jit(solution)/shard_map/ppermute | solution.py:41
  53.3 20.8 %collective-permute-start.11 = (bf16[128,1024]{1,0:T(8,128)(2,1)S(1)}, bf16[128,1024]{1,0:T(8,128)(2,1)S(1)}, u32[]{:S(2)}, u32[]{:S(2)}) collective-permute-start(bf16[128,1024]{1,0:T(8,128)(2,1)S(1)} %collective-permute-done.10), channel_id=1, source_target_pairs={{0,4},{4,8},{8,12},{12,0},{1,5},{5,9},{9,13},{13,1},{2,6},{6,10},{... | collective-permute-start | bytes 786440 | tf_op jit(solution)/shard_map/ppermute | solution.py:41
  57.3 21.5 %collective-permute-start.19 = (bf16[128,1024]{1,0:T(8,128)(2,1)S(1)}, bf16[128,1024]{1,0:T(8,128)(2,1)S(1)}, u32[]{:S(2)}, u32[]{:S(2)}) collective-permute-start(bf16[128,1024]{1,0:T(8,128)(2,1)S(1)} %collective-permute-done.1), channel_id=1, source_target_pairs={{0,16},{16,0},{1,17},{17,1},{2,18},{18,2},{3,19},{19,3},{4,20},{20... | collective-permute-start | bytes 786440 | tf_op jit(solution)/shard_map/ppermute | solution.py:46
  60.3 22.2 %collective-permute-start.20 = (bf16[128,1024]{1,0:T(8,128)(2,1)S(1)}, bf16[128,1024]{1,0:T(8,128)(2,1)S(1)}, u32[]{:S(2)}, u32[]{:S(2)}) collective-permute-start(bf16[128,1024]{1,0:T(8,128)(2,1)S(1)} %collective-permute-done.4), channel_id=1, source_target_pairs={{0,16},{16,0},{1,17},{17,1},{2,18},{18,2},{3,19},{19,3},{4,20},{20... | collective-permute-start | bytes 786440 | tf_op jit(solution)/shard_map/ppermute | solution.py:46
  64.5 18.2 %collective-permute-start.21 = (bf16[128,1024]{1,0:T(8,128)(2,1)S(1)}, bf16[128,1024]{1,0:T(8,128)(2,1)S(1)}, u32[]{:S(2)}, u32[]{:S(2)}) collective-permute-start(bf16[128,1024]{1,0:T(8,128)(2,1)S(1)} %collective-permute-done.7), channel_id=1, source_target_pairs={{0,16},{16,0},{1,17},{17,1},{2,18},{18,2},{3,19},{19,3},{4,20},{20... | collective-permute-start | bytes 786440 | tf_op jit(solution)/shard_map/ppermute | solution.py:46
  70.2 14.2 %collective-permute-start.22 = (bf16[128,1024]{1,0:T(8,128)(2,1)S(1)}, bf16[128,1024]{1,0:T(8,128)(2,1)S(1)}, u32[]{:S(2)}, u32[]{:S(2)}) collective-permute-start(bf16[128,1024]{1,0:T(8,128)(2,1)S(1)} %collective-permute-done.10), channel_id=1, source_target_pairs={{0,16},{16,0},{1,17},{17,1},{2,18},{18,2},{3,19},{19,3},{4,20},{20... | collective-permute-start | bytes 786440 | tf_op jit(solution)/shard_map/ppermute | solution.py:46
  75.7 53.3 %collective-permute-start.12 = (bf16[8,384,128]{2,0,1:T(8,128)(2,1)S(1)}, bf16[8,384,128]{2,0,1:T(8,128)(2,1)S(1)}, u32[]{:S(2)}, u32[]{:S(2)}) collective-permute-start(bf16[8,384,128]{2,0,1:T(8,128)(2,1)S(1)} %pad_maximum_fusion.1), channel_id=1, source_target_pairs={{0,4},{4,8},{8,12},{12,0},{1,5},{5,9},{9,13},{13,1},{2,6},{6,10},{... | collective-permute-start | bytes 2359304 | tf_op jit(solution)/shard_map/ppermute | solution.py:68
  78.8 64.5 %collective-permute-start.13 = (bf16[8,384,128]{2,0,1:T(8,128)(2,1)S(1)}, bf16[8,384,128]{2,0,1:T(8,128)(2,1)S(1)}, u32[]{:S(2)}, u32[]{:S(2)}) collective-permute-start(bf16[8,384,128]{2,0,1:T(8,128)(2,1)S(1)} %pad_maximum_fusion.2), channel_id=1, source_target_pairs={{0,8},{4,12},{8,0},{12,4},{1,9},{5,13},{9,1},{13,5},{2,10},{6,14},... | collective-permute-start | bytes 2359304 | tf_op jit(solution)/shard_map/ppermute | solution.py:68
  82.5 64.7 %collective-permute-start.14 = (bf16[8,384,128]{2,0,1:T(8,128)(2,1)S(1)}, bf16[8,384,128]{2,0,1:T(8,128)(2,1)S(1)}, u32[]{:S(2)}, u32[]{:S(2)}) collective-permute-start(bf16[8,384,128]{2,0,1:T(8,128)(2,1)S(1)} %pad_maximum_fusion.3), channel_id=1, source_target_pairs={{0,12},{4,0},{8,4},{12,8},{1,13},{5,1},{9,5},{13,9},{2,14},{6,2},{... | collective-permute-start | bytes 2359304 | tf_op jit(solution)/shard_map/ppermute | solution.py:68
  84.4 13.3 %collective-permute-start.24 = (bf16[128,1024]{1,0:T(8,128)(2,1)S(1)}, bf16[128,1024]{1,0:T(8,128)(2,1)S(1)}, u32[]{:S(2)}, u32[]{:S(2)}) collective-permute-start(bf16[128,1024]{1,0:T(8,128)(2,1)S(1)} %collective-permute-done.5), channel_id=1, source_target_pairs={{0,16},{16,0},{1,17},{17,1},{2,18},{18,2},{3,19},{19,3},{4,20},{20... | collective-permute-start | bytes 786440 | tf_op jit(solution)/shard_map/ppermute | solution.py:46
  165.1 11.5 %all-to-all-start = ((bf16[4,96,512]{2,1,0:T(8,128)(2,1)}), bf16[4,96,512]{2,1,0:T(8,128)(2,1)S(1)}, u32[]{:S(2)}, u32[]{:S(2)}) async-start(bf16[4,96,512]{2,1,0:T(8,128)(2,1)} %bitcast.79), calls=%async_computation | async-start | bytes 786432 | tf_op jit(solution)/shard_map/all_to_all | solution.py:146
  170.5 11.2 %collective-permute-start.28 = (bf16[62,1024]{1,0:T(8,128)(2,1)S(1)}, bf16[62,1024]{1,0:T(8,128)(2,1)S(1)}, u32[]{:S(2)}, u32[]{:S(2)}) collective-permute-start(bf16[62,1024]{1,0:T(8,128)(2,1)S(1)} %copy-done.8), channel_id=1, source_target_pairs={{0,2},{1,3},{2,0},{3,1},{4,6},{5,7},{6,4},{7,5},{8,10},{9,11},{10,... | collective-permute-start | bytes 380936 | tf_op jit(solution)/shard_map/ppermute | solution.py:106
  (19 other events, 278.6 us)

commit v15 on v14

--- a/solution.py
+++ b/solution.py
@@ -131,6 +131,7 @@
         base_all = term if base_all is None else base_all + term
         partial = jnp.dot(term, weights[:, :rank], preferred_element_type=jnp.float32)
         low_sum = partial if low_sum is None else low_sum + partial
+    base_all, low_sum = lax.optimization_barrier((base_all, low_sum))
     low_rank = low_sum.astype(jnp.bfloat16)
     lifted = lax.dot_general(
         low_rank,

time: 183 us -> 180 us (0.984)
  matrix products: 25.8 us -> 18.4 us
  other arithmetic: 4.65 us -> 8.37 us
    dot_general x1, matrix products: 13.7 us -> 6.41 us  [on_device(): jnp.dot(crossed, weights[:, 2 * rank:], preferred_element_type=jnp.float32)]
    add x0 -> x1, other arithmetic: none -> 3.72 us  [on_device(): base_all = term if base_all is None else base_all + term]
    unnamed x47 -> x41, local copies, waits for them, and re-layouts: 12.5 us -> 12.5 us
  transfers between devices with their start and end apart: 31 -> 31, of which waited for: 15 -> 15; matrix products, arithmetic and copies ran while one was open for 21% -> 22% of each run, Pallas kernels for 0% -> 0%
where the time goes in v15:
time: 180 us; the launch traced here: 179 us
  waiting for transfers between devices  77 us (43%)
  starting transfers between devices  43.5 us (24%)
  local copies, waits for them, and re-layouts  31.5 us (18%)
  matrix products  18.4 us (10%)
  other arithmetic  8.37 us (5%)
    ppermute x3, waiting for transfers between devices, exchange_rows(): lax.ppermute(piece, 'feat', [(source, (source + shift) % feat_count) for...  36.6 us
    ppermute x12, waiting for transfers between devices, weight_parts(): forwarded = lax.ppermute(rings[chunk], 'groups', pairs)  18.3 us
    ppermute x12, starting transfers between devices, weight_parts(): rings[chunk] = lax.ppermute(rings[chunk], 'feat', ring)  15.7 us
    ppermute x12, waiting for transfers between devices, weight_parts(): rings[chunk] = lax.ppermute(rings[chunk], 'feat', ring)  15.6 us
    ppermute x12, starting transfers between devices, weight_parts(): forwarded = lax.ppermute(rings[chunk], 'groups', pairs)  15.5 us
    unnamed x41, local copies, waits for them, and re-layouts  12.5 us
    squeeze x1, local copies, waits for them, and re-layouts, on_device(): pooled_second[0]  12 us
    dot_general x1, matrix products, on_device(): jnp.dot(crossed, weights[:, 2 * rank:], preferred_element_type=jnp.float32)  6.41 us
  transfers between devices with their start and end apart: 31, of which 15 were waited for; matrix products, arithmetic and copies ran while one was open for 22% of the time, Pallas kernels for 0%

profile of v15, /device:TPU:8, one launch (start us, length us, event | category | flops | bytes accessed | tf_op | source)
XLA Modules:
  0.0 179.3 jit_solution(12965417882208986839)
XLA Ops:
  0.0 3.2 %pad_maximum_fusion = (bf16[1024,1024]{1,0:T(8,128)(2,1)S(1)}, bf16[4096,1024]{1,0:T(8,128)(2,1)}) fusion(bf16[1024,512]{1,0:T(8,128)(2,1)} %bitcast.164, bf16[1024,256]{1,0:T(8,128)(2,1)} %bitcast.165, bf16[1024,256]{1,0:T(8,128)(2,1)} %bitcast.166), kind=kLoop, calls=%fused_computation.26 | loop fusion | flops 6291455 | bytes 6291456 | tf_op jit(solution)/shard_map/concatenate | solution.py:108
  7.3 1.8 collective-permute-start.9
  9.4 12.0 %copy_bitcast_fusion = (bf16[4,1536,128]{2,0,1:T(4,128)(2,1)S(1)}, bf16[4,1536,128]{2,0,1:T(4,128)(2,1)S(1)}) fusion(bf16[1,4,1536,128]{3,2,1,0:T(8,128)(2,1)} %param.14, bf16[1,4,1536,128]{3,2,1,0:T(8,128)(2,1)} %param.13), kind=kLoop, calls=%fused_computation.27 | loop fusion | bytes 6291456 | tf_op jit(solution)/shard_map/squeeze | solution.py:112
  28.6 1.7 constant_dynamic-update-slice_fusion.23
  36.4 2.0 %collective-permute-start.10 = (bf16[128,1024]{1,0:T(8,128)(2,1)}, bf16[128,1024]{1,0:T(8,128)(2,1)S(1)}, u32[]{:S(2)}, u32[]{:S(2)}) collective-permute-start(bf16[128,1024]{1,0:T(8,128)(2,1)} %collective-permute-done.9), channel_id=1, source_target_pairs={{0,4},{4,8},{8,12},{12,0},{1,5},{5,9},{9,13},{13,1},{2,6},{6,10},{... | collective-permute-start | bytes 786440 | tf_op jit(solution)/shard_map/ppermute | solution.py:41
  49.3 4.0 %collective-permute-done.10 = bf16[128,1024]{1,0:T(8,128)(2,1)S(1)} collective-permute-done((bf16[128,1024]{1,0:T(8,128)(2,1)}, bf16[128,1024]{1,0:T(8,128)(2,1)S(1)}, u32[]{:S(2)}, u32[]{:S(2)}) %collective-permute-start.10) | collective-permute-done | bytes 262176 | tf_op jit(solution)/shard_map/ppermute | solution.py:41
  60.8 3.8 %collective-permute-done.5 = bf16[128,1024]{1,0:T(8,128)(2,1)S(1)} collective-permute-done((bf16[128,1024]{1,0:T(8,128)(2,1)S(1)}, bf16[128,1024]{1,0:T(8,128)(2,1)S(1)}, u32[]{:S(2)}, u32[]{:S(2)}) %collective-permute-start.5) | collective-permute-done | bytes 262176 | tf_op jit(solution)/shard_map/ppermute | solution.py:41
  66.1 4.1 %collective-permute-done.8 = bf16[128,1024]{1,0:T(8,128)(2,1)S(1)} collective-permute-done((bf16[128,1024]{1,0:T(8,128)(2,1)S(1)}, bf16[128,1024]{1,0:T(8,128)(2,1)S(1)}, u32[]{:S(2)}, u32[]{:S(2)}) %collective-permute-start.8) | collective-permute-done | bytes 262176 | tf_op jit(solution)/shard_map/ppermute | solution.py:41
  71.7 2.5 %collective-permute-done.11 = bf16[128,1024]{1,0:T(8,128)(2,1)S(1)} collective-permute-done((bf16[128,1024]{1,0:T(8,128)(2,1)S(1)}, bf16[128,1024]{1,0:T(8,128)(2,1)S(1)}, u32[]{:S(2)}, u32[]{:S(2)}) %collective-permute-start.11) | collective-permute-done | bytes 262176 | tf_op jit(solution)/shard_map/ppermute | solution.py:41
  75.7 1.8 %collective-permute-start.12 = (bf16[8,384,128]{2,0,1:T(8,128)(2,1)S(1)}, bf16[8,384,128]{2,0,1:T(8,128)(2,1)S(1)}, u32[]{:S(2)}, u32[]{:S(2)}) collective-permute-start(bf16[8,384,128]{2,0,1:T(8,128)(2,1)S(1)} %pad_maximum_fusion.1), channel_id=1, source_target_pairs={{0,4},{4,8},{8,12},{12,0},{1,5},{5,9},{9,13},{13,1},{2,6},{6,10},{... | collective-permute-start | bytes 2359304 | tf_op jit(solution)/shard_map/ppermute | solution.py:68
  79.0 3.2 %collective-permute-start.13 = (bf16[8,384,128]{2,0,1:T(8,128)(2,1)S(1)}, bf16[8,384,128]{2,0,1:T(8,128)(2,1)S(1)}, u32[]{:S(2)}, u32[]{:S(2)}) collective-permute-start(bf16[8,384,128]{2,0,1:T(8,128)(2,1)S(1)} %pad_maximum_fusion.2), channel_id=1, source_target_pairs={{0,8},{4,12},{8,0},{12,4},{1,9},{5,13},{9,1},{13,5},{2,10},{6,14},... | collective-permute-start | bytes 2359304 | tf_op jit(solution)/shard_map/ppermute | solution.py:68
  85.1 7.0 %collective-permute-done.23 = bf16[128,1024]{1,0:T(8,128)(2,1)S(1)} collective-permute-done((bf16[128,1024]{1,0:T(8,128)(2,1)S(1)}, bf16[128,1024]{1,0:T(8,128)(2,1)S(1)}, u32[]{:S(2)}, u32[]{:S(2)}) %collective-permute-start.23) | collective-permute-done | bytes 262176 | tf_op jit(solution)/shard_map/ppermute | solution.py:46
  93.7 4.0 %collective-permute-done.24 = bf16[128,1024]{1,0:T(8,128)(2,1)S(1)} collective-permute-done((bf16[128,1024]{1,0:T(8,128)(2,1)S(1)}, bf16[128,1024]{1,0:T(8,128)(2,1)S(1)}, u32[]{:S(2)}, u32[]{:S(2)}) %collective-permute-start.24) | collective-permute-done | bytes 262176 | tf_op jit(solution)/shard_map/ppermute | solution.py:46
  99.3 4.0 %collective-permute-done.25 = bf16[128,1024]{1,0:T(8,128)(2,1)S(1)} collective-permute-done((bf16[128,1024]{1,0:T(8,128)(2,1)S(1)}, bf16[128,1024]{1,0:T(8,128)(2,1)S(1)}, u32[]{:S(2)}, u32[]{:S(2)}) %collective-permute-start.25) | collective-permute-done | bytes 262176 | tf_op jit(solution)/shard_map/ppermute | solution.py:46
  103.3 2.8 %collective-permute-done.26 = bf16[128,1024]{1,0:T(8,128)(2,1)S(1)} collective-permute-done((bf16[128,1024]{1,0:T(8,128)(2,1)S(1)}, bf16[128,1024]{1,0:T(8,128)(2,1)S(1)}, u32[]{:S(2)}, u32[]{:S(2)}) %collective-permute-start.26) | collective-permute-done | bytes 262176 | tf_op jit(solution)/shard_map/ppermute | solution.py:46
  106.1 23.1 %collective-permute-done.12 = bf16[8,384,128]{2,0,1:T(8,128)(2,1)S(1)} collective-permute-done((bf16[8,384,128]{2,0,1:T(8,128)(2,1)S(1)}, bf16[8,384,128]{2,0,1:T(8,128)(2,1)S(1)}, u32[]{:S(2)}, u32[]{:S(2)}) %collective-permute-start.12) | collective-permute-done | bytes 786464 | tf_op jit(solution)/shard_map/ppermute | solution.py:68
  131.5 12.0 %collective-permute-done.13 = bf16[8,384,128]{2,0,1:T(8,128)(2,1)S(1)} collective-permute-done((bf16[8,384,128]{2,0,1:T(8,128)(2,1)S(1)}, bf16[8,384,128]{2,0,1:T(8,128)(2,1)S(1)}, u32[]{:S(2)}, u32[]{:S(2)}) %collective-permute-start.13) | collective-permute-done | bytes 786464 | tf_op jit(solution)/shard_map/ppermute | solution.py:68
  149.6 3.7 %bitcast_add_fusion = bf16[384,4096]{1,0:T(8,128)(2,1)S(1)} fusion(bf16[48,8,32,128]{3,2,1,0:T(8,128)(2,1)S(1)} %bitcast.161, bf16[48,8,32,128]{3,2,1,0:T(8,128)(2,1)S(1)} %bitcast.159, bf16[48,8,32,128]{3,2,1,0:T(8,128)(2,1)S(1)} %bitcast.157, bf16[48,8,32,128]{3,2,1,0:T(8,128)(2,1)S(1)} %bitcast.154), kind=kLoop, calls=%fused_computation.12 | loop fusion | flops 4718592 | bytes 15728640 | tf_op jit(solution)/shard_map/add | solution.py:131
  153.4 1.9 %fusion.45 = bf16[384,256]{1,0:T(8,128)(2,1)} fusion(f32[384,256]{1,0:T(8,128)S(1)} %fusion.3, f32[384,256]{1,0:T(8,128)S(1)} %fusion.5, f32[384,256]{1,0:T(8,128)S(1)} %fusion.7, bf16[4096,1024]{1,0:T(8,128)(2,1)S(1)} %constant_dynamic-update-slice_fusion, bf16[48,8,32,128]{3,2,1,0:T(8,128)(2,1)S(1)} %bitcast.155), kind=kOutput, calls=%fused_computation.43 | convolution fusion | flops 805699584 | bytes 6619136 | tf_op jit(solution)/shard_map/dot_general | solution.py:132
  155.3 6.4 %fusion.27 = bf16[384,512]{1,0:T(8,128)(2,1)} fusion(bf16[4096,1024]{1,0:T(8,128)(2,1)} %copy-done.3, bf16[384,4096]{1,0:T(8,128)(2,1)S(1)} %bitcast_add_fusion, f32[4096]{0:T(1024)S(1)} %bitcast.168, f32[512]{0:T(512)S(1)} %bitcast.169, bf16[384,256]{1,0:T(8,128)(2,1)} %fusion.45), kind=kOutput, calls=%fused_computation.35 | convolution fusion | flops 2424176640 | bytes 10045440 | tf_op jit(solution)/shard_map/dot_general | solution.py:145
  161.7 3.6 %all-to-all-start = ((bf16[4,96,512]{2,1,0:T(8,128)(2,1)}), bf16[4,96,512]{2,1,0:T(8,128)(2,1)S(1)}, u32[]{:S(2)}, u32[]{:S(2)}) async-start(bf16[4,96,512]{2,1,0:T(8,128)(2,1)} %bitcast.79), calls=%async_computation | async-start | bytes 786432 | tf_op jit(solution)/shard_map/all_to_all | solution.py:147
  167.1 1.9 %collective-permute-start.28 = (bf16[62,1024]{1,0:T(8,128)(2,1)S(1)}, bf16[62,1024]{1,0:T(8,128)(2,1)S(1)}, u32[]{:S(2)}, u32[]{:S(2)}) collective-permute-start(bf16[62,1024]{1,0:T(8,128)(2,1)S(1)} %copy-done.5), channel_id=1, source_target_pairs={{0,2},{1,3},{2,0},{3,1},{4,6},{5,7},{6,4},{7,5},{8,10},{9,11},{10,... | collective-permute-start | bytes 380936 | tf_op jit(solution)/shard_map/ppermute | solution.py:106
  169.0 4.1 %all-to-all-done = bf16[4,96,512]{2,1,0:T(8,128)(2,1)S(1)} async-done(((bf16[4,96,512]{2,1,0:T(8,128)(2,1)}), bf16[4,96,512]{2,1,0:T(8,128)(2,1)S(1)}, u32[]{:S(2)}, u32[]{:S(2)}) %all-to-all-start) | async-done | bytes 393248 | tf_op jit(solution)/shard_map/all_to_all | solution.py:147
  176.0 2.3 %collective-permute-done.28 = bf16[62,1024]{1,0:T(8,128)(2,1)S(1)} collective-permute-done((bf16[62,1024]{1,0:T(8,128)(2,1)S(1)}, bf16[62,1024]{1,0:T(8,128)(2,1)S(1)}, u32[]{:S(2)}, u32[]{:S(2)}) %collective-permute-start.28) | collective-permute-done | bytes 127008 | tf_op jit(solution)/shard_map/ppermute | solution.py:106
  (133 shorter events, 61.9 us)
Async XLA Ops:
  4.1 17.4 %collective-permute-start = (bf16[128,1024]{1,0:T(8,128)(2,1)}, bf16[128,1024]{1,0:T(8,128)(2,1)}, u32[]{:S(2)}, u32[]{:S(2)}) collective-permute-start(bf16[128,1024]{1,0:T(8,128)(2,1)} %get-tuple-element.15), channel_id=1, source_target_pairs={{0,4},{4,8},{8,12},{12,0},{1,5},{5,9},{9,13},{13,1},{2,6},{6,10},{... | collective-permute-start | bytes 786440 | tf_op jit(solution)/shard_map/ppermute | solution.py:41
  5.7 17.4 %collective-permute-start.3 = (bf16[128,1024]{1,0:T(8,128)(2,1)}, bf16[128,1024]{1,0:T(8,128)(2,1)}, u32[]{:S(2)}, u32[]{:S(2)}) collective-permute-start(bf16[128,1024]{1,0:T(8,128)(2,1)} %get-tuple-element.14), channel_id=1, source_target_pairs={{0,4},{4,8},{8,12},{12,0},{1,5},{5,9},{9,13},{13,1},{2,6},{6,10},{... | collective-permute-start | bytes 786440 | tf_op jit(solution)/shard_map/ppermute | solution.py:41
  7.3 23.1 %collective-permute-start.6 = (bf16[128,1024]{1,0:T(8,128)(2,1)}, bf16[128,1024]{1,0:T(8,128)(2,1)}, u32[]{:S(2)}, u32[]{:S(2)}) collective-permute-start(bf16[128,1024]{1,0:T(8,128)(2,1)} %get-tuple-element.16), channel_id=1, source_target_pairs={{0,4},{4,8},{8,12},{12,0},{1,5},{5,9},{9,13},{13,1},{2,6},{6,10},{... | collective-permute-start | bytes 786440 | tf_op jit(solution)/shard_map/ppermute | solution.py:41
  7.3 27.8 %collective-permute-start.9 = (bf16[128,1024]{1,0:T(8,128)(2,1)S(1)}, bf16[128,1024]{1,0:T(8,128)(2,1)}, u32[]{:S(2)}, u32[]{:S(2)}) collective-permute-start(bf16[128,1024]{1,0:T(8,128)(2,1)S(1)} %get-tuple-element.13), channel_id=1, source_target_pairs={{0,4},{4,8},{8,12},{12,0},{1,5},{5,9},{9,13},{13,1},{2,6},{6,10},{... | collective-permute-start | bytes 786440 | tf_op jit(solution)/shard_map/ppermute | solution.py:41
  23.1 13.3 %collective-permute-start.16 = (bf16[128,1024]{1,0:T(8,128)(2,1)}, bf16[128,1024]{1,0:T(8,128)(2,1)}, u32[]{:S(2)}, u32[]{:S(2)}) collective-permute-start(bf16[128,1024]{1,0:T(8,128)(2,1)} %collective-permute-done.3), channel_id=1, source_target_pairs={{0,16},{16,0},{1,17},{17,1},{2,18},{18,2},{3,19},{19,3},{4,20},{20... | collective-permute-start | bytes 786440 | tf_op jit(solution)/shard_map/ppermute | solution.py:46
  27.0 17.9 %collective-permute-start.1 = (bf16[128,1024]{1,0:T(8,128)(2,1)}, bf16[128,1024]{1,0:T(8,128)(2,1)S(1)}, u32[]{:S(2)}, u32[]{:S(2)}) collective-permute-start(bf16[128,1024]{1,0:T(8,128)(2,1)} %collective-permute-done), channel_id=1, source_target_pairs={{0,4},{4,8},{8,12},{12,0},{1,5},{5,9},{9,13},{13,1},{2,6},{6,10},{... | collective-permute-start | bytes 786440 | tf_op jit(solution)/shard_map/ppermute | solution.py:41
  30.3 16.1 %collective-permute-start.4 = (bf16[128,1024]{1,0:T(8,128)(2,1)}, bf16[128,1024]{1,0:T(8,128)(2,1)S(1)}, u32[]{:S(2)}, u32[]{:S(2)}) collective-permute-start(bf16[128,1024]{1,0:T(8,128)(2,1)} %collective-permute-done.3), channel_id=1, source_target_pairs={{0,4},{4,8},{8,12},{12,0},{1,5},{5,9},{9,13},{13,1},{2,6},{6,10},{... | collective-permute-start | bytes 786440 | tf_op jit(solution)/shard_map/ppermute | solution.py:41
  35.1 12.6 %collective-permute-start.7 = (bf16[128,1024]{1,0:T(8,128)(2,1)}, bf16[128,1024]{1,0:T(8,128)(2,1)S(1)}, u32[]{:S(2)}, u32[]{:S(2)}) collective-permute-start(bf16[128,1024]{1,0:T(8,128)(2,1)} %collective-permute-done.6), channel_id=1, source_target_pairs={{0,4},{4,8},{8,12},{12,0},{1,5},{5,9},{9,13},{13,1},{2,6},{6,10},{... | collective-permute-start | bytes 786440 | tf_op jit(solution)/shard_map/ppermute | solution.py:41
  36.4 17.0 %collective-permute-start.10 = (bf16[128,1024]{1,0:T(8,128)(2,1)}, bf16[128,1024]{1,0:T(8,128)(2,1)S(1)}, u32[]{:S(2)}, u32[]{:S(2)}) collective-permute-start(bf16[128,1024]{1,0:T(8,128)(2,1)} %collective-permute-done.9), channel_id=1, source_target_pairs={{0,4},{4,8},{8,12},{12,0},{1,5},{5,9},{9,13},{13,1},{2,6},{6,10},{... | collective-permute-start | bytes 786440 | tf_op jit(solution)/shard_map/ppermute | solution.py:41
  41.6 15.6 %collective-permute-start.18 = (bf16[128,1024]{1,0:T(8,128)(2,1)}, bf16[128,1024]{1,0:T(8,128)(2,1)S(1)}, u32[]{:S(2)}, u32[]{:S(2)}) collective-permute-start(bf16[128,1024]{1,0:T(8,128)(2,1)} %collective-permute-done.9), channel_id=1, source_target_pairs={{0,16},{16,0},{1,17},{17,1},{2,18},{18,2},{3,19},{19,3},{4,20},{20... | collective-permute-start | bytes 786440 | tf_op jit(solution)/shard_map/ppermute | solution.py:46
  44.8 15.4 %collective-permute-start.2 = (bf16[128,1024]{1,0:T(8,128)(2,1)S(1)}, bf16[128,1024]{1,0:T(8,128)(2,1)S(1)}, u32[]{:S(2)}, u32[]{:S(2)}) collective-permute-start(bf16[128,1024]{1,0:T(8,128)(2,1)S(1)} %collective-permute-done.1), channel_id=1, source_target_pairs={{0,4},{4,8},{8,12},{12,0},{1,5},{5,9},{9,13},{13,1},{2,6},{6,10},{... | collective-permute-start | bytes 786440 | tf_op jit(solution)/shard_map/ppermute | solution.py:41
  46.4 18.1 %collective-permute-start.5 = (bf16[128,1024]{1,0:T(8,128)(2,1)S(1)}, bf16[128,1024]{1,0:T(8,128)(2,1)S(1)}, u32[]{:S(2)}, u32[]{:S(2)}) collective-permute-start(bf16[128,1024]{1,0:T(8,128)(2,1)S(1)} %collective-permute-done.4), channel_id=1, source_target_pairs={{0,4},{4,8},{8,12},{12,0},{1,5},{5,9},{9,13},{13,1},{2,6},{6,10},{... | collective-permute-start | bytes 786440 | tf_op jit(solution)/shard_map/ppermute | solution.py:41
  47.7 22.5 %collective-permute-start.8 = (bf16[128,1024]{1,0:T(8,128)(2,1)S(1)}, bf16[128,1024]{1,0:T(8,128)(2,1)S(1)}, u32[]{:S(2)}, u32[]{:S(2)}) collective-permute-start(bf16[128,1024]{1,0:T(8,128)(2,1)S(1)} %collective-permute-done.7), channel_id=1, source_target_pairs={{0,4},{4,8},{8,12},{12,0},{1,5},{5,9},{9,13},{13,1},{2,6},{6,10},{... | collective-permute-start | bytes 786440 | tf_op jit(solution)/shard_map/ppermute | solution.py:41
  53.3 20.8 %collective-permute-start.11 = (bf16[128,1024]{1,0:T(8,128)(2,1)S(1)}, bf16[128,1024]{1,0:T(8,128)(2,1)S(1)}, u32[]{:S(2)}, u32[]{:S(2)}) collective-permute-start(bf16[128,1024]{1,0:T(8,128)(2,1)S(1)} %collective-permute-done.10), channel_id=1, source_target_pairs={{0,4},{4,8},{8,12},{12,0},{1,5},{5,9},{9,13},{13,1},{2,6},{6,10},{... | collective-permute-start | bytes 786440 | tf_op jit(solution)/shard_map/ppermute | solution.py:41
  57.3 21.7 %collective-permute-start.19 = (bf16[128,1024]{1,0:T(8,128)(2,1)S(1)}, bf16[128,1024]{1,0:T(8,128)(2,1)S(1)}, u32[]{:S(2)}, u32[]{:S(2)}) collective-permute-start(bf16[128,1024]{1,0:T(8,128)(2,1)S(1)} %collective-permute-done.1), channel_id=1, source_target_pairs={{0,16},{16,0},{1,17},{17,1},{2,18},{18,2},{3,19},{19,3},{4,20},{20... | collective-permute-start | bytes 786440 | tf_op jit(solution)/shard_map/ppermute | solution.py:46
  60.3 22.4 %collective-permute-start.20 = (bf16[128,1024]{1,0:T(8,128)(2,1)S(1)}, bf16[128,1024]{1,0:T(8,128)(2,1)S(1)}, u32[]{:S(2)}, u32[]{:S(2)}) collective-permute-start(bf16[128,1024]{1,0:T(8,128)(2,1)S(1)} %collective-permute-done.4), channel_id=1, source_target_pairs={{0,16},{16,0},{1,17},{17,1},{2,18},{18,2},{3,19},{19,3},{4,20},{20... | collective-permute-start | bytes 786440 | tf_op jit(solution)/shard_map/ppermute | solution.py:46
  64.6 18.2 %collective-permute-start.21 = (bf16[128,1024]{1,0:T(8,128)(2,1)S(1)}, bf16[128,1024]{1,0:T(8,128)(2,1)S(1)}, u32[]{:S(2)}, u32[]{:S(2)}) collective-permute-start(bf16[128,1024]{1,0:T(8,128)(2,1)S(1)} %collective-permute-done.7), channel_id=1, source_target_pairs={{0,16},{16,0},{1,17},{17,1},{2,18},{18,2},{3,19},{19,3},{4,20},{20... | collective-permute-start | bytes 786440 | tf_op jit(solution)/shard_map/ppermute | solution.py:46
  70.2 14.2 %collective-permute-start.22 = (bf16[128,1024]{1,0:T(8,128)(2,1)S(1)}, bf16[128,1024]{1,0:T(8,128)(2,1)S(1)}, u32[]{:S(2)}, u32[]{:S(2)}) collective-permute-start(bf16[128,1024]{1,0:T(8,128)(2,1)S(1)} %collective-permute-done.10), channel_id=1, source_target_pairs={{0,16},{16,0},{1,17},{17,1},{2,18},{18,2},{3,19},{19,3},{4,20},{20... | collective-permute-start | bytes 786440 | tf_op jit(solution)/shard_map/ppermute | solution.py:46
  75.7 53.5 %collective-permute-start.12 = (bf16[8,384,128]{2,0,1:T(8,128)(2,1)S(1)}, bf16[8,384,128]{2,0,1:T(8,128)(2,1)S(1)}, u32[]{:S(2)}, u32[]{:S(2)}) collective-permute-start(bf16[8,384,128]{2,0,1:T(8,128)(2,1)S(1)} %pad_maximum_fusion.1), channel_id=1, source_target_pairs={{0,4},{4,8},{8,12},{12,0},{1,5},{5,9},{9,13},{13,1},{2,6},{6,10},{... | collective-permute-start | bytes 2359304 | tf_op jit(solution)/shard_map/ppermute | solution.py:68
  79.0 64.5 %collective-permute-start.13 = (bf16[8,384,128]{2,0,1:T(8,128)(2,1)S(1)}, bf16[8,384,128]{2,0,1:T(8,128)(2,1)S(1)}, u32[]{:S(2)}, u32[]{:S(2)}) collective-permute-start(bf16[8,384,128]{2,0,1:T(8,128)(2,1)S(1)} %pad_maximum_fusion.2), channel_id=1, source_target_pairs={{0,8},{4,12},{8,0},{12,4},{1,9},{5,13},{9,1},{13,5},{2,10},{6,14},... | collective-permute-start | bytes 2359304 | tf_op jit(solution)/shard_map/ppermute | solution.py:68
  82.7 64.7 %collective-permute-start.14 = (bf16[8,384,128]{2,0,1:T(8,128)(2,1)S(1)}, bf16[8,384,128]{2,0,1:T(8,128)(2,1)S(1)}, u32[]{:S(2)}, u32[]{:S(2)}) collective-permute-start(bf16[8,384,128]{2,0,1:T(8,128)(2,1)S(1)} %pad_maximum_fusion.3), channel_id=1, source_target_pairs={{0,12},{4,0},{8,4},{12,8},{1,13},{5,1},{9,5},{13,9},{2,14},{6,2},{... | collective-permute-start | bytes 2359304 | tf_op jit(solution)/shard_map/ppermute | solution.py:68
  84.4 13.3 %collective-permute-start.24 = (bf16[128,1024]{1,0:T(8,128)(2,1)S(1)}, bf16[128,1024]{1,0:T(8,128)(2,1)S(1)}, u32[]{:S(2)}, u32[]{:S(2)}) collective-permute-start(bf16[128,1024]{1,0:T(8,128)(2,1)S(1)} %collective-permute-done.5), channel_id=1, source_target_pairs={{0,16},{16,0},{1,17},{17,1},{2,18},{18,2},{3,19},{19,3},{4,20},{20... | collective-permute-start | bytes 786440 | tf_op jit(solution)/shard_map/ppermute | solution.py:46
  161.7 11.5 %all-to-all-start = ((bf16[4,96,512]{2,1,0:T(8,128)(2,1)}), bf16[4,96,512]{2,1,0:T(8,128)(2,1)S(1)}, u32[]{:S(2)}, u32[]{:S(2)}) async-start(bf16[4,96,512]{2,1,0:T(8,128)(2,1)} %bitcast.79), calls=%async_computation | async-start | bytes 786432 | tf_op jit(solution)/shard_map/all_to_all | solution.py:147
  167.1 11.2 %collective-permute-start.28 = (bf16[62,1024]{1,0:T(8,128)(2,1)S(1)}, bf16[62,1024]{1,0:T(8,128)(2,1)S(1)}, u32[]{:S(2)}, u32[]{:S(2)}) collective-permute-start(bf16[62,1024]{1,0:T(8,128)(2,1)S(1)} %copy-done.5), channel_id=1, source_target_pairs={{0,2},{1,3},{2,0},{3,1},{4,6},{5,7},{6,4},{7,5},{8,10},{9,11},{10,... | collective-permute-start | bytes 380936 | tf_op jit(solution)/shard_map/ppermute | solution.py:106
  (16 other events, 244.1 us)

commit v16 on v15

--- a/solution.py
+++ b/solution.py
@@ -109,7 +109,7 @@
     parts, last_rows = weight_parts(weights_here, feat_count, group_count, share_count, entry_count)
 
     first_rows, second_rows, _ = lax.optimization_barrier(
-        (pooled_first[0], pooled_second[0], last_rows)
+        (pooled_first[0], pooled_second[0], (last_rows, hidden_pieces))
     )
     pieces, slot_ids = exchange_rows(first_rows, second_rows, feat_count)
     row_count = pieces[0].shape[1]

time: 180 us -> 190 us (1.056)
  waiting for transfers between devices: 77 us -> 92.1 us
  starting transfers between devices: 43.5 us -> 37.6 us
    ppermute x12, waiting for transfers between devices: 15.6 us -> 24.6 us  [weight_parts(): rings[chunk] = lax.ppermute(rings[chunk], 'feat', ring)]
    ppermute x12, starting transfers between devices: 15.5 us -> 11.3 us  [weight_parts(): forwarded = lax.ppermute(rings[chunk], 'groups', pairs)]
    ppermute x12, waiting for transfers between devices: 18.3 us -> 22.3 us  [weight_parts(): forwarded = lax.ppermute(rings[chunk], 'groups', pairs)]
    all_to_all x1, waiting for transfers between devices: 4.14 us -> 7.33 us  [on_device(): lax.all_to_all(compressed, 'tower', split_axis=0, concat_axis=1, tiled=True)]
    ppermute x3, starting transfers between devices: 3.73 us -> 1.5 us  [on_device(): hidden_pieces.append(lax.ppermute(mlp_weight, 'tower', pairs))]
    unnamed x41 -> x43, local copies, waits for them, and re-layouts: 12.5 us -> 11.5 us
  transfers between devices with their start and end apart: 31 -> 31, of which waited for: 15 -> 16; matrix products, arithmetic and copies ran while one was open for 22% -> 19% of each run, Pallas kernels for 0% -> 0%
where the time goes in v16:
time: 190 us; the launch traced here: 189 us
  waiting for transfers between devices  92.1 us (48%)
  starting transfers between devices  37.6 us (20%)
  local copies, waits for them, and re-layouts  30.5 us (16%)
  matrix products  20.2 us (11%)
  other arithmetic  8.37 us (4%)
    ppermute x3, waiting for transfers between devices, exchange_rows(): lax.ppermute(piece, 'feat', [(source, (source + shift) % feat_count) for...  36.5 us
    ppermute x12, waiting for transfers between devices, weight_parts(): rings[chunk] = lax.ppermute(rings[chunk], 'feat', ring)  24.6 us
    ppermute x12, waiting for transfers between devices, weight_parts(): forwarded = lax.ppermute(rings[chunk], 'groups', pairs)  22.3 us
    ppermute x12, starting transfers between devices, weight_parts(): rings[chunk] = lax.ppermute(rings[chunk], 'feat', ring)  16.2 us
    squeeze x1, local copies, waits for them, and re-layouts, on_device(): pooled_second[0]  12 us
    unnamed x43, local copies, waits for them, and re-layouts  11.5 us
    ppermute x12, starting transfers between devices, weight_parts(): forwarded = lax.ppermute(rings[chunk], 'groups', pairs)  11.3 us
    all_to_all x1, waiting for transfers between devices, on_device(): lax.all_to_all(compressed, 'tower', split_axis=0, concat_axis=1, tiled=True)  7.33 us
  transfers between devices with their start and end apart: 31, of which 16 were waited for; matrix products, arithmetic and copies ran while one was open for 19% of the time, Pallas kernels for 0%

profile of v16, /device:TPU:8, one launch (start us, length us, event | category | flops | bytes accessed | tf_op | source)
XLA Modules:
  0.0 189.4 jit_solution(15826306876240627738)
XLA Ops:
  0.0 3.2 %pad_maximum_fusion = (bf16[1024,1024]{1,0:T(8,128)(2,1)S(1)}, bf16[4096,1024]{1,0:T(8,128)(2,1)}) fusion(bf16[1024,512]{1,0:T(8,128)(2,1)} %bitcast.164, bf16[1024,256]{1,0:T(8,128)(2,1)} %bitcast.165, bf16[1024,256]{1,0:T(8,128)(2,1)} %bitcast.166), kind=kLoop, calls=%fused_computation.26 | loop fusion | flops 6291455 | bytes 6291456 | tf_op jit(solution)/shard_map/concatenate | solution.py:108
  7.3 1.8 collective-permute-start.9
  9.4 12.0 %copy_bitcast_fusion = (bf16[4,1536,128]{2,0,1:T(4,128)(2,1)S(1)}, bf16[4,1536,128]{2,0,1:T(4,128)(2,1)S(1)}) fusion(bf16[1,4,1536,128]{3,2,1,0:T(8,128)(2,1)} %param.14, bf16[1,4,1536,128]{3,2,1,0:T(8,128)(2,1)} %param.13), kind=kLoop, calls=%fused_computation.27 | loop fusion | bytes 6291456 | tf_op jit(solution)/shard_map/squeeze | solution.py:112
  27.0 1.7 constant_dynamic-update-slice_fusion.23
  33.7 1.7 constant_dynamic-update-slice_fusion.21
  47.1 3.3 %collective-permute-done.4 = bf16[128,1024]{1,0:T(8,128)(2,1)S(1)} collective-permute-done((bf16[128,1024]{1,0:T(8,128)(2,1)}, bf16[128,1024]{1,0:T(8,128)(2,1)S(1)}, u32[]{:S(2)}, u32[]{:S(2)}) %collective-permute-start.4) | collective-permute-done | bytes 262176 | tf_op jit(solution)/shard_map/ppermute | solution.py:41
  51.9 4.0 %collective-permute-done.7 = bf16[128,1024]{1,0:T(8,128)(2,1)S(1)} collective-permute-done((bf16[128,1024]{1,0:T(8,128)(2,1)}, bf16[128,1024]{1,0:T(8,128)(2,1)S(1)}, u32[]{:S(2)}, u32[]{:S(2)}) %collective-permute-start.7) | collective-permute-done | bytes 262176 | tf_op jit(solution)/shard_map/ppermute | solution.py:41
  57.5 4.0 %collective-permute-done.10 = bf16[128,1024]{1,0:T(8,128)(2,1)S(1)} collective-permute-done((bf16[128,1024]{1,0:T(8,128)(2,1)}, bf16[128,1024]{1,0:T(8,128)(2,1)S(1)}, u32[]{:S(2)}, u32[]{:S(2)}) %collective-permute-start.10) | collective-permute-done | bytes 262176 | tf_op jit(solution)/shard_map/ppermute | solution.py:41
  63.2 1.7 constant_dynamic-update-slice_fusion.17
  69.7 3.1 %collective-permute-done.5 = bf16[128,1024]{1,0:T(8,128)(2,1)S(1)} collective-permute-done((bf16[128,1024]{1,0:T(8,128)(2,1)S(1)}, bf16[128,1024]{1,0:T(8,128)(2,1)S(1)}, u32[]{:S(2)}, u32[]{:S(2)}) %collective-permute-start.5) | collective-permute-done | bytes 262176 | tf_op jit(solution)/shard_map/ppermute | solution.py:41
  73.3 5.1 %collective-permute-done.8 = bf16[128,1024]{1,0:T(8,128)(2,1)S(1)} collective-permute-done((bf16[128,1024]{1,0:T(8,128)(2,1)S(1)}, bf16[128,1024]{1,0:T(8,128)(2,1)S(1)}, u32[]{:S(2)}, u32[]{:S(2)}) %collective-permute-start.8) | collective-permute-done | bytes 262176 | tf_op jit(solution)/shard_map/ppermute | solution.py:41
  78.9 5.0 %collective-permute-done.11 = bf16[128,1024]{1,0:T(8,128)(2,1)S(1)} collective-permute-done((bf16[128,1024]{1,0:T(8,128)(2,1)S(1)}, bf16[128,1024]{1,0:T(8,128)(2,1)S(1)}, u32[]{:S(2)}, u32[]{:S(2)}) %collective-permute-start.11) | collective-permute-done | bytes 262176 | tf_op jit(solution)/shard_map/ppermute | solution.py:41
  85.5 1.8 collective-permute-start.15
  88.8 3.2 %collective-permute-start.16 = (bf16[8,384,128]{2,0,1:T(8,128)(2,1)S(1)}, bf16[8,384,128]{2,0,1:T(8,128)(2,1)S(1)}, u32[]{:S(2)}, u32[]{:S(2)}) collective-permute-start(bf16[8,384,128]{2,0,1:T(8,128)(2,1)S(1)} %pad_maximum_fusion.2), channel_id=1, source_target_pairs={{0,8},{4,12},{8,0},{12,4},{1,9},{5,13},{9,1},{13,5},{2,10},{6,14},... | collective-permute-start | bytes 2359304 | tf_op jit(solution)/shard_map/ppermute | solution.py:68
  94.9 7.0 %collective-permute-done.26 = bf16[128,1024]{1,0:T(8,128)(2,1)S(1)} collective-permute-done((bf16[128,1024]{1,0:T(8,128)(2,1)S(1)}, bf16[128,1024]{1,0:T(8,128)(2,1)S(1)}, u32[]{:S(2)}, u32[]{:S(2)}) %collective-permute-start.26) | collective-permute-done | bytes 262176 | tf_op jit(solution)/shard_map/ppermute | solution.py:46
  102.4 5.1 %collective-permute-done.27 = bf16[128,1024]{1,0:T(8,128)(2,1)S(1)} collective-permute-done((bf16[128,1024]{1,0:T(8,128)(2,1)S(1)}, bf16[128,1024]{1,0:T(8,128)(2,1)S(1)}, u32[]{:S(2)}, u32[]{:S(2)}) %collective-permute-start.27) | collective-permute-done | bytes 262176 | tf_op jit(solution)/shard_map/ppermute | solution.py:46
  108.0 5.1 %collective-permute-done.28 = bf16[128,1024]{1,0:T(8,128)(2,1)S(1)} collective-permute-done((bf16[128,1024]{1,0:T(8,128)(2,1)S(1)}, bf16[128,1024]{1,0:T(8,128)(2,1)S(1)}, u32[]{:S(2)}, u32[]{:S(2)}) %collective-permute-start.28) | collective-permute-done | bytes 262176 | tf_op jit(solution)/shard_map/ppermute | solution.py:46
  113.2 4.1 %collective-permute-done.29 = bf16[128,1024]{1,0:T(8,128)(2,1)S(1)} collective-permute-done((bf16[128,1024]{1,0:T(8,128)(2,1)S(1)}, bf16[128,1024]{1,0:T(8,128)(2,1)S(1)}, u32[]{:S(2)}, u32[]{:S(2)}) %collective-permute-start.29) | collective-permute-done | bytes 262176 | tf_op jit(solution)/shard_map/ppermute | solution.py:46
  119.6 35.2 %collective-permute-done.16 = bf16[8,384,128]{2,0,1:T(8,128)(2,1)S(1)} collective-permute-done((bf16[8,384,128]{2,0,1:T(8,128)(2,1)S(1)}, bf16[8,384,128]{2,0,1:T(8,128)(2,1)S(1)}, u32[]{:S(2)}, u32[]{:S(2)}) %collective-permute-start.16) | collective-permute-done | bytes 786464 | tf_op jit(solution)/shard_map/ppermute | solution.py:68
  160.8 3.7 %bitcast_add_fusion = bf16[384,4096]{1,0:T(8,128)(2,1)S(1)} fusion(bf16[48,8,32,128]{3,2,1,0:T(8,128)(2,1)S(1)} %bitcast.161, bf16[48,8,32,128]{3,2,1,0:T(8,128)(2,1)S(1)} %bitcast.159, bf16[48,8,32,128]{3,2,1,0:T(8,128)(2,1)S(1)} %bitcast.157, bf16[48,8,32,128]{3,2,1,0:T(8,128)(2,1)S(1)} %bitcast.154), kind=kLoop, calls=%fused_computation.12 | loop fusion | flops 4718592 | bytes 15728640 | tf_op jit(solution)/shard_map/add | solution.py:131
  164.6 1.9 fusion.45
  166.4 6.4 %fusion.27 = bf16[384,512]{1,0:T(8,128)(2,1)} fusion(bf16[4096,1024]{1,0:T(8,128)(2,1)} %copy-done.3, bf16[384,4096]{1,0:T(8,128)(2,1)S(1)} %bitcast_add_fusion, f32[4096]{0:T(1024)S(1)} %bitcast.168, f32[512]{0:T(512)S(1)} %bitcast.169, bf16[384,256]{1,0:T(8,128)(2,1)} %fusion.45), kind=kOutput, calls=%fused_computation.35 | convolution fusion | flops 2424176640 | bytes 10045440 | tf_op jit(solution)/shard_map/dot_general | solution.py:145
  172.8 3.6 %all-to-all-start = ((bf16[4,96,512]{2,1,0:T(8,128)(2,1)}), bf16[4,96,512]{2,1,0:T(8,128)(2,1)S(1)}, u32[]{:S(2)}, u32[]{:S(2)}) async-start(bf16[4,96,512]{2,1,0:T(8,128)(2,1)} %bitcast.79), calls=%async_computation | async-start | bytes 786432 | tf_op jit(solution)/shard_map/all_to_all | solution.py:147
  176.5 7.3 %all-to-all-done = bf16[4,96,512]{2,1,0:T(8,128)(2,1)S(1)} async-done(((bf16[4,96,512]{2,1,0:T(8,128)(2,1)}), bf16[4,96,512]{2,1,0:T(8,128)(2,1)S(1)}, u32[]{:S(2)}, u32[]{:S(2)}) %all-to-all-start) | async-done | bytes 393248 | tf_op jit(solution)/shard_map/all_to_all | solution.py:147
  (135 shorter events, 57.9 us)
Async XLA Ops:
  4.1 17.4 %collective-permute-start = (bf16[128,1024]{1,0:T(8,128)(2,1)}, bf16[128,1024]{1,0:T(8,128)(2,1)}, u32[]{:S(2)}, u32[]{:S(2)}) collective-permute-start(bf16[128,1024]{1,0:T(8,128)(2,1)} %get-tuple-element.15), channel_id=1, source_target_pairs={{0,4},{4,8},{8,12},{12,0},{1,5},{5,9},{9,13},{13,1},{2,6},{6,10},{... | collective-permute-start | bytes 786440 | tf_op jit(solution)/shard_map/ppermute | solution.py:41
  5.7 20.7 %collective-permute-start.3 = (bf16[128,1024]{1,0:T(8,128)(2,1)}, bf16[128,1024]{1,0:T(8,128)(2,1)}, u32[]{:S(2)}, u32[]{:S(2)}) collective-permute-start(bf16[128,1024]{1,0:T(8,128)(2,1)} %get-tuple-element.14), channel_id=1, source_target_pairs={{0,4},{4,8},{8,12},{12,0},{1,5},{5,9},{9,13},{13,1},{2,6},{6,10},{... | collective-permute-start | bytes 786440 | tf_op jit(solution)/shard_map/ppermute | solution.py:41
  7.3 21.4 %collective-permute-start.6 = (bf16[128,1024]{1,0:T(8,128)(2,1)}, bf16[128,1024]{1,0:T(8,128)(2,1)}, u32[]{:S(2)}, u32[]{:S(2)}) collective-permute-start(bf16[128,1024]{1,0:T(8,128)(2,1)} %get-tuple-element.16), channel_id=1, source_target_pairs={{0,4},{4,8},{8,12},{12,0},{1,5},{5,9},{9,13},{13,1},{2,6},{6,10},{... | collective-permute-start | bytes 786440 | tf_op jit(solution)/shard_map/ppermute | solution.py:41
  7.3 31.2 %collective-permute-start.9 = (bf16[128,1024]{1,0:T(8,128)(2,1)S(1)}, bf16[128,1024]{1,0:T(8,128)(2,1)}, u32[]{:S(2)}, u32[]{:S(2)}) collective-permute-start(bf16[128,1024]{1,0:T(8,128)(2,1)S(1)} %get-tuple-element.13), channel_id=1, source_target_pairs={{0,4},{4,8},{8,12},{12,0},{1,5},{5,9},{9,13},{13,1},{2,6},{6,10},{... | collective-permute-start | bytes 786440 | tf_op jit(solution)/shard_map/ppermute | solution.py:41
  9.1 26.3 %collective-permute-start.12 = (bf16[62,1024]{1,0:T(8,128)(2,1)}, bf16[62,1024]{1,0:T(8,128)(2,1)}, u32[]{:S(2)}, u32[]{:S(2)}) collective-permute-start(bf16[62,1024]{1,0:T(8,128)(2,1)} %param.22), channel_id=1, source_target_pairs={{0,1},{1,2},{2,3},{3,0},{4,5},{5,6},{6,7},{7,4},{8,9},{9,10},{10,1... | collective-permute-start | bytes 380936 | tf_op jit(solution)/shard_map/ppermute | solution.py:106
  26.4 12.8 %collective-permute-start.19 = (bf16[128,1024]{1,0:T(8,128)(2,1)}, bf16[128,1024]{1,0:T(8,128)(2,1)S(1)}, u32[]{:S(2)}, u32[]{:S(2)}) collective-permute-start(bf16[128,1024]{1,0:T(8,128)(2,1)} %collective-permute-done.3), channel_id=1, source_target_pairs={{0,16},{16,0},{1,17},{17,1},{2,18},{18,2},{3,19},{19,3},{4,20},{20... | collective-permute-start | bytes 786440 | tf_op jit(solution)/shard_map/ppermute | solution.py:46
  30.5 11.1 %collective-permute-start.20 = (bf16[128,1024]{1,0:T(8,128)(2,1)}, bf16[128,1024]{1,0:T(8,128)(2,1)S(1)}, u32[]{:S(2)}, u32[]{:S(2)}) collective-permute-start(bf16[128,1024]{1,0:T(8,128)(2,1)} %collective-permute-done.6), channel_id=1, source_target_pairs={{0,16},{16,0},{1,17},{17,1},{2,18},{18,2},{3,19},{19,3},{4,20},{20... | collective-permute-start | bytes 786440 | tf_op jit(solution)/shard_map/ppermute | solution.py:46
  36.9 13.4 %collective-permute-start.4 = (bf16[128,1024]{1,0:T(8,128)(2,1)}, bf16[128,1024]{1,0:T(8,128)(2,1)S(1)}, u32[]{:S(2)}, u32[]{:S(2)}) collective-permute-start(bf16[128,1024]{1,0:T(8,128)(2,1)} %collective-permute-done.3), channel_id=1, source_target_pairs={{0,4},{4,8},{8,12},{12,0},{1,5},{5,9},{9,13},{13,1},{2,6},{6,10},{... | collective-permute-start | bytes 786440 | tf_op jit(solution)/shard_map/ppermute | solution.py:41
  38.5 17.5 %collective-permute-start.7 = (bf16[128,1024]{1,0:T(8,128)(2,1)}, bf16[128,1024]{1,0:T(8,128)(2,1)S(1)}, u32[]{:S(2)}, u32[]{:S(2)}) collective-permute-start(bf16[128,1024]{1,0:T(8,128)(2,1)} %collective-permute-done.6), channel_id=1, source_target_pairs={{0,4},{4,8},{8,12},{12,0},{1,5},{5,9},{9,13},{13,1},{2,6},{6,10},{... | collective-permute-start | bytes 786440 | tf_op jit(solution)/shard_map/ppermute | solution.py:41
  39.2 22.4 %collective-permute-start.10 = (bf16[128,1024]{1,0:T(8,128)(2,1)}, bf16[128,1024]{1,0:T(8,128)(2,1)S(1)}, u32[]{:S(2)}, u32[]{:S(2)}) collective-permute-start(bf16[128,1024]{1,0:T(8,128)(2,1)} %collective-permute-done.9), channel_id=1, source_target_pairs={{0,4},{4,8},{8,12},{12,0},{1,5},{5,9},{9,13},{13,1},{2,6},{6,10},{... | collective-permute-start | bytes 786440 | tf_op jit(solution)/shard_map/ppermute | solution.py:41
  41.6 23.2 %collective-permute-start.21 = (bf16[128,1024]{1,0:T(8,128)(2,1)}, bf16[128,1024]{1,0:T(8,128)(2,1)S(1)}, u32[]{:S(2)}, u32[]{:S(2)}) collective-permute-start(bf16[128,1024]{1,0:T(8,128)(2,1)} %collective-permute-done.9), channel_id=1, source_target_pairs={{0,16},{16,0},{1,17},{17,1},{2,18},{18,2},{3,19},{19,3},{4,20},{20... | collective-permute-start | bytes 786440 | tf_op jit(solution)/shard_map/ppermute | solution.py:46
  45.5 22.7 %collective-permute-start.2 = (bf16[128,1024]{1,0:T(8,128)(2,1)S(1)}, bf16[128,1024]{1,0:T(8,128)(2,1)S(1)}, u32[]{:S(2)}, u32[]{:S(2)}) collective-permute-start(bf16[128,1024]{1,0:T(8,128)(2,1)S(1)} %collective-permute-done.1), channel_id=1, source_target_pairs={{0,4},{4,8},{8,12},{12,0},{1,5},{5,9},{9,13},{13,1},{2,6},{6,10},{... | collective-permute-start | bytes 786440 | tf_op jit(solution)/shard_map/ppermute | solution.py:41
  50.3 22.5 %collective-permute-start.5 = (bf16[128,1024]{1,0:T(8,128)(2,1)S(1)}, bf16[128,1024]{1,0:T(8,128)(2,1)S(1)}, u32[]{:S(2)}, u32[]{:S(2)}) collective-permute-start(bf16[128,1024]{1,0:T(8,128)(2,1)S(1)} %collective-permute-done.4), channel_id=1, source_target_pairs={{0,4},{4,8},{8,12},{12,0},{1,5},{5,9},{9,13},{13,1},{2,6},{6,10},{... | collective-permute-start | bytes 786440 | tf_op jit(solution)/shard_map/ppermute | solution.py:41
  56.0 22.5 %collective-permute-start.8 = (bf16[128,1024]{1,0:T(8,128)(2,1)S(1)}, bf16[128,1024]{1,0:T(8,128)(2,1)S(1)}, u32[]{:S(2)}, u32[]{:S(2)}) collective-permute-start(bf16[128,1024]{1,0:T(8,128)(2,1)S(1)} %collective-permute-done.7), channel_id=1, source_target_pairs={{0,4},{4,8},{8,12},{12,0},{1,5},{5,9},{9,13},{13,1},{2,6},{6,10},{... | collective-permute-start | bytes 786440 | tf_op jit(solution)/shard_map/ppermute | solution.py:41
  61.6 22.4 %collective-permute-start.11 = (bf16[128,1024]{1,0:T(8,128)(2,1)S(1)}, bf16[128,1024]{1,0:T(8,128)(2,1)S(1)}, u32[]{:S(2)}, u32[]{:S(2)}) collective-permute-start(bf16[128,1024]{1,0:T(8,128)(2,1)S(1)} %collective-permute-done.10), channel_id=1, source_target_pairs={{0,4},{4,8},{8,12},{12,0},{1,5},{5,9},{9,13},{13,1},{2,6},{6,10},{... | collective-permute-start | bytes 786440 | tf_op jit(solution)/shard_map/ppermute | solution.py:41
  67.7 21.1 %collective-permute-start.22 = (bf16[128,1024]{1,0:T(8,128)(2,1)S(1)}, bf16[128,1024]{1,0:T(8,128)(2,1)S(1)}, u32[]{:S(2)}, u32[]{:S(2)}) collective-permute-start(bf16[128,1024]{1,0:T(8,128)(2,1)S(1)} %collective-permute-done.1), channel_id=1, source_target_pairs={{0,16},{16,0},{1,17},{17,1},{2,18},{18,2},{3,19},{19,3},{4,20},{20... | collective-permute-start | bytes 786440 | tf_op jit(solution)/shard_map/ppermute | solution.py:46
  68.2 24.3 %collective-permute-start.23 = (bf16[128,1024]{1,0:T(8,128)(2,1)S(1)}, bf16[128,1024]{1,0:T(8,128)(2,1)S(1)}, u32[]{:S(2)}, u32[]{:S(2)}) collective-permute-start(bf16[128,1024]{1,0:T(8,128)(2,1)S(1)} %collective-permute-done.4), channel_id=1, source_target_pairs={{0,16},{16,0},{1,17},{17,1},{2,18},{18,2},{3,19},{19,3},{4,20},{20... | collective-permute-start | bytes 786440 | tf_op jit(solution)/shard_map/ppermute | solution.py:46
  72.8 19.8 %collective-permute-start.24 = (bf16[128,1024]{1,0:T(8,128)(2,1)S(1)}, bf16[128,1024]{1,0:T(8,128)(2,1)S(1)}, u32[]{:S(2)}, u32[]{:S(2)}) collective-permute-start(bf16[128,1024]{1,0:T(8,128)(2,1)S(1)} %collective-permute-done.7), channel_id=1, source_target_pairs={{0,16},{16,0},{1,17},{17,1},{2,18},{18,2},{3,19},{19,3},{4,20},{20... | collective-permute-start | bytes 786440 | tf_op jit(solution)/shard_map/ppermute | solution.py:46
  78.4 14.7 %collective-permute-start.25 = (bf16[128,1024]{1,0:T(8,128)(2,1)S(1)}, bf16[128,1024]{1,0:T(8,128)(2,1)S(1)}, u32[]{:S(2)}, u32[]{:S(2)}) collective-permute-start(bf16[128,1024]{1,0:T(8,128)(2,1)S(1)} %collective-permute-done.10), channel_id=1, source_target_pairs={{0,16},{16,0},{1,17},{17,1},{2,18},{18,2},{3,19},{19,3},{4,20},{20... | collective-permute-start | bytes 786440 | tf_op jit(solution)/shard_map/ppermute | solution.py:46
  85.5 31.8 %collective-permute-start.15 = (bf16[8,384,128]{2,0,1:T(8,128)(2,1)S(1)}, bf16[8,384,128]{2,0,1:T(8,128)(2,1)S(1)}, u32[]{:S(2)}, u32[]{:S(2)}) collective-permute-start(bf16[8,384,128]{2,0,1:T(8,128)(2,1)S(1)} %pad_maximum_fusion.1), channel_id=1, source_target_pairs={{0,4},{4,8},{8,12},{12,0},{1,5},{5,9},{9,13},{13,1},{2,6},{6,10},{... | collective-permute-start | bytes 2359304 | tf_op jit(solution)/shard_map/ppermute | solution.py:68
  88.8 66.0 %collective-permute-start.16 = (bf16[8,384,128]{2,0,1:T(8,128)(2,1)S(1)}, bf16[8,384,128]{2,0,1:T(8,128)(2,1)S(1)}, u32[]{:S(2)}, u32[]{:S(2)}) collective-permute-start(bf16[8,384,128]{2,0,1:T(8,128)(2,1)S(1)} %pad_maximum_fusion.2), channel_id=1, source_target_pairs={{0,8},{4,12},{8,0},{12,4},{1,9},{5,13},{9,1},{13,5},{2,10},{6,14},... | collective-permute-start | bytes 2359304 | tf_op jit(solution)/shard_map/ppermute | solution.py:68
  92.5 66.0 %collective-permute-start.17 = (bf16[8,384,128]{2,0,1:T(8,128)(2,1)S(1)}, bf16[8,384,128]{2,0,1:T(8,128)(2,1)S(1)}, u32[]{:S(2)}, u32[]{:S(2)}) collective-permute-start(bf16[8,384,128]{2,0,1:T(8,128)(2,1)S(1)} %pad_maximum_fusion.3), channel_id=1, source_target_pairs={{0,12},{4,0},{8,4},{12,8},{1,13},{5,1},{9,5},{13,9},{2,14},{6,2},{... | collective-permute-start | bytes 2359304 | tf_op jit(solution)/shard_map/ppermute | solution.py:68
  93.1 14.4 %collective-permute-start.27 = (bf16[128,1024]{1,0:T(8,128)(2,1)S(1)}, bf16[128,1024]{1,0:T(8,128)(2,1)S(1)}, u32[]{:S(2)}, u32[]{:S(2)}) collective-permute-start(bf16[128,1024]{1,0:T(8,128)(2,1)S(1)} %collective-permute-done.5), channel_id=1, source_target_pairs={{0,16},{16,0},{1,17},{17,1},{2,18},{18,2},{3,19},{19,3},{4,20},{20... | collective-permute-start | bytes 786440 | tf_op jit(solution)/shard_map/ppermute | solution.py:46
  101.9 11.2 %collective-permute-start.28 = (bf16[128,1024]{1,0:T(8,128)(2,1)S(1)}, bf16[128,1024]{1,0:T(8,128)(2,1)S(1)}, u32[]{:S(2)}, u32[]{:S(2)}) collective-permute-start(bf16[128,1024]{1,0:T(8,128)(2,1)S(1)} %collective-permute-done.8), channel_id=1, source_target_pairs={{0,16},{16,0},{1,17},{17,1},{2,18},{18,2},{3,19},{19,3},{4,20},{20... | collective-permute-start | bytes 786440 | tf_op jit(solution)/shard_map/ppermute | solution.py:46
  (17 other events, 239.9 us)

commit v17 on v10

--- a/solution.py
+++ b/solution.py
@@ -109,7 +109,7 @@
     parts, last_rows = weight_parts(weights_here, feat_count, group_count, share_count, entry_count)
 
     first_rows, second_rows, _ = lax.optimization_barrier(
-        (pooled_first[0], pooled_second[0], last_rows)
+        (pooled_first[0], pooled_second[0], last_rows[: max(1, len(last_rows) - 1)])
     )
     pieces, slot_ids = exchange_rows(first_rows, second_rows, feat_count)
     row_count = pieces[0].shape[1]

time: 179 us -> 180 us (level)
  waiting for transfers between devices: 71.9 us -> 75.1 us
    ppermute x3, waiting for transfers between devices: 36.5 us -> 42.1 us  [exchange_rows(): lax.ppermute(piece, 'feat', [(source, (source + shift) % feat_count) for...]
    ppermute x12, waiting for transfers between devices: 17.3 us -> 13.8 us  [weight_parts(): rings[chunk] = lax.ppermute(rings[chunk], 'feat', ring)]
  transfers between devices with their start and end apart: 31 -> 31, of which waited for: 13 -> 13; matrix products, arithmetic and copies ran while one was open for 26% -> 25% of each run, Pallas kernels for 0% -> 0%
where the time goes in v17:
time: 180 us
  waiting for transfers between devices  75.1 us (42%)
  local copies, waits for them, and re-layouts  41.3 us (23%)
  starting transfers between devices  41.3 us (23%)
  matrix products  17.4 us (10%)
  other arithmetic  4.66 us (3%)
    ppermute x3, waiting for transfers between devices, exchange_rows(): lax.ppermute(piece, 'feat', [(source, (source + shift) % feat_count) for...  42.1 us
    unnamed x37, local copies, waits for them, and re-layouts  21.6 us
    ppermute x12, starting transfers between devices, weight_parts(): forwarded = lax.ppermute(rings[chunk], 'groups', pairs)  15.5 us
    ppermute x12, starting transfers between devices, weight_parts(): rings[chunk] = lax.ppermute(rings[chunk], 'feat', ring)  15.2 us
    ppermute x12, waiting for transfers between devices, weight_parts(): rings[chunk] = lax.ppermute(rings[chunk], 'feat', ring)  13.8 us
    squeeze x1, local copies, waits for them, and re-layouts, on_device(): pooled_second[0]  12 us
    ppermute x12, waiting for transfers between devices, weight_parts(): forwarded = lax.ppermute(rings[chunk], 'groups', pairs)  11.4 us
    dot_general x1, matrix products, on_device(): jnp.dot(crossed, weights[:, 2 * rank:], preferred_element_type=jnp.float32)  7.08 us
  transfers between devices with their start and end apart: 31, of which 13 were waited for; matrix products, arithmetic and copies ran while one was open for 25% of the time, Pallas kernels for 0%

profile of v17, /device:TPU:0, one launch (start us, length us, event | category | flops | bytes accessed | tf_op | source)
XLA Modules:
  0.0 180.1 jit_solution(10790248773180558601)
XLA Ops:
  0.0 3.2 %pad_maximum_fusion = (bf16[1024,1024]{1,0:T(8,128)(2,1)S(1)}, bf16[4096,1024]{1,0:T(8,128)(2,1)}) fusion(bf16[1024,512]{1,0:T(8,128)(2,1)} %bitcast.138, bf16[1024,256]{1,0:T(8,128)(2,1)} %bitcast.139, bf16[1024,256]{1,0:T(8,128)(2,1)} %bitcast.140), kind=kLoop, calls=%fused_computation.16 | loop fusion | flops 6291455 | bytes 6291456 | tf_op jit(solution)/shard_map/concatenate | solution.py:108
  4.1 3.0 %collective-permute-start = (bf16[128,1024]{1,0:T(8,128)(2,1)}, bf16[128,1024]{1,0:T(8,128)(2,1)}, u32[]{:S(2)}, u32[]{:S(2)}) collective-permute-start(bf16[128,1024]{1,0:T(8,128)(2,1)} %get-tuple-element.11), channel_id=1, source_target_pairs={{0,4},{4,8},{8,12},{12,0},{1,5},{5,9},{9,13},{13,1},{2,6},{6,10},{... | collective-permute-start | bytes 786440 | tf_op jit(solution)/shard_map/ppermute | solution.py:41
  10.7 12.0 %copy_bitcast_fusion = (bf16[4,1536,128]{2,0,1:T(4,128)(2,1)S(1)}, bf16[4,1536,128]{2,0,1:T(4,128)(2,1)S(1)}) fusion(bf16[1,4,1536,128]{3,2,1,0:T(8,128)(2,1)} %param.14, bf16[1,4,1536,128]{3,2,1,0:T(8,128)(2,1)} %param.13), kind=kLoop, calls=%fused_computation.17 | loop fusion | bytes 6291456 | tf_op jit(solution)/shard_map/squeeze | solution.py:112
  22.8 1.8 collective-permute-start.12
  34.8 1.7 constant_dynamic-update-slice_fusion.22
  41.0 1.7 constant_dynamic-update-slice_fusion.19
  43.8 2.0 %collective-permute-start.20 = (bf16[128,1024]{1,0:T(8,128)(2,1)}, bf16[128,1024]{1,0:T(8,128)(2,1)S(1)}, u32[]{:S(2)}, u32[]{:S(2)}) collective-permute-start(bf16[128,1024]{1,0:T(8,128)(2,1)} %collective-permute-done.15), channel_id=1, source_target_pairs={{0,4},{4,8},{8,12},{12,0},{1,5},{5,9},{9,13},{13,1},{2,6},{6,10},{... | collective-permute-start | bytes 786440 | tf_op jit(solution)/shard_map/ppermute | solution.py:41
  45.8 1.9 %collective-permute-start.2 = (bf16[128,1024]{1,0:T(8,128)(2,1)S(1)}, bf16[128,1024]{1,0:T(8,128)(2,1)S(1)}, u32[]{:S(2)}, u32[]{:S(2)}) collective-permute-start(bf16[128,1024]{1,0:T(8,128)(2,1)S(1)} %collective-permute-done.1), channel_id=1, source_target_pairs={{0,4},{4,8},{8,12},{12,0},{1,5},{5,9},{9,13},{13,1},{2,6},{6,10},{... | collective-permute-start | bytes 786440 | tf_op jit(solution)/shard_map/ppermute | solution.py:41
  48.0 2.4 %collective-permute-done.7 = bf16[128,1024]{1,0:T(8,128)(2,1)S(1)} collective-permute-done((bf16[128,1024]{1,0:T(8,128)(2,1)}, bf16[128,1024]{1,0:T(8,128)(2,1)S(1)}, u32[]{:S(2)}, u32[]{:S(2)}) %collective-permute-start.7) | collective-permute-done | bytes 262176 | tf_op jit(solution)/shard_map/ppermute | solution.py:41
  51.1 1.7 constant_dynamic-update-slice_fusion.17
  57.6 4.1 %collective-permute-done.2 = bf16[128,1024]{1,0:T(8,128)(2,1)S(1)} collective-permute-done((bf16[128,1024]{1,0:T(8,128)(2,1)S(1)}, bf16[128,1024]{1,0:T(8,128)(2,1)S(1)}, u32[]{:S(2)}, u32[]{:S(2)}) %collective-permute-start.2) | collective-permute-done | bytes 262176 | tf_op jit(solution)/shard_map/ppermute | solution.py:41
  63.2 4.1 %collective-permute-done.5 = bf16[128,1024]{1,0:T(8,128)(2,1)S(1)} collective-permute-done((bf16[128,1024]{1,0:T(8,128)(2,1)S(1)}, bf16[128,1024]{1,0:T(8,128)(2,1)S(1)}, u32[]{:S(2)}, u32[]{:S(2)}) %collective-permute-start.5) | collective-permute-done | bytes 262176 | tf_op jit(solution)/shard_map/ppermute | solution.py:41
  68.8 3.0 %collective-permute-done.8 = bf16[128,1024]{1,0:T(8,128)(2,1)S(1)} collective-permute-done((bf16[128,1024]{1,0:T(8,128)(2,1)S(1)}, bf16[128,1024]{1,0:T(8,128)(2,1)S(1)}, u32[]{:S(2)}, u32[]{:S(2)}) %collective-permute-start.8) | collective-permute-done | bytes 262176 | tf_op jit(solution)/shard_map/ppermute | solution.py:41
  73.4 4.1 %collective-permute-start.11 = (bf16[8,384,128]{2,0,1:T(8,128)(2,1)S(1)}, bf16[8,384,128]{2,0,1:T(8,128)(2,1)S(1)}, u32[]{:S(2)}, u32[]{:S(2)}) collective-permute-start(bf16[8,384,128]{2,0,1:T(8,128)(2,1)S(1)} %pad_maximum_fusion.3), channel_id=1, source_target_pairs={{0,12},{4,0},{8,4},{12,8},{1,13},{5,1},{9,5},{13,9},{2,14},{6,2},{... | collective-permute-start | bytes 2359304 | tf_op jit(solution)/shard_map/ppermute | solution.py:68
  86.2 3.9 %collective-permute-done.22 = bf16[128,1024]{1,0:T(8,128)(2,1)S(1)} collective-permute-done((bf16[128,1024]{1,0:T(8,128)(2,1)S(1)}, bf16[128,1024]{1,0:T(8,128)(2,1)S(1)}, u32[]{:S(2)}, u32[]{:S(2)}) %collective-permute-start.22) | collective-permute-done | bytes 262176 | tf_op jit(solution)/shard_map/ppermute | solution.py:46
  93.6 2.1 %collective-permute-done.23 = bf16[128,1024]{1,0:T(8,128)(2,1)S(1)} collective-permute-done((bf16[128,1024]{1,0:T(8,128)(2,1)S(1)}, bf16[128,1024]{1,0:T(8,128)(2,1)S(1)}, u32[]{:S(2)}, u32[]{:S(2)}) %collective-permute-start.23) | collective-permute-done | bytes 262176 | tf_op jit(solution)/shard_map/ppermute | solution.py:46
  98.6 2.6 %collective-permute-done.24 = bf16[128,1024]{1,0:T(8,128)(2,1)S(1)} collective-permute-done((bf16[128,1024]{1,0:T(8,128)(2,1)S(1)}, bf16[128,1024]{1,0:T(8,128)(2,1)S(1)}, u32[]{:S(2)}, u32[]{:S(2)}) %collective-permute-start.24) | collective-permute-done | bytes 262176 | tf_op jit(solution)/shard_map/ppermute | solution.py:46
  106.2 42.1 %collective-permute-done.10 = bf16[8,384,128]{2,0,1:T(8,128)(2,1)S(1)} collective-permute-done((bf16[8,384,128]{2,0,1:T(8,128)(2,1)S(1)}, bf16[8,384,128]{2,0,1:T(8,128)(2,1)S(1)}, u32[]{:S(2)}, u32[]{:S(2)}) %collective-permute-start.10) | collective-permute-done | bytes 786464 | tf_op jit(solution)/shard_map/ppermute | solution.py:68
  152.2 3.4 %fusion.24 = bf16[384,256]{1,0:T(8,128)(2,1)} fusion(bf16[4096,1024]{1,0:T(8,128)(2,1)} %constant_dynamic-update-slice_fusion, bf16[48,8,32,128]{3,2,1,0:T(8,128)(2,1)S(1)} %bitcast.134), kind=kOutput, calls=%fused_computation.28 | convolution fusion | flops 805404672 | bytes 5439488 | tf_op jit(solution)/shard_map/dot_general | solution.py:132
  155.5 7.1 %fusion.15 = bf16[384,512]{1,0:T(8,128)(2,1)} fusion(bf16[4096,1024]{1,0:T(8,128)(2,1)} %constant_dynamic-update-slice_fusion, bf16[384,256]{1,0:T(8,128)(2,1)} %fusion.24, f32[4096]{0:T(1024)S(1)} %bitcast.142, bf16[48,8,32,128]{3,2,1,0:T(8,128)(2,1)S(1)} %bitcast.135, f32[512]{0:T(512)S(1)} %bitcast.143), kind=kOutput, calls=%fused_computation.21 | convolution fusion | flops 2424176640 | bytes 10045440 | tf_op jit(solution)/shard_map/dot_general | solution.py:143
  162.6 3.5 %all-to-all-start = ((bf16[4,96,512]{2,1,0:T(8,128)(2,1)}), bf16[4,96,512]{2,1,0:T(8,128)(2,1)S(1)}, u32[]{:S(2)}, u32[]{:S(2)}) async-start(bf16[4,96,512]{2,1,0:T(8,128)(2,1)} %bitcast.76), calls=%async_computation | async-start | bytes 786432 | tf_op jit(solution)/shard_map/all_to_all | solution.py:145
  166.1 1.7 collective-permute-start.29
  168.6 5.4 %all-to-all-done = bf16[4,96,512]{2,1,0:T(8,128)(2,1)S(1)} async-done(((bf16[4,96,512]{2,1,0:T(8,128)(2,1)}), bf16[4,96,512]{2,1,0:T(8,128)(2,1)S(1)}, u32[]{:S(2)}, u32[]{:S(2)}) %all-to-all-start) | async-done | bytes 393248 | tf_op jit(solution)/shard_map/all_to_all | solution.py:145
  176.8 2.3 %collective-permute-done.28 = bf16[62,1024]{1,0:T(8,128)(2,1)S(1)} collective-permute-done((bf16[62,1024]{1,0:T(8,128)(2,1)S(1)}, bf16[62,1024]{1,0:T(8,128)(2,1)S(1)}, u32[]{:S(2)}, u32[]{:S(2)}) %collective-permute-start.28) | collective-permute-done | bytes 127008 | tf_op jit(solution)/shard_map/ppermute | solution.py:106
  (125 shorter events, 59.0 us)
Async XLA Ops:
  4.1 18.6 %collective-permute-start = (bf16[128,1024]{1,0:T(8,128)(2,1)}, bf16[128,1024]{1,0:T(8,128)(2,1)}, u32[]{:S(2)}, u32[]{:S(2)}) collective-permute-start(bf16[128,1024]{1,0:T(8,128)(2,1)} %get-tuple-element.11), channel_id=1, source_target_pairs={{0,4},{4,8},{8,12},{12,0},{1,5},{5,9},{9,13},{13,1},{2,6},{6,10},{... | collective-permute-start | bytes 786440 | tf_op jit(solution)/shard_map/ppermute | solution.py:41
  7.1 22.4 %collective-permute-start.3 = (bf16[128,1024]{1,0:T(8,128)(2,1)}, bf16[128,1024]{1,0:T(8,128)(2,1)}, u32[]{:S(2)}, u32[]{:S(2)}) collective-permute-start(bf16[128,1024]{1,0:T(8,128)(2,1)} %get-tuple-element.10), channel_id=1, source_target_pairs={{0,4},{4,8},{8,12},{12,0},{1,5},{5,9},{9,13},{13,1},{2,6},{6,10},{... | collective-permute-start | bytes 786440 | tf_op jit(solution)/shard_map/ppermute | solution.py:41
  8.7 23.0 %collective-permute-start.6 = (bf16[128,1024]{1,0:T(8,128)(2,1)}, bf16[128,1024]{1,0:T(8,128)(2,1)}, u32[]{:S(2)}, u32[]{:S(2)}) collective-permute-start(bf16[128,1024]{1,0:T(8,128)(2,1)} %get-tuple-element.12), channel_id=1, source_target_pairs={{0,4},{4,8},{8,12},{12,0},{1,5},{5,9},{9,13},{13,1},{2,6},{6,10},{... | collective-permute-start | bytes 786440 | tf_op jit(solution)/shard_map/ppermute | solution.py:41
  10.3 26.2 %collective-permute-start.15 = (bf16[128,1024]{1,0:T(8,128)(2,1)S(1)}, bf16[128,1024]{1,0:T(8,128)(2,1)}, u32[]{:S(2)}, u32[]{:S(2)}) collective-permute-start(bf16[128,1024]{1,0:T(8,128)(2,1)S(1)} %get-tuple-element.9), channel_id=1, source_target_pairs={{0,4},{4,8},{8,12},{12,0},{1,5},{5,9},{9,13},{13,1},{2,6},{6,10},{... | collective-permute-start | bytes 786440 | tf_op jit(solution)/shard_map/ppermute | solution.py:41
  27.9 17.9 %collective-permute-start.1 = (bf16[128,1024]{1,0:T(8,128)(2,1)}, bf16[128,1024]{1,0:T(8,128)(2,1)S(1)}, u32[]{:S(2)}, u32[]{:S(2)}) collective-permute-start(bf16[128,1024]{1,0:T(8,128)(2,1)} %collective-permute-done), channel_id=1, source_target_pairs={{0,4},{4,8},{8,12},{12,0},{1,5},{5,9},{9,13},{13,1},{2,6},{6,10},{... | collective-permute-start | bytes 786440 | tf_op jit(solution)/shard_map/ppermute | solution.py:41
  31.7 16.0 %collective-permute-start.4 = (bf16[128,1024]{1,0:T(8,128)(2,1)}, bf16[128,1024]{1,0:T(8,128)(2,1)S(1)}, u32[]{:S(2)}, u32[]{:S(2)}) collective-permute-start(bf16[128,1024]{1,0:T(8,128)(2,1)} %collective-permute-done.3), channel_id=1, source_target_pairs={{0,4},{4,8},{8,12},{12,0},{1,5},{5,9},{9,13},{13,1},{2,6},{6,10},{... | collective-permute-start | bytes 786440 | tf_op jit(solution)/shard_map/ppermute | solution.py:41
  36.5 13.9 %collective-permute-start.7 = (bf16[128,1024]{1,0:T(8,128)(2,1)}, bf16[128,1024]{1,0:T(8,128)(2,1)S(1)}, u32[]{:S(2)}, u32[]{:S(2)}) collective-permute-start(bf16[128,1024]{1,0:T(8,128)(2,1)} %collective-permute-done.6), channel_id=1, source_target_pairs={{0,4},{4,8},{8,12},{12,0},{1,5},{5,9},{9,13},{13,1},{2,6},{6,10},{... | collective-permute-start | bytes 786440 | tf_op jit(solution)/shard_map/ppermute | solution.py:41
  39.7 13.1 %collective-permute-start.16 = (bf16[128,1024]{1,0:T(8,128)(2,1)}, bf16[128,1024]{1,0:T(8,128)(2,1)S(1)}, u32[]{:S(2)}, u32[]{:S(2)}) collective-permute-start(bf16[128,1024]{1,0:T(8,128)(2,1)} %collective-permute-done.15), channel_id=1, source_target_pairs={{0,16},{16,0},{1,17},{17,1},{2,18},{18,2},{3,19},{19,3},{4,20},{20... | collective-permute-start | bytes 786440 | tf_op jit(solution)/shard_map/ppermute | solution.py:46
  43.8 12.2 %collective-permute-start.20 = (bf16[128,1024]{1,0:T(8,128)(2,1)}, bf16[128,1024]{1,0:T(8,128)(2,1)S(1)}, u32[]{:S(2)}, u32[]{:S(2)}) collective-permute-start(bf16[128,1024]{1,0:T(8,128)(2,1)} %collective-permute-done.15), channel_id=1, source_target_pairs={{0,4},{4,8},{8,12},{12,0},{1,5},{5,9},{9,13},{13,1},{2,6},{6,10},{... | collective-permute-start | bytes 786440 | tf_op jit(solution)/shard_map/ppermute | solution.py:41
  45.8 15.9 %collective-permute-start.2 = (bf16[128,1024]{1,0:T(8,128)(2,1)S(1)}, bf16[128,1024]{1,0:T(8,128)(2,1)S(1)}, u32[]{:S(2)}, u32[]{:S(2)}) collective-permute-start(bf16[128,1024]{1,0:T(8,128)(2,1)S(1)} %collective-permute-done.1), channel_id=1, source_target_pairs={{0,4},{4,8},{8,12},{12,0},{1,5},{5,9},{9,13},{13,1},{2,6},{6,10},{... | collective-permute-start | bytes 786440 | tf_op jit(solution)/shard_map/ppermute | solution.py:41
  47.7 19.6 %collective-permute-start.5 = (bf16[128,1024]{1,0:T(8,128)(2,1)S(1)}, bf16[128,1024]{1,0:T(8,128)(2,1)S(1)}, u32[]{:S(2)}, u32[]{:S(2)}) collective-permute-start(bf16[128,1024]{1,0:T(8,128)(2,1)S(1)} %collective-permute-done.4), channel_id=1, source_target_pairs={{0,4},{4,8},{8,12},{12,0},{1,5},{5,9},{9,13},{13,1},{2,6},{6,10},{... | collective-permute-start | bytes 786440 | tf_op jit(solution)/shard_map/ppermute | solution.py:41
  50.4 21.4 %collective-permute-start.8 = (bf16[128,1024]{1,0:T(8,128)(2,1)S(1)}, bf16[128,1024]{1,0:T(8,128)(2,1)S(1)}, u32[]{:S(2)}, u32[]{:S(2)}) collective-permute-start(bf16[128,1024]{1,0:T(8,128)(2,1)S(1)} %collective-permute-done.7), channel_id=1, source_target_pairs={{0,4},{4,8},{8,12},{12,0},{1,5},{5,9},{9,13},{13,1},{2,6},{6,10},{... | collective-permute-start | bytes 786440 | tf_op jit(solution)/shard_map/ppermute | solution.py:41
  52.8 20.6 %collective-permute-start.17 = (bf16[128,1024]{1,0:T(8,128)(2,1)S(1)}, bf16[128,1024]{1,0:T(8,128)(2,1)S(1)}, u32[]{:S(2)}, u32[]{:S(2)}) collective-permute-start(bf16[128,1024]{1,0:T(8,128)(2,1)S(1)} %collective-permute-done.1), channel_id=1, source_target_pairs={{0,16},{16,0},{1,17},{17,1},{2,18},{18,2},{3,19},{19,3},{4,20},{20... | collective-permute-start | bytes 786440 | tf_op jit(solution)/shard_map/ppermute | solution.py:46
  56.0 23.3 %collective-permute-start.18 = (bf16[128,1024]{1,0:T(8,128)(2,1)S(1)}, bf16[128,1024]{1,0:T(8,128)(2,1)S(1)}, u32[]{:S(2)}, u32[]{:S(2)}) collective-permute-start(bf16[128,1024]{1,0:T(8,128)(2,1)S(1)} %collective-permute-done.4), channel_id=1, source_target_pairs={{0,16},{16,0},{1,17},{17,1},{2,18},{18,2},{3,19},{19,3},{4,20},{20... | collective-permute-start | bytes 786440 | tf_op jit(solution)/shard_map/ppermute | solution.py:46
  61.7 19.1 %collective-permute-start.19 = (bf16[128,1024]{1,0:T(8,128)(2,1)S(1)}, bf16[128,1024]{1,0:T(8,128)(2,1)S(1)}, u32[]{:S(2)}, u32[]{:S(2)}) collective-permute-start(bf16[128,1024]{1,0:T(8,128)(2,1)S(1)} %collective-permute-done.7), channel_id=1, source_target_pairs={{0,16},{16,0},{1,17},{17,1},{2,18},{18,2},{3,19},{19,3},{4,20},{20... | collective-permute-start | bytes 786440 | tf_op jit(solution)/shard_map/ppermute | solution.py:46
  67.3 16.5 %collective-permute-start.21 = (bf16[128,1024]{1,0:T(8,128)(2,1)S(1)}, bf16[128,1024]{1,0:T(8,128)(2,1)S(1)}, u32[]{:S(2)}, u32[]{:S(2)}) collective-permute-start(bf16[128,1024]{1,0:T(8,128)(2,1)S(1)} %collective-permute-done.20), channel_id=1, source_target_pairs={{0,16},{16,0},{1,17},{17,1},{2,18},{18,2},{3,19},{19,3},{4,20},{20... | collective-permute-start | bytes 786440 | tf_op jit(solution)/shard_map/ppermute | solution.py:46
  71.8 21.2 %collective-permute-start.25 = (bf16[128,1024]{1,0:T(8,128)(2,1)S(1)}, bf16[128,1024]{1,0:T(8,128)(2,1)S(1)}, u32[]{:S(2)}, u32[]{:S(2)}) collective-permute-start(bf16[128,1024]{1,0:T(8,128)(2,1)S(1)} %collective-permute-done.20), channel_id=1, source_target_pairs={{0,4},{4,8},{8,12},{12,0},{1,5},{5,9},{9,13},{13,1},{2,6},{6,10},{... | collective-permute-start | bytes 786440 | tf_op jit(solution)/shard_map/ppermute | solution.py:41
  73.4 31.7 %collective-permute-start.11 = (bf16[8,384,128]{2,0,1:T(8,128)(2,1)S(1)}, bf16[8,384,128]{2,0,1:T(8,128)(2,1)S(1)}, u32[]{:S(2)}, u32[]{:S(2)}) collective-permute-start(bf16[8,384,128]{2,0,1:T(8,128)(2,1)S(1)} %pad_maximum_fusion.3), channel_id=1, source_target_pairs={{0,12},{4,0},{8,4},{12,8},{1,13},{5,1},{9,5},{13,9},{2,14},{6,2},{... | collective-permute-start | bytes 2359304 | tf_op jit(solution)/shard_map/ppermute | solution.py:68
  79.3 69.0 %collective-permute-start.10 = (bf16[8,384,128]{2,0,1:T(8,128)(2,1)S(1)}, bf16[8,384,128]{2,0,1:T(8,128)(2,1)S(1)}, u32[]{:S(2)}, u32[]{:S(2)}) collective-permute-start(bf16[8,384,128]{2,0,1:T(8,128)(2,1)S(1)} %pad_maximum_fusion.2), channel_id=1, source_target_pairs={{0,8},{4,12},{8,0},{12,4},{1,9},{5,13},{9,1},{13,5},{2,10},{6,14},... | collective-permute-start | bytes 2359304 | tf_op jit(solution)/shard_map/ppermute | solution.py:68
  83.8 11.9 %collective-permute-start.23 = (bf16[128,1024]{1,0:T(8,128)(2,1)S(1)}, bf16[128,1024]{1,0:T(8,128)(2,1)S(1)}, u32[]{:S(2)}, u32[]{:S(2)}) collective-permute-start(bf16[128,1024]{1,0:T(8,128)(2,1)S(1)} %collective-permute-done.5), channel_id=1, source_target_pairs={{0,16},{16,0},{1,17},{17,1},{2,18},{18,2},{3,19},{19,3},{4,20},{20... | collective-permute-start | bytes 786440 | tf_op jit(solution)/shard_map/ppermute | solution.py:46
  90.0 11.2 %collective-permute-start.24 = (bf16[128,1024]{1,0:T(8,128)(2,1)S(1)}, bf16[128,1024]{1,0:T(8,128)(2,1)S(1)}, u32[]{:S(2)}, u32[]{:S(2)}) collective-permute-start(bf16[128,1024]{1,0:T(8,128)(2,1)S(1)} %collective-permute-done.8), channel_id=1, source_target_pairs={{0,16},{16,0},{1,17},{17,1},{2,18},{18,2},{3,19},{19,3},{4,20},{20... | collective-permute-start | bytes 786440 | tf_op jit(solution)/shard_map/ppermute | solution.py:46
  93.0 56.4 %collective-permute-start.9 = (bf16[8,384,128]{2,0,1:T(8,128)(2,1)S(1)}, bf16[8,384,128]{2,0,1:T(8,128)(2,1)S(1)}, u32[]{:S(2)}, u32[]{:S(2)}) collective-permute-start(bf16[8,384,128]{2,0,1:T(8,128)(2,1)S(1)} %pad_maximum_fusion.1), channel_id=1, source_target_pairs={{0,4},{4,8},{8,12},{12,0},{1,5},{5,9},{9,13},{13,1},{2,6},{6,10},{... | collective-permute-start | bytes 2359304 | tf_op jit(solution)/shard_map/ppermute | solution.py:68
  162.6 11.3 %all-to-all-start = ((bf16[4,96,512]{2,1,0:T(8,128)(2,1)}), bf16[4,96,512]{2,1,0:T(8,128)(2,1)S(1)}, u32[]{:S(2)}, u32[]{:S(2)}) async-start(bf16[4,96,512]{2,1,0:T(8,128)(2,1)} %bitcast.76), calls=%async_computation | async-start | bytes 786432 | tf_op jit(solution)/shard_map/all_to_all | solution.py:145
  167.8 11.3 %collective-permute-start.28 = (bf16[62,1024]{1,0:T(8,128)(2,1)S(1)}, bf16[62,1024]{1,0:T(8,128)(2,1)S(1)}, u32[]{:S(2)}, u32[]{:S(2)}) collective-permute-start(bf16[62,1024]{1,0:T(8,128)(2,1)S(1)} %copy-done.3), channel_id=1, source_target_pairs={{0,2},{1,3},{2,0},{3,1},{4,6},{5,7},{6,4},{7,5},{8,10},{9,11},{10,... | collective-permute-start | bytes 380936 | tf_op jit(solution)/shard_map/ppermute | solution.py:106
  (14 other events, 200.4 us)

commit v18 on v10

--- a/solution.py
+++ b/solution.py
@@ -41,11 +41,12 @@
             rings[chunk] = lax.ppermute(rings[chunk], "feat", ring)
             first_block = source_block * blocks_here + chunk * chunk_blocks
             parts.append((rings[chunk], first_block + group * blocks_piece + chunk_range))
-            for shift in range(1, share_count):
-                pairs = [(source, (source + shift) % group_count) for source in range(group_count)]
-                forwarded = lax.ppermute(rings[chunk], "groups", pairs)
-                from_group = (group - shift) % group_count
-                parts.append((forwarded, first_block + from_group * blocks_piece + chunk_range))
+        arrived = jnp.concatenate(rings, 0) if chunk_count > 1 else rings[0]
+        for shift in range(1, share_count):
+            pairs = [(source, (source + shift) % group_count) for source in range(group_count)]
+            forwarded = lax.ppermute(arrived, "groups", pairs)
+            from_group = (group - shift) % group_count
+            parts.append((forwarded, source_block * blocks_here + from_group * blocks_piece + block_range))
     travelling = rings
     return parts, travelling
 

time: 179 us -> 184 us (1.028)
  waiting for transfers between devices: 71.9 us -> 104 us
  starting transfers between devices: 41.8 us -> 25.5 us
  local copies, waits for them, and re-layouts: 42.2 us -> 30.1 us
    ppermute x12, waiting for transfers between devices: 17.3 us -> 39.6 us  [weight_parts(): rings[chunk] = lax.ppermute(rings[chunk], 'feat', ring)]
    ppermute x3, waiting for transfers between devices: 36.5 us -> 56.3 us  [exchange_rows(): lax.ppermute(piece, 'feat', [(source, (source + shift) % feat_count) for...]
    ppermute x12 -> x3, starting transfers between devices: 17 us -> 5.15 us  [weight_parts(): forwarded = lax.ppermute(arrived, 'groups', pairs)]
    ppermute x12 -> x3, waiting for transfers between devices: 10.3 us -> 0.01 us  [weight_parts(): forwarded = lax.ppermute(arrived, 'groups', pairs)]
    unnamed x37 -> x32, local copies, waits for them, and re-layouts: 22.5 us -> 13.7 us
    ppermute x12, starting transfers between devices: 16 us -> 11.2 us  [weight_parts(): rings[chunk] = lax.ppermute(rings[chunk], 'feat', ring)]
    squeeze x1, local copies, waits for them, and re-layouts: 12 us -> 8.15 us  [on_device(): pooled_second[0]]
  transfers between devices with their start and end apart: 31 -> 22, of which waited for: 13 -> 13; matrix products, arithmetic and copies ran while one was open for 26% -> 20% of each run, Pallas kernels for 0% -> 0%
where the time goes in v18:
time: 184 us; the launch traced here: 183 us
  waiting for transfers between devices  104 us (57%)
  local copies, waits for them, and re-layouts  30.1 us (16%)
  starting transfers between devices  25.5 us (14%)
  matrix products  17.4 us (9%)
  other arithmetic  6.13 us (3%)
    ppermute x3, waiting for transfers between devices, exchange_rows(): lax.ppermute(piece, 'feat', [(source, (source + shift) % feat_count) for...  56.3 us
    ppermute x12, waiting for transfers between devices, weight_parts(): rings[chunk] = lax.ppermute(rings[chunk], 'feat', ring)  39.6 us
    unnamed x32, local copies, waits for them, and re-layouts  13.7 us
    ppermute x12, starting transfers between devices, weight_parts(): rings[chunk] = lax.ppermute(rings[chunk], 'feat', ring)  11.2 us
    squeeze x1, local copies, waits for them, and re-layouts, on_device(): pooled_second[0]  8.15 us
    dot_general x1, matrix products, on_device(): jnp.dot(crossed, weights[:, 2 * rank:], preferred_element_type=jnp.float32)  7.09 us
    all_to_all x1, waiting for transfers between devices, on_device(): lax.all_to_all(compressed, 'tower', split_axis=0, concat_axis=1, tiled=True)  5.38 us
    ppermute x3, starting transfers between devices, weight_parts(): forwarded = lax.ppermute(arrived, 'groups', pairs)  5.15 us
  transfers between devices with their start and end apart: 22, of which 13 were waited for; matrix products, arithmetic and copies ran while one was open for 20% of the time, Pallas kernels for 0%

profile of v18, /device:TPU:0, one launch (start us, length us, event | category | flops | bytes accessed | tf_op | source)
XLA Modules:
  0.0 183.2 jit_solution(6428423437346709811)
XLA Ops:
  0.0 3.3 %pad_maximum_fusion = (bf16[1024,1024]{1,0:T(8,128)(2,1)S(1)}, bf16[4096,1024]{1,0:T(8,128)(2,1)}) fusion(bf16[1024,512]{1,0:T(8,128)(2,1)} %bitcast.120, bf16[1024,256]{1,0:T(8,128)(2,1)} %bitcast.121, bf16[1024,256]{1,0:T(8,128)(2,1)} %bitcast.122), kind=kLoop, calls=%fused_computation.16 | loop fusion | flops 6291455 | bytes 6291456 | tf_op jit(solution)/shard_map/concatenate | solution.py:109
  4.4 3.0 %collective-permute-start = (bf16[128,1024]{1,0:T(8,128)(2,1)}, bf16[128,1024]{1,0:T(8,128)(2,1)}, u32[]{:S(2)}, u32[]{:S(2)}) collective-permute-start(bf16[128,1024]{1,0:T(8,128)(2,1)} %get-tuple-element.11), channel_id=1, source_target_pairs={{0,4},{4,8},{8,12},{12,0},{1,5},{5,9},{9,13},{13,1},{2,6},{6,10},{... | collective-permute-start | bytes 786440 | tf_op jit(solution)/shard_map/ppermute | solution.py:41
  14.4 8.1 %copy_bitcast_fusion = (bf16[4,1536,128]{2,0,1:T(4,128)(2,1)S(1)}, bf16[4,1536,128]{2,0,1:T(4,128)(2,1)S(1)}) fusion(bf16[1,4,1536,128]{3,2,1,0:T(8,128)(2,1)S(1)} %copy-done.2, bf16[1,4,1536,128]{3,2,1,0:T(8,128)(2,1)S(1)} %copy-done.3), kind=kLoop, calls=%fused_computation.17 | loop fusion | bytes 6291456 | tf_op jit(solution)/shard_map/squeeze | solution.py:113
  22.6 1.8 collective-permute-start.1
  26.0 2.0 %collective-permute-done.6 = bf16[128,1024]{1,0:T(8,128)(2,1)S(1)} collective-permute-done((bf16[128,1024]{1,0:T(8,128)(2,1)}, bf16[128,1024]{1,0:T(8,128)(2,1)S(1)}, u32[]{:S(2)}, u32[]{:S(2)}) %collective-permute-start.6) | collective-permute-done | bytes 262176 | tf_op jit(solution)/shard_map/ppermute | solution.py:41
  28.0 5.7 %collective-permute-done.9 = bf16[128,1024]{1,0:T(8,128)(2,1)} collective-permute-done((bf16[128,1024]{1,0:T(8,128)(2,1)}, bf16[128,1024]{1,0:T(8,128)(2,1)}, u32[]{:S(2)}, u32[]{:S(2)}) %collective-permute-start.9) | collective-permute-done | bytes 262176 | tf_op jit(solution)/shard_map/ppermute | solution.py:41
  34.9 1.8 collective-permute-start.15
  41.4 3.4 %collective-permute-done.4 = bf16[128,1024]{1,0:T(8,128)(2,1)S(1)} collective-permute-done((bf16[128,1024]{1,0:T(8,128)(2,1)}, bf16[128,1024]{1,0:T(8,128)(2,1)S(1)}, u32[]{:S(2)}, u32[]{:S(2)}) %collective-permute-start.4) | collective-permute-done | bytes 262176 | tf_op jit(solution)/shard_map/ppermute | solution.py:41
  44.9 5.6 %collective-permute-done.7 = bf16[128,1024]{1,0:T(8,128)(2,1)S(1)} collective-permute-done((bf16[128,1024]{1,0:T(8,128)(2,1)S(1)}, bf16[128,1024]{1,0:T(8,128)(2,1)S(1)}, u32[]{:S(2)}, u32[]{:S(2)}) %collective-permute-start.7) | collective-permute-done | bytes 262176 | tf_op jit(solution)/shard_map/ppermute | solution.py:41
  50.5 5.6 %collective-permute-done.10 = bf16[128,1024]{1,0:T(8,128)(2,1)S(1)} collective-permute-done((bf16[128,1024]{1,0:T(8,128)(2,1)}, bf16[128,1024]{1,0:T(8,128)(2,1)S(1)}, u32[]{:S(2)}, u32[]{:S(2)}) %collective-permute-start.10) | collective-permute-done | bytes 262176 | tf_op jit(solution)/shard_map/ppermute | solution.py:41
  58.6 3.1 %collective-permute-done.2 = bf16[128,1024]{1,0:T(8,128)(2,1)S(1)} collective-permute-done((bf16[128,1024]{1,0:T(8,128)(2,1)S(1)}, bf16[128,1024]{1,0:T(8,128)(2,1)S(1)}, u32[]{:S(2)}, u32[]{:S(2)}) %collective-permute-start.2) | collective-permute-done | bytes 262176 | tf_op jit(solution)/shard_map/ppermute | solution.py:41
  61.7 1.8 collective-permute-start.16
  63.5 3.9 %collective-permute-done.5 = bf16[128,1024]{1,0:T(8,128)(2,1)S(1)} collective-permute-done((bf16[128,1024]{1,0:T(8,128)(2,1)S(1)}, bf16[128,1024]{1,0:T(8,128)(2,1)S(1)}, u32[]{:S(2)}, u32[]{:S(2)}) %collective-permute-start.5) | collective-permute-done | bytes 262176 | tf_op jit(solution)/shard_map/ppermute | solution.py:41
  67.3 5.6 %collective-permute-done.8 = bf16[128,1024]{1,0:T(8,128)(2,1)S(1)} collective-permute-done((bf16[128,1024]{1,0:T(8,128)(2,1)S(1)}, bf16[128,1024]{1,0:T(8,128)(2,1)S(1)}, u32[]{:S(2)}, u32[]{:S(2)}) %collective-permute-start.8) | collective-permute-done | bytes 262176 | tf_op jit(solution)/shard_map/ppermute | solution.py:41
  72.9 4.8 %collective-permute-done.11 = bf16[128,1024]{1,0:T(8,128)(2,1)S(1)} collective-permute-done((bf16[128,1024]{1,0:T(8,128)(2,1)S(1)}, bf16[128,1024]{1,0:T(8,128)(2,1)S(1)}, u32[]{:S(2)}, u32[]{:S(2)}) %collective-permute-start.11) | collective-permute-done | bytes 262176 | tf_op jit(solution)/shard_map/ppermute | solution.py:41
  80.9 1.8 collective-permute-start.14
  91.4 9.3 %collective-permute-done.14 = bf16[8,384,128]{2,0,1:T(8,128)(2,1)S(1)} collective-permute-done((bf16[8,384,128]{2,0,1:T(8,128)(2,1)S(1)}, bf16[8,384,128]{2,0,1:T(8,128)(2,1)S(1)}, u32[]{:S(2)}, u32[]{:S(2)}) %collective-permute-start.14) | collective-permute-done | bytes 786464 | tf_op jit(solution)/shard_map/ppermute | solution.py:69
  101.8 47.0 %collective-permute-done.13 = bf16[8,384,128]{2,0,1:T(8,128)(2,1)S(1)} collective-permute-done((bf16[8,384,128]{2,0,1:T(8,128)(2,1)S(1)}, bf16[8,384,128]{2,0,1:T(8,128)(2,1)S(1)}, u32[]{:S(2)}, u32[]{:S(2)}) %collective-permute-start.13) | collective-permute-done | bytes 786464 | tf_op jit(solution)/shard_map/ppermute | solution.py:69
  155.2 3.3 %fusion.24 = bf16[384,256]{1,0:T(8,128)(2,1)} fusion(bf16[4096,1024]{1,0:T(8,128)(2,1)} %constant_dynamic-update-slice_fusion, bf16[48,8,32,128]{3,2,1,0:T(8,128)(2,1)S(1)} %bitcast.116), kind=kOutput, calls=%fused_computation.28 | convolution fusion | flops 805404672 | bytes 5439488 | tf_op jit(solution)/shard_map/dot_general | solution.py:133
  158.6 7.1 %fusion.15 = bf16[384,512]{1,0:T(8,128)(2,1)} fusion(bf16[4096,1024]{1,0:T(8,128)(2,1)} %constant_dynamic-update-slice_fusion, bf16[384,256]{1,0:T(8,128)(2,1)} %fusion.24, f32[4096]{0:T(1024)S(1)} %bitcast.124, bf16[48,8,32,128]{3,2,1,0:T(8,128)(2,1)S(1)} %bitcast.117, f32[512]{0:T(512)S(1)} %bitcast.125), kind=kOutput, calls=%fused_computation.21 | convolution fusion | flops 2424176640 | bytes 10045440 | tf_op jit(solution)/shard_map/dot_general | solution.py:144
  165.7 3.6 %all-to-all-start = ((bf16[4,96,512]{2,1,0:T(8,128)(2,1)}), bf16[4,96,512]{2,1,0:T(8,128)(2,1)S(1)}, u32[]{:S(2)}, u32[]{:S(2)}) async-start(bf16[4,96,512]{2,1,0:T(8,128)(2,1)} %bitcast.55), calls=%async_computation | async-start | bytes 786432 | tf_op jit(solution)/shard_map/all_to_all | solution.py:146
  169.3 1.7 collective-permute-start.20
  171.8 5.4 %all-to-all-done = bf16[4,96,512]{2,1,0:T(8,128)(2,1)S(1)} async-done(((bf16[4,96,512]{2,1,0:T(8,128)(2,1)}), bf16[4,96,512]{2,1,0:T(8,128)(2,1)S(1)}, u32[]{:S(2)}, u32[]{:S(2)}) %all-to-all-start) | async-done | bytes 393248 | tf_op jit(solution)/shard_map/all_to_all | solution.py:146
  180.0 2.3 %collective-permute-done.19 = bf16[62,1024]{1,0:T(8,128)(2,1)S(1)} collective-permute-done((bf16[62,1024]{1,0:T(8,128)(2,1)S(1)}, bf16[62,1024]{1,0:T(8,128)(2,1)S(1)}, u32[]{:S(2)}, u32[]{:S(2)}) %collective-permute-start.19) | collective-permute-done | bytes 127008 | tf_op jit(solution)/shard_map/ppermute | solution.py:107
  (110 shorter events, 41.7 us)
Async XLA Ops:
  4.4 18.3 %collective-permute-start = (bf16[128,1024]{1,0:T(8,128)(2,1)}, bf16[128,1024]{1,0:T(8,128)(2,1)}, u32[]{:S(2)}, u32[]{:S(2)}) collective-permute-start(bf16[128,1024]{1,0:T(8,128)(2,1)} %get-tuple-element.11), channel_id=1, source_target_pairs={{0,4},{4,8},{8,12},{12,0},{1,5},{5,9},{9,13},{13,1},{2,6},{6,10},{... | collective-permute-start | bytes 786440 | tf_op jit(solution)/shard_map/ppermute | solution.py:41
  7.4 17.0 %collective-permute-start.3 = (bf16[128,1024]{1,0:T(8,128)(2,1)}, bf16[128,1024]{1,0:T(8,128)(2,1)}, u32[]{:S(2)}, u32[]{:S(2)}) collective-permute-start(bf16[128,1024]{1,0:T(8,128)(2,1)} %get-tuple-element.10), channel_id=1, source_target_pairs={{0,4},{4,8},{8,12},{12,0},{1,5},{5,9},{9,13},{13,1},{2,6},{6,10},{... | collective-permute-start | bytes 786440 | tf_op jit(solution)/shard_map/ppermute | solution.py:41
  9.0 19.0 %collective-permute-start.6 = (bf16[128,1024]{1,0:T(8,128)(2,1)}, bf16[128,1024]{1,0:T(8,128)(2,1)S(1)}, u32[]{:S(2)}, u32[]{:S(2)}) collective-permute-start(bf16[128,1024]{1,0:T(8,128)(2,1)} %get-tuple-element.12), channel_id=1, source_target_pairs={{0,4},{4,8},{8,12},{12,0},{1,5},{5,9},{9,13},{13,1},{2,6},{6,10},{... | collective-permute-start | bytes 786440 | tf_op jit(solution)/shard_map/ppermute | solution.py:41
  10.5 23.2 %collective-permute-start.9 = (bf16[128,1024]{1,0:T(8,128)(2,1)}, bf16[128,1024]{1,0:T(8,128)(2,1)}, u32[]{:S(2)}, u32[]{:S(2)}) collective-permute-start(bf16[128,1024]{1,0:T(8,128)(2,1)} %get-tuple-element.9), channel_id=1, source_target_pairs={{0,4},{4,8},{8,12},{12,0},{1,5},{5,9},{9,13},{13,1},{2,6},{6,10},{... | collective-permute-start | bytes 786440 | tf_op jit(solution)/shard_map/ppermute | solution.py:41
  22.6 17.5 %collective-permute-start.1 = (bf16[128,1024]{1,0:T(8,128)(2,1)}, bf16[128,1024]{1,0:T(8,128)(2,1)S(1)}, u32[]{:S(2)}, u32[]{:S(2)}) collective-permute-start(bf16[128,1024]{1,0:T(8,128)(2,1)} %collective-permute-done), channel_id=1, source_target_pairs={{0,4},{4,8},{8,12},{12,0},{1,5},{5,9},{9,13},{13,1},{2,6},{6,10},{... | collective-permute-start | bytes 786440 | tf_op jit(solution)/shard_map/ppermute | solution.py:41
  24.4 20.4 %collective-permute-start.4 = (bf16[128,1024]{1,0:T(8,128)(2,1)}, bf16[128,1024]{1,0:T(8,128)(2,1)S(1)}, u32[]{:S(2)}, u32[]{:S(2)}) collective-permute-start(bf16[128,1024]{1,0:T(8,128)(2,1)} %collective-permute-done.3), channel_id=1, source_target_pairs={{0,4},{4,8},{8,12},{12,0},{1,5},{5,9},{9,13},{13,1},{2,6},{6,10},{... | collective-permute-start | bytes 786440 | tf_op jit(solution)/shard_map/ppermute | solution.py:41
  28.0 22.5 %collective-permute-start.7 = (bf16[128,1024]{1,0:T(8,128)(2,1)S(1)}, bf16[128,1024]{1,0:T(8,128)(2,1)S(1)}, u32[]{:S(2)}, u32[]{:S(2)}) collective-permute-start(bf16[128,1024]{1,0:T(8,128)(2,1)S(1)} %collective-permute-done.6), channel_id=1, source_target_pairs={{0,4},{4,8},{8,12},{12,0},{1,5},{5,9},{9,13},{13,1},{2,6},{6,10},{... | collective-permute-start | bytes 786440 | tf_op jit(solution)/shard_map/ppermute | solution.py:41
  33.7 22.4 %collective-permute-start.10 = (bf16[128,1024]{1,0:T(8,128)(2,1)}, bf16[128,1024]{1,0:T(8,128)(2,1)S(1)}, u32[]{:S(2)}, u32[]{:S(2)}) collective-permute-start(bf16[128,1024]{1,0:T(8,128)(2,1)} %collective-permute-done.9), channel_id=1, source_target_pairs={{0,4},{4,8},{8,12},{12,0},{1,5},{5,9},{9,13},{13,1},{2,6},{6,10},{... | collective-permute-start | bytes 786440 | tf_op jit(solution)/shard_map/ppermute | solution.py:41
  34.9 48.7 %collective-permute-start.15 = (bf16[512,1024]{1,0:T(8,128)(2,1)S(1)}, bf16[512,1024]{1,0:T(8,128)(2,1)S(1)}, u32[]{:S(2)}, u32[]{:S(2)}) collective-permute-start(bf16[512,1024]{1,0:T(8,128)(2,1)S(1)} %pad_maximum_fusion.1), channel_id=1, source_target_pairs={{0,16},{16,0},{1,17},{17,1},{2,18},{18,2},{3,19},{19,3},{4,20},{20... | collective-permute-start | bytes 3145736 | tf_op jit(solution)/shard_map/ppermute | solution.py:47
  40.1 21.6 %collective-permute-start.2 = (bf16[128,1024]{1,0:T(8,128)(2,1)S(1)}, bf16[128,1024]{1,0:T(8,128)(2,1)S(1)}, u32[]{:S(2)}, u32[]{:S(2)}) collective-permute-start(bf16[128,1024]{1,0:T(8,128)(2,1)S(1)} %collective-permute-done.1), channel_id=1, source_target_pairs={{0,4},{4,8},{8,12},{12,0},{1,5},{5,9},{9,13},{13,1},{2,6},{6,10},{... | collective-permute-start | bytes 786440 | tf_op jit(solution)/shard_map/ppermute | solution.py:41
  44.8 22.5 %collective-permute-start.5 = (bf16[128,1024]{1,0:T(8,128)(2,1)S(1)}, bf16[128,1024]{1,0:T(8,128)(2,1)S(1)}, u32[]{:S(2)}, u32[]{:S(2)}) collective-permute-start(bf16[128,1024]{1,0:T(8,128)(2,1)S(1)} %collective-permute-done.4), channel_id=1, source_target_pairs={{0,4},{4,8},{8,12},{12,0},{1,5},{5,9},{9,13},{13,1},{2,6},{6,10},{... | collective-permute-start | bytes 786440 | tf_op jit(solution)/shard_map/ppermute | solution.py:41
  50.5 22.5 %collective-permute-start.8 = (bf16[128,1024]{1,0:T(8,128)(2,1)S(1)}, bf16[128,1024]{1,0:T(8,128)(2,1)S(1)}, u32[]{:S(2)}, u32[]{:S(2)}) collective-permute-start(bf16[128,1024]{1,0:T(8,128)(2,1)S(1)} %collective-permute-done.7), channel_id=1, source_target_pairs={{0,4},{4,8},{8,12},{12,0},{1,5},{5,9},{9,13},{13,1},{2,6},{6,10},{... | collective-permute-start | bytes 786440 | tf_op jit(solution)/shard_map/ppermute | solution.py:41
  56.1 21.6 %collective-permute-start.11 = (bf16[128,1024]{1,0:T(8,128)(2,1)S(1)}, bf16[128,1024]{1,0:T(8,128)(2,1)S(1)}, u32[]{:S(2)}, u32[]{:S(2)}) collective-permute-start(bf16[128,1024]{1,0:T(8,128)(2,1)S(1)} %collective-permute-done.10), channel_id=1, source_target_pairs={{0,4},{4,8},{8,12},{12,0},{1,5},{5,9},{9,13},{13,1},{2,6},{6,10},{... | collective-permute-start | bytes 786440 | tf_op jit(solution)/shard_map/ppermute | solution.py:41
  61.7 27.2 %collective-permute-start.16 = (bf16[512,1024]{1,0:T(8,128)(2,1)S(1)}, bf16[512,1024]{1,0:T(8,128)(2,1)S(1)}, u32[]{:S(2)}, u32[]{:S(2)}) collective-permute-start(bf16[512,1024]{1,0:T(8,128)(2,1)S(1)} %pad_maximum_fusion.2), channel_id=1, source_target_pairs={{0,16},{16,0},{1,17},{17,1},{2,18},{18,2},{3,19},{19,3},{4,20},{20... | collective-permute-start | bytes 3145736 | tf_op jit(solution)/shard_map/ppermute | solution.py:47
  77.8 76.3 %collective-permute-start.17 = (bf16[512,1024]{1,0:T(8,128)(2,1)S(1)}, bf16[512,1024]{1,0:T(8,128)(2,1)S(1)}, u32[]{:S(2)}, u32[]{:S(2)}) collective-permute-start(bf16[512,1024]{1,0:T(8,128)(2,1)S(1)} %pad_maximum_fusion.3), channel_id=1, source_target_pairs={{0,16},{16,0},{1,17},{17,1},{2,18},{18,2},{3,19},{19,3},{4,20},{20... | collective-permute-start | bytes 3145736 | tf_op jit(solution)/shard_map/ppermute | solution.py:47
  80.9 19.8 %collective-permute-start.14 = (bf16[8,384,128]{2,0,1:T(8,128)(2,1)S(1)}, bf16[8,384,128]{2,0,1:T(8,128)(2,1)S(1)}, u32[]{:S(2)}, u32[]{:S(2)}) collective-permute-start(bf16[8,384,128]{2,0,1:T(8,128)(2,1)S(1)} %pad_maximum_fusion.6), channel_id=1, source_target_pairs={{0,12},{4,0},{8,4},{12,8},{1,13},{5,1},{9,5},{13,9},{2,14},{6,2},{... | collective-permute-start | bytes 2359304 | tf_op jit(solution)/shard_map/ppermute | solution.py:69
  83.1 65.7 %collective-permute-start.13 = (bf16[8,384,128]{2,0,1:T(8,128)(2,1)S(1)}, bf16[8,384,128]{2,0,1:T(8,128)(2,1)S(1)}, u32[]{:S(2)}, u32[]{:S(2)}) collective-permute-start(bf16[8,384,128]{2,0,1:T(8,128)(2,1)S(1)} %pad_maximum_fusion.5), channel_id=1, source_target_pairs={{0,8},{4,12},{8,0},{12,4},{1,9},{5,13},{9,1},{13,5},{2,10},{6,14},... | collective-permute-start | bytes 2359304 | tf_op jit(solution)/shard_map/ppermute | solution.py:69
  83.6 66.3 %collective-permute-start.12 = (bf16[8,384,128]{2,0,1:T(8,128)(2,1)S(1)}, bf16[8,384,128]{2,0,1:T(8,128)(2,1)S(1)}, u32[]{:S(2)}, u32[]{:S(2)}) collective-permute-start(bf16[8,384,128]{2,0,1:T(8,128)(2,1)S(1)} %pad_maximum_fusion.4), channel_id=1, source_target_pairs={{0,4},{4,8},{8,12},{12,0},{1,5},{5,9},{9,13},{13,1},{2,6},{6,10},{... | collective-permute-start | bytes 2359304 | tf_op jit(solution)/shard_map/ppermute | solution.py:69
  158.6 20.5 %copy-start.4 = (bf16[96,128]{1,0:T(8,128)(2,1)S(1)}, bf16[96,128]{1,0:T(8,128)(2,1)}, u32[]{:S(2)}) copy-start(bf16[96,128]{1,0:T(8,128)(2,1)} %param.21) | copy-start | bytes 73732
  165.7 16.6 %copy-start.6 = (f32[1024]{0:T(1024)S(1)}, f32[1024]{0:T(1024)}, u32[]{:S(2)}) copy-start(f32[1024]{0:T(1024)} %param.23) | copy-start | bytes 12292
  165.7 11.5 %all-to-all-start = ((bf16[4,96,512]{2,1,0:T(8,128)(2,1)}), bf16[4,96,512]{2,1,0:T(8,128)(2,1)S(1)}, u32[]{:S(2)}, u32[]{:S(2)}) async-start(bf16[4,96,512]{2,1,0:T(8,128)(2,1)} %bitcast.55), calls=%async_computation | async-start | bytes 786432 | tf_op jit(solution)/shard_map/all_to_all | solution.py:146
  169.3 10.4 %collective-permute-start.20 = (bf16[62,1024]{1,0:T(8,128)(2,1)S(1)}, bf16[62,1024]{1,0:T(8,128)(2,1)S(1)}, u32[]{:S(2)}, u32[]{:S(2)}) collective-permute-start(bf16[62,1024]{1,0:T(8,128)(2,1)S(1)} %copy-done.5), channel_id=1, source_target_pairs={{0,3},{1,0},{2,1},{3,2},{4,7},{5,4},{6,5},{7,6},{8,11},{9,8},{10,9... | collective-permute-start | bytes 380936 | tf_op jit(solution)/shard_map/ppermute | solution.py:107
  171.0 8.4 %collective-permute-start.18 = (bf16[62,1024]{1,0:T(8,128)(2,1)S(1)}, bf16[62,1024]{1,0:T(8,128)(2,1)S(1)}, u32[]{:S(2)}, u32[]{:S(2)}) collective-permute-start(bf16[62,1024]{1,0:T(8,128)(2,1)S(1)} %copy-done.5), channel_id=1, source_target_pairs={{0,1},{1,2},{2,3},{3,0},{4,5},{5,6},{6,7},{7,4},{8,9},{9,10},{10,1... | collective-permute-start | bytes 380936 | tf_op jit(solution)/shard_map/ppermute | solution.py:107
  171.0 11.3 %collective-permute-start.19 = (bf16[62,1024]{1,0:T(8,128)(2,1)S(1)}, bf16[62,1024]{1,0:T(8,128)(2,1)S(1)}, u32[]{:S(2)}, u32[]{:S(2)}) collective-permute-start(bf16[62,1024]{1,0:T(8,128)(2,1)S(1)} %copy-done.5), channel_id=1, source_target_pairs={{0,2},{1,3},{2,0},{3,1},{4,6},{5,7},{6,4},{7,5},{8,10},{9,11},{10,... | collective-permute-start | bytes 380936 | tf_op jit(solution)/shard_map/ppermute | solution.py:107
  (7 other events, 82.4 us)

commit v19 on v10

--- a/solution.py
+++ b/solution.py
@@ -34,10 +34,11 @@
         lax.slice_in_dim(travelling, chunk * chunk_rows, (chunk + 1) * chunk_rows, axis=0)
         for chunk in range(chunk_count)
     ]
-    ring = [(source, (source + 1) % feat_count) for source in range(feat_count)]
     for step in range(1, feat_count):
-        source_block = (owner - step) % feat_count
         for chunk in range(chunk_count):
+            way = 1 if chunk % 2 == 0 else -1
+            ring = [(source, (source + way) % feat_count) for source in range(feat_count)]
+            source_block = (owner - way * step) % feat_count
             rings[chunk] = lax.ppermute(rings[chunk], "feat", ring)
             first_block = source_block * blocks_here + chunk * chunk_blocks
             parts.append((rings[chunk], first_block + group * blocks_piece + chunk_range))

time: 179 us -> 181 us (1.011)
  starting transfers between devices: 41.8 us -> 45.5 us
    ppermute x12, starting transfers between devices: 16 us -> 20.4 us  [weight_parts(): rings[chunk] = lax.ppermute(rings[chunk], 'feat', ring)]
    ppermute x12, waiting for transfers between devices: 17.3 us -> 15.1 us  [weight_parts(): rings[chunk] = lax.ppermute(rings[chunk], 'feat', ring)]
  transfers between devices with their start and end apart: 31 -> 31, of which waited for: 13 -> 12; matrix products, arithmetic and copies ran while one was open for 26% -> 25% of each run, Pallas kernels for 0% -> 0%
where the time goes in v19:
time: 181 us
  waiting for transfers between devices  70.9 us (39%)
  starting transfers between devices  45.5 us (25%)
  local copies, waits for them, and re-layouts  42.2 us (23%)
  matrix products  17.4 us (10%)
  other arithmetic  4.67 us (3%)
    ppermute x3, waiting for transfers between devices, exchange_rows(): lax.ppermute(piece, 'feat', [(source, (source + shift) % feat_count) for...  36.8 us
    unnamed x37, local copies, waits for them, and re-layouts  22.5 us
    ppermute x12, starting transfers between devices, weight_parts(): rings[chunk] = lax.ppermute(rings[chunk], 'feat', ring)  20.4 us
    ppermute x12, starting transfers between devices, weight_parts(): forwarded = lax.ppermute(rings[chunk], 'groups', pairs)  16.3 us
    ppermute x12, waiting for transfers between devices, weight_parts(): rings[chunk] = lax.ppermute(rings[chunk], 'feat', ring)  15.1 us
    squeeze x1, local copies, waits for them, and re-layouts, on_device(): pooled_second[0]  12 us
    ppermute x12, waiting for transfers between devices, weight_parts(): forwarded = lax.ppermute(rings[chunk], 'groups', pairs)  11.4 us
    dot_general x1, matrix products, on_device(): jnp.dot(crossed, weights[:, 2 * rank:], preferred_element_type=jnp.float32)  7.07 us
  transfers between devices with their start and end apart: 31, of which 12 were waited for; matrix products, arithmetic and copies ran while one was open for 25% of the time, Pallas kernels for 0%

profile of v19, /device:TPU:0, one launch (start us, length us, event | category | flops | bytes accessed | tf_op | source)
XLA Modules:
  0.0 181.0 jit_solution(8334762665704480261)
XLA Ops:
  0.0 3.2 %pad_maximum_fusion = (bf16[1024,1024]{1,0:T(8,128)(2,1)S(1)}, bf16[4096,1024]{1,0:T(8,128)(2,1)}) fusion(bf16[1024,512]{1,0:T(8,128)(2,1)} %bitcast.138, bf16[1024,256]{1,0:T(8,128)(2,1)} %bitcast.139, bf16[1024,256]{1,0:T(8,128)(2,1)} %bitcast.140), kind=kLoop, calls=%fused_computation.16 | loop fusion | flops 6291455 | bytes 6291456 | tf_op jit(solution)/shard_map/concatenate | solution.py:109
  4.1 3.0 %collective-permute-start = (bf16[128,1024]{1,0:T(8,128)(2,1)}, bf16[128,1024]{1,0:T(8,128)(2,1)}, u32[]{:S(2)}, u32[]{:S(2)}) collective-permute-start(bf16[128,1024]{1,0:T(8,128)(2,1)} %get-tuple-element.11), channel_id=1, source_target_pairs={{0,4},{4,8},{8,12},{12,0},{1,5},{5,9},{9,13},{13,1},{2,6},{6,10},{... | collective-permute-start | bytes 786440 | tf_op jit(solution)/shard_map/ppermute | solution.py:42
  7.1 2.0 %collective-permute-start.3 = (bf16[128,1024]{1,0:T(8,128)(2,1)}, bf16[128,1024]{1,0:T(8,128)(2,1)}, u32[]{:S(2)}, u32[]{:S(2)}) collective-permute-start(bf16[128,1024]{1,0:T(8,128)(2,1)} %get-tuple-element.10), channel_id=1, source_target_pairs={{0,12},{4,0},{8,4},{12,8},{1,13},{5,1},{9,5},{13,9},{2,14},{6,2},{... | collective-permute-start | bytes 786440 | tf_op jit(solution)/shard_map/ppermute | solution.py:42
  9.2 3.8 %collective-permute-start.9 = (bf16[128,1024]{1,0:T(8,128)(2,1)S(1)}, bf16[128,1024]{1,0:T(8,128)(2,1)}, u32[]{:S(2)}, u32[]{:S(2)}) collective-permute-start(bf16[128,1024]{1,0:T(8,128)(2,1)S(1)} %get-tuple-element.9), channel_id=1, source_target_pairs={{0,12},{4,0},{8,4},{12,8},{1,13},{5,1},{9,5},{13,9},{2,14},{6,2},{... | collective-permute-start | bytes 786440 | tf_op jit(solution)/shard_map/ppermute | solution.py:42
  13.3 12.0 %copy_bitcast_fusion = (bf16[4,1536,128]{2,0,1:T(4,128)(2,1)S(1)}, bf16[4,1536,128]{2,0,1:T(4,128)(2,1)S(1)}) fusion(bf16[1,4,1536,128]{3,2,1,0:T(8,128)(2,1)} %param.14, bf16[1,4,1536,128]{3,2,1,0:T(8,128)(2,1)} %param.13), kind=kLoop, calls=%fused_computation.17 | loop fusion | bytes 6291456 | tf_op jit(solution)/shard_map/squeeze | solution.py:113
  25.4 1.8 collective-permute-start.15
  32.7 3.8 %collective-permute-start.4 = (bf16[128,1024]{1,0:T(8,128)(2,1)}, bf16[128,1024]{1,0:T(8,128)(2,1)S(1)}, u32[]{:S(2)}, u32[]{:S(2)}) collective-permute-start(bf16[128,1024]{1,0:T(8,128)(2,1)} %collective-permute-done.3), channel_id=1, source_target_pairs={{0,12},{4,0},{8,4},{12,8},{1,13},{5,1},{9,5},{13,9},{2,14},{6,2},{... | collective-permute-start | bytes 786440 | tf_op jit(solution)/shard_map/ppermute | solution.py:42
  39.9 3.8 %collective-permute-start.10 = (bf16[128,1024]{1,0:T(8,128)(2,1)}, bf16[128,1024]{1,0:T(8,128)(2,1)S(1)}, u32[]{:S(2)}, u32[]{:S(2)}) collective-permute-start(bf16[128,1024]{1,0:T(8,128)(2,1)} %collective-permute-done.9), channel_id=1, source_target_pairs={{0,12},{4,0},{8,4},{12,8},{1,13},{5,1},{9,5},{13,9},{2,14},{6,2},{... | collective-permute-start | bytes 786440 | tf_op jit(solution)/shard_map/ppermute | solution.py:42
  49.1 3.8 %collective-permute-start.5 = (bf16[128,1024]{1,0:T(8,128)(2,1)S(1)}, bf16[128,1024]{1,0:T(8,128)(2,1)S(1)}, u32[]{:S(2)}, u32[]{:S(2)}) collective-permute-start(bf16[128,1024]{1,0:T(8,128)(2,1)S(1)} %collective-permute-done.4), channel_id=1, source_target_pairs={{0,12},{4,0},{8,4},{12,8},{1,13},{5,1},{9,5},{13,9},{2,14},{6,2},{... | collective-permute-start | bytes 786440 | tf_op jit(solution)/shard_map/ppermute | solution.py:42
  53.4 5.7 %collective-permute-done.10 = bf16[128,1024]{1,0:T(8,128)(2,1)S(1)} collective-permute-done((bf16[128,1024]{1,0:T(8,128)(2,1)}, bf16[128,1024]{1,0:T(8,128)(2,1)S(1)}, u32[]{:S(2)}, u32[]{:S(2)}) %collective-permute-start.10) | collective-permute-done | bytes 262176 | tf_op jit(solution)/shard_map/ppermute | solution.py:42
  61.6 1.9 %collective-permute-start.19 = (bf16[128,1024]{1,0:T(8,128)(2,1)S(1)}, bf16[128,1024]{1,0:T(8,128)(2,1)S(1)}, u32[]{:S(2)}, u32[]{:S(2)}) collective-permute-start(bf16[128,1024]{1,0:T(8,128)(2,1)S(1)} %collective-permute-done.1), channel_id=1, source_target_pairs={{0,16},{16,0},{1,17},{17,1},{2,18},{18,2},{3,19},{19,3},{4,20},{20... | collective-permute-start | bytes 786440 | tf_op jit(solution)/shard_map/ppermute | solution.py:47
  66.4 4.0 %collective-permute-done.5 = bf16[128,1024]{1,0:T(8,128)(2,1)S(1)} collective-permute-done((bf16[128,1024]{1,0:T(8,128)(2,1)S(1)}, bf16[128,1024]{1,0:T(8,128)(2,1)S(1)}, u32[]{:S(2)}, u32[]{:S(2)}) %collective-permute-start.5) | collective-permute-done | bytes 262176 | tf_op jit(solution)/shard_map/ppermute | solution.py:42
  70.4 1.9 %collective-permute-start.21 = (bf16[128,1024]{1,0:T(8,128)(2,1)S(1)}, bf16[128,1024]{1,0:T(8,128)(2,1)S(1)}, u32[]{:S(2)}, u32[]{:S(2)}) collective-permute-start(bf16[128,1024]{1,0:T(8,128)(2,1)S(1)} %collective-permute-done.7), channel_id=1, source_target_pairs={{0,16},{16,0},{1,17},{17,1},{2,18},{18,2},{3,19},{19,3},{4,20},{20... | collective-permute-start | bytes 786440 | tf_op jit(solution)/shard_map/ppermute | solution.py:47
  72.3 3.6 %collective-permute-done.8 = bf16[128,1024]{1,0:T(8,128)(2,1)S(1)} collective-permute-done((bf16[128,1024]{1,0:T(8,128)(2,1)S(1)}, bf16[128,1024]{1,0:T(8,128)(2,1)S(1)}, u32[]{:S(2)}, u32[]{:S(2)}) %collective-permute-start.8) | collective-permute-done | bytes 262176 | tf_op jit(solution)/shard_map/ppermute | solution.py:42
  91.9 4.3 %collective-permute-done.23 = bf16[128,1024]{1,0:T(8,128)(2,1)S(1)} collective-permute-done((bf16[128,1024]{1,0:T(8,128)(2,1)S(1)}, bf16[128,1024]{1,0:T(8,128)(2,1)S(1)}, u32[]{:S(2)}, u32[]{:S(2)}) %collective-permute-start.23) | collective-permute-done | bytes 262176 | tf_op jit(solution)/shard_map/ppermute | solution.py:47
  99.2 2.6 %collective-permute-done.24 = bf16[128,1024]{1,0:T(8,128)(2,1)S(1)} collective-permute-done((bf16[128,1024]{1,0:T(8,128)(2,1)S(1)}, bf16[128,1024]{1,0:T(8,128)(2,1)S(1)}, u32[]{:S(2)}, u32[]{:S(2)}) %collective-permute-start.24) | collective-permute-done | bytes 262176 | tf_op jit(solution)/shard_map/ppermute | solution.py:47
  104.8 2.6 %collective-permute-done.25 = bf16[128,1024]{1,0:T(8,128)(2,1)S(1)} collective-permute-done((bf16[128,1024]{1,0:T(8,128)(2,1)S(1)}, bf16[128,1024]{1,0:T(8,128)(2,1)S(1)}, u32[]{:S(2)}, u32[]{:S(2)}) %collective-permute-start.25) | collective-permute-done | bytes 262176 | tf_op jit(solution)/shard_map/ppermute | solution.py:47
  108.9 1.7 collective-permute-done.26
  112.5 36.8 %collective-permute-done.13 = bf16[8,384,128]{2,0,1:T(8,128)(2,1)S(1)} collective-permute-done((bf16[8,384,128]{2,0,1:T(8,128)(2,1)S(1)}, bf16[8,384,128]{2,0,1:T(8,128)(2,1)S(1)}, u32[]{:S(2)}, u32[]{:S(2)}) %collective-permute-start.13) | collective-permute-done | bytes 786464 | tf_op jit(solution)/shard_map/ppermute | solution.py:69
  153.1 3.3 %fusion.24 = bf16[384,256]{1,0:T(8,128)(2,1)} fusion(bf16[4096,1024]{1,0:T(8,128)(2,1)} %constant_dynamic-update-slice_fusion, bf16[48,8,32,128]{3,2,1,0:T(8,128)(2,1)S(1)} %bitcast.134), kind=kOutput, calls=%fused_computation.28 | convolution fusion | flops 805404672 | bytes 5439488 | tf_op jit(solution)/shard_map/dot_general | solution.py:133
  156.5 7.1 %fusion.15 = bf16[384,512]{1,0:T(8,128)(2,1)} fusion(bf16[4096,1024]{1,0:T(8,128)(2,1)} %constant_dynamic-update-slice_fusion, bf16[384,256]{1,0:T(8,128)(2,1)} %fusion.24, f32[4096]{0:T(1024)S(1)} %bitcast.142, bf16[48,8,32,128]{3,2,1,0:T(8,128)(2,1)S(1)} %bitcast.135, f32[512]{0:T(512)S(1)} %bitcast.143), kind=kOutput, calls=%fused_computation.21 | convolution fusion | flops 2424176640 | bytes 10045440 | tf_op jit(solution)/shard_map/dot_general | solution.py:144
  163.5 3.5 %all-to-all-start = ((bf16[4,96,512]{2,1,0:T(8,128)(2,1)}), bf16[4,96,512]{2,1,0:T(8,128)(2,1)S(1)}, u32[]{:S(2)}, u32[]{:S(2)}) async-start(bf16[4,96,512]{2,1,0:T(8,128)(2,1)} %bitcast.76), calls=%async_computation | async-start | bytes 786432 | tf_op jit(solution)/shard_map/all_to_all | solution.py:146
  169.5 5.4 %all-to-all-done = bf16[4,96,512]{2,1,0:T(8,128)(2,1)S(1)} async-done(((bf16[4,96,512]{2,1,0:T(8,128)(2,1)}), bf16[4,96,512]{2,1,0:T(8,128)(2,1)S(1)}, u32[]{:S(2)}, u32[]{:S(2)}) %all-to-all-start) | async-done | bytes 393248 | tf_op jit(solution)/shard_map/all_to_all | solution.py:146
  177.7 2.3 %collective-permute-done.28 = bf16[62,1024]{1,0:T(8,128)(2,1)S(1)} collective-permute-done((bf16[62,1024]{1,0:T(8,128)(2,1)S(1)}, bf16[62,1024]{1,0:T(8,128)(2,1)S(1)}, u32[]{:S(2)}, u32[]{:S(2)}) %collective-permute-start.28) | collective-permute-done | bytes 127008 | tf_op jit(solution)/shard_map/ppermute | solution.py:107
  (125 shorter events, 56.5 us)
Async XLA Ops:
  4.1 21.3 %collective-permute-start = (bf16[128,1024]{1,0:T(8,128)(2,1)}, bf16[128,1024]{1,0:T(8,128)(2,1)}, u32[]{:S(2)}, u32[]{:S(2)}) collective-permute-start(bf16[128,1024]{1,0:T(8,128)(2,1)} %get-tuple-element.11), channel_id=1, source_target_pairs={{0,4},{4,8},{8,12},{12,0},{1,5},{5,9},{9,13},{13,1},{2,6},{6,10},{... | collective-permute-start | bytes 786440 | tf_op jit(solution)/shard_map/ppermute | solution.py:42
  7.1 20.1 %collective-permute-start.3 = (bf16[128,1024]{1,0:T(8,128)(2,1)}, bf16[128,1024]{1,0:T(8,128)(2,1)}, u32[]{:S(2)}, u32[]{:S(2)}) collective-permute-start(bf16[128,1024]{1,0:T(8,128)(2,1)} %get-tuple-element.10), channel_id=1, source_target_pairs={{0,12},{4,0},{8,4},{12,8},{1,13},{5,1},{9,5},{13,9},{2,14},{6,2},{... | collective-permute-start | bytes 786440 | tf_op jit(solution)/shard_map/ppermute | solution.py:42
  9.2 23.5 %collective-permute-start.6 = (bf16[128,1024]{1,0:T(8,128)(2,1)}, bf16[128,1024]{1,0:T(8,128)(2,1)}, u32[]{:S(2)}, u32[]{:S(2)}) collective-permute-start(bf16[128,1024]{1,0:T(8,128)(2,1)} %get-tuple-element.12), channel_id=1, source_target_pairs={{0,4},{4,8},{8,12},{12,0},{1,5},{5,9},{9,13},{13,1},{2,6},{6,10},{... | collective-permute-start | bytes 786440 | tf_op jit(solution)/shard_map/ppermute | solution.py:42
  9.2 30.7 %collective-permute-start.9 = (bf16[128,1024]{1,0:T(8,128)(2,1)S(1)}, bf16[128,1024]{1,0:T(8,128)(2,1)}, u32[]{:S(2)}, u32[]{:S(2)}) collective-permute-start(bf16[128,1024]{1,0:T(8,128)(2,1)S(1)} %get-tuple-element.9), channel_id=1, source_target_pairs={{0,12},{4,0},{8,4},{12,8},{1,13},{5,1},{9,5},{13,9},{2,14},{6,2},{... | collective-permute-start | bytes 786440 | tf_op jit(solution)/shard_map/ppermute | solution.py:42
  27.2 12.7 %collective-permute-start.16 = (bf16[128,1024]{1,0:T(8,128)(2,1)}, bf16[128,1024]{1,0:T(8,128)(2,1)}, u32[]{:S(2)}, u32[]{:S(2)}) collective-permute-start(bf16[128,1024]{1,0:T(8,128)(2,1)} %collective-permute-done.3), channel_id=1, source_target_pairs={{0,16},{16,0},{1,17},{17,1},{2,18},{18,2},{3,19},{19,3},{4,20},{20... | collective-permute-start | bytes 786440 | tf_op jit(solution)/shard_map/ppermute | solution.py:47
  30.9 18.2 %collective-permute-start.1 = (bf16[128,1024]{1,0:T(8,128)(2,1)}, bf16[128,1024]{1,0:T(8,128)(2,1)S(1)}, u32[]{:S(2)}, u32[]{:S(2)}) collective-permute-start(bf16[128,1024]{1,0:T(8,128)(2,1)} %collective-permute-done), channel_id=1, source_target_pairs={{0,4},{4,8},{8,12},{12,0},{1,5},{5,9},{9,13},{13,1},{2,6},{6,10},{... | collective-permute-start | bytes 786440 | tf_op jit(solution)/shard_map/ppermute | solution.py:42
  32.7 16.4 %collective-permute-start.4 = (bf16[128,1024]{1,0:T(8,128)(2,1)}, bf16[128,1024]{1,0:T(8,128)(2,1)S(1)}, u32[]{:S(2)}, u32[]{:S(2)}) collective-permute-start(bf16[128,1024]{1,0:T(8,128)(2,1)} %collective-permute-done.3), channel_id=1, source_target_pairs={{0,12},{4,0},{8,4},{12,8},{1,13},{5,1},{9,5},{13,9},{2,14},{6,2},{... | collective-permute-start | bytes 786440 | tf_op jit(solution)/shard_map/ppermute | solution.py:42
  39.9 13.5 %collective-permute-start.7 = (bf16[128,1024]{1,0:T(8,128)(2,1)}, bf16[128,1024]{1,0:T(8,128)(2,1)S(1)}, u32[]{:S(2)}, u32[]{:S(2)}) collective-permute-start(bf16[128,1024]{1,0:T(8,128)(2,1)} %collective-permute-done.6), channel_id=1, source_target_pairs={{0,4},{4,8},{8,12},{12,0},{1,5},{5,9},{9,13},{13,1},{2,6},{6,10},{... | collective-permute-start | bytes 786440 | tf_op jit(solution)/shard_map/ppermute | solution.py:42
  39.9 19.2 %collective-permute-start.10 = (bf16[128,1024]{1,0:T(8,128)(2,1)}, bf16[128,1024]{1,0:T(8,128)(2,1)S(1)}, u32[]{:S(2)}, u32[]{:S(2)}) collective-permute-start(bf16[128,1024]{1,0:T(8,128)(2,1)} %collective-permute-done.9), channel_id=1, source_target_pairs={{0,12},{4,0},{8,4},{12,8},{1,13},{5,1},{9,5},{13,9},{2,14},{6,2},{... | collective-permute-start | bytes 786440 | tf_op jit(solution)/shard_map/ppermute | solution.py:42
  47.1 14.5 %collective-permute-start.18 = (bf16[128,1024]{1,0:T(8,128)(2,1)}, bf16[128,1024]{1,0:T(8,128)(2,1)S(1)}, u32[]{:S(2)}, u32[]{:S(2)}) collective-permute-start(bf16[128,1024]{1,0:T(8,128)(2,1)} %collective-permute-done.9), channel_id=1, source_target_pairs={{0,16},{16,0},{1,17},{17,1},{2,18},{18,2},{3,19},{19,3},{4,20},{20... | collective-permute-start | bytes 786440 | tf_op jit(solution)/shard_map/ppermute | solution.py:47
  49.1 15.9 %collective-permute-start.2 = (bf16[128,1024]{1,0:T(8,128)(2,1)S(1)}, bf16[128,1024]{1,0:T(8,128)(2,1)S(1)}, u32[]{:S(2)}, u32[]{:S(2)}) collective-permute-start(bf16[128,1024]{1,0:T(8,128)(2,1)S(1)} %collective-permute-done.1), channel_id=1, source_target_pairs={{0,4},{4,8},{8,12},{12,0},{1,5},{5,9},{9,13},{13,1},{2,6},{6,10},{... | collective-permute-start | bytes 786440 | tf_op jit(solution)/shard_map/ppermute | solution.py:42
  49.1 21.3 %collective-permute-start.5 = (bf16[128,1024]{1,0:T(8,128)(2,1)S(1)}, bf16[128,1024]{1,0:T(8,128)(2,1)S(1)}, u32[]{:S(2)}, u32[]{:S(2)}) collective-permute-start(bf16[128,1024]{1,0:T(8,128)(2,1)S(1)} %collective-permute-done.4), channel_id=1, source_target_pairs={{0,12},{4,0},{8,4},{12,8},{1,13},{5,1},{9,5},{13,9},{2,14},{6,2},{... | collective-permute-start | bytes 786440 | tf_op jit(solution)/shard_map/ppermute | solution.py:42
  53.4 22.5 %collective-permute-start.8 = (bf16[128,1024]{1,0:T(8,128)(2,1)S(1)}, bf16[128,1024]{1,0:T(8,128)(2,1)S(1)}, u32[]{:S(2)}, u32[]{:S(2)}) collective-permute-start(bf16[128,1024]{1,0:T(8,128)(2,1)S(1)} %collective-permute-done.7), channel_id=1, source_target_pairs={{0,4},{4,8},{8,12},{12,0},{1,5},{5,9},{9,13},{13,1},{2,6},{6,10},{... | collective-permute-start | bytes 786440 | tf_op jit(solution)/shard_map/ppermute | solution.py:42
  59.2 19.7 %collective-permute-start.11 = (bf16[128,1024]{1,0:T(8,128)(2,1)S(1)}, bf16[128,1024]{1,0:T(8,128)(2,1)S(1)}, u32[]{:S(2)}, u32[]{:S(2)}) collective-permute-start(bf16[128,1024]{1,0:T(8,128)(2,1)S(1)} %collective-permute-done.10), channel_id=1, source_target_pairs={{0,12},{4,0},{8,4},{12,8},{1,13},{5,1},{9,5},{13,9},{2,14},{6,2},{... | collective-permute-start | bytes 786440 | tf_op jit(solution)/shard_map/ppermute | solution.py:42
  61.6 19.8 %collective-permute-start.19 = (bf16[128,1024]{1,0:T(8,128)(2,1)S(1)}, bf16[128,1024]{1,0:T(8,128)(2,1)S(1)}, u32[]{:S(2)}, u32[]{:S(2)}) collective-permute-start(bf16[128,1024]{1,0:T(8,128)(2,1)S(1)} %collective-permute-done.1), channel_id=1, source_target_pairs={{0,16},{16,0},{1,17},{17,1},{2,18},{18,2},{3,19},{19,3},{4,20},{20... | collective-permute-start | bytes 786440 | tf_op jit(solution)/shard_map/ppermute | solution.py:47
  64.9 18.9 %collective-permute-start.20 = (bf16[128,1024]{1,0:T(8,128)(2,1)S(1)}, bf16[128,1024]{1,0:T(8,128)(2,1)S(1)}, u32[]{:S(2)}, u32[]{:S(2)}) collective-permute-start(bf16[128,1024]{1,0:T(8,128)(2,1)S(1)} %collective-permute-done.4), channel_id=1, source_target_pairs={{0,16},{16,0},{1,17},{17,1},{2,18},{18,2},{3,19},{19,3},{4,20},{20... | collective-permute-start | bytes 786440 | tf_op jit(solution)/shard_map/ppermute | solution.py:47
  70.4 16.6 %collective-permute-start.21 = (bf16[128,1024]{1,0:T(8,128)(2,1)S(1)}, bf16[128,1024]{1,0:T(8,128)(2,1)S(1)}, u32[]{:S(2)}, u32[]{:S(2)}) collective-permute-start(bf16[128,1024]{1,0:T(8,128)(2,1)S(1)} %collective-permute-done.7), channel_id=1, source_target_pairs={{0,16},{16,0},{1,17},{17,1},{2,18},{18,2},{3,19},{19,3},{4,20},{20... | collective-permute-start | bytes 786440 | tf_op jit(solution)/shard_map/ppermute | solution.py:47
  75.9 14.0 %collective-permute-start.22 = (bf16[128,1024]{1,0:T(8,128)(2,1)S(1)}, bf16[128,1024]{1,0:T(8,128)(2,1)S(1)}, u32[]{:S(2)}, u32[]{:S(2)}) collective-permute-start(bf16[128,1024]{1,0:T(8,128)(2,1)S(1)} %collective-permute-done.10), channel_id=1, source_target_pairs={{0,16},{16,0},{1,17},{17,1},{2,18},{18,2},{3,19},{19,3},{4,20},{20... | collective-permute-start | bytes 786440 | tf_op jit(solution)/shard_map/ppermute | solution.py:47
  80.4 31.1 %collective-permute-start.14 = (bf16[8,384,128]{2,0,1:T(8,128)(2,1)S(1)}, bf16[8,384,128]{2,0,1:T(8,128)(2,1)S(1)}, u32[]{:S(2)}, u32[]{:S(2)}) collective-permute-start(bf16[8,384,128]{2,0,1:T(8,128)(2,1)S(1)} %pad_maximum_fusion.3), channel_id=1, source_target_pairs={{0,12},{4,0},{8,4},{12,8},{1,13},{5,1},{9,5},{13,9},{2,14},{6,2},{... | collective-permute-start | bytes 2359304 | tf_op jit(solution)/shard_map/ppermute | solution.py:69
  81.3 67.9 %collective-permute-start.13 = (bf16[8,384,128]{2,0,1:T(8,128)(2,1)S(1)}, bf16[8,384,128]{2,0,1:T(8,128)(2,1)S(1)}, u32[]{:S(2)}, u32[]{:S(2)}) collective-permute-start(bf16[8,384,128]{2,0,1:T(8,128)(2,1)S(1)} %pad_maximum_fusion.2), channel_id=1, source_target_pairs={{0,8},{4,12},{8,0},{12,4},{1,9},{5,13},{9,1},{13,5},{2,10},{6,14},... | collective-permute-start | bytes 2359304 | tf_op jit(solution)/shard_map/ppermute | solution.py:69
  83.8 66.6 %collective-permute-start.12 = (bf16[8,384,128]{2,0,1:T(8,128)(2,1)S(1)}, bf16[8,384,128]{2,0,1:T(8,128)(2,1)S(1)}, u32[]{:S(2)}, u32[]{:S(2)}) collective-permute-start(bf16[8,384,128]{2,0,1:T(8,128)(2,1)S(1)} %pad_maximum_fusion.1), channel_id=1, source_target_pairs={{0,4},{4,8},{8,12},{12,0},{1,5},{5,9},{9,13},{13,1},{2,6},{6,10},{... | collective-permute-start | bytes 2359304 | tf_op jit(solution)/shard_map/ppermute | solution.py:69
  89.9 11.9 %collective-permute-start.24 = (bf16[128,1024]{1,0:T(8,128)(2,1)S(1)}, bf16[128,1024]{1,0:T(8,128)(2,1)S(1)}, u32[]{:S(2)}, u32[]{:S(2)}) collective-permute-start(bf16[128,1024]{1,0:T(8,128)(2,1)S(1)} %collective-permute-done.5), channel_id=1, source_target_pairs={{0,16},{16,0},{1,17},{17,1},{2,18},{18,2},{3,19},{19,3},{4,20},{20... | collective-permute-start | bytes 786440 | tf_op jit(solution)/shard_map/ppermute | solution.py:47
  163.5 11.3 %all-to-all-start = ((bf16[4,96,512]{2,1,0:T(8,128)(2,1)}), bf16[4,96,512]{2,1,0:T(8,128)(2,1)S(1)}, u32[]{:S(2)}, u32[]{:S(2)}) async-start(bf16[4,96,512]{2,1,0:T(8,128)(2,1)} %bitcast.76), calls=%async_computation | async-start | bytes 786432 | tf_op jit(solution)/shard_map/all_to_all | solution.py:146
  168.8 11.3 %collective-permute-start.28 = (bf16[62,1024]{1,0:T(8,128)(2,1)S(1)}, bf16[62,1024]{1,0:T(8,128)(2,1)S(1)}, u32[]{:S(2)}, u32[]{:S(2)}) collective-permute-start(bf16[62,1024]{1,0:T(8,128)(2,1)S(1)} %copy-done.3), channel_id=1, source_target_pairs={{0,2},{1,3},{2,0},{3,1},{4,6},{5,7},{6,4},{7,5},{8,10},{9,11},{10,... | collective-permute-start | bytes 380936 | tf_op jit(solution)/shard_map/ppermute | solution.py:107
  (14 other events, 210.8 us)

commit v20 on v10

--- a/solution.py
+++ b/solution.py
@@ -55,7 +55,8 @@
     share = row_count // feat_count
     owner = lax.axis_index("feat")
     pieces, ids = [], []
-    for shift in range(feat_count):
+    order = sorted(range(feat_count), key=lambda shift: -min(shift, feat_count - shift))
+    for shift in order:
         target = (owner + shift) % feat_count
         piece = jnp.concatenate(
             [

time: 179 us -> 179 us (level)
  no operation moved by 1% of the time
where the time goes in v20:
time: 179 us
  waiting for transfers between devices  71.9 us (40%)
  local copies, waits for them, and re-layouts  42.2 us (24%)
  starting transfers between devices  41.8 us (23%)
  matrix products  17.7 us (10%)
  other arithmetic  4.66 us (3%)
    ppermute x3, waiting for transfers between devices, exchange_rows(): lax.ppermute(piece, 'feat', [(source, (source + shift) % feat_count) for...  36.5 us
    unnamed x37, local copies, waits for them, and re-layouts  22.5 us
    ppermute x12, waiting for transfers between devices, weight_parts(): rings[chunk] = lax.ppermute(rings[chunk], 'feat', ring)  17.3 us
    ppermute x12, starting transfers between devices, weight_parts(): forwarded = lax.ppermute(rings[chunk], 'groups', pairs)  17 us
    ppermute x12, starting transfers between devices, weight_parts(): rings[chunk] = lax.ppermute(rings[chunk], 'feat', ring)  16 us
    squeeze x1, local copies, waits for them, and re-layouts, on_device(): pooled_second[0]  12 us
    ppermute x12, waiting for transfers between devices, weight_parts(): forwarded = lax.ppermute(rings[chunk], 'groups', pairs)  10.3 us
    dot_general x1, matrix products, on_device(): jnp.dot(crossed, weights[:, 2 * rank:], preferred_element_type=jnp.float32)  7.28 us
  transfers between devices with their start and end apart: 31, of which 13 were waited for; matrix products, arithmetic and copies ran while one was open for 26% of the time, Pallas kernels for 0%

profile of v20, /device:TPU:0, one launch (start us, length us, event | category | flops | bytes accessed | tf_op | source)
XLA Modules:
  0.0 178.7 jit_solution(11021439870377466674)
XLA Ops:
  0.0 3.2 %pad_maximum_fusion = (bf16[1024,1024]{1,0:T(8,128)(2,1)S(1)}, bf16[4096,1024]{1,0:T(8,128)(2,1)}) fusion(bf16[1024,512]{1,0:T(8,128)(2,1)} %bitcast.138, bf16[1024,256]{1,0:T(8,128)(2,1)} %bitcast.139, bf16[1024,256]{1,0:T(8,128)(2,1)} %bitcast.140), kind=kLoop, calls=%fused_computation.16 | loop fusion | flops 6291455 | bytes 6291456 | tf_op jit(solution)/shard_map/concatenate | solution.py:109
  4.1 3.0 %collective-permute-start = (bf16[128,1024]{1,0:T(8,128)(2,1)}, bf16[128,1024]{1,0:T(8,128)(2,1)}, u32[]{:S(2)}, u32[]{:S(2)}) collective-permute-start(bf16[128,1024]{1,0:T(8,128)(2,1)} %get-tuple-element.11), channel_id=1, source_target_pairs={{0,4},{4,8},{8,12},{12,0},{1,5},{5,9},{9,13},{13,1},{2,6},{6,10},{... | collective-permute-start | bytes 786440 | tf_op jit(solution)/shard_map/ppermute | solution.py:41
  10.7 12.0 %copy_bitcast_fusion = (bf16[4,1536,128]{2,0,1:T(4,128)(2,1)S(1)}, bf16[4,1536,128]{2,0,1:T(4,128)(2,1)S(1)}) fusion(bf16[1,4,1536,128]{3,2,1,0:T(8,128)(2,1)} %param.14, bf16[1,4,1536,128]{3,2,1,0:T(8,128)(2,1)} %param.13), kind=kLoop, calls=%fused_computation.17 | loop fusion | bytes 6291456 | tf_op jit(solution)/shard_map/squeeze | solution.py:113
  22.8 1.8 collective-permute-start.15
  28.2 1.8 %collective-permute-start.1 = (bf16[128,1024]{1,0:T(8,128)(2,1)}, bf16[128,1024]{1,0:T(8,128)(2,1)S(1)}, u32[]{:S(2)}, u32[]{:S(2)}) collective-permute-start(bf16[128,1024]{1,0:T(8,128)(2,1)} %collective-permute-done), channel_id=1, source_target_pairs={{0,4},{4,8},{8,12},{12,0},{1,5},{5,9},{9,13},{13,1},{2,6},{6,10},{... | collective-permute-start | bytes 786440 | tf_op jit(solution)/shard_map/ppermute | solution.py:41
  30.0 1.7 constant_dynamic-update-slice_fusion.23
  44.3 1.7 constant_dynamic-update-slice_fusion.19
  46.0 1.9 %collective-permute-start.2 = (bf16[128,1024]{1,0:T(8,128)(2,1)S(1)}, bf16[128,1024]{1,0:T(8,128)(2,1)S(1)}, u32[]{:S(2)}, u32[]{:S(2)}) collective-permute-start(bf16[128,1024]{1,0:T(8,128)(2,1)S(1)} %collective-permute-done.1), channel_id=1, source_target_pairs={{0,4},{4,8},{8,12},{12,0},{1,5},{5,9},{9,13},{13,1},{2,6},{6,10},{... | collective-permute-start | bytes 786440 | tf_op jit(solution)/shard_map/ppermute | solution.py:41
  50.8 5.6 %collective-permute-done.10 = bf16[128,1024]{1,0:T(8,128)(2,1)S(1)} collective-permute-done((bf16[128,1024]{1,0:T(8,128)(2,1)}, bf16[128,1024]{1,0:T(8,128)(2,1)S(1)}, u32[]{:S(2)}, u32[]{:S(2)}) %collective-permute-start.10) | collective-permute-done | bytes 262176 | tf_op jit(solution)/shard_map/ppermute | solution.py:41
  63.7 3.9 %collective-permute-done.5 = bf16[128,1024]{1,0:T(8,128)(2,1)S(1)} collective-permute-done((bf16[128,1024]{1,0:T(8,128)(2,1)S(1)}, bf16[128,1024]{1,0:T(8,128)(2,1)S(1)}, u32[]{:S(2)}, u32[]{:S(2)}) %collective-permute-start.5) | collective-permute-done | bytes 262176 | tf_op jit(solution)/shard_map/ppermute | solution.py:41
  69.3 3.9 %collective-permute-done.8 = bf16[128,1024]{1,0:T(8,128)(2,1)S(1)} collective-permute-done((bf16[128,1024]{1,0:T(8,128)(2,1)S(1)}, bf16[128,1024]{1,0:T(8,128)(2,1)S(1)}, u32[]{:S(2)}, u32[]{:S(2)}) %collective-permute-start.8) | collective-permute-done | bytes 262176 | tf_op jit(solution)/shard_map/ppermute | solution.py:41
  74.9 2.5 %collective-permute-done.11 = bf16[128,1024]{1,0:T(8,128)(2,1)S(1)} collective-permute-done((bf16[128,1024]{1,0:T(8,128)(2,1)S(1)}, bf16[128,1024]{1,0:T(8,128)(2,1)S(1)}, u32[]{:S(2)}, u32[]{:S(2)}) %collective-permute-start.11) | collective-permute-done | bytes 262176 | tf_op jit(solution)/shard_map/ppermute | solution.py:41
  79.0 1.8 %collective-permute-start.14 = (bf16[8,384,128]{2,0,1:T(8,128)(2,1)S(1)}, bf16[8,384,128]{2,0,1:T(8,128)(2,1)S(1)}, u32[]{:S(2)}, u32[]{:S(2)}) collective-permute-start(bf16[8,384,128]{2,0,1:T(8,128)(2,1)S(1)} %pad_maximum_fusion.3), channel_id=1, source_target_pairs={{0,12},{4,0},{8,4},{12,8},{1,13},{5,1},{9,5},{13,9},{2,14},{6,2},{... | collective-permute-start | bytes 2359304 | tf_op jit(solution)/shard_map/ppermute | solution.py:69
  90.6 4.3 %collective-permute-done.23 = bf16[128,1024]{1,0:T(8,128)(2,1)S(1)} collective-permute-done((bf16[128,1024]{1,0:T(8,128)(2,1)S(1)}, bf16[128,1024]{1,0:T(8,128)(2,1)S(1)}, u32[]{:S(2)}, u32[]{:S(2)}) %collective-permute-start.23) | collective-permute-done | bytes 262176 | tf_op jit(solution)/shard_map/ppermute | solution.py:46
  97.9 2.6 %collective-permute-done.24 = bf16[128,1024]{1,0:T(8,128)(2,1)S(1)} collective-permute-done((bf16[128,1024]{1,0:T(8,128)(2,1)S(1)}, bf16[128,1024]{1,0:T(8,128)(2,1)S(1)}, u32[]{:S(2)}, u32[]{:S(2)}) %collective-permute-start.24) | collective-permute-done | bytes 262176 | tf_op jit(solution)/shard_map/ppermute | solution.py:46
  103.5 2.1 %collective-permute-done.25 = bf16[128,1024]{1,0:T(8,128)(2,1)S(1)} collective-permute-done((bf16[128,1024]{1,0:T(8,128)(2,1)S(1)}, bf16[128,1024]{1,0:T(8,128)(2,1)S(1)}, u32[]{:S(2)}, u32[]{:S(2)}) %collective-permute-start.25) | collective-permute-done | bytes 262176 | tf_op jit(solution)/shard_map/ppermute | solution.py:46
  110.2 36.5 %collective-permute-done.12 = bf16[8,384,128]{2,0,1:T(8,128)(2,1)S(1)} collective-permute-done((bf16[8,384,128]{2,0,1:T(8,128)(2,1)S(1)}, bf16[8,384,128]{2,0,1:T(8,128)(2,1)S(1)}, u32[]{:S(2)}, u32[]{:S(2)}) %collective-permute-start.12) | collective-permute-done | bytes 786464 | tf_op jit(solution)/shard_map/ppermute | solution.py:69
  148.9 1.8 add_convert_fusion
  150.6 3.4 %fusion.24 = bf16[384,256]{1,0:T(8,128)(2,1)} fusion(bf16[4096,1024]{1,0:T(8,128)(2,1)} %constant_dynamic-update-slice_fusion, bf16[48,8,32,128]{3,2,1,0:T(8,128)(2,1)S(1)} %bitcast.134), kind=kOutput, calls=%fused_computation.28 | convolution fusion | flops 805404672 | bytes 5439488 | tf_op jit(solution)/shard_map/dot_general | solution.py:133
  154.0 7.3 %fusion.15 = bf16[384,512]{1,0:T(8,128)(2,1)} fusion(bf16[4096,1024]{1,0:T(8,128)(2,1)} %constant_dynamic-update-slice_fusion, bf16[384,256]{1,0:T(8,128)(2,1)} %fusion.24, f32[4096]{0:T(1024)S(1)} %bitcast.143, bf16[48,8,32,128]{3,2,1,0:T(8,128)(2,1)S(1)} %bitcast.135, f32[512]{0:T(512)S(1)} %bitcast.144), kind=kOutput, calls=%fused_computation.21 | convolution fusion | flops 2424176640 | bytes 10045440 | tf_op jit(solution)/shard_map/dot_general | solution.py:144
  161.3 3.5 %all-to-all-start = ((bf16[4,96,512]{2,1,0:T(8,128)(2,1)}), bf16[4,96,512]{2,1,0:T(8,128)(2,1)S(1)}, u32[]{:S(2)}, u32[]{:S(2)}) async-start(bf16[4,96,512]{2,1,0:T(8,128)(2,1)} %bitcast.141), calls=%async_computation | async-start | bytes 786432 | tf_op jit(solution)/shard_map/all_to_all | solution.py:146
  164.8 1.7 collective-permute-start.29
  167.3 5.4 %all-to-all-done = bf16[4,96,512]{2,1,0:T(8,128)(2,1)S(1)} async-done(((bf16[4,96,512]{2,1,0:T(8,128)(2,1)}), bf16[4,96,512]{2,1,0:T(8,128)(2,1)S(1)}, u32[]{:S(2)}, u32[]{:S(2)}) %all-to-all-start) | async-done | bytes 393248 | tf_op jit(solution)/shard_map/all_to_all | solution.py:146
  175.4 2.3 %collective-permute-done.28 = bf16[62,1024]{1,0:T(8,128)(2,1)S(1)} collective-permute-done((bf16[62,1024]{1,0:T(8,128)(2,1)S(1)}, bf16[62,1024]{1,0:T(8,128)(2,1)S(1)}, u32[]{:S(2)}, u32[]{:S(2)}) %collective-permute-start.28) | collective-permute-done | bytes 127008 | tf_op jit(solution)/shard_map/ppermute | solution.py:107
  (125 shorter events, 62.7 us)
Async XLA Ops:
  4.1 18.6 %collective-permute-start = (bf16[128,1024]{1,0:T(8,128)(2,1)}, bf16[128,1024]{1,0:T(8,128)(2,1)}, u32[]{:S(2)}, u32[]{:S(2)}) collective-permute-start(bf16[128,1024]{1,0:T(8,128)(2,1)} %get-tuple-element.11), channel_id=1, source_target_pairs={{0,4},{4,8},{8,12},{12,0},{1,5},{5,9},{9,13},{13,1},{2,6},{6,10},{... | collective-permute-start | bytes 786440 | tf_op jit(solution)/shard_map/ppermute | solution.py:41
  7.1 17.4 %collective-permute-start.3 = (bf16[128,1024]{1,0:T(8,128)(2,1)}, bf16[128,1024]{1,0:T(8,128)(2,1)}, u32[]{:S(2)}, u32[]{:S(2)}) collective-permute-start(bf16[128,1024]{1,0:T(8,128)(2,1)} %get-tuple-element.10), channel_id=1, source_target_pairs={{0,4},{4,8},{8,12},{12,0},{1,5},{5,9},{9,13},{13,1},{2,6},{6,10},{... | collective-permute-start | bytes 786440 | tf_op jit(solution)/shard_map/ppermute | solution.py:41
  8.7 23.0 %collective-permute-start.6 = (bf16[128,1024]{1,0:T(8,128)(2,1)}, bf16[128,1024]{1,0:T(8,128)(2,1)}, u32[]{:S(2)}, u32[]{:S(2)}) collective-permute-start(bf16[128,1024]{1,0:T(8,128)(2,1)} %get-tuple-element.12), channel_id=1, source_target_pairs={{0,4},{4,8},{8,12},{12,0},{1,5},{5,9},{9,13},{13,1},{2,6},{6,10},{... | collective-permute-start | bytes 786440 | tf_op jit(solution)/shard_map/ppermute | solution.py:41
  10.3 26.2 %collective-permute-start.9 = (bf16[128,1024]{1,0:T(8,128)(2,1)S(1)}, bf16[128,1024]{1,0:T(8,128)(2,1)}, u32[]{:S(2)}, u32[]{:S(2)}) collective-permute-start(bf16[128,1024]{1,0:T(8,128)(2,1)S(1)} %get-tuple-element.9), channel_id=1, source_target_pairs={{0,4},{4,8},{8,12},{12,0},{1,5},{5,9},{9,13},{13,1},{2,6},{6,10},{... | collective-permute-start | bytes 786440 | tf_op jit(solution)/shard_map/ppermute | solution.py:41
  24.5 13.6 %collective-permute-start.16 = (bf16[128,1024]{1,0:T(8,128)(2,1)}, bf16[128,1024]{1,0:T(8,128)(2,1)}, u32[]{:S(2)}, u32[]{:S(2)}) collective-permute-start(bf16[128,1024]{1,0:T(8,128)(2,1)} %collective-permute-done.3), channel_id=1, source_target_pairs={{0,16},{16,0},{1,17},{17,1},{2,18},{18,2},{3,19},{19,3},{4,20},{20... | collective-permute-start | bytes 786440 | tf_op jit(solution)/shard_map/ppermute | solution.py:46
  28.2 17.7 %collective-permute-start.1 = (bf16[128,1024]{1,0:T(8,128)(2,1)}, bf16[128,1024]{1,0:T(8,128)(2,1)S(1)}, u32[]{:S(2)}, u32[]{:S(2)}) collective-permute-start(bf16[128,1024]{1,0:T(8,128)(2,1)} %collective-permute-done), channel_id=1, source_target_pairs={{0,4},{4,8},{8,12},{12,0},{1,5},{5,9},{9,13},{13,1},{2,6},{6,10},{... | collective-permute-start | bytes 786440 | tf_op jit(solution)/shard_map/ppermute | solution.py:41
  31.8 16.2 %collective-permute-start.4 = (bf16[128,1024]{1,0:T(8,128)(2,1)}, bf16[128,1024]{1,0:T(8,128)(2,1)S(1)}, u32[]{:S(2)}, u32[]{:S(2)}) collective-permute-start(bf16[128,1024]{1,0:T(8,128)(2,1)} %collective-permute-done.3), channel_id=1, source_target_pairs={{0,4},{4,8},{8,12},{12,0},{1,5},{5,9},{9,13},{13,1},{2,6},{6,10},{... | collective-permute-start | bytes 786440 | tf_op jit(solution)/shard_map/ppermute | solution.py:41
  36.5 14.2 %collective-permute-start.7 = (bf16[128,1024]{1,0:T(8,128)(2,1)}, bf16[128,1024]{1,0:T(8,128)(2,1)S(1)}, u32[]{:S(2)}, u32[]{:S(2)}) collective-permute-start(bf16[128,1024]{1,0:T(8,128)(2,1)} %collective-permute-done.6), channel_id=1, source_target_pairs={{0,4},{4,8},{8,12},{12,0},{1,5},{5,9},{9,13},{13,1},{2,6},{6,10},{... | collective-permute-start | bytes 786440 | tf_op jit(solution)/shard_map/ppermute | solution.py:41
  38.1 18.3 %collective-permute-start.10 = (bf16[128,1024]{1,0:T(8,128)(2,1)}, bf16[128,1024]{1,0:T(8,128)(2,1)S(1)}, u32[]{:S(2)}, u32[]{:S(2)}) collective-permute-start(bf16[128,1024]{1,0:T(8,128)(2,1)} %collective-permute-done.9), channel_id=1, source_target_pairs={{0,4},{4,8},{8,12},{12,0},{1,5},{5,9},{9,13},{13,1},{2,6},{6,10},{... | collective-permute-start | bytes 786440 | tf_op jit(solution)/shard_map/ppermute | solution.py:41
  42.7 16.1 %collective-permute-start.18 = (bf16[128,1024]{1,0:T(8,128)(2,1)}, bf16[128,1024]{1,0:T(8,128)(2,1)S(1)}, u32[]{:S(2)}, u32[]{:S(2)}) collective-permute-start(bf16[128,1024]{1,0:T(8,128)(2,1)} %collective-permute-done.9), channel_id=1, source_target_pairs={{0,16},{16,0},{1,17},{17,1},{2,18},{18,2},{3,19},{19,3},{4,20},{20... | collective-permute-start | bytes 786440 | tf_op jit(solution)/shard_map/ppermute | solution.py:46
  46.0 16.1 %collective-permute-start.2 = (bf16[128,1024]{1,0:T(8,128)(2,1)S(1)}, bf16[128,1024]{1,0:T(8,128)(2,1)S(1)}, u32[]{:S(2)}, u32[]{:S(2)}) collective-permute-start(bf16[128,1024]{1,0:T(8,128)(2,1)S(1)} %collective-permute-done.1), channel_id=1, source_target_pairs={{0,4},{4,8},{8,12},{12,0},{1,5},{5,9},{9,13},{13,1},{2,6},{6,10},{... | collective-permute-start | bytes 786440 | tf_op jit(solution)/shard_map/ppermute | solution.py:41
  47.9 19.7 %collective-permute-start.5 = (bf16[128,1024]{1,0:T(8,128)(2,1)S(1)}, bf16[128,1024]{1,0:T(8,128)(2,1)S(1)}, u32[]{:S(2)}, u32[]{:S(2)}) collective-permute-start(bf16[128,1024]{1,0:T(8,128)(2,1)S(1)} %collective-permute-done.4), channel_id=1, source_target_pairs={{0,4},{4,8},{8,12},{12,0},{1,5},{5,9},{9,13},{13,1},{2,6},{6,10},{... | collective-permute-start | bytes 786440 | tf_op jit(solution)/shard_map/ppermute | solution.py:41
  50.8 22.5 %collective-permute-start.8 = (bf16[128,1024]{1,0:T(8,128)(2,1)S(1)}, bf16[128,1024]{1,0:T(8,128)(2,1)S(1)}, u32[]{:S(2)}, u32[]{:S(2)}) collective-permute-start(bf16[128,1024]{1,0:T(8,128)(2,1)S(1)} %collective-permute-done.7), channel_id=1, source_target_pairs={{0,4},{4,8},{8,12},{12,0},{1,5},{5,9},{9,13},{13,1},{2,6},{6,10},{... | collective-permute-start | bytes 786440 | tf_op jit(solution)/shard_map/ppermute | solution.py:41
  56.4 21.1 %collective-permute-start.11 = (bf16[128,1024]{1,0:T(8,128)(2,1)S(1)}, bf16[128,1024]{1,0:T(8,128)(2,1)S(1)}, u32[]{:S(2)}, u32[]{:S(2)}) collective-permute-start(bf16[128,1024]{1,0:T(8,128)(2,1)S(1)} %collective-permute-done.10), channel_id=1, source_target_pairs={{0,4},{4,8},{8,12},{12,0},{1,5},{5,9},{9,13},{13,1},{2,6},{6,10},{... | collective-permute-start | bytes 786440 | tf_op jit(solution)/shard_map/ppermute | solution.py:41
  58.8 22.4 %collective-permute-start.19 = (bf16[128,1024]{1,0:T(8,128)(2,1)S(1)}, bf16[128,1024]{1,0:T(8,128)(2,1)S(1)}, u32[]{:S(2)}, u32[]{:S(2)}) collective-permute-start(bf16[128,1024]{1,0:T(8,128)(2,1)S(1)} %collective-permute-done.1), channel_id=1, source_target_pairs={{0,16},{16,0},{1,17},{17,1},{2,18},{18,2},{3,19},{19,3},{4,20},{20... | collective-permute-start | bytes 786440 | tf_op jit(solution)/shard_map/ppermute | solution.py:46
  62.0 21.2 %collective-permute-start.20 = (bf16[128,1024]{1,0:T(8,128)(2,1)S(1)}, bf16[128,1024]{1,0:T(8,128)(2,1)S(1)}, u32[]{:S(2)}, u32[]{:S(2)}) collective-permute-start(bf16[128,1024]{1,0:T(8,128)(2,1)S(1)} %collective-permute-done.4), channel_id=1, source_target_pairs={{0,16},{16,0},{1,17},{17,1},{2,18},{18,2},{3,19},{19,3},{4,20},{20... | collective-permute-start | bytes 786440 | tf_op jit(solution)/shard_map/ppermute | solution.py:46
  67.6 18.0 %collective-permute-start.21 = (bf16[128,1024]{1,0:T(8,128)(2,1)S(1)}, bf16[128,1024]{1,0:T(8,128)(2,1)S(1)}, u32[]{:S(2)}, u32[]{:S(2)}) collective-permute-start(bf16[128,1024]{1,0:T(8,128)(2,1)S(1)} %collective-permute-done.7), channel_id=1, source_target_pairs={{0,16},{16,0},{1,17},{17,1},{2,18},{18,2},{3,19},{19,3},{4,20},{20... | collective-permute-start | bytes 786440 | tf_op jit(solution)/shard_map/ppermute | solution.py:46
  73.2 15.4 %collective-permute-start.22 = (bf16[128,1024]{1,0:T(8,128)(2,1)S(1)}, bf16[128,1024]{1,0:T(8,128)(2,1)S(1)}, u32[]{:S(2)}, u32[]{:S(2)}) collective-permute-start(bf16[128,1024]{1,0:T(8,128)(2,1)S(1)} %collective-permute-done.10), channel_id=1, source_target_pairs={{0,16},{16,0},{1,17},{17,1},{2,18},{18,2},{3,19},{19,3},{4,20},{20... | collective-permute-start | bytes 786440 | tf_op jit(solution)/shard_map/ppermute | solution.py:46
  79.0 30.1 %collective-permute-start.14 = (bf16[8,384,128]{2,0,1:T(8,128)(2,1)S(1)}, bf16[8,384,128]{2,0,1:T(8,128)(2,1)S(1)}, u32[]{:S(2)}, u32[]{:S(2)}) collective-permute-start(bf16[8,384,128]{2,0,1:T(8,128)(2,1)S(1)} %pad_maximum_fusion.3), channel_id=1, source_target_pairs={{0,12},{4,0},{8,4},{12,8},{1,13},{5,1},{9,5},{13,9},{2,14},{6,2},{... | collective-permute-start | bytes 2359304 | tf_op jit(solution)/shard_map/ppermute | solution.py:69
  81.2 65.5 %collective-permute-start.12 = (bf16[8,384,128]{2,0,1:T(8,128)(2,1)S(1)}, bf16[8,384,128]{2,0,1:T(8,128)(2,1)S(1)}, u32[]{:S(2)}, u32[]{:S(2)}) collective-permute-start(bf16[8,384,128]{2,0,1:T(8,128)(2,1)S(1)} %pad_maximum_fusion.1), channel_id=1, source_target_pairs={{0,8},{4,12},{8,0},{12,4},{1,9},{5,13},{9,1},{13,5},{2,10},{6,14},... | collective-permute-start | bytes 2359304 | tf_op jit(solution)/shard_map/ppermute | solution.py:69
  83.2 64.6 %collective-permute-start.13 = (bf16[8,384,128]{2,0,1:T(8,128)(2,1)S(1)}, bf16[8,384,128]{2,0,1:T(8,128)(2,1)S(1)}, u32[]{:S(2)}, u32[]{:S(2)}) collective-permute-start(bf16[8,384,128]{2,0,1:T(8,128)(2,1)S(1)} %pad_maximum_fusion.2), channel_id=1, source_target_pairs={{0,4},{4,8},{8,12},{12,0},{1,5},{5,9},{9,13},{13,1},{2,6},{6,10},{... | collective-permute-start | bytes 2359304 | tf_op jit(solution)/shard_map/ppermute | solution.py:69
  88.6 11.9 %collective-permute-start.24 = (bf16[128,1024]{1,0:T(8,128)(2,1)S(1)}, bf16[128,1024]{1,0:T(8,128)(2,1)S(1)}, u32[]{:S(2)}, u32[]{:S(2)}) collective-permute-start(bf16[128,1024]{1,0:T(8,128)(2,1)S(1)} %collective-permute-done.5), channel_id=1, source_target_pairs={{0,16},{16,0},{1,17},{17,1},{2,18},{18,2},{3,19},{19,3},{4,20},{20... | collective-permute-start | bytes 786440 | tf_op jit(solution)/shard_map/ppermute | solution.py:46
  161.3 11.3 %all-to-all-start = ((bf16[4,96,512]{2,1,0:T(8,128)(2,1)}), bf16[4,96,512]{2,1,0:T(8,128)(2,1)S(1)}, u32[]{:S(2)}, u32[]{:S(2)}) async-start(bf16[4,96,512]{2,1,0:T(8,128)(2,1)} %bitcast.141), calls=%async_computation | async-start | bytes 786432 | tf_op jit(solution)/shard_map/all_to_all | solution.py:146
  166.5 11.3 %collective-permute-start.28 = (bf16[62,1024]{1,0:T(8,128)(2,1)S(1)}, bf16[62,1024]{1,0:T(8,128)(2,1)S(1)}, u32[]{:S(2)}, u32[]{:S(2)}) collective-permute-start(bf16[62,1024]{1,0:T(8,128)(2,1)S(1)} %copy-done.3), channel_id=1, source_target_pairs={{0,2},{1,3},{2,0},{3,1},{4,6},{5,7},{6,4},{7,5},{8,10},{9,11},{10,... | collective-permute-start | bytes 380936 | tf_op jit(solution)/shard_map/ppermute | solution.py:107
  (14 other events, 200.2 us)
